TPU v7x, 512 devices: a whole 4x4x16 slice. The times are simulated.
512 devices in a mesh: req: 128 (over x, z, core), mlp: 4 (over y).
Axes of the slice: x: 4, y: 4, z: 16, core: 2. Of those that a mesh axis runs over, the one named last changes fastest.
Arguments:
- queries: bfloat16 [32768, 8, 256], P('req', 'mlp'), may hold values from -7 to 7
- new_kv: bfloat16 [32768, 8, 512], P('req', 'mlp'), may hold values from -6 to 6
- cache_pool: bfloat16 [768, 128, 8, 512], P('req', None, 'mlp'), may hold values from -6 to 6
- page_table: int32 [128, 6], P('req'), may hold values from 0 to 5, each once within a row
- assignment: int32 [128], P('req'), may hold values from 0 to 127, each once
- lengths: int32 [128], replicated, may hold values from 1 to 768, 24576 in all
- lambda_vectors: float32 [4, 128], replicated, may hold values from -0.4 to 0.4
- subln_gain: float32 [256], replicated, may hold values from 0.5 to 1.5
- residual: bfloat16 [32768, 2048], P('req', 'mlp'), may hold values from -70 to 70
- out_weight: bfloat16 [2048, 2048], P('req', 'mlp'), may hold values from -0.125 to 0.125
- norm_gain: float32 [2048], replicated, may hold values from 0.5 to 1.5
- gate_weight: bfloat16 [2048, 3072], P('req', 'mlp'), may hold values from -0.125 to 0.125
- up_weight: bfloat16 [2048, 3072], P('req', 'mlp'), may hold values from -0.125 to 0.125
- down_weight_t: bfloat16 [2048, 3072], P('req', 'mlp'), may hold values from -0.109375 to 0.109375
Outputs:
- layer_out: bfloat16 [32768, 2048], P('req', 'mlp')
Inputs may be any that keep to these rules, and one draw needn't show every extreme that they name: `page_table`: row g lists the cache pages of slot g in logical order as offsets from page g * 6; each offset once in a row. `assignment`: every request is served by exactly one slot. `lengths`: indexed by request; some request has exactly 768 cached tokens.
All inputs are finite; a program needn't handle non-finite values.
Results may differ from a plain program's by a relative error of at most 0.011.
Values may be sent and summed in bfloat16 or wider, within the bound.
No kernel may reach another device: no remote copies, remote signals or barrier semaphores. Data moves between devices by JAX's collectives and lax.ppermute only.
A program may use at most 64 MiB of HBM per device.

v0:
```python
import jax
import jax.numpy as jnp
from jax import lax
from jax.sharding import PartitionSpec as P

D = 2048


NEG_FILL = -1e30
LAMBDA_BASE = 0.2


def map_block(carried, query_rows, key_half, value_rows, visible, score_scale):
    running_max, running_sum, running_acc = carried
    score = (
        jnp.einsum("nhd,khd->nhk", query_rows, key_half, preferred_element_type=jnp.float32)
        * score_scale
    )
    score = jnp.where(visible[:, None, :], score, NEG_FILL)
    newest = jnp.maximum(running_max, jnp.max(score, axis=2))
    exp_terms = jnp.where(visible[:, None, :], jnp.exp(score - newest[:, :, None]), 0.0)
    shrink = jnp.exp(running_max - newest)
    running_sum = running_sum * shrink + jnp.sum(exp_terms, axis=2)
    running_acc = running_acc * shrink[:, :, None] + jnp.einsum(
        "nhk,khd->nhd",
        exp_terms.astype(jnp.bfloat16),
        value_rows,
        preferred_element_type=jnp.float32,
    )
    return (newest, running_sum, running_acc)


def both_maps(carried, query_rows, key_rows, visible, half_size):
    score_scale = half_size ** (-0.5)
    value_rows = key_rows[:, :, 2 * half_size :]
    map_one = map_block(
        carried[0],
        query_rows[:, :, :half_size],
        key_rows[:, :, :half_size],
        value_rows,
        visible,
        score_scale,
    )
    map_two = map_block(
        carried[1],
        query_rows[:, :, half_size:],
        key_rows[:, :, half_size : 2 * half_size],
        value_rows,
        visible,
        score_scale,
    )
    return (map_one, map_two)


def attend(
    queries, new_kv, cache_pool, page_table, assignment, lengths, lambda_vectors, subln_gain
):
    row_count, head_count, value_width = queries.shape
    half_size = value_width // 2
    page_len = cache_pool.shape[1]
    request = assignment[0]
    cached = jnp.sum(
        jnp.where(jnp.arange(lengths.shape[0], dtype=jnp.int32) == request, lengths, 0)
    )

    def fresh_state():
        return (
            jnp.full((row_count, head_count), NEG_FILL, jnp.float32),
            jnp.zeros((row_count, head_count), jnp.float32),
            jnp.zeros((row_count, head_count, value_width), jnp.float32),
        )

    table_row = page_table[0]

    def page_step(page_index, carried):
        physical = table_row[page_index]
        page_rows = lax.dynamic_index_in_dim(cache_pool, physical, 0, keepdims=False)
        positions = page_index * page_len + jnp.arange(page_len, dtype=jnp.int32)
        visible = jnp.broadcast_to((positions < cached)[None, :], (row_count, page_len))
        return both_maps(carried, queries, page_rows, visible, half_size)

    page_count = (cached + page_len - 1) // page_len
    carried = lax.fori_loop(jnp.int32(0), page_count, page_step, (fresh_state(), fresh_state()))
    token_pos = jnp.arange(row_count, dtype=jnp.int32)
    carried = both_maps(
        carried, queries, new_kv, token_pos[None, :] <= token_pos[:, None], half_size
    )
    lambda_now = (
        jnp.exp(jnp.sum(lambda_vectors[0] * lambda_vectors[1]))
        - jnp.exp(jnp.sum(lambda_vectors[2] * lambda_vectors[3]))
        + LAMBDA_BASE
    )
    mix_out = (
        carried[0][2] / carried[0][1][:, :, None]
        - lambda_now * carried[1][2] / carried[1][1][:, :, None]
    )
    mix_out = (
        mix_out
        * lax.rsqrt(jnp.mean(mix_out * mix_out, axis=2, keepdims=True) + 1e-05)
        * subln_gain
        * (1.0 - LAMBDA_BASE)
    )
    return mix_out.astype(jnp.bfloat16).reshape(row_count, head_count * value_width)


def per_device(
    queries,
    new_kv,
    cache_pool,
    page_table,
    assignment,
    lengths,
    lambda_vectors,
    subln_gain,
    residual,
    out_weight,
    norm_gain,
    gate_weight,
    up_weight,
    down_weight_t,
):
    attn_out = attend(
        queries, new_kv, cache_pool, page_table, assignment, lengths, lambda_vectors, subln_gain
    )
    heads_all = lax.all_gather(attn_out, "mlp", axis=1, tiled=True)
    columns = heads_all
    projected = jnp.dot(
        columns,
        lax.all_gather(out_weight, "req", axis=0, tiled=True),
        preferred_element_type=jnp.float32,
    )
    stream = (residual.astype(jnp.float32) + projected).astype(jnp.bfloat16)
    stream_f = stream.astype(jnp.float32)
    squares = lax.psum(jnp.sum(stream_f * stream_f, axis=1), "mlp")
    slice_width = stream_f.shape[1]
    local_gain = lax.dynamic_slice_in_dim(
        norm_gain, lax.axis_index("mlp") * slice_width, slice_width
    )
    normed_part = (stream_f * lax.rsqrt(squares / D + 1e-05)[:, None] * local_gain).astype(
        jnp.bfloat16
    )
    normed = lax.all_gather(normed_part, "mlp", axis=1, tiled=True)
    columns = normed
    gate_value = jnp.dot(
        columns,
        lax.all_gather(gate_weight, "req", axis=0, tiled=True),
        preferred_element_type=jnp.float32,
    )
    up_value = jnp.dot(
        columns,
        lax.all_gather(up_weight, "req", axis=0, tiled=True),
        preferred_element_type=jnp.float32,
    )
    hidden_act = (jax.nn.silu(gate_value) * up_value).astype(jnp.bfloat16)
    partial_value = lax.dot_general(
        hidden_act,
        lax.all_gather(down_weight_t, "req", axis=0, tiled=True),
        (((1,), (1,)), ((), ())),
        preferred_element_type=jnp.float32,
    )
    summed = lax.psum_scatter(
        partial_value.astype(jnp.bfloat16), "mlp", scatter_dimension=1, tiled=True
    ).astype(jnp.float32)
    return (stream_f + summed).astype(jnp.bfloat16)


def solution(mesh):
    in_specs = (
        P("req", "mlp", None),
        P("req", "mlp", None),
        P("req", None, "mlp", None),
        P("req", None),
        P("req"),
        P(),
        P(),
        P(),
        P("req", "mlp"),
        P("req", "mlp"),
        P(),
        P("req", "mlp"),
        P("req", "mlp"),
        P("req", "mlp"),
    )
    out_specs = P("req", "mlp")
    return jax.shard_map(
        per_device, mesh=mesh, in_specs=in_specs, out_specs=out_specs, check_vma=False
    )
```

profile of v0, /device:TPU:1, one launch (start us, length us, event | category | flops | bytes accessed | tf_op | source)
XLA Modules:
  0.0 740.7 jit_solution(16968464529783752565)
XLA Ops:
  7.2 1.4 fusion.56
  9.3 1.2 fusion.62
  10.5 1.0 copy.20
  11.6 6.5 while.20
  11.6 1.3 dynamic_slice.15
  14.9 1.1 constant_dynamic-slice_fusion.2
  16.0 0.7 add_compare_fusion.2
  17.3 0.4 fusion.92
  17.7 0.4 fusion.91
  18.2 0.2 fusion.63
  18.7 0.7 multiply_reduce_fusion.2
  21.3 0.3 fusion.36
  21.6 0.3 multiply_reduce_fusion.1
  21.9 0.8 multiply_convert_fusion.1
  22.8 0.7 all-gather.9.cloned.1.call-update
  23.6 0.8 dynamic_slice.10
  24.3 66.4 %all-gather.7.cloned.1.call-done = bf16[256,2048]{0,1:T(8,128)(2,1)} async-done(((bf16[256,512]{0,1:T(8,128)(2,1)}), bf16[256,2048]{0,1:T(8,128)(2,1)}) %all-gather.7.cloned.1.call-update) | async-done | bytes 1048592 | tf_op jit(solution)/shard_map/all_gather | solution.py:125
  90.7 144.7 %all-gather.9.cloned.1.call-done = bf16[2048,512]{1,0:T(8,128)(2,1)} async-done(((bf16[16,512]{1,0:T(8,128)(2,1)}), bf16[2048,512]{1,0:T(8,128)(2,1)}) %all-gather.9.cloned.1.call-update) | async-done | bytes 2097168 | tf_op jit(solution)/shard_map/all_gather | solution.py:129
  235.4 2.7 multiply_reduce_fusion
  238.1 8.5 %psum.7 = f32[256]{0:T(256)S(1)} all-reduce(f32[256]{0:T(256)S(1)} %get-tuple-element.143), channel_id=1, replica_groups=mesh['req'=128,'mlp'=4] {'mlp'}, use_global_device_ids=true, to_apply=%region_15.16 | all-reduce | flops 256 | bytes 2048 | tf_op jit(solution)/shard_map/psum | solution.py:134
  246.6 0.8 multiply_convert_fusion
  247.5 0.5 all-gather.13.cloned.1.call-update
  248.0 0.5 all-gather.15.cloned.1.call-update
  248.6 0.5 all-gather.17.cloned.1.call-update
  249.2 24.8 %all-gather.11.cloned.1.call-done = bf16[256,2048]{1,0:T(8,128)(2,1)} async-done(((bf16[256,512]{1,0:T(8,128)(2,1)}), bf16[256,2048]{1,0:T(8,128)(2,1)}) %all-gather.11.cloned.1.call-update) | async-done | bytes 1048592 | tf_op jit(solution)/shard_map/all_gather | solution.py:142
  274.0 145.9 %all-gather.13.cloned.1.call-done = bf16[2048,768]{1,0:T(8,128)(2,1)} async-done(((bf16[16,768]{1,0:T(8,128)(2,1)}), bf16[2048,768]{1,0:T(8,128)(2,1)}) %all-gather.13.cloned.1.call-update) | async-done | bytes 3145744 | tf_op jit(solution)/shard_map/all_gather | solution.py:146
  420.0 3.2 fusion.65
  423.2 137.1 %all-gather.15.cloned.1.call-done = bf16[2048,768]{1,0:T(8,128)(2,1)} async-done(((bf16[16,768]{1,0:T(8,128)(2,1)}), bf16[2048,768]{1,0:T(8,128)(2,1)}) %all-gather.15.cloned.1.call-update) | async-done | bytes 3145744 | tf_op jit(solution)/shard_map/all_gather | solution.py:151
  560.3 140.3 %all-gather.17.cloned.1.call-done = bf16[2048,768]{1,0:T(8,128)(2,1)} async-done(((bf16[16,768]{1,0:T(8,128)(2,1)}), bf16[2048,768]{1,0:T(8,128)(2,1)}) %all-gather.17.cloned.1.call-update) | async-done | bytes 3145744 | tf_op jit(solution)/shard_map/all_gather | solution.py:157
  700.6 6.0 convolution_convert_fusion
  706.6 25.6 %reduce-scatter.2.cloned.1.call-done = bf16[256,512]{1,0:T(8,128)(2,1)} async-done(((bf16[256,2048]{1,0:T(8,128)(2,1)}), bf16[256,512]{1,0:T(8,128)(2,1)}) %reduce-scatter.2.cloned.1.call-update) | async-done | bytes 262160 | tf_op jit(solution)/shard_map/reduce_scatter | solution.py:161
  732.2 1.7 add_convert_fusion
  (44 shorter events, 1.7 us)
Async XLA Ops:
  6.5 84.2 %all-gather.7.cloned.1.call-start = ((), (), s32[]{:S(2)}) async-start(), calls=%async_computation.1 | async-start | bytes 1310720 | tf_op jit(solution)/shard_map/all_gather | solution.py:125
  11.6 7.1 copy-start
  11.6 9.2 %slice-start = ((bf16[256,2,512]{2,1,0:T(2,128)(2,1)}), bf16[256,2,256]{2,1,0:T(2,128)(2,1)S(1)}, s32[]{:S(2)}) async-start(bf16[256,2,512]{2,1,0:T(2,128)(2,1)} %param.17), calls=%async_computation.8 | async-start | bytes 524288 | tf_op jit(solution)/shard_map/slice | solution.py:35
  21.2 0.7 copy-start.1
  21.3 214.1 %copy-start.3 = (bf16[256,512]{1,0:T(8,128)(2,1)S(1)}, bf16[256,512]{1,0:T(8,128)(2,1)}, u32[]{:S(2)}) copy-start(bf16[256,512]{1,0:T(8,128)(2,1)} %param.24) | copy-start | bytes 786436
  22.8 212.6 %all-gather.9.cloned.1.call-start = ((), (), s32[]{:S(2)}) async-start(), calls=%async_computation.2 | async-start | bytes 2113536 | tf_op jit(solution)/shard_map/all_gather | solution.py:129
  23.5 250.5 %all-gather.11.cloned.1.call-start = ((), (), s32[]{:S(2)}) async-start(), calls=%async_computation.3 | async-start | bytes 1310720 | tf_op jit(solution)/shard_map/all_gather | solution.py:142
  247.4 172.6 %all-gather.13.cloned.1.call-start = ((), (), s32[]{:S(2)}) async-start(), calls=%async_computation.4 | async-start | bytes 3170304 | tf_op jit(solution)/shard_map/all_gather | solution.py:146
  248.0 312.3 %all-gather.15.cloned.1.call-start = ((), (), s32[]{:S(2)}) async-start(), calls=%async_computation.5 | async-start | bytes 3170304 | tf_op jit(solution)/shard_map/all_gather | solution.py:151
  248.6 452.0 %all-gather.17.cloned.1.call-start = ((), (), s32[]{:S(2)}) async-start(), calls=%async_computation.6 | async-start | bytes 3170304 | tf_op jit(solution)/shard_map/all_gather | solution.py:157
  249.2 483.0 %reduce-scatter.2.cloned.1.call-start = ((), (), s32[]{:S(2)}) async-start(), calls=%async_computation.7 | async-start | bytes 1310720 | tf_op jit(solution)/shard_map/reduce_scatter | solution.py:161
  274.0 426.5 %copy-start.2 = (bf16[256,2048]{1,0:T(8,128)(2,1)S(1)}, bf16[256,2048]{1,0:T(8,128)(2,1)}, u32[]{:S(2)}) copy-start(bf16[256,2048]{1,0:T(8,128)(2,1)} %all-gather.11.cloned.1.call-done) | copy-start | bytes 3145732
Sparse Core Ops, SparseCore 0:
  22.9 67.7 all-gather.6
  93.8 141.4 all-gather.8
  247.5 26.4 all-gather.10
  277.0 142.9 all-gather.12
  422.9 137.2 all-gather.14
  563.3 137.2 all-gather.16
  706.7 25.4 reduce-scatter.1
where the time goes:
time: 742 us; the launch traced here: 741 us
  waiting for transfers between devices  687 us (93%)
  between operations  16.5 us (2%)
  matrix products  14.2 us (2%)
  blocking collectives  8.46 us (1%)
    all_gather x1, waiting for transfers between devices, per_device(): lax.all_gather(gate_weight, 'req', axis=0, tiled=True)  146 us
    all_gather x1, waiting for transfers between devices, per_device(): lax.all_gather(out_weight, 'req', axis=0, tiled=True)  145 us
    all_gather x1, waiting for transfers between devices, per_device(): lax.all_gather(down_weight_t, 'req', axis=0, tiled=True)  140 us
    all_gather x1, waiting for transfers between devices, per_device(): lax.all_gather(up_weight, 'req', axis=0, tiled=True)  137 us
    all_gather x1, waiting for transfers between devices, per_device(): heads_all = lax.all_gather(attn_out, 'mlp', axis=1, tiled=True)  66.4 us
    reduce_scatter x1, waiting for transfers between devices, per_device(): lax.psum_scatter(partial_value.astype(jnp.bfloat16), 'mlp', scatter_dimen...  25.6 us
    all_gather x1, waiting for transfers between devices, per_device(): normed = lax.all_gather(normed_part, 'mlp', axis=1, tiled=True)  24.8 us
  transfers between devices with their start and end apart: 7, of which 7 were waited for; matrix products, arithmetic and copies ran while one was open for 1% of the time, Pallas kernels for 0%

commit v1 on v0

--- a/solution.py
+++ b/solution.py
@@ -119,49 +119,37 @@
     up_weight,
     down_weight_t,
 ):
+    widths = [out_weight.shape[1], gate_weight.shape[1], up_weight.shape[1], down_weight_t.shape[1]]
+    packed = jnp.concatenate([out_weight, gate_weight, up_weight, down_weight_t], axis=1)
+    gathered = lax.all_gather(packed, "req", axis=0, tiled=True)
+    bounds = [0]
+    for w in widths:
+        bounds.append(bounds[-1] + w)
+    out_full, gate_full, up_full, down_full = [
+        gathered[:, bounds[i] : bounds[i + 1]] for i in range(4)
+    ]
     attn_out = attend(
         queries, new_kv, cache_pool, page_table, assignment, lengths, lambda_vectors, subln_gain
     )
     heads_all = lax.all_gather(attn_out, "mlp", axis=1, tiled=True)
-    columns = heads_all
-    projected = jnp.dot(
-        columns,
-        lax.all_gather(out_weight, "req", axis=0, tiled=True),
-        preferred_element_type=jnp.float32,
-    )
+    projected = jnp.dot(heads_all, out_full, preferred_element_type=jnp.float32)
     stream = (residual.astype(jnp.float32) + projected).astype(jnp.bfloat16)
-    stream_f = stream.astype(jnp.float32)
-    squares = lax.psum(jnp.sum(stream_f * stream_f, axis=1), "mlp")
-    slice_width = stream_f.shape[1]
-    local_gain = lax.dynamic_slice_in_dim(
-        norm_gain, lax.axis_index("mlp") * slice_width, slice_width
-    )
-    normed_part = (stream_f * lax.rsqrt(squares / D + 1e-05)[:, None] * local_gain).astype(
-        jnp.bfloat16
-    )
-    normed = lax.all_gather(normed_part, "mlp", axis=1, tiled=True)
-    columns = normed
-    gate_value = jnp.dot(
-        columns,
-        lax.all_gather(gate_weight, "req", axis=0, tiled=True),
-        preferred_element_type=jnp.float32,
-    )
-    up_value = jnp.dot(
-        columns,
-        lax.all_gather(up_weight, "req", axis=0, tiled=True),
-        preferred_element_type=jnp.float32,
-    )
+    stream_all = lax.all_gather(stream, "mlp", axis=1, tiled=True).astype(jnp.float32)
+    squares = jnp.sum(stream_all * stream_all, axis=1, keepdims=True)
+    normed = (stream_all * lax.rsqrt(squares / D + 1e-05) * norm_gain).astype(jnp.bfloat16)
+    gate_value = jnp.dot(normed, gate_full, preferred_element_type=jnp.float32)
+    up_value = jnp.dot(normed, up_full, preferred_element_type=jnp.float32)
     hidden_act = (jax.nn.silu(gate_value) * up_value).astype(jnp.bfloat16)
     partial_value = lax.dot_general(
         hidden_act,
-        lax.all_gather(down_weight_t, "req", axis=0, tiled=True),
+        down_full,
         (((1,), (1,)), ((), ())),
         preferred_element_type=jnp.float32,
     )
     summed = lax.psum_scatter(
         partial_value.astype(jnp.bfloat16), "mlp", scatter_dimension=1, tiled=True
     ).astype(jnp.float32)
-    return (stream_f + summed).astype(jnp.bfloat16)
+    return (stream.astype(jnp.float32) + summed).astype(jnp.bfloat16)
 
 
 def solution(mesh):

time: 742 us -> 324 us (0.44)
  waiting for transfers between devices: 687 us -> 277 us
  blocking collectives: 8.46 us -> 0 us
    all_gather x5 -> x2, waiting for transfers between devices: 593 us -> 182 us  [the longest x1 156 us: per_device(): gathered = lax.all_gather(packed, 'req', axis=0, tiled=True)]
    psum x1 -> x0, blocking collectives: 8.46 us -> none  [per_device(): squares = lax.psum(jnp.sum(stream_f * stream_f, axis=1), 'mlp')]
  transfers between devices with their start and end apart: 7 -> 4, of which waited for: 7 -> 4; matrix products, arithmetic and copies ran while one was open for 1% -> 0% of each run, Pallas kernels for 0% -> 0%
where the time goes in v1:
time: 324 us; the launch traced here: 323 us
  waiting for transfers between devices  277 us (85%)
  between operations  16.2 us (5%)
  matrix products  15 us (5%)
  other arithmetic  7.88 us (2%)
  local copies, waits for them, and re-layouts  4.51 us (1%)
    all_gather x1, waiting for transfers between devices, per_device(): gathered = lax.all_gather(packed, 'req', axis=0, tiled=True)  156 us
    all_gather x1, waiting for transfers between devices, per_device(): heads_all = lax.all_gather(attn_out, 'mlp', axis=1, tiled=True)  64.3 us
    reduce_scatter x1, waiting for transfers between devices, per_device(): lax.psum_scatter(partial_value.astype(jnp.bfloat16), 'mlp', scatter_dimen...  31.3 us
    all_gather x1, waiting for transfers between devices, per_device(): lax.all_gather(stream, 'mlp', axis=1, tiled=True).astype(jnp.float32)  25.5 us
  transfers between devices with their start and end apart: 4, of which 4 were waited for; matrix products, arithmetic and copies ran while one was open for 0% of the time, Pallas kernels for 0%

profile of v1, /device:TPU:1, one launch (start us, length us, event | category | flops | bytes accessed | tf_op | source)
XLA Modules:
  0.0 323.1 jit_solution(15329398589124734857)
XLA Ops:
  7.2 1.4 fusion.89
  9.3 1.2 fusion.95
  10.5 1.0 copy.20
  11.6 5.8 %while.20 = (s32[]{:T(128)}, f32[256,2]{0,1:T(2,128)S(1)}, f32[256,2]{0,1:T(2,128)S(1)}, f32[256,2,256]{0,2,1:T(8,128)S(1)}, f32[256,2]{0,1:T(2,128)S(1)}, /*ind...) while((s32[]{:T(128)}, f32[256,2]{0,1:T(2,128)S(1)}, ...), condition=%wide.region_6.7_spmd, body=%wide.region_1.6_spmd.sunk | while | flops 102369544 | bytes 5442045 | solution.py:83
  11.7 0.6 dynamic_slice.11
  14.2 1.1 constant_dynamic-slice_fusion.2
  15.4 0.7 add_compare_fusion.2
  16.1 0.2 fusion.114
  16.3 0.2 fusion.115
  16.5 0.1 fusion.116
  16.7 0.4 fusion.118
  17.1 0.4 fusion.117
  17.5 0.2 fusion.96
  17.7 0.2 fusion.97
  18.0 0.7 multiply_reduce_fusion.1
  20.1 0.2 copy.36
  20.3 0.2 fusion.69
  20.6 0.3 fusion.58
  20.9 0.3 multiply_reduce_fusion
  21.3 0.3 copy-done.7
  21.5 0.8 multiply_convert_fusion
  22.5 0.6 pad_maximum_fusion
  23.2 0.0 all-gather.8.cloned.1.call-start
  23.2 64.3 %all-gather.4.cloned.1.call-done = bf16[256,2048]{0,1:T(8,128)(2,1)} async-done(((bf16[256,512]{0,1:T(8,128)(2,1)}), bf16[256,2048]{0,1:T(8,128)(2,1)}) %all-gather.4.cloned.1.call-update) | async-done | bytes 1048592 | tf_op jit(solution)/shard_map/all_gather | solution.py:134
  87.5 156.2 %all-gather.6.cloned.1.call-done = bf16[2048,2816]{1,0:T(8,128)(2,1)} async-done(((bf16[16,2816]{1,0:T(8,128)(2,1)}), bf16[2048,2816]{1,0:T(8,128)(2,1)}) %all-gather.6.cloned.1.call-update) | async-done | bytes 11534352 | tf_op jit(solution)/shard_map/all_gather | solution.py:124
  243.6 3.3 %fusion.59 = bf16[256,512]{1,0:T(8,128)(2,1)} fusion(bf16[256,2048]{0,1:T(8,128)(2,1)} %all-gather.4.cloned.1.call-done, bf16[2048,2816]{1,0:T(8,128)(2,1)} %all-gather.6.cloned.1.call-done, bf16[256,512]{1,0:T(8,128)(2,1)S(1)} %copy-done.8), kind=kOutput, calls=%fused_computation.68 | convolution fusion | flops 537264128 | bytes 3670016 | tf_op jit(solution)/shard_map/dot_general | solution.py:135
  247.1 25.5 %all-gather.8.cloned.1.call-done = bf16[256,2048]{1,0:T(8,128)(2,1)} async-done(((bf16[256,512]{1,0:T(8,128)(2,1)}), bf16[256,2048]{1,0:T(8,128)(2,1)}) %all-gather.8.cloned.1.call-update) | async-done | bytes 1048592 | tf_op jit(solution)/shard_map/all_gather | solution.py:137
  272.6 1.5 fusion.35
  274.1 3.3 %fusion.30 = f32[256,768]{1,0:T(8,128)S(1)} fusion(bf16[2048,2816]{1,0:T(8,128)(2,1)} %all-gather.6.cloned.1.call-done, bf16[256,2048]{1,0:T(8,128)(2,1)} %all-gather.8.cloned.1.call-done, f32[2048]{0:T(1024)S(1)} %copy-done.9, f32[256]{0:T(256)S(1)} %add_rsqrt_fusion.1), kind=kOutput, calls=%fused_computation.41 | convolution fusion | flops 807403520 | bytes 4989952 | tf_op jit(solution)/shard_map/dot_general | solution.py:140
  277.5 6.1 %fusion.32 = bf16[256,2048]{1,0:T(8,128)(2,1)} fusion(bf16[2048,2816]{1,0:T(8,128)(2,1)} %all-gather.6.cloned.1.call-done, f32[256,768]{1,0:T(8,128)S(1)} %fusion.30, bf16[256,2048]{1,0:T(8,128)(2,1)S(1)} %copy-done.1, f32[2048]{0:T(1024)S(1)} %copy-done.9, f32[256]{0:T(256)S(1)} %add_rsqrt_fusion.1), kind=kOutput, calls=%fused_computation.45 | convolution fusion | flops 1614413824 | bytes 9184256 | tf_op jit(solution)/shard_map/dot_general | solution.py:143
  283.6 31.3 %reduce-scatter.2.cloned.1.call-done = bf16[256,512]{1,0:T(8,128)(2,1)} async-done(((bf16[256,2048]{1,0:T(8,128)(2,1)}), bf16[256,512]{1,0:T(8,128)(2,1)}) %reduce-scatter.2.cloned.1.call-update) | async-done | bytes 262160 | tf_op jit(solution)/shard_map/reduce_scatter | solution.py:149
  314.9 1.7 add_convert_fusion
  (48 shorter events, 0.4 us)
Async XLA Ops:
  6.5 5.1 %copy-start.10 = (s32[1,6]{1,0:T(1,128)S(1)}, s32[1,6]{1,0:T(1,128)}, u32[]{:S(2)}) copy-start(s32[1,6]{1,0:T(1,128)} %param.19) | copy-start | bytes 76
  6.5 80.9 %all-gather.4.cloned.1.call-start = ((), (), s32[]{:S(2)}) async-start(), calls=%async_computation.1 | async-start | bytes 1310720 | tf_op jit(solution)/shard_map/all_gather | solution.py:134
  11.6 6.4 %copy-start.6 = (f32[4,128]{1,0:T(4,128)S(1)}, f32[4,128]{1,0:T(4,128)}, u32[]{:S(2)}) copy-start(f32[4,128]{1,0:T(4,128)} %param.22) | copy-start | bytes 6148
  11.6 8.5 %slice-start = ((bf16[256,2,512]{2,1,0:T(2,128)(2,1)}), bf16[256,2,256]{2,1,0:T(2,128)(2,1)S(1)}, s32[]{:S(2)}) async-start(bf16[256,2,512]{2,1,0:T(2,128)(2,1)} %param.17), calls=%async_computation.5 | async-start | bytes 524288 | tf_op jit(solution)/shard_map/slice | solution.py:35
  20.9 0.7 copy-start.7
  20.9 1.6 copy-start.2
  20.9 1.6 copy-start.3
  20.9 1.6 copy-start.4
  20.9 1.6 copy-start.5
  20.9 222.7 %copy-start.8 = (bf16[256,512]{1,0:T(8,128)(2,1)S(1)}, bf16[256,512]{1,0:T(8,128)(2,1)}, u32[]{:S(2)}) copy-start(bf16[256,512]{1,0:T(8,128)(2,1)} %param.24) | copy-start | bytes 786436
  22.4 221.2 %all-gather.6.cloned.1.call-start = ((), (), s32[]{:S(2)}) async-start(), calls=%async_computation.2 | async-start | bytes 11624448 | tf_op jit(solution)/shard_map/all_gather | solution.py:124
  23.1 251.0 %copy-start.9 = (f32[2048]{0:T(1024)S(1)}, f32[2048]{0:T(1024)}, u32[]{:S(2)}) copy-start(f32[2048]{0:T(1024)} %param.26) | copy-start | bytes 24580
  23.2 249.4 %all-gather.8.cloned.1.call-start = ((), (), s32[]{:S(2)}) async-start(), calls=%async_computation.3 | async-start | bytes 1310720 | tf_op jit(solution)/shard_map/all_gather | solution.py:137
  247.0 67.9 %reduce-scatter.2.cloned.1.call-start = ((), (), s32[]{:S(2)}) async-start(), calls=%async_computation.4 | async-start | bytes 1310720 | tf_op jit(solution)/shard_map/reduce_scatter | solution.py:149
  274.1 3.3 %copy-start.1 = (bf16[256,2048]{1,0:T(8,128)(2,1)S(1)}, bf16[256,2048]{1,0:T(8,128)(2,1)}, u32[]{:S(2)}) copy-start(bf16[256,2048]{1,0:T(8,128)(2,1)} %all-gather.8.cloned.1.call-done) | copy-start | bytes 3145732
  277.5 37.4 %copy-start = (bf16[256,512]{1,0:T(8,128)(2,1)S(1)}, bf16[256,512]{1,0:T(8,128)(2,1)}, u32[]{:S(2)}) copy-start(bf16[256,512]{1,0:T(8,128)(2,1)} %fusion.59) | copy-start | bytes 786436
Sparse Core Ops, SparseCore 0:
  22.5 64.9 all-gather.3
  90.6 152.9 all-gather.5
  247.1 25.4 all-gather.7
  283.7 31.1 reduce-scatter.1

commit v2 on v1

--- a/solution.py
+++ b/solution.py
@@ -101,6 +101,34 @@
         * (1.0 - LAMBDA_BASE)
     )
     return mix_out.astype(jnp.bfloat16).reshape(row_count, head_count * value_width)
+
+
+def mlp_gather(block, axis_size):
+    index = lax.axis_index("mlp")
+    pieces = [block]
+    for shift in range(1, axis_size):
+        pieces.append(
+            lax.ppermute(block, "mlp", [(i, (i + shift) % axis_size) for i in range(axis_size)])
+        )
+    stacked = jnp.stack(pieces, axis=0)
+    source_of = (index - jnp.arange(axis_size, dtype=jnp.int32)) % axis_size
+    gathered = jnp.take(stacked, source_of, axis=0)
+    return jnp.concatenate([gathered[k] for k in range(axis_size)], axis=1)
+
+
+def mlp_reduce_scatter(partial_value, axis_size):
+    index = lax.axis_index("mlp")
+    width = partial_value.shape[1] // axis_size
+    blocks = partial_value.reshape(partial_value.shape[0], axis_size, width)
+    total = lax.dynamic_index_in_dim(blocks, index, 1, keepdims=False).astype(jnp.float32)
+    for shift in range(1, axis_size):
+        target = (index + shift) % axis_size
+        outgoing = lax.dynamic_index_in_dim(blocks, target, 1, keepdims=False)
+        incoming = lax.ppermute(
+            outgoing, "mlp", [(i, (i + shift) % axis_size) for i in range(axis_size)]
+        )
+        total = total + incoming.astype(jnp.float32)
+    return total
 
 
 def per_device(
@@ -131,10 +159,11 @@
     attn_out = attend(
         queries, new_kv, cache_pool, page_table, assignment, lengths, lambda_vectors, subln_gain
     )
-    heads_all = lax.all_gather(attn_out, "mlp", axis=1, tiled=True)
+    mlp_size = D // residual.shape[1]
+    heads_all = mlp_gather(attn_out, mlp_size)
     projected = jnp.dot(heads_all, out_full, preferred_element_type=jnp.float32)
     stream = (residual.astype(jnp.float32) + projected).astype(jnp.bfloat16)
-    stream_all = lax.all_gather(stream, "mlp", axis=1, tiled=True).astype(jnp.float32)
+    stream_all = mlp_gather(stream, mlp_size).astype(jnp.float32)
     squares = jnp.sum(stream_all * stream_all, axis=1, keepdims=True)
     normed = (stream_all * lax.rsqrt(squares / D + 1e-05) * norm_gain).astype(jnp.bfloat16)
     gate_value = jnp.dot(normed, gate_full, preferred_element_type=jnp.float32)
@@ -146,9 +175,7 @@
         (((1,), (1,)), ((), ())),
         preferred_element_type=jnp.float32,
     )
-    summed = lax.psum_scatter(
-        partial_value.astype(jnp.bfloat16), "mlp", scatter_dimension=1, tiled=True
-    ).astype(jnp.float32)
+    summed = mlp_reduce_scatter(partial_value.astype(jnp.bfloat16), mlp_size)
     return (stream.astype(jnp.float32) + summed).astype(jnp.bfloat16)
 
 

time: 324 us -> 228 us (0.70)
  waiting for transfers between devices: 277 us -> 146 us
  starting transfers between devices: 0.13 us -> 33.2 us
    all_gather x2 -> x0, waiting for transfers between devices: 89.8 us -> none  [the longest x1 64.3 us: per_device(): heads_all = lax.all_gather(attn_out, 'mlp', axis=1, tiled=True)]
    ppermute x0 -> x9, starting transfers between devices: none -> 33.2 us  [the longest x6 22.1 us: mlp_gather(): lax.ppermute(block, 'mlp', [(i, (i + shift) % axis_size) for i in range(a...]
    reduce_scatter x1 -> x0, waiting for transfers between devices: 31.3 us -> none  [per_device(): lax.psum_scatter(partial_value.astype(jnp.bfloat16), 'mlp', scatter_dimen...]
    all_gather x1, waiting for transfers between devices: 156 us -> 125 us  [per_device(): gathered = lax.all_gather(packed, 'req', axis=0, tiled=True)]
    ppermute x0 -> x9, waiting for transfers between devices: none -> 20.7 us  [the longest x6 13.6 us: mlp_gather(): lax.ppermute(block, 'mlp', [(i, (i + shift) % axis_size) for i in range(a...]
  transfers between devices with their start and end apart: 4 -> 10, of which waited for: 4 -> 7; matrix products, arithmetic and copies ran while one was open for 0% -> 5% of each run, Pallas kernels for 0% -> 0%
where the time goes in v2:
time: 228 us; the launch traced here: 225 us
  waiting for transfers between devices  146 us (64%)
  starting transfers between devices  33.2 us (15%)
  between operations  16.5 us (7%)
  matrix products  12.6 us (6%)
  local copies, waits for them, and re-layouts  7.58 us (3%)
  other arithmetic  7.25 us (3%)
    all_gather x1, waiting for transfers between devices, per_device(): gathered = lax.all_gather(packed, 'req', axis=0, tiled=True)  125 us
    ppermute x6, starting transfers between devices, mlp_gather(): lax.ppermute(block, 'mlp', [(i, (i + shift) % axis_size) for i in range(a...  22.1 us
    ppermute x6, waiting for transfers between devices, mlp_gather(): lax.ppermute(block, 'mlp', [(i, (i + shift) % axis_size) for i in range(a...  13.6 us
    ppermute x3, starting transfers between devices, mlp_reduce_scatter(): lax.ppermute(outgoing, 'mlp', [(i, (i + shift) % axis_size) for i in rang...  11.2 us
    ppermute x3, waiting for transfers between devices, mlp_reduce_scatter(): lax.ppermute(outgoing, 'mlp', [(i, (i + shift) % axis_size) for i in rang...  7.13 us
    dot_general x1, matrix products, per_device(): lax.dot_general(hidden_act, down_full, (((1,), (1,)), ((), ())), preferre...  5.05 us
  transfers between devices with their start and end apart: 10, of which 7 were waited for; matrix products, arithmetic and copies ran while one was open for 5% of the time, Pallas kernels for 0%

profile of v2, /device:TPU:1, one launch (start us, length us, event | category | flops | bytes accessed | tf_op | source)
XLA Modules:
  0.0 225.3 jit_solution(5736969011411162520)
XLA Ops:
  6.5 1.5 pad_maximum_fusion.3
  8.7 1.3 fusion.100
  10.7 1.0 copy.33
  11.6 1.5 multiply_reduce_fusion.1
  14.5 1.1 slice.80
  16.5 5.8 %while.20 = (s32[]{:T(128)}, f32[256,2]{0,1:T(2,128)S(1)}, f32[256,2]{0,1:T(2,128)S(1)}, f32[256,2,256]{0,2,1:T(8,128)S(1)}, f32[256,2]{0,1:T(2,128)S(1)}, /*ind...) while((s32[]{:T(128)}, f32[256,2]{0,1:T(2,128)S(1)}, ...), condition=%wide.region_6.7_spmd, body=%wide.region_1.6_spmd.sunk | while | flops 102369544 | bytes 5442045 | solution.py:83
  16.5 0.7 dynamic_slice.32
  19.1 1.1 constant_dynamic-slice_fusion.6
  20.2 0.6 add_compare_fusion.2
  21.9 0.4 fusion.129
  23.9 4.0 %collective-permute-start = (bf16[256,512]{0,1:T(8,128)(2,1)S(1)}, bf16[256,512]{0,1:T(8,128)(2,1)S(1)}, u32[]{:S(2)}, u32[]{:S(2)}) collective-permute-start(bf16[256,512]{0,1:T(8,128)(2,1)S(1)} %bitcast.90), channel_id=1, source_target_pairs={{0,1},{1,2},{2,3},{3,0},{4,5},{5,6},{6,7},{7,4},{8,9},{9,10},{10,1... | collective-permute-start | bytes 786440 | tf_op jit(solution)/shard_map/ppermute | solution.py:111
  27.9 4.5 %collective-permute-start.1 = (bf16[256,512]{0,1:T(8,128)(2,1)S(1)}, bf16[256,512]{0,1:T(8,128)(2,1)S(1)}, u32[]{:S(2)}, u32[]{:S(2)}) collective-permute-start(bf16[256,512]{0,1:T(8,128)(2,1)S(1)} %bitcast.91), channel_id=1, source_target_pairs={{0,2},{1,3},{2,0},{3,1},{4,6},{5,7},{6,4},{7,5},{8,10},{9,11},{10,... | collective-permute-start | bytes 786440 | tf_op jit(solution)/shard_map/ppermute | solution.py:111
  32.5 3.0 %collective-permute-start.2 = (bf16[256,512]{0,1:T(8,128)(2,1)S(1)}, bf16[256,512]{0,1:T(8,128)(2,1)S(1)}, u32[]{:S(2)}, u32[]{:S(2)}) collective-permute-start(bf16[256,512]{0,1:T(8,128)(2,1)S(1)} %bitcast.92), channel_id=1, source_target_pairs={{0,3},{1,0},{2,1},{3,2},{4,7},{5,4},{6,5},{7,6},{8,11},{9,8},{10,9... | collective-permute-start | bytes 786440 | tf_op jit(solution)/shard_map/ppermute | solution.py:111
  35.5 5.6 %collective-permute-done.1 = bf16[256,512]{0,1:T(8,128)(2,1)S(1)} collective-permute-done((bf16[256,512]{0,1:T(8,128)(2,1)S(1)}, bf16[256,512]{0,1:T(8,128)(2,1)S(1)}, u32[]{:S(2)}, u32[]{:S(2)}) %collective-permute-start.1) | collective-permute-done | bytes 262176 | tf_op jit(solution)/shard_map/ppermute | solution.py:111
  41.3 0.6 gather_fusion
  42.1 125.4 %all-gather.2.cloned.1.call-done = bf16[2048,2816]{1,0:T(8,128)(2,1)} async-done(((bf16[16,2816]{1,0:T(8,128)(2,1)}), bf16[2048,2816]{1,0:T(8,128)(2,1)}) %all-gather.2.cloned.1.call-update) | async-done | bytes 11534352 | tf_op jit(solution)/shard_map/all_gather | solution.py:152
  167.6 2.3 %fusion.59 = bf16[256,512]{1,0:T(8,128)(2,1)S(1)} fusion(bf16[2048,2816]{1,0:T(8,128)(2,1)} %all-gather.2.cloned.1.call-done, bf16[256,512]{0,1:T(8,128)(2,1)S(1)} %get-tuple-element.157, bf16[256,512]{0,1:T(8,128)(2,1)S(1)} %get-tuple-element.158, bf16[256,512]{0,1:T(8,128)(2,1)S(1)} %get-tuple-element.159, bf16[256,512]{0,1:T(8,128)(2,1)S(1)} %get-tuple-element.156, ...), kind=kOutput, calls=%fused_computation.70 | convolution fusion | flops 541458432 | bytes 3670016 | tf_op jit(solution)/shard_map/dot_general | solution.py:164
  169.9 3.1 %collective-permute-start.3 = (bf16[256,512]{1,0:T(8,128)(2,1)S(1)}, bf16[256,512]{1,0:T(8,128)(2,1)S(1)}, u32[]{:S(2)}, u32[]{:S(2)}) collective-permute-start(bf16[256,512]{1,0:T(8,128)(2,1)S(1)} %fusion.59), channel_id=1, source_target_pairs={{0,1},{1,2},{2,3},{3,0},{4,5},{5,6},{6,7},{7,4},{8,9},{9,10},{10,1... | collective-permute-start | bytes 786440 | tf_op jit(solution)/shard_map/ppermute | solution.py:111
  173.0 4.3 %collective-permute-start.4 = (bf16[256,512]{1,0:T(8,128)(2,1)S(1)}, bf16[256,512]{1,0:T(8,128)(2,1)S(1)}, u32[]{:S(2)}, u32[]{:S(2)}) collective-permute-start(bf16[256,512]{1,0:T(8,128)(2,1)S(1)} %fusion.59), channel_id=1, source_target_pairs={{0,2},{1,3},{2,0},{3,1},{4,6},{5,7},{6,4},{7,5},{8,10},{9,11},{10,... | collective-permute-start | bytes 786440 | tf_op jit(solution)/shard_map/ppermute | solution.py:111
  177.4 3.1 %collective-permute-start.5 = (bf16[256,512]{1,0:T(8,128)(2,1)S(1)}, bf16[256,512]{1,0:T(8,128)(2,1)S(1)}, u32[]{:S(2)}, u32[]{:S(2)}) collective-permute-start(bf16[256,512]{1,0:T(8,128)(2,1)S(1)} %fusion.59), channel_id=1, source_target_pairs={{0,3},{1,0},{2,1},{3,2},{4,7},{5,4},{6,5},{7,6},{8,11},{9,8},{10,9... | collective-permute-start | bytes 786440 | tf_op jit(solution)/shard_map/ppermute | solution.py:111
  180.6 6.6 %collective-permute-done.4 = bf16[256,512]{1,0:T(8,128)(2,1)S(1)} collective-permute-done((bf16[256,512]{1,0:T(8,128)(2,1)S(1)}, bf16[256,512]{1,0:T(8,128)(2,1)S(1)}, u32[]{:S(2)}, u32[]{:S(2)}) %collective-permute-start.4) | collective-permute-done | bytes 262176 | tf_op jit(solution)/shard_map/ppermute | solution.py:111
  187.2 1.2 collective-permute-done.5
  188.6 0.6 gather_fusion.1
  190.1 2.9 %fusion.30 = f32[256,768]{1,0:T(8,128)S(1)} fusion(bf16[2048,2816]{1,0:T(8,128)(2,1)} %all-gather.2.cloned.1.call-done, f32[2048]{0:T(1024)S(1)} %copy-done.3, f32[256]{0:T(256)S(1)} %add_rsqrt_fusion.1, bf16[256,512]{1,0:T(8,128)(2,1)S(1)} %get-tuple-element.153, bf16[256,512]{1,0:T(8,128)(2,1)S(1)} %get-tuple-element.154, ...), kind=kOutput, calls=%fused_computation.43 | convolution fusion | flops 811073536 | bytes 4989952 | tf_op jit(solution)/shard_map/dot_general | solution.py:169
  193.0 5.1 %fusion.32 = bf16[256,2048]{1,0:T(8,128)(2,1)S(1)} fusion(bf16[2048,2816]{1,0:T(8,128)(2,1)} %all-gather.2.cloned.1.call-done, f32[256,768]{1,0:T(8,128)S(1)} %fusion.30, f32[2048]{0:T(1024)S(1)} %copy-done.3, f32[256]{0:T(256)S(1)} %add_rsqrt_fusion.1, bf16[256,512]{1,0:T(8,128)(2,1)S(1)} %get-tuple-element.153, ...), kind=kOutput, calls=%fused_computation.47 | convolution fusion | flops 1618083840 | bytes 9184256 | tf_op jit(solution)/shard_map/dot_general | solution.py:172
  198.0 0.5 copy.41
  198.8 4.9 %collective-permute-start.6 = (bf16[256,512]{1,0:T(8,128)(2,1)S(1)}, bf16[256,512]{1,0:T(8,128)(2,1)S(1)}, u32[]{:S(2)}, u32[]{:S(2)}) collective-permute-start(bf16[256,512]{1,0:T(8,128)(2,1)S(1)} %bitcast.95), channel_id=1, source_target_pairs={{0,1},{1,2},{2,3},{3,0},{4,5},{5,6},{6,7},{7,4},{8,9},{9,10},{10,1... | collective-permute-start | bytes 786440 | tf_op jit(solution)/shard_map/ppermute | solution.py:127
  203.9 3.2 %collective-permute-start.7 = (bf16[256,512]{1,0:T(8,128)(2,1)S(1)}, bf16[256,512]{1,0:T(8,128)(2,1)S(1)}, u32[]{:S(2)}, u32[]{:S(2)}) collective-permute-start(bf16[256,512]{1,0:T(8,128)(2,1)S(1)} %bitcast.96), channel_id=1, source_target_pairs={{0,2},{1,3},{2,0},{3,1},{4,6},{5,7},{6,4},{7,5},{8,10},{9,11},{10,... | collective-permute-start | bytes 786440 | tf_op jit(solution)/shard_map/ppermute | solution.py:127
  207.3 3.0 %collective-permute-start.8 = (bf16[256,512]{1,0:T(8,128)(2,1)S(1)}, bf16[256,512]{1,0:T(8,128)(2,1)S(1)}, u32[]{:S(2)}, u32[]{:S(2)}) collective-permute-start(bf16[256,512]{1,0:T(8,128)(2,1)S(1)} %bitcast.97), channel_id=1, source_target_pairs={{0,3},{1,0},{2,1},{3,2},{4,7},{5,4},{6,5},{7,6},{8,11},{9,8},{10,9... | collective-permute-start | bytes 786440 | tf_op jit(solution)/shard_map/ppermute | solution.py:127
  210.5 6.0 %collective-permute-done.7 = bf16[256,512]{1,0:T(8,128)(2,1)S(1)} collective-permute-done((bf16[256,512]{1,0:T(8,128)(2,1)S(1)}, bf16[256,512]{1,0:T(8,128)(2,1)S(1)}, u32[]{:S(2)}, u32[]{:S(2)}) %collective-permute-start.7) | collective-permute-done | bytes 262176 | tf_op jit(solution)/shard_map/ppermute | solution.py:127
  216.5 1.1 collective-permute-done.8
  217.6 0.9 fusion.79
  (61 shorter events, 5.5 us)
Async XLA Ops:
  6.5 9.4 %copy-start = (bf16[256,2,512]{2,1,0:T(2,128)(2,1)S(1)}, bf16[256,2,512]{2,1,0:T(2,128)(2,1)}, u32[]{:S(2)}) copy-start(bf16[256,2,512]{2,1,0:T(2,128)(2,1)} %param.19) | copy-start | bytes 1572868
  6.5 161.0 %all-gather.2.cloned.1.call-start = ((), (), s32[]{:S(2)}) async-start(), calls=%async_computation | async-start | bytes 11624448 | tf_op jit(solution)/shard_map/all_gather | solution.py:152
  10.6 5.9 %copy-start.4 = (s32[1,6]{1,0:T(1,128)S(1)}, s32[1,6]{1,0:T(1,128)}, u32[]{:S(2)}) copy-start(s32[1,6]{1,0:T(1,128)} %param.21) | copy-start | bytes 76
  23.1 0.7 copy-start.1
  23.9 11.6 %collective-permute-start = (bf16[256,512]{0,1:T(8,128)(2,1)S(1)}, bf16[256,512]{0,1:T(8,128)(2,1)S(1)}, u32[]{:S(2)}, u32[]{:S(2)}) collective-permute-start(bf16[256,512]{0,1:T(8,128)(2,1)S(1)} %bitcast.90), channel_id=1, source_target_pairs={{0,1},{1,2},{2,3},{3,0},{4,5},{5,6},{6,7},{7,4},{8,9},{9,10},{10,1... | collective-permute-start | bytes 786440 | tf_op jit(solution)/shard_map/ppermute | solution.py:111
  27.9 13.2 %collective-permute-start.1 = (bf16[256,512]{0,1:T(8,128)(2,1)S(1)}, bf16[256,512]{0,1:T(8,128)(2,1)S(1)}, u32[]{:S(2)}, u32[]{:S(2)}) collective-permute-start(bf16[256,512]{0,1:T(8,128)(2,1)S(1)} %bitcast.91), channel_id=1, source_target_pairs={{0,2},{1,3},{2,0},{3,1},{4,6},{5,7},{6,4},{7,5},{8,10},{9,11},{10,... | collective-permute-start | bytes 786440 | tf_op jit(solution)/shard_map/ppermute | solution.py:111
  32.5 8.6 %collective-permute-start.2 = (bf16[256,512]{0,1:T(8,128)(2,1)S(1)}, bf16[256,512]{0,1:T(8,128)(2,1)S(1)}, u32[]{:S(2)}, u32[]{:S(2)}) collective-permute-start(bf16[256,512]{0,1:T(8,128)(2,1)S(1)} %bitcast.92), channel_id=1, source_target_pairs={{0,3},{1,0},{2,1},{3,2},{4,7},{5,4},{6,5},{7,6},{8,11},{9,8},{10,9... | collective-permute-start | bytes 786440 | tf_op jit(solution)/shard_map/ppermute | solution.py:111
  41.9 125.7 %copy-start.2 = (bf16[256,512]{1,0:T(8,128)(2,1)S(1)}, bf16[256,512]{1,0:T(8,128)(2,1)}, u32[]{:S(2)}) copy-start(bf16[256,512]{1,0:T(8,128)(2,1)} %param.26) | copy-start | bytes 786436
  169.9 10.8 %collective-permute-start.3 = (bf16[256,512]{1,0:T(8,128)(2,1)S(1)}, bf16[256,512]{1,0:T(8,128)(2,1)S(1)}, u32[]{:S(2)}, u32[]{:S(2)}) collective-permute-start(bf16[256,512]{1,0:T(8,128)(2,1)S(1)} %fusion.59), channel_id=1, source_target_pairs={{0,1},{1,2},{2,3},{3,0},{4,5},{5,6},{6,7},{7,4},{8,9},{9,10},{10,1... | collective-permute-start | bytes 786440 | tf_op jit(solution)/shard_map/ppermute | solution.py:111
  173.0 14.2 %collective-permute-start.4 = (bf16[256,512]{1,0:T(8,128)(2,1)S(1)}, bf16[256,512]{1,0:T(8,128)(2,1)S(1)}, u32[]{:S(2)}, u32[]{:S(2)}) collective-permute-start(bf16[256,512]{1,0:T(8,128)(2,1)S(1)} %fusion.59), channel_id=1, source_target_pairs={{0,2},{1,3},{2,0},{3,1},{4,6},{5,7},{6,4},{7,5},{8,10},{9,11},{10,... | collective-permute-start | bytes 786440 | tf_op jit(solution)/shard_map/ppermute | solution.py:111
  177.4 11.1 %collective-permute-start.5 = (bf16[256,512]{1,0:T(8,128)(2,1)S(1)}, bf16[256,512]{1,0:T(8,128)(2,1)S(1)}, u32[]{:S(2)}, u32[]{:S(2)}) collective-permute-start(bf16[256,512]{1,0:T(8,128)(2,1)S(1)} %fusion.59), channel_id=1, source_target_pairs={{0,3},{1,0},{2,1},{3,2},{4,7},{5,4},{6,5},{7,6},{8,11},{9,8},{10,9... | collective-permute-start | bytes 786440 | tf_op jit(solution)/shard_map/ppermute | solution.py:111
  189.4 0.7 copy-start.3
  198.8 11.6 %collective-permute-start.6 = (bf16[256,512]{1,0:T(8,128)(2,1)S(1)}, bf16[256,512]{1,0:T(8,128)(2,1)S(1)}, u32[]{:S(2)}, u32[]{:S(2)}) collective-permute-start(bf16[256,512]{1,0:T(8,128)(2,1)S(1)} %bitcast.95), channel_id=1, source_target_pairs={{0,1},{1,2},{2,3},{3,0},{4,5},{5,6},{6,7},{7,4},{8,9},{9,10},{10,1... | collective-permute-start | bytes 786440 | tf_op jit(solution)/shard_map/ppermute | solution.py:127
  203.9 12.6 %collective-permute-start.7 = (bf16[256,512]{1,0:T(8,128)(2,1)S(1)}, bf16[256,512]{1,0:T(8,128)(2,1)S(1)}, u32[]{:S(2)}, u32[]{:S(2)}) collective-permute-start(bf16[256,512]{1,0:T(8,128)(2,1)S(1)} %bitcast.96), channel_id=1, source_target_pairs={{0,2},{1,3},{2,0},{3,1},{4,6},{5,7},{6,4},{7,5},{8,10},{9,11},{10,... | collective-permute-start | bytes 786440 | tf_op jit(solution)/shard_map/ppermute | solution.py:127
  207.3 10.3 %collective-permute-start.8 = (bf16[256,512]{1,0:T(8,128)(2,1)S(1)}, bf16[256,512]{1,0:T(8,128)(2,1)S(1)}, u32[]{:S(2)}, u32[]{:S(2)}) collective-permute-start(bf16[256,512]{1,0:T(8,128)(2,1)S(1)} %bitcast.97), channel_id=1, source_target_pairs={{0,3},{1,0},{2,1},{3,2},{4,7},{5,4},{6,5},{7,6},{8,11},{9,8},{10,9... | collective-permute-start | bytes 786440 | tf_op jit(solution)/shard_map/ppermute | solution.py:127
Sparse Core Ops, SparseCore 0:
  10.5 157.0 all-gather.1

commit v3 on v2

--- a/solution.py
+++ b/solution.py
@@ -129,6 +129,31 @@
         )
         total = total + incoming.astype(jnp.float32)
     return total
+
+
+DOUBLING_BITS = (4, 3, 6, 2, 5, 1, 0)
+
+
+def req_gather_by_permutes(block):
+    size = lax.axis_size("req")
+    index = lax.axis_index("req")
+    rows, width = block.shape
+    bits = [b for b in DOUBLING_BITS if (1 << b) < size]
+    out = block
+    for bit in bits:
+        partner = lax.ppermute(out, "req", [(r, r ^ (1 << bit)) for r in range(size)])
+        upper = (index >> bit) & 1
+        out = jnp.where(
+            upper == 1,
+            jnp.concatenate([partner, out], axis=0),
+            jnp.concatenate([out, partner], axis=0),
+        )
+    count = len(bits)
+    out = out.reshape((2,) * count + (rows, width))
+    axis_of_bit = {bits[count - 1 - j]: j for j in range(count)}
+    order = [axis_of_bit[b] for b in range(count - 1, -1, -1)]
+    out = out.transpose(order + [count, count + 1])
+    return out.reshape(size * rows, width)
 
 
 def per_device(
@@ -147,15 +172,16 @@
     up_weight,
     down_weight_t,
 ):
-    widths = [out_weight.shape[1], gate_weight.shape[1], up_weight.shape[1], down_weight_t.shape[1]]
-    packed = jnp.concatenate([out_weight, gate_weight, up_weight, down_weight_t], axis=1)
+    widths = [gate_weight.shape[1], up_weight.shape[1], down_weight_t.shape[1]]
+    packed = jnp.concatenate([gate_weight, up_weight, down_weight_t], axis=1)
     gathered = lax.all_gather(packed, "req", axis=0, tiled=True)
     bounds = [0]
     for w in widths:
         bounds.append(bounds[-1] + w)
-    out_full, gate_full, up_full, down_full = [
-        gathered[:, bounds[i] : bounds[i + 1]] for i in range(4)
+    gate_full, up_full, down_full = [
+        gathered[:, bounds[i] : bounds[i + 1]] for i in range(3)
     ]
+    out_full = req_gather_by_permutes(out_weight)
     attn_out = attend(
         queries, new_kv, cache_pool, page_table, assignment, lengths, lambda_vectors, subln_gain
     )

time: 228 us -> 204 us (0.89)
  waiting for transfers between devices: 146 us -> 51.7 us
  starting transfers between devices: 33.2 us -> 97.6 us
  other arithmetic: 7.25 us -> 10.2 us
    all_gather x1, waiting for transfers between devices: 125 us -> 0.09 us  [per_device(): gathered = lax.all_gather(packed, 'req', axis=0, tiled=True)]
    ppermute x0 -> x7, starting transfers between devices: none -> 64.5 us  [req_gather_by_permutes(): partner = lax.ppermute(out, 'req', [(r, r ^ 1 << bit) for r in range(size)])]
    ppermute x0 -> x7, waiting for transfers between devices: none -> 29.2 us  [req_gather_by_permutes(): partner = lax.ppermute(out, 'req', [(r, r ^ 1 << bit) for r in range(size)])]
    select_n x0 -> x7, other arithmetic: none -> 3.9 us  [req_gather_by_permutes(): jnp.where(upper == 1, jnp.concatenate([partner, out], axis=0), jnp.concat...]
    dot_general x4, matrix products: 1.38 us -> 4.22 us  [map_block(): jnp.einsum('nhk,khd->nhd', exp_terms.astype(jnp.bfloat16), value_rows, pr...]
    ppermute x6, waiting for transfers between devices: 13.6 us -> 15.9 us  [mlp_gather(): lax.ppermute(block, 'mlp', [(i, (i + shift) % axis_size) for i in range(a...]
  transfers between devices with their start and end apart: 10 -> 17, of which waited for: 7 -> 13; matrix products, arithmetic and copies ran while one was open for 5% -> 10% of each run, Pallas kernels for 0% -> 0%
where the time goes in v3:
time: 204 us; the launch traced here: 201 us
  starting transfers between devices  97.6 us (48%)
  waiting for transfers between devices  51.7 us (25%)
  between operations  16.6 us (8%)
  matrix products  13.8 us (7%)
  other arithmetic  10.2 us (5%)
  local copies, waits for them, and re-layouts  8.68 us (4%)
  loops' own time  2.18 us (1%)
    ppermute x7, starting transfers between devices, req_gather_by_permutes(): partner = lax.ppermute(out, 'req', [(r, r ^ 1 << bit) for r in range(size)])  64.5 us
    ppermute x7, waiting for transfers between devices, req_gather_by_permutes(): partner = lax.ppermute(out, 'req', [(r, r ^ 1 << bit) for r in range(size)])  29.2 us
    ppermute x6, starting transfers between devices, mlp_gather(): lax.ppermute(block, 'mlp', [(i, (i + shift) % axis_size) for i in range(a...  21.3 us
    ppermute x6, waiting for transfers between devices, mlp_gather(): lax.ppermute(block, 'mlp', [(i, (i + shift) % axis_size) for i in range(a...  15.9 us
    ppermute x3, starting transfers between devices, mlp_reduce_scatter(): lax.ppermute(outgoing, 'mlp', [(i, (i + shift) % axis_size) for i in rang...  11.8 us
    ppermute x3, waiting for transfers between devices, mlp_reduce_scatter(): lax.ppermute(outgoing, 'mlp', [(i, (i + shift) % axis_size) for i in rang...  6.48 us
    dot_general x1, matrix products, per_device(): lax.dot_general(hidden_act, down_full, (((1,), (1,)), ((), ())), preferre...  5.06 us
    dot_general x4, matrix products, map_block(): jnp.einsum('nhk,khd->nhd', exp_terms.astype(jnp.bfloat16), value_rows, pr...  4.22 us
  transfers between devices with their start and end apart: 17, of which 13 were waited for; matrix products, arithmetic and copies ran while one was open for 10% of the time, Pallas kernels for 0%

profile of v3, /device:TPU:1, one launch (start us, length us, event | category | flops | bytes accessed | tf_op | source)
XLA Modules:
  0.0 200.7 jit_solution(727697755887194875)
XLA Ops:
  6.5 1.4 pad_maximum_fusion.3
  8.0 16.3 %collective-permute-start.3 = (bf16[16,512]{1,0:T(8,128)(2,1)}, bf16[16,512]{1,0:T(8,128)(2,1)S(1)}, u32[]{:S(2)}, u32[]{:S(2)}) collective-permute-start(bf16[16,512]{1,0:T(8,128)(2,1)} %param.27), channel_id=1, source_target_pairs={{0,64},{4,68},{8,72},{12,76},{16,80},{20,84},{24,88},{28,92},{32,9... | collective-permute-start | bytes 49160 | tf_op jit(solution)/shard_map/ppermute | solution.py:144
  29.1 6.0 %while.20 = (s32[]{:T(128)}, f32[256,2]{0,1:T(2,128)S(1)}, f32[256,2]{0,1:T(2,128)S(1)}, f32[256,2,256]{0,2,1:T(8,128)S(1)}, f32[256,2]{0,1:T(2,128)S(1)}, /*ind...) while((s32[]{:T(128)}, f32[256,2]{0,1:T(2,128)S(1)}, ...), condition=%wide.region_6.7_spmd, body=%wide.region_1.6_spmd.sunk | while | flops 102369544 | bytes 5442045 | solution.py:83
  35.2 4.0 %collective-permute-start.4 = (bf16[32,512]{1,0:T(8,128)(2,1)S(1)}, bf16[32,512]{1,0:T(8,128)(2,1)S(1)}, u32[]{:S(2)}, u32[]{:S(2)}) collective-permute-start(bf16[32,512]{1,0:T(8,128)(2,1)S(1)} %maximum_select_fusion.6), channel_id=1, source_target_pairs={{0,32},{4,36},{8,40},{12,44},{16,48},{20,52},{24,56},{28,60},{32,0... | collective-permute-start | bytes 98312 | tf_op jit(solution)/shard_map/ppermute | solution.py:144
  39.5 4.3 %collective-permute-done.4 = bf16[32,512]{1,0:T(8,128)(2,1)S(1)} collective-permute-done((bf16[32,512]{1,0:T(8,128)(2,1)S(1)}, bf16[32,512]{1,0:T(8,128)(2,1)S(1)}, u32[]{:S(2)}, u32[]{:S(2)}) %collective-permute-start.4) | collective-permute-done | bytes 32800 | tf_op jit(solution)/shard_map/ppermute | solution.py:144
  43.8 10.6 %collective-permute-start.5 = (bf16[64,512]{1,0:T(8,128)(2,1)S(1)}, bf16[64,512]{1,0:T(8,128)(2,1)S(1)}, u32[]{:S(2)}, u32[]{:S(2)}) collective-permute-start(bf16[64,512]{1,0:T(8,128)(2,1)S(1)} %maximum_select_fusion.5), channel_id=1, source_target_pairs={{0,256},{4,260},{8,264},{12,268},{16,272},{20,276},{24,280},{28,28... | collective-permute-start | bytes 196616 | tf_op jit(solution)/shard_map/ppermute | solution.py:144
  54.8 1.4 collective-permute-done.5
  56.2 27.3 %collective-permute-start.6 = (bf16[128,512]{1,0:T(8,128)(2,1)S(1)}, bf16[128,512]{1,0:T(8,128)(2,1)S(1)}, u32[]{:S(2)}, u32[]{:S(2)}) collective-permute-start(bf16[128,512]{1,0:T(8,128)(2,1)S(1)} %maximum_select_fusion.4), channel_id=1, source_target_pairs={{0,16},{4,20},{8,24},{12,28},{16,0},{20,4},{24,8},{28,12},{32,48},... | collective-permute-start | bytes 393224 | tf_op jit(solution)/shard_map/ppermute | solution.py:144
  83.7 4.1 %collective-permute-done.6 = bf16[128,512]{1,0:T(8,128)(2,1)S(1)} collective-permute-done((bf16[128,512]{1,0:T(8,128)(2,1)S(1)}, bf16[128,512]{1,0:T(8,128)(2,1)S(1)}, u32[]{:S(2)}, u32[]{:S(2)}) %collective-permute-start.6) | collective-permute-done | bytes 131104 | tf_op jit(solution)/shard_map/ppermute | solution.py:144
  87.9 1.9 collective-permute-start.7
  92.6 4.0 %collective-permute-done.7 = bf16[256,512]{1,0:T(8,128)(2,1)} collective-permute-done((bf16[256,512]{1,0:T(8,128)(2,1)S(1)}, bf16[256,512]{1,0:T(8,128)(2,1)}, u32[]{:S(2)}, u32[]{:S(2)}) %collective-permute-start.7) | collective-permute-done | bytes 262176 | tf_op jit(solution)/shard_map/ppermute | solution.py:144
  97.8 1.9 collective-permute-start.8
  99.7 2.0 %fusion.53 = f32[256,2,256]{0,2,1:T(8,128)} fusion(bf16[256,2,256]{0,2,1:T(8,128)(2,1)} %copy.73, f32[256,2,256]{0,2,1:T(8,128)S(1)} %get-tuple-element.77, f32[256,2,256]{0,2,1:T(8,128)S(1)} %get-tuple-element.177, f32[256,2]{0,1:T(2,128)S(1)} %get-tuple-element.152, f32[256,2]{0,1:T(2,128)S(1)} %max.13, f32[256,2]{0,1:T(2,128)S(1)} %get-tuple-element.153, ...), kind=kOutput, calls=%fused_computation.68 | convolution fusion | flops 68026368 | bytes 1906692 | tf_op jit(solution)/shard_map/nhk,khd->nhd/dot_general | solution.py:24
  101.7 1.4 multiply_reduce_fusion
  103.2 15.4 %collective-permute-done.8 = bf16[512,512]{1,0:T(8,128)(2,1)S(1)} collective-permute-done((bf16[512,512]{1,0:T(8,128)(2,1)S(1)}, bf16[512,512]{1,0:T(8,128)(2,1)S(1)}, u32[]{:S(2)}, u32[]{:S(2)}) %collective-permute-start.8) | collective-permute-done | bytes 524320 | tf_op jit(solution)/shard_map/ppermute | solution.py:144
  119.1 2.4 %collective-permute-start.9 = (bf16[1024,512]{1,0:T(8,128)(2,1)S(1)}, bf16[1024,512]{1,0:T(8,128)(2,1)}, u32[]{:S(2)}, u32[]{:S(2)}) collective-permute-start(bf16[1024,512]{1,0:T(8,128)(2,1)S(1)} %maximum_select_fusion.1), channel_id=1, source_target_pairs={{0,4},{4,0},{8,12},{12,8},{16,20},{20,16},{24,28},{28,24},{32,36},... | collective-permute-start | bytes 3145736 | tf_op jit(solution)/shard_map/ppermute | solution.py:144
  121.6 3.3 %collective-permute-start = (bf16[256,512]{0,1:T(8,128)(2,1)S(1)}, bf16[256,512]{0,1:T(8,128)(2,1)S(1)}, u32[]{:S(2)}, u32[]{:S(2)}) collective-permute-start(bf16[256,512]{0,1:T(8,128)(2,1)S(1)} %bitcast.97), channel_id=1, source_target_pairs={{0,1},{1,2},{2,3},{3,0},{4,5},{5,6},{6,7},{7,4},{8,9},{9,10},{10,1... | collective-permute-start | bytes 786440 | tf_op jit(solution)/shard_map/ppermute | solution.py:111
  124.9 4.6 %collective-permute-start.1 = (bf16[256,512]{0,1:T(8,128)(2,1)S(1)}, bf16[256,512]{0,1:T(8,128)(2,1)S(1)}, u32[]{:S(2)}, u32[]{:S(2)}) collective-permute-start(bf16[256,512]{0,1:T(8,128)(2,1)S(1)} %bitcast.98), channel_id=1, source_target_pairs={{0,2},{1,3},{2,0},{3,1},{4,6},{5,7},{6,4},{7,5},{8,10},{9,11},{10,... | collective-permute-start | bytes 786440 | tf_op jit(solution)/shard_map/ppermute | solution.py:111
  129.5 2.8 %collective-permute-start.2 = (bf16[256,512]{0,1:T(8,128)(2,1)S(1)}, bf16[256,512]{0,1:T(8,128)(2,1)S(1)}, u32[]{:S(2)}, u32[]{:S(2)}) collective-permute-start(bf16[256,512]{0,1:T(8,128)(2,1)S(1)} %bitcast.99), channel_id=1, source_target_pairs={{0,3},{1,0},{2,1},{3,2},{4,7},{5,4},{6,5},{7,6},{8,11},{9,8},{10,9... | collective-permute-start | bytes 786440 | tf_op jit(solution)/shard_map/ppermute | solution.py:111
  133.1 6.6 %collective-permute-done.1 = bf16[256,512]{0,1:T(8,128)(2,1)S(1)} collective-permute-done((bf16[256,512]{0,1:T(8,128)(2,1)S(1)}, bf16[256,512]{0,1:T(8,128)(2,1)S(1)}, u32[]{:S(2)}, u32[]{:S(2)}) %collective-permute-start.1) | collective-permute-done | bytes 262176 | tf_op jit(solution)/shard_map/ppermute | solution.py:111
  139.7 1.4 collective-permute-done.2
  142.0 2.2 %maximum_select_fusion = bf16[2048,512]{1,0:T(8,128)(2,1)S(1)} fusion(bf16[1024,512]{1,0:T(8,128)(2,1)S(1)} %maximum_select_fusion.1, bf16[1024,512]{1,0:T(8,128)(2,1)} %collective-permute-done.9, pred[]{:T(512)S(6)} %eq.36), kind=kLoop, calls=%fused_computation.51 | loop fusion | flops 9437184 | bytes 4194305 | tf_op jit(solution)/shard_map/jit(_where)/select_n | solution.py:146
  145.9 4.4 %collective-permute-start.10 = (bf16[256,512]{1,0:T(8,128)(2,1)S(1)}, bf16[256,512]{1,0:T(8,128)(2,1)S(1)}, u32[]{:S(2)}, u32[]{:S(2)}) collective-permute-start(bf16[256,512]{1,0:T(8,128)(2,1)S(1)} %fusion.54), channel_id=1, source_target_pairs={{0,1},{1,2},{2,3},{3,0},{4,5},{5,6},{6,7},{7,4},{8,9},{9,10},{10,1... | collective-permute-start | bytes 786440 | tf_op jit(solution)/shard_map/ppermute | solution.py:111
  150.3 3.3 %collective-permute-start.11 = (bf16[256,512]{1,0:T(8,128)(2,1)S(1)}, bf16[256,512]{1,0:T(8,128)(2,1)S(1)}, u32[]{:S(2)}, u32[]{:S(2)}) collective-permute-start(bf16[256,512]{1,0:T(8,128)(2,1)S(1)} %fusion.54), channel_id=1, source_target_pairs={{0,2},{1,3},{2,0},{3,1},{4,6},{5,7},{6,4},{7,5},{8,10},{9,11},{10,... | collective-permute-start | bytes 786440 | tf_op jit(solution)/shard_map/ppermute | solution.py:111
  153.6 3.0 %collective-permute-start.12 = (bf16[256,512]{1,0:T(8,128)(2,1)S(1)}, bf16[256,512]{1,0:T(8,128)(2,1)S(1)}, u32[]{:S(2)}, u32[]{:S(2)}) collective-permute-start(bf16[256,512]{1,0:T(8,128)(2,1)S(1)} %fusion.54), channel_id=1, source_target_pairs={{0,3},{1,0},{2,1},{3,2},{4,7},{5,4},{6,5},{7,6},{8,11},{9,8},{10,9... | collective-permute-start | bytes 786440 | tf_op jit(solution)/shard_map/ppermute | solution.py:111
  156.6 6.6 %collective-permute-done.11 = bf16[256,512]{1,0:T(8,128)(2,1)S(1)} collective-permute-done((bf16[256,512]{1,0:T(8,128)(2,1)S(1)}, bf16[256,512]{1,0:T(8,128)(2,1)S(1)}, u32[]{:S(2)}, u32[]{:S(2)}) %collective-permute-start.11) | collective-permute-done | bytes 262176 | tf_op jit(solution)/shard_map/ppermute | solution.py:111
  165.5 2.9 %fusion.30 = f32[256,768]{1,0:T(8,128)S(1)} fusion(bf16[2048,2304]{1,0:T(8,128)(2,1)} %all-gather.2.cloned.1.call-done, f32[2048]{0:T(1024)S(1)} %copy-done.5, f32[256]{0:T(256)S(1)} %add_rsqrt_fusion.1, bf16[256,512]{1,0:T(8,128)(2,1)S(1)} %get-tuple-element.165, bf16[256,512]{1,0:T(8,128)(2,1)S(1)} %get-tuple-element.166, ...), kind=kOutput, calls=%fused_computation.43 | convolution fusion | flops 811073536 | bytes 4989952 | tf_op jit(solution)/shard_map/dot_general | solution.py:195
  168.4 5.1 %fusion.32 = bf16[256,2048]{1,0:T(8,128)(2,1)S(1)} fusion(bf16[2048,2304]{1,0:T(8,128)(2,1)} %all-gather.2.cloned.1.call-done, f32[256,768]{1,0:T(8,128)S(1)} %fusion.30, f32[2048]{0:T(1024)S(1)} %copy-done.5, f32[256]{0:T(256)S(1)} %add_rsqrt_fusion.1, bf16[256,512]{1,0:T(8,128)(2,1)S(1)} %get-tuple-element.165, ...), kind=kOutput, calls=%fused_computation.47 | convolution fusion | flops 1618083840 | bytes 9184256 | tf_op jit(solution)/shard_map/dot_general | solution.py:198
  174.3 5.6 %collective-permute-start.13 = (bf16[256,512]{1,0:T(8,128)(2,1)S(1)}, bf16[256,512]{1,0:T(8,128)(2,1)S(1)}, u32[]{:S(2)}, u32[]{:S(2)}) collective-permute-start(bf16[256,512]{1,0:T(8,128)(2,1)S(1)} %bitcast.102), channel_id=1, source_target_pairs={{0,1},{1,2},{2,3},{3,0},{4,5},{5,6},{6,7},{7,4},{8,9},{9,10},{10,1... | collective-permute-start | bytes 786440 | tf_op jit(solution)/shard_map/ppermute | solution.py:127
  180.0 2.6 %collective-permute-start.14 = (bf16[256,512]{1,0:T(8,128)(2,1)S(1)}, bf16[256,512]{1,0:T(8,128)(2,1)S(1)}, u32[]{:S(2)}, u32[]{:S(2)}) collective-permute-start(bf16[256,512]{1,0:T(8,128)(2,1)S(1)} %bitcast.103), channel_id=1, source_target_pairs={{0,2},{1,3},{2,0},{3,1},{4,6},{5,7},{6,4},{7,5},{8,10},{9,11},{10,... | collective-permute-start | bytes 786440 | tf_op jit(solution)/shard_map/ppermute | solution.py:127
  182.7 3.6 %collective-permute-start.15 = (bf16[256,512]{1,0:T(8,128)(2,1)S(1)}, bf16[256,512]{1,0:T(8,128)(2,1)S(1)}, u32[]{:S(2)}, u32[]{:S(2)}) collective-permute-start(bf16[256,512]{1,0:T(8,128)(2,1)S(1)} %bitcast.104), channel_id=1, source_target_pairs={{0,3},{1,0},{2,1},{3,2},{4,7},{5,4},{6,5},{7,6},{8,11},{9,8},{10,9... | collective-permute-start | bytes 786440 | tf_op jit(solution)/shard_map/ppermute | solution.py:127
  186.6 5.2 %collective-permute-done.14 = bf16[256,512]{1,0:T(8,128)(2,1)S(1)} collective-permute-done((bf16[256,512]{1,0:T(8,128)(2,1)S(1)}, bf16[256,512]{1,0:T(8,128)(2,1)S(1)}, u32[]{:S(2)}, u32[]{:S(2)}) %collective-permute-start.14) | collective-permute-done | bytes 262176 | tf_op jit(solution)/shard_map/ppermute | solution.py:127
  (88 shorter events, 20.5 us)
Async XLA Ops:
  6.5 22.6 %copy-start.6 = (s32[1,6]{1,0:T(1,128)S(1)}, s32[1,6]{1,0:T(1,128)}, u32[]{:S(2)}) copy-start(s32[1,6]{1,0:T(1,128)} %param.21) | copy-start | bytes 76
  6.5 158.8 %all-gather.2.cloned.1.call-start = ((), (), s32[]{:S(2)}) async-start(), calls=%async_computation | async-start | bytes 9510912 | tf_op jit(solution)/shard_map/all_gather | solution.py:177
  8.0 27.2 %collective-permute-start.3 = (bf16[16,512]{1,0:T(8,128)(2,1)}, bf16[16,512]{1,0:T(8,128)(2,1)S(1)}, u32[]{:S(2)}, u32[]{:S(2)}) collective-permute-start(bf16[16,512]{1,0:T(8,128)(2,1)} %param.27), channel_id=1, source_target_pairs={{0,64},{4,68},{8,72},{12,76},{16,80},{20,84},{24,88},{28,92},{32,9... | collective-permute-start | bytes 49160 | tf_op jit(solution)/shard_map/ppermute | solution.py:144
  29.1 6.1 %copy-start.1 = (bf16[16,512]{1,0:T(8,128)(2,1)S(1)}, bf16[16,512]{1,0:T(8,128)(2,1)}, u32[]{:S(2)}) copy-start(bf16[16,512]{1,0:T(8,128)(2,1)} %param.27) | copy-start | bytes 49156
  35.1 54.7 %copy-start.2 = (f32[4,128]{1,0:T(4,128)S(1)}, f32[4,128]{1,0:T(4,128)}, u32[]{:S(2)}) copy-start(f32[4,128]{1,0:T(4,128)} %param.24) | copy-start | bytes 6148
  35.2 8.6 %collective-permute-start.4 = (bf16[32,512]{1,0:T(8,128)(2,1)S(1)}, bf16[32,512]{1,0:T(8,128)(2,1)S(1)}, u32[]{:S(2)}, u32[]{:S(2)}) collective-permute-start(bf16[32,512]{1,0:T(8,128)(2,1)S(1)} %maximum_select_fusion.6), channel_id=1, source_target_pairs={{0,32},{4,36},{8,40},{12,44},{16,48},{20,52},{24,56},{28,60},{32,0... | collective-permute-start | bytes 98312 | tf_op jit(solution)/shard_map/ppermute | solution.py:144
  39.2 52.5 %slice-start = ((bf16[256,2,512]{2,1,0:T(2,128)(2,1)}), bf16[256,2,256]{2,1,0:T(2,128)(2,1)S(1)}, s32[]{:S(2)}) async-start(bf16[256,2,512]{2,1,0:T(2,128)(2,1)} %param.19), calls=%async_computation.1 | async-start | bytes 524288 | tf_op jit(solution)/shard_map/slice | solution.py:35
  43.8 12.3 %collective-permute-start.5 = (bf16[64,512]{1,0:T(8,128)(2,1)S(1)}, bf16[64,512]{1,0:T(8,128)(2,1)S(1)}, u32[]{:S(2)}, u32[]{:S(2)}) collective-permute-start(bf16[64,512]{1,0:T(8,128)(2,1)S(1)} %maximum_select_fusion.5), channel_id=1, source_target_pairs={{0,256},{4,260},{8,264},{12,268},{16,272},{20,276},{24,280},{28,28... | collective-permute-start | bytes 196616 | tf_op jit(solution)/shard_map/ppermute | solution.py:144
  56.2 31.6 %collective-permute-start.6 = (bf16[128,512]{1,0:T(8,128)(2,1)S(1)}, bf16[128,512]{1,0:T(8,128)(2,1)S(1)}, u32[]{:S(2)}, u32[]{:S(2)}) collective-permute-start(bf16[128,512]{1,0:T(8,128)(2,1)S(1)} %maximum_select_fusion.4), channel_id=1, source_target_pairs={{0,16},{4,20},{8,24},{12,28},{16,0},{20,4},{24,8},{28,12},{32,48},... | collective-permute-start | bytes 393224 | tf_op jit(solution)/shard_map/ppermute | solution.py:144
  87.9 8.7 %collective-permute-start.7 = (bf16[256,512]{1,0:T(8,128)(2,1)S(1)}, bf16[256,512]{1,0:T(8,128)(2,1)}, u32[]{:S(2)}, u32[]{:S(2)}) collective-permute-start(bf16[256,512]{1,0:T(8,128)(2,1)S(1)} %maximum_select_fusion.3), channel_id=1, source_target_pairs={{0,128},{4,132},{8,136},{12,140},{16,144},{20,148},{24,152},{28,15... | collective-permute-start | bytes 786440 | tf_op jit(solution)/shard_map/ppermute | solution.py:144
  92.6 9.1 %copy-start = (bf16[256,2,256]{0,2,1:T(8,128)(2,1)S(1)}, bf16[256,2,256]{0,2,1:T(8,128)(2,1)}, u32[]{:S(2)}) copy-start(bf16[256,2,256]{0,2,1:T(8,128)(2,1)} %copy.73) | copy-start | bytes 786436
  97.8 20.8 %collective-permute-start.8 = (bf16[512,512]{1,0:T(8,128)(2,1)S(1)}, bf16[512,512]{1,0:T(8,128)(2,1)S(1)}, u32[]{:S(2)}, u32[]{:S(2)}) collective-permute-start(bf16[512,512]{1,0:T(8,128)(2,1)S(1)} %maximum_select_fusion.2), channel_id=1, source_target_pairs={{0,8},{4,12},{8,0},{12,4},{16,24},{20,28},{24,16},{28,20},{32,40},... | collective-permute-start | bytes 1572872 | tf_op jit(solution)/shard_map/ppermute | solution.py:144
  101.7 19.8 %copy-start.3 = (f32[256]{0:T(256)S(1)}, f32[256]{0:T(256)}, u32[]{:S(2)}) copy-start(f32[256]{0:T(256)} %param.25) | copy-start | bytes 3076
  119.1 23.0 %collective-permute-start.9 = (bf16[1024,512]{1,0:T(8,128)(2,1)S(1)}, bf16[1024,512]{1,0:T(8,128)(2,1)}, u32[]{:S(2)}, u32[]{:S(2)}) collective-permute-start(bf16[1024,512]{1,0:T(8,128)(2,1)S(1)} %maximum_select_fusion.1), channel_id=1, source_target_pairs={{0,4},{4,0},{8,12},{12,8},{16,20},{20,16},{24,28},{28,24},{32,36},... | collective-permute-start | bytes 3145736 | tf_op jit(solution)/shard_map/ppermute | solution.py:144
  121.6 11.5 %collective-permute-start = (bf16[256,512]{0,1:T(8,128)(2,1)S(1)}, bf16[256,512]{0,1:T(8,128)(2,1)S(1)}, u32[]{:S(2)}, u32[]{:S(2)}) collective-permute-start(bf16[256,512]{0,1:T(8,128)(2,1)S(1)} %bitcast.97), channel_id=1, source_target_pairs={{0,1},{1,2},{2,3},{3,0},{4,5},{5,6},{6,7},{7,4},{8,9},{9,10},{10,1... | collective-permute-start | bytes 786440 | tf_op jit(solution)/shard_map/ppermute | solution.py:111
  124.9 14.7 %collective-permute-start.1 = (bf16[256,512]{0,1:T(8,128)(2,1)S(1)}, bf16[256,512]{0,1:T(8,128)(2,1)S(1)}, u32[]{:S(2)}, u32[]{:S(2)}) collective-permute-start(bf16[256,512]{0,1:T(8,128)(2,1)S(1)} %bitcast.98), channel_id=1, source_target_pairs={{0,2},{1,3},{2,0},{3,1},{4,6},{5,7},{6,4},{7,5},{8,10},{9,11},{10,... | collective-permute-start | bytes 786440 | tf_op jit(solution)/shard_map/ppermute | solution.py:111
  129.5 11.5 %collective-permute-start.2 = (bf16[256,512]{0,1:T(8,128)(2,1)S(1)}, bf16[256,512]{0,1:T(8,128)(2,1)S(1)}, u32[]{:S(2)}, u32[]{:S(2)}) collective-permute-start(bf16[256,512]{0,1:T(8,128)(2,1)S(1)} %bitcast.99), channel_id=1, source_target_pairs={{0,3},{1,0},{2,1},{3,2},{4,7},{5,4},{6,5},{7,6},{8,11},{9,8},{10,9... | collective-permute-start | bytes 786440 | tf_op jit(solution)/shard_map/ppermute | solution.py:111
  144.2 1.0 copy-start.4
  145.9 10.7 %collective-permute-start.10 = (bf16[256,512]{1,0:T(8,128)(2,1)S(1)}, bf16[256,512]{1,0:T(8,128)(2,1)S(1)}, u32[]{:S(2)}, u32[]{:S(2)}) collective-permute-start(bf16[256,512]{1,0:T(8,128)(2,1)S(1)} %fusion.54), channel_id=1, source_target_pairs={{0,1},{1,2},{2,3},{3,0},{4,5},{5,6},{6,7},{7,4},{8,9},{9,10},{10,1... | collective-permute-start | bytes 786440 | tf_op jit(solution)/shard_map/ppermute | solution.py:111
  150.3 12.9 %collective-permute-start.11 = (bf16[256,512]{1,0:T(8,128)(2,1)S(1)}, bf16[256,512]{1,0:T(8,128)(2,1)S(1)}, u32[]{:S(2)}, u32[]{:S(2)}) collective-permute-start(bf16[256,512]{1,0:T(8,128)(2,1)S(1)} %fusion.54), channel_id=1, source_target_pairs={{0,2},{1,3},{2,0},{3,1},{4,6},{5,7},{6,4},{7,5},{8,10},{9,11},{10,... | collective-permute-start | bytes 786440 | tf_op jit(solution)/shard_map/ppermute | solution.py:111
  153.6 10.3 %collective-permute-start.12 = (bf16[256,512]{1,0:T(8,128)(2,1)S(1)}, bf16[256,512]{1,0:T(8,128)(2,1)S(1)}, u32[]{:S(2)}, u32[]{:S(2)}) collective-permute-start(bf16[256,512]{1,0:T(8,128)(2,1)S(1)} %fusion.54), channel_id=1, source_target_pairs={{0,3},{1,0},{2,1},{3,2},{4,7},{5,4},{6,5},{7,6},{8,11},{9,8},{10,9... | collective-permute-start | bytes 786440 | tf_op jit(solution)/shard_map/ppermute | solution.py:111
  164.8 0.7 copy-start.5
  174.3 12.3 %collective-permute-start.13 = (bf16[256,512]{1,0:T(8,128)(2,1)S(1)}, bf16[256,512]{1,0:T(8,128)(2,1)S(1)}, u32[]{:S(2)}, u32[]{:S(2)}) collective-permute-start(bf16[256,512]{1,0:T(8,128)(2,1)S(1)} %bitcast.102), channel_id=1, source_target_pairs={{0,1},{1,2},{2,3},{3,0},{4,5},{5,6},{6,7},{7,4},{8,9},{9,10},{10,1... | collective-permute-start | bytes 786440 | tf_op jit(solution)/shard_map/ppermute | solution.py:127
  180.0 11.8 %collective-permute-start.14 = (bf16[256,512]{1,0:T(8,128)(2,1)S(1)}, bf16[256,512]{1,0:T(8,128)(2,1)S(1)}, u32[]{:S(2)}, u32[]{:S(2)}) collective-permute-start(bf16[256,512]{1,0:T(8,128)(2,1)S(1)} %bitcast.103), channel_id=1, source_target_pairs={{0,2},{1,3},{2,0},{3,1},{4,6},{5,7},{6,4},{7,5},{8,10},{9,11},{10,... | collective-permute-start | bytes 786440 | tf_op jit(solution)/shard_map/ppermute | solution.py:127
  182.7 10.3 %collective-permute-start.15 = (bf16[256,512]{1,0:T(8,128)(2,1)S(1)}, bf16[256,512]{1,0:T(8,128)(2,1)S(1)}, u32[]{:S(2)}, u32[]{:S(2)}) collective-permute-start(bf16[256,512]{1,0:T(8,128)(2,1)S(1)} %bitcast.104), channel_id=1, source_target_pairs={{0,3},{1,0},{2,1},{3,2},{4,7},{5,4},{6,5},{7,6},{8,11},{9,8},{10,9... | collective-permute-start | bytes 786440 | tf_op jit(solution)/shard_map/ppermute | solution.py:127
Sparse Core Ops, SparseCore 0:
  10.5 154.7 all-gather.1

commit v4 on v3

--- a/solution.py
+++ b/solution.py
@@ -10,90 +10,56 @@
 LAMBDA_BASE = 0.2
 
 
-def map_block(carried, query_rows, key_half, value_rows, visible, score_scale):
-    running_max, running_sum, running_acc = carried
-    score = (
-        jnp.einsum("nhd,khd->nhk", query_rows, key_half, preferred_element_type=jnp.float32)
-        * score_scale
-    )
-    score = jnp.where(visible[:, None, :], score, NEG_FILL)
-    newest = jnp.maximum(running_max, jnp.max(score, axis=2))
-    exp_terms = jnp.where(visible[:, None, :], jnp.exp(score - newest[:, :, None]), 0.0)
-    shrink = jnp.exp(running_max - newest)
-    running_sum = running_sum * shrink + jnp.sum(exp_terms, axis=2)
-    running_acc = running_acc * shrink[:, :, None] + jnp.einsum(
-        "nhk,khd->nhd",
-        exp_terms.astype(jnp.bfloat16),
-        value_rows,
-        preferred_element_type=jnp.float32,
-    )
-    return (newest, running_sum, running_acc)
-
-
-def both_maps(carried, query_rows, key_rows, visible, half_size):
-    score_scale = half_size ** (-0.5)
-    value_rows = key_rows[:, :, 2 * half_size :]
-    map_one = map_block(
-        carried[0],
-        query_rows[:, :, :half_size],
-        key_rows[:, :, :half_size],
-        value_rows,
-        visible,
-        score_scale,
-    )
-    map_two = map_block(
-        carried[1],
-        query_rows[:, :, half_size:],
-        key_rows[:, :, half_size : 2 * half_size],
-        value_rows,
-        visible,
-        score_scale,
-    )
-    return (map_one, map_two)
-
-
 def attend(
     queries, new_kv, cache_pool, page_table, assignment, lengths, lambda_vectors, subln_gain
 ):
     row_count, head_count, value_width = queries.shape
     half_size = value_width // 2
-    page_len = cache_pool.shape[1]
+    score_scale = half_size ** (-0.5)
     request = assignment[0]
     cached = jnp.sum(
         jnp.where(jnp.arange(lengths.shape[0], dtype=jnp.int32) == request, lengths, 0)
     )
+    pages = jnp.take(cache_pool, page_table[0], axis=0)
+    cached_rows = pages.reshape(-1, head_count, cache_pool.shape[3])
+    cache_len = cached_rows.shape[0]
+    key_rows = jnp.concatenate([cached_rows, new_kv], axis=0)
+    positions = jnp.arange(cache_len, dtype=jnp.int32)
+    token_pos = jnp.arange(row_count, dtype=jnp.int32)
+    visible = jnp.concatenate(
+        [
+            jnp.broadcast_to((positions < cached)[None, :], (row_count, cache_len)),
+            token_pos[None, :] <= token_pos[:, None],
+        ],
+        axis=1,
+    )
+    value_rows = key_rows[:, :, 2 * half_size :]
 
-    def fresh_state():
-        return (
-            jnp.full((row_count, head_count), NEG_FILL, jnp.float32),
-            jnp.zeros((row_count, head_count), jnp.float32),
-            jnp.zeros((row_count, head_count, value_width), jnp.float32),
+    def one_map(query_rows, key_half):
+        score = (
+            jnp.einsum("nhd,khd->nhk", query_rows, key_half, preferred_element_type=jnp.float32)
+            * score_scale
         )
+        score = jnp.where(visible[:, None, :], score, NEG_FILL)
+        row_max = jnp.max(score, axis=2, keepdims=True)
+        exp_terms = jnp.where(visible[:, None, :], jnp.exp(score - row_max), 0.0)
+        exp_total = jnp.sum(exp_terms, axis=2)
+        mixed = jnp.einsum(
+            "nhk,khd->nhd",
+            exp_terms.astype(jnp.bfloat16),
+            value_rows,
+            preferred_element_type=jnp.float32,
+        )
+        return mixed / exp_total[:, :, None]
 
-    table_row = page_table[0]
-
-    def page_step(page_index, carried):
-        physical = table_row[page_index]
-        page_rows = lax.dynamic_index_in_dim(cache_pool, physical, 0, keepdims=False)
-        positions = page_index * page_len + jnp.arange(page_len, dtype=jnp.int32)
-        visible = jnp.broadcast_to((positions < cached)[None, :], (row_count, page_len))
-        return both_maps(carried, queries, page_rows, visible, half_size)
-
-    page_count = (cached + page_len - 1) // page_len
-    carried = lax.fori_loop(jnp.int32(0), page_count, page_step, (fresh_state(), fresh_state()))
-    token_pos = jnp.arange(row_count, dtype=jnp.int32)
-    carried = both_maps(
-        carried, queries, new_kv, token_pos[None, :] <= token_pos[:, None], half_size
-    )
+    map_one = one_map(queries[:, :, :half_size], key_rows[:, :, :half_size])
+    map_two = one_map(queries[:, :, half_size:], key_rows[:, :, half_size : 2 * half_size])
     lambda_now = (
         jnp.exp(jnp.sum(lambda_vectors[0] * lambda_vectors[1]))
         - jnp.exp(jnp.sum(lambda_vectors[2] * lambda_vectors[3]))
         + LAMBDA_BASE
     )
-    mix_out = (
-        carried[0][2] / carried[0][1][:, :, None]
-        - lambda_now * carried[1][2] / carried[1][1][:, :, None]
-    )
+    mix_out = map_one - lambda_now * map_two
     mix_out = (
         mix_out
         * lax.rsqrt(jnp.mean(mix_out * mix_out, axis=2, keepdims=True) + 1e-05)

time: 204 us -> 208 us (1.020)
  starting transfers between devices: 97.6 us -> 73.2 us
  local copies, waits for them, and re-layouts: 8.68 us -> 18 us
  other arithmetic: 10.2 us -> 18.8 us
  matrix products: 13.8 us -> 21 us
  waiting for transfers between devices: 51.7 us -> 58.5 us
  loops' own time: 2.18 us -> 0 us
    all_gather x1, waiting for transfers between devices: 0.09 us -> 24.8 us  [per_device(): gathered = lax.all_gather(packed, 'req', axis=0, tiled=True)]
    ppermute x7, starting transfers between devices: 64.5 us -> 41.1 us  [req_gather_by_permutes(): partner = lax.ppermute(out, 'req', [(r, r ^ 1 << bit) for r in range(size)])]
    ppermute x7, waiting for transfers between devices: 29.2 us -> 10.4 us  [req_gather_by_permutes(): partner = lax.ppermute(out, 'req', [(r, r ^ 1 << bit) for r in range(size)])]
    gather x0 -> x2, local copies, waits for them, and re-layouts: none -> 5.42 us  [attend(): pages = jnp.take(cache_pool, page_table[0], axis=0)]
    sub x0 -> x2, matrix products: none -> 4.31 us  [one_map(): exp_terms = jnp.where(visible[:, None, :], jnp.exp(score - row_max), 0.0)]
    gather x2, local copies, waits for them, and re-layouts: 1.23 us -> 4.69 us  [mlp_gather(): gathered = jnp.take(stacked, source_of, axis=0)]
    select_n x7, other arithmetic: 3.9 us -> 6.98 us  [req_gather_by_permutes(): jnp.where(upper == 1, jnp.concatenate([partner, out], axis=0), jnp.concat...]
    another operation x2, other arithmetic: 0.26 us -> 3.15 us  [mlp_gather(): stacked = jnp.stack(pieces, axis=0)]
  transfers between devices with their start and end apart: 17 -> 17, of which waited for: 13 -> 12; matrix products, arithmetic and copies ran while one was open for 10% -> 20% of each run, Pallas kernels for 0% -> 0%
where the time goes in v4:
time: 208 us; the launch traced here: 205 us
  starting transfers between devices  73.2 us (35%)
  waiting for transfers between devices  58.5 us (28%)
  matrix products  21 us (10%)
  other arithmetic  18.8 us (9%)
  local copies, waits for them, and re-layouts  18 us (9%)
  between operations  16 us (8%)
    ppermute x7, starting transfers between devices, req_gather_by_permutes(): partner = lax.ppermute(out, 'req', [(r, r ^ 1 << bit) for r in range(size)])  41.1 us
    all_gather x1, waiting for transfers between devices, per_device(): gathered = lax.all_gather(packed, 'req', axis=0, tiled=True)  24.8 us
    ppermute x6, starting transfers between devices, mlp_gather(): lax.ppermute(block, 'mlp', [(i, (i + shift) % axis_size) for i in range(a...  21.5 us
    ppermute x6, waiting for transfers between devices, mlp_gather(): lax.ppermute(block, 'mlp', [(i, (i + shift) % axis_size) for i in range(a...  15.7 us
    ppermute x3, starting transfers between devices, mlp_reduce_scatter(): lax.ppermute(outgoing, 'mlp', [(i, (i + shift) % axis_size) for i in rang...  10.6 us
    ppermute x7, waiting for transfers between devices, req_gather_by_permutes(): partner = lax.ppermute(out, 'req', [(r, r ^ 1 << bit) for r in range(size)])  10.4 us
    ppermute x3, waiting for transfers between devices, mlp_reduce_scatter(): lax.ppermute(outgoing, 'mlp', [(i, (i + shift) % axis_size) for i in rang...  7.56 us
    dot_general x2, matrix products, one_map(): jnp.einsum('nhk,khd->nhd', exp_terms.astype(jnp.bfloat16), value_rows, pr...  7.08 us
  transfers between devices with their start and end apart: 17, of which 12 were waited for; matrix products, arithmetic and copies ran while one was open for 20% of the time, Pallas kernels for 0%

profile of v4, /device:TPU:1, one launch (start us, length us, event | category | flops | bytes accessed | tf_op | source)
XLA Modules:
  0.0 205.5 jit_solution(577571821508282695)
XLA Ops:
  8.1 16.3 %collective-permute-start.3 = (bf16[16,512]{1,0:T(8,128)(2,1)}, bf16[16,512]{1,0:T(8,128)(2,1)S(1)}, u32[]{:S(2)}, u32[]{:S(2)}) collective-permute-start(bf16[16,512]{1,0:T(8,128)(2,1)} %param.25), channel_id=1, source_target_pairs={{0,64},{4,68},{8,72},{12,76},{16,80},{20,84},{24,88},{28,92},{32,9... | collective-permute-start | bytes 49160 | tf_op jit(solution)/shard_map/ppermute | solution.py:110
  25.0 5.1 %gather_fusion = bf16[6,128,2,512]{3,2,1,0:T(2,128)(2,1)S(1)} fusion(bf16[6,128,2,512]{3,2,1,0:T(2,128)(2,1)S(1)} %copy-done, s32[1024]{0:T(1024)S(1)} %pad_clamp_fusion.1), kind=kCustom, calls=%fused_computation.2 | custom fusion | bytes 3145752 | tf_op jit(solution)/shard_map/jit(_take)/gather | solution.py:23
  34.0 4.0 %collective-permute-start.4 = (bf16[32,512]{1,0:T(8,128)(2,1)S(1)}, bf16[32,512]{1,0:T(8,128)(2,1)S(1)}, u32[]{:S(2)}, u32[]{:S(2)}) collective-permute-start(bf16[32,512]{1,0:T(8,128)(2,1)S(1)} %maximum_select_fusion.6), channel_id=1, source_target_pairs={{0,32},{4,36},{8,40},{12,44},{16,48},{20,52},{24,56},{28,60},{32,0... | collective-permute-start | bytes 98312 | tf_op jit(solution)/shard_map/ppermute | solution.py:110
  40.2 2.4 %collective-permute-done.4 = bf16[32,512]{1,0:T(8,128)(2,1)S(1)} collective-permute-done((bf16[32,512]{1,0:T(8,128)(2,1)S(1)}, bf16[32,512]{1,0:T(8,128)(2,1)S(1)}, u32[]{:S(2)}, u32[]{:S(2)}) %collective-permute-start.4) | collective-permute-done | bytes 32800 | tf_op jit(solution)/shard_map/ppermute | solution.py:110
  42.6 4.7 %collective-permute-start.5 = (bf16[64,512]{1,0:T(8,128)(2,1)S(1)}, bf16[64,512]{1,0:T(8,128)(2,1)}, u32[]{:S(2)}, u32[]{:S(2)}) collective-permute-start(bf16[64,512]{1,0:T(8,128)(2,1)S(1)} %maximum_select_fusion.5), channel_id=1, source_target_pairs={{0,256},{4,260},{8,264},{12,268},{16,272},{20,276},{24,280},{28,28... | collective-permute-start | bytes 196616 | tf_op jit(solution)/shard_map/ppermute | solution.py:110
  50.3 3.1 %collective-permute-start.6 = (bf16[128,512]{1,0:T(8,128)(2,1)S(1)}, bf16[128,512]{1,0:T(8,128)(2,1)}, u32[]{:S(2)}, u32[]{:S(2)}) collective-permute-start(bf16[128,512]{1,0:T(8,128)(2,1)S(1)} %maximum_select_fusion.4), channel_id=1, source_target_pairs={{0,16},{4,20},{8,24},{12,28},{16,0},{20,4},{24,8},{28,12},{32,48},... | collective-permute-start | bytes 393224 | tf_op jit(solution)/shard_map/ppermute | solution.py:110
  53.4 3.2 %fusion.22 = f32[256,2,256]{0,2,1:T(8,128)} fusion(f32[256,2]{0,1:T(2,128)S(1)} %fusion.125, pred[256,1024]{0,1:T(8,128)(4,1)S(1)} %pad_add_fusion, bf16[768,2,512]{2,0,1:T(8,128)(2,1)S(1)} %bitcast_select_fusion.4, bf16[256,2,512]{2,0,1:T(8,128)(2,1)} %copy.37, bf16[256,2,128]{2,1,0:T(2,128)(2,1)} %get-tuple-element.21), kind=kOutput, calls=%fused_computation.34 | convolution fusion | flops 408552960 | bytes 5376000 | tf_op jit(solution)/shard_map/nhk,khd->nhd/dot_general | solution.py:47
  56.6 2.2 %collective-permute-done.6 = bf16[128,512]{1,0:T(8,128)(2,1)} collective-permute-done((bf16[128,512]{1,0:T(8,128)(2,1)S(1)}, bf16[128,512]{1,0:T(8,128)(2,1)}, u32[]{:S(2)}, u32[]{:S(2)}) %collective-permute-start.6) | collective-permute-done | bytes 131104 | tf_op jit(solution)/shard_map/ppermute | solution.py:110
  59.9 3.1 %collective-permute-start.7 = (bf16[256,512]{1,0:T(8,128)(2,1)S(1)}, bf16[256,512]{1,0:T(8,128)(2,1)}, u32[]{:S(2)}, u32[]{:S(2)}) collective-permute-start(bf16[256,512]{1,0:T(8,128)(2,1)S(1)} %maximum_select_fusion.3), channel_id=1, source_target_pairs={{0,128},{4,132},{8,136},{12,140},{16,144},{20,148},{24,152},{28,15... | collective-permute-start | bytes 786440 | tf_op jit(solution)/shard_map/ppermute | solution.py:110
  63.0 2.3 %fusion.130 = f32[256,2]{0,1:T(2,128)S(1)} fusion(pred[256,1024]{0,1:T(8,128)(4,1)} %copy-done.5, bf16[256,2,512]{2,0,1:T(8,128)(2,1)} %copy.37, bf16[768,2,512]{2,0,1:T(8,128)(2,1)S(1)} %bitcast_select_fusion.4, bf16[256,2,128]{2,1,0:T(2,128)(2,1)} %get-tuple-element.20), kind=kOutput, calls=%fused_computation.147 | convolution fusion | flops 137888768 | bytes 2492416 | tf_op jit(solution)/shard_map/sub | solution.py:45
  65.3 2.1 %collective-permute-done.7 = bf16[256,512]{1,0:T(8,128)(2,1)} collective-permute-done((bf16[256,512]{1,0:T(8,128)(2,1)S(1)}, bf16[256,512]{1,0:T(8,128)(2,1)}, u32[]{:S(2)}, u32[]{:S(2)}) %collective-permute-start.7) | collective-permute-done | bytes 262176 | tf_op jit(solution)/shard_map/ppermute | solution.py:110
  72.5 3.9 %multiply_reduce_fusion = (f32[256,2]{0,1:T(2,128)S(1)}, f32[256,2,256]{0,2,1:T(8,128)}) fusion(f32[256,2,256]{0,2,1:T(8,128)} %fusion.22, f32[256,2]{0,1:T(2,128)S(1)} %fusion.130, pred[256,1024]{0,1:T(8,128)(4,1)} %copy-done.5, bf16[256,2,512]{2,0,1:T(8,128)(2,1)} %copy.37, bf16[768,2,512]{2,0,1:T(8,128)(2,1)} %copy-done.1, ...), kind=kOutput, calls=%fused_computation.79 | convolution fusion | flops 409076736 | bytes 5902340 | tf_op jit(solution)/shard_map/nhk,khd->nhd/dot_general | solution.py:47
  76.3 3.6 %collective-permute-done.8 = bf16[512,512]{1,0:T(8,128)(2,1)} collective-permute-done((bf16[512,512]{1,0:T(8,128)(2,1)S(1)}, bf16[512,512]{1,0:T(8,128)(2,1)}, u32[]{:S(2)}, u32[]{:S(2)}) %collective-permute-start.8) | collective-permute-done | bytes 524320 | tf_op jit(solution)/shard_map/ppermute | solution.py:110
  81.6 8.0 %collective-permute-start.9 = (bf16[1024,512]{1,0:T(8,128)(2,1)S(1)}, bf16[1024,512]{1,0:T(8,128)(2,1)}, u32[]{:S(2)}, u32[]{:S(2)}) collective-permute-start(bf16[1024,512]{1,0:T(8,128)(2,1)S(1)} %maximum_select_fusion.1), channel_id=1, source_target_pairs={{0,4},{4,0},{8,12},{12,8},{16,20},{20,16},{24,28},{28,24},{32,36},... | collective-permute-start | bytes 3145736 | tf_op jit(solution)/shard_map/ppermute | solution.py:110
  89.8 3.2 %collective-permute-start = (bf16[256,512]{0,1:T(8,128)(2,1)S(1)}, bf16[256,512]{0,1:T(8,128)(2,1)S(1)}, u32[]{:S(2)}, u32[]{:S(2)}) collective-permute-start(bf16[256,512]{0,1:T(8,128)(2,1)S(1)} %bitcast.88), channel_id=1, source_target_pairs={{0,1},{1,2},{2,3},{3,0},{4,5},{5,6},{6,7},{7,4},{8,9},{9,10},{10,1... | collective-permute-start | bytes 786440 | tf_op jit(solution)/shard_map/ppermute | solution.py:77
  93.0 4.5 %collective-permute-start.1 = (bf16[256,512]{0,1:T(8,128)(2,1)S(1)}, bf16[256,512]{0,1:T(8,128)(2,1)S(1)}, u32[]{:S(2)}, u32[]{:S(2)}) collective-permute-start(bf16[256,512]{0,1:T(8,128)(2,1)S(1)} %bitcast.89), channel_id=1, source_target_pairs={{0,2},{1,3},{2,0},{3,1},{4,6},{5,7},{6,4},{7,5},{8,10},{9,11},{10,... | collective-permute-start | bytes 786440 | tf_op jit(solution)/shard_map/ppermute | solution.py:77
  97.5 2.9 %collective-permute-start.2 = (bf16[256,512]{0,1:T(8,128)(2,1)S(1)}, bf16[256,512]{0,1:T(8,128)(2,1)}, u32[]{:S(2)}, u32[]{:S(2)}) collective-permute-start(bf16[256,512]{0,1:T(8,128)(2,1)S(1)} %bitcast.90), channel_id=1, source_target_pairs={{0,3},{1,0},{2,1},{3,2},{4,7},{5,4},{6,5},{7,6},{8,11},{9,8},{10,9... | collective-permute-start | bytes 786440 | tf_op jit(solution)/shard_map/ppermute | solution.py:77
  100.9 6.7 %collective-permute-done.1 = bf16[256,512]{0,1:T(8,128)(2,1)S(1)} collective-permute-done((bf16[256,512]{0,1:T(8,128)(2,1)S(1)}, bf16[256,512]{0,1:T(8,128)(2,1)S(1)}, u32[]{:S(2)}, u32[]{:S(2)}) %collective-permute-start.1) | collective-permute-done | bytes 262176 | tf_op jit(solution)/shard_map/ppermute | solution.py:77
  108.8 2.1 %pad_maximum_fusion = bf16[4,256,512]{1,2,0:T(8,128)(2,1)} fusion(bf16[1,256,512]{1,2,0:T(8,128)(2,1)} %bitcast.14, bf16[1,256,512]{1,2,0:T(8,128)(2,1)S(1)} %bitcast.100, bf16[1,256,512]{1,2,0:T(8,128)(2,1)S(1)} %bitcast.99, bf16[1,256,512]{1,2,0:T(8,128)(2,1)S(1)} %bitcast.91), kind=kLoop, calls=%fused_computation.40 | loop fusion | flops 1572864 | bytes 2097152 | tf_op jit(solution)/shard_map/stack | solution.py:79
  110.9 2.8 %gather_fusion.1 = bf16[4,256,512]{1,2,0:T(8,128)(2,1)} fusion(bf16[4,256,512]{1,2,0:T(8,128)(2,1)} %pad_maximum_fusion, s32[1024]{0:T(1024)S(1)} %pad_clamp_fusion), kind=kCustom, calls=%fused_computation.clone | custom fusion | bytes 2097168 | tf_op jit(solution)/shard_map/jit(_take)/gather | solution.py:81
  115.2 2.1 %maximum_select_fusion = bf16[2048,512]{1,0:T(8,128)(2,1)S(1)} fusion(bf16[1024,512]{1,0:T(8,128)(2,1)S(1)} %maximum_select_fusion.1, bf16[1024,512]{1,0:T(8,128)(2,1)} %collective-permute-done.9, pred[]{:T(512)S(6)} %eq.36), kind=kLoop, calls=%fused_computation.21 | loop fusion | flops 9437184 | bytes 4194305 | tf_op jit(solution)/shard_map/jit(_where)/select_n | solution.py:112
  119.0 4.7 %collective-permute-start.10 = (bf16[256,512]{1,0:T(8,128)(2,1)S(1)}, bf16[256,512]{1,0:T(8,128)(2,1)S(1)}, u32[]{:S(2)}, u32[]{:S(2)}) collective-permute-start(bf16[256,512]{1,0:T(8,128)(2,1)S(1)} %fusion.26), channel_id=1, source_target_pairs={{0,1},{1,2},{2,3},{3,0},{4,5},{5,6},{6,7},{7,4},{8,9},{9,10},{10,1... | collective-permute-start | bytes 786440 | tf_op jit(solution)/shard_map/ppermute | solution.py:77
  123.7 3.3 %collective-permute-start.11 = (bf16[256,512]{1,0:T(8,128)(2,1)S(1)}, bf16[256,512]{1,0:T(8,128)(2,1)S(1)}, u32[]{:S(2)}, u32[]{:S(2)}) collective-permute-start(bf16[256,512]{1,0:T(8,128)(2,1)S(1)} %fusion.26), channel_id=1, source_target_pairs={{0,2},{1,3},{2,0},{3,1},{4,6},{5,7},{6,4},{7,5},{8,10},{9,11},{10,... | collective-permute-start | bytes 786440 | tf_op jit(solution)/shard_map/ppermute | solution.py:77
  127.0 2.9 %collective-permute-start.12 = (bf16[256,512]{1,0:T(8,128)(2,1)S(1)}, bf16[256,512]{1,0:T(8,128)(2,1)S(1)}, u32[]{:S(2)}, u32[]{:S(2)}) collective-permute-start(bf16[256,512]{1,0:T(8,128)(2,1)S(1)} %fusion.26), channel_id=1, source_target_pairs={{0,3},{1,0},{2,1},{3,2},{4,7},{5,4},{6,5},{7,6},{8,11},{9,8},{10,9... | collective-permute-start | bytes 786440 | tf_op jit(solution)/shard_map/ppermute | solution.py:77
  130.0 6.6 %collective-permute-done.11 = bf16[256,512]{1,0:T(8,128)(2,1)S(1)} collective-permute-done((bf16[256,512]{1,0:T(8,128)(2,1)S(1)}, bf16[256,512]{1,0:T(8,128)(2,1)S(1)}, u32[]{:S(2)}, u32[]{:S(2)}) %collective-permute-start.11) | collective-permute-done | bytes 262176 | tf_op jit(solution)/shard_map/ppermute | solution.py:77
  140.9 24.8 %all-gather.2.cloned.1.call-done = bf16[2048,2304]{1,0:T(8,128)(2,1)} async-done(((bf16[16,2304]{1,0:T(8,128)(2,1)}), bf16[2048,2304]{1,0:T(8,128)(2,1)}) %all-gather.2.cloned.1.call-update) | async-done | bytes 9437200 | tf_op jit(solution)/shard_map/all_gather | solution.py:143
  165.7 2.9 %fusion.6 = f32[256,768]{1,0:T(8,128)S(1)} fusion(bf16[2048,2304]{1,0:T(8,128)(2,1)} %all-gather.2.cloned.1.call-done, f32[2048]{0:T(1024)S(1)} %copy-done.13, f32[256]{0:T(256)S(1)} %add_rsqrt_fusion.1, bf16[256,512]{1,0:T(8,128)(2,1)S(1)} %get-tuple-element.13, bf16[256,512]{1,0:T(8,128)(2,1)S(1)} %get-tuple-element.14, ...), kind=kOutput, calls=%fused_computation.9 | convolution fusion | flops 811073536 | bytes 4989952 | tf_op jit(solution)/shard_map/dot_general | solution.py:161
  168.6 6.0 %fusion.8 = bf16[256,2048]{1,0:T(8,128)(2,1)} fusion(bf16[2048,2304]{1,0:T(8,128)(2,1)} %all-gather.2.cloned.1.call-done, f32[256,768]{1,0:T(8,128)S(1)} %fusion.6, f32[2048]{0:T(1024)S(1)} %copy-done.13, f32[256]{0:T(256)S(1)} %add_rsqrt_fusion.1, bf16[256,512]{1,0:T(8,128)(2,1)S(1)} %get-tuple-element.13, bf16[256,512]{1,0:T(8,128)(2,1)S(1)} %get-tuple-element.14, ...), kind=kOutput, calls=%fused_computation.15 | convolution fusion | flops 1618083840 | bytes 9184256 | tf_op jit(solution)/shard_map/dot_general | solution.py:164
  178.1 3.2 %collective-permute-start.13 = (bf16[256,512]{1,0:T(8,128)(2,1)S(1)}, bf16[256,512]{1,0:T(8,128)(2,1)}, u32[]{:S(2)}, u32[]{:S(2)}) collective-permute-start(bf16[256,512]{1,0:T(8,128)(2,1)S(1)} %bitcast.93), channel_id=1, source_target_pairs={{0,1},{1,2},{2,3},{3,0},{4,5},{5,6},{6,7},{7,4},{8,9},{9,10},{10,1... | collective-permute-start | bytes 786440 | tf_op jit(solution)/shard_map/ppermute | solution.py:93
  181.4 4.3 %collective-permute-start.14 = (bf16[256,512]{1,0:T(8,128)(2,1)S(1)}, bf16[256,512]{1,0:T(8,128)(2,1)}, u32[]{:S(2)}, u32[]{:S(2)}) collective-permute-start(bf16[256,512]{1,0:T(8,128)(2,1)S(1)} %bitcast.94), channel_id=1, source_target_pairs={{0,2},{1,3},{2,0},{3,1},{4,6},{5,7},{6,4},{7,5},{8,10},{9,11},{10,... | collective-permute-start | bytes 786440 | tf_op jit(solution)/shard_map/ppermute | solution.py:93
  185.9 3.1 %collective-permute-start.15 = (bf16[256,512]{1,0:T(8,128)(2,1)S(1)}, bf16[256,512]{1,0:T(8,128)(2,1)S(1)}, u32[]{:S(2)}, u32[]{:S(2)}) collective-permute-start(bf16[256,512]{1,0:T(8,128)(2,1)S(1)} %bitcast.95), channel_id=1, source_target_pairs={{0,3},{1,0},{2,1},{3,2},{4,7},{5,4},{6,5},{7,6},{8,11},{9,8},{10,9... | collective-permute-start | bytes 786440 | tf_op jit(solution)/shard_map/ppermute | solution.py:93
  189.2 6.4 %collective-permute-done.14 = bf16[256,512]{1,0:T(8,128)(2,1)} collective-permute-done((bf16[256,512]{1,0:T(8,128)(2,1)S(1)}, bf16[256,512]{1,0:T(8,128)(2,1)}, u32[]{:S(2)}, u32[]{:S(2)}) %collective-permute-start.14) | collective-permute-done | bytes 262176 | tf_op jit(solution)/shard_map/ppermute | solution.py:93
  (88 shorter events, 32.8 us)
Async XLA Ops:
  6.5 18.5 %copy-start = (bf16[6,128,2,512]{3,2,1,0:T(2,128)(2,1)S(1)}, bf16[6,128,2,512]{3,2,1,0:T(2,128)(2,1)}, u32[]{:S(2)}) copy-start(bf16[6,128,2,512]{3,2,1,0:T(2,128)(2,1)} %param.18) | copy-start | bytes 4718596
  6.5 159.2 %all-gather.2.cloned.1.call-start = ((), (), s32[]{:S(2)}) async-start(), calls=%async_computation | async-start | bytes 9510912 | tf_op jit(solution)/shard_map/all_gather | solution.py:143
  8.1 25.8 %collective-permute-start.3 = (bf16[16,512]{1,0:T(8,128)(2,1)}, bf16[16,512]{1,0:T(8,128)(2,1)S(1)}, u32[]{:S(2)}, u32[]{:S(2)}) collective-permute-start(bf16[16,512]{1,0:T(8,128)(2,1)} %param.25), channel_id=1, source_target_pairs={{0,64},{4,68},{8,72},{12,76},{16,80},{20,84},{24,88},{28,92},{32,9... | collective-permute-start | bytes 49160 | tf_op jit(solution)/shard_map/ppermute | solution.py:110
  30.2 1.0 copy-start.14
  30.2 1.7 copy-start.15
  30.2 1.8 copy-start.6
  30.5 3.4 %copy-start.9 = (bf16[16,512]{1,0:T(8,128)(2,1)S(1)}, bf16[16,512]{1,0:T(8,128)(2,1)}, u32[]{:S(2)}) copy-start(bf16[16,512]{1,0:T(8,128)(2,1)} %param.25) | copy-start | bytes 49156
  33.2 29.8 %copy-start.1 = (bf16[768,2,512]{2,0,1:T(8,128)(2,1)}, bf16[768,2,512]{2,0,1:T(8,128)(2,1)S(1)}, u32[]{:S(2)}) copy-start(bf16[768,2,512]{2,0,1:T(8,128)(2,1)S(1)} %bitcast_select_fusion.4) | copy-start | bytes 4718596
  34.0 8.6 %collective-permute-start.4 = (bf16[32,512]{1,0:T(8,128)(2,1)S(1)}, bf16[32,512]{1,0:T(8,128)(2,1)S(1)}, u32[]{:S(2)}, u32[]{:S(2)}) collective-permute-start(bf16[32,512]{1,0:T(8,128)(2,1)S(1)} %maximum_select_fusion.6), channel_id=1, source_target_pairs={{0,32},{4,36},{8,40},{12,44},{16,48},{20,52},{24,56},{28,60},{32,0... | collective-permute-start | bytes 98312 | tf_op jit(solution)/shard_map/ppermute | solution.py:110
  38.2 15.2 %copy-start.5 = (pred[256,1024]{0,1:T(8,128)(4,1)}, pred[256,1024]{0,1:T(8,128)(4,1)S(1)}, u32[]{:S(2)}) copy-start(pred[256,1024]{0,1:T(8,128)(4,1)S(1)} %pad_add_fusion) | copy-start | bytes 786436
  42.6 6.7 %copy-start.7 = (bf16[64,512]{1,0:T(8,128)(2,1)}, bf16[64,512]{1,0:T(8,128)(2,1)S(1)}, u32[]{:S(2)}) copy-start(bf16[64,512]{1,0:T(8,128)(2,1)S(1)} %maximum_select_fusion.5) | copy-start | bytes 196612
  42.6 6.7 %collective-permute-start.5 = (bf16[64,512]{1,0:T(8,128)(2,1)S(1)}, bf16[64,512]{1,0:T(8,128)(2,1)}, u32[]{:S(2)}, u32[]{:S(2)}) collective-permute-start(bf16[64,512]{1,0:T(8,128)(2,1)S(1)} %maximum_select_fusion.5), channel_id=1, source_target_pairs={{0,256},{4,260},{8,264},{12,268},{16,272},{20,276},{24,280},{28,28... | collective-permute-start | bytes 196616 | tf_op jit(solution)/shard_map/ppermute | solution.py:110
  50.3 8.5 %collective-permute-start.6 = (bf16[128,512]{1,0:T(8,128)(2,1)S(1)}, bf16[128,512]{1,0:T(8,128)(2,1)}, u32[]{:S(2)}, u32[]{:S(2)}) collective-permute-start(bf16[128,512]{1,0:T(8,128)(2,1)S(1)} %maximum_select_fusion.4), channel_id=1, source_target_pairs={{0,16},{4,20},{8,24},{12,28},{16,0},{20,4},{24,8},{28,12},{32,48},... | collective-permute-start | bytes 393224 | tf_op jit(solution)/shard_map/ppermute | solution.py:110
  59.9 7.5 %collective-permute-start.7 = (bf16[256,512]{1,0:T(8,128)(2,1)S(1)}, bf16[256,512]{1,0:T(8,128)(2,1)}, u32[]{:S(2)}, u32[]{:S(2)}) collective-permute-start(bf16[256,512]{1,0:T(8,128)(2,1)S(1)} %maximum_select_fusion.3), channel_id=1, source_target_pairs={{0,128},{4,132},{8,136},{12,140},{16,144},{20,148},{24,152},{28,15... | collective-permute-start | bytes 786440 | tf_op jit(solution)/shard_map/ppermute | solution.py:110
  63.0 7.5 %copy-start.10 = (f32[4,128]{1,0:T(4,128)S(1)}, f32[4,128]{1,0:T(4,128)}, u32[]{:S(2)}) copy-start(f32[4,128]{1,0:T(4,128)} %param.22) | copy-start | bytes 6148
  63.0 9.5 %copy-start.8 = (bf16[256,2,128]{2,1,0:T(2,128)(2,1)S(1)}, bf16[256,2,128]{2,1,0:T(2,128)(2,1)}, u32[]{:S(2)}) copy-start(bf16[256,2,128]{2,1,0:T(2,128)(2,1)} %get-tuple-element.20) | copy-start | bytes 393220
  68.6 11.4 %collective-permute-start.8 = (bf16[512,512]{1,0:T(8,128)(2,1)S(1)}, bf16[512,512]{1,0:T(8,128)(2,1)}, u32[]{:S(2)}, u32[]{:S(2)}) collective-permute-start(bf16[512,512]{1,0:T(8,128)(2,1)S(1)} %maximum_select_fusion.2), channel_id=1, source_target_pairs={{0,8},{4,12},{8,0},{12,4},{16,24},{20,28},{24,16},{28,20},{32,40},... | collective-permute-start | bytes 1572872 | tf_op jit(solution)/shard_map/ppermute | solution.py:110
  76.3 13.3 %copy-start.4 = (f32[256,2,256]{0,2,1:T(8,128)S(1)}, f32[256,2,256]{0,2,1:T(8,128)}, u32[]{:S(2)}) copy-start(f32[256,2,256]{0,2,1:T(8,128)} %get-tuple-element.23) | copy-start | bytes 1572868
  76.3 13.3 %copy-start.11 = (f32[256]{0:T(256)S(1)}, f32[256]{0:T(256)}, u32[]{:S(2)}) copy-start(f32[256]{0:T(256)} %param.23) | copy-start | bytes 3076
  81.6 33.6 %collective-permute-start.9 = (bf16[1024,512]{1,0:T(8,128)(2,1)S(1)}, bf16[1024,512]{1,0:T(8,128)(2,1)}, u32[]{:S(2)}, u32[]{:S(2)}) collective-permute-start(bf16[1024,512]{1,0:T(8,128)(2,1)S(1)} %maximum_select_fusion.1), channel_id=1, source_target_pairs={{0,4},{4,0},{8,12},{12,8},{16,20},{20,16},{24,28},{28,24},{32,36},... | collective-permute-start | bytes 3145736 | tf_op jit(solution)/shard_map/ppermute | solution.py:110
  89.8 11.1 %collective-permute-start = (bf16[256,512]{0,1:T(8,128)(2,1)S(1)}, bf16[256,512]{0,1:T(8,128)(2,1)S(1)}, u32[]{:S(2)}, u32[]{:S(2)}) collective-permute-start(bf16[256,512]{0,1:T(8,128)(2,1)S(1)} %bitcast.88), channel_id=1, source_target_pairs={{0,1},{1,2},{2,3},{3,0},{4,5},{5,6},{6,7},{7,4},{8,9},{9,10},{10,1... | collective-permute-start | bytes 786440 | tf_op jit(solution)/shard_map/ppermute | solution.py:77
  93.0 14.6 %collective-permute-start.1 = (bf16[256,512]{0,1:T(8,128)(2,1)S(1)}, bf16[256,512]{0,1:T(8,128)(2,1)S(1)}, u32[]{:S(2)}, u32[]{:S(2)}) collective-permute-start(bf16[256,512]{0,1:T(8,128)(2,1)S(1)} %bitcast.89), channel_id=1, source_target_pairs={{0,2},{1,3},{2,0},{3,1},{4,6},{5,7},{6,4},{7,5},{8,10},{9,11},{10,... | collective-permute-start | bytes 786440 | tf_op jit(solution)/shard_map/ppermute | solution.py:77
  97.5 11.3 %collective-permute-start.2 = (bf16[256,512]{0,1:T(8,128)(2,1)S(1)}, bf16[256,512]{0,1:T(8,128)(2,1)}, u32[]{:S(2)}, u32[]{:S(2)}) collective-permute-start(bf16[256,512]{0,1:T(8,128)(2,1)S(1)} %bitcast.90), channel_id=1, source_target_pairs={{0,3},{1,0},{2,1},{3,2},{4,7},{5,4},{6,5},{7,6},{8,11},{9,8},{10,9... | collective-permute-start | bytes 786440 | tf_op jit(solution)/shard_map/ppermute | solution.py:77
  119.0 18.4 %copy-start.2 = (bf16[256,512]{1,0:T(8,128)(2,1)}, bf16[256,512]{1,0:T(8,128)(2,1)S(1)}, u32[]{:S(2)}) copy-start(bf16[256,512]{1,0:T(8,128)(2,1)S(1)} %fusion.26) | copy-start | bytes 786436
  119.0 11.0 %collective-permute-start.10 = (bf16[256,512]{1,0:T(8,128)(2,1)S(1)}, bf16[256,512]{1,0:T(8,128)(2,1)S(1)}, u32[]{:S(2)}, u32[]{:S(2)}) collective-permute-start(bf16[256,512]{1,0:T(8,128)(2,1)S(1)} %fusion.26), channel_id=1, source_target_pairs={{0,1},{1,2},{2,3},{3,0},{4,5},{5,6},{6,7},{7,4},{8,9},{9,10},{10,1... | collective-permute-start | bytes 786440 | tf_op jit(solution)/shard_map/ppermute | solution.py:77
  123.7 12.9 %collective-permute-start.11 = (bf16[256,512]{1,0:T(8,128)(2,1)S(1)}, bf16[256,512]{1,0:T(8,128)(2,1)S(1)}, u32[]{:S(2)}, u32[]{:S(2)}) collective-permute-start(bf16[256,512]{1,0:T(8,128)(2,1)S(1)} %fusion.26), channel_id=1, source_target_pairs={{0,2},{1,3},{2,0},{3,1},{4,6},{5,7},{6,4},{7,5},{8,10},{9,11},{10,... | collective-permute-start | bytes 786440 | tf_op jit(solution)/shard_map/ppermute | solution.py:77
  127.0 10.4 %collective-permute-start.12 = (bf16[256,512]{1,0:T(8,128)(2,1)S(1)}, bf16[256,512]{1,0:T(8,128)(2,1)S(1)}, u32[]{:S(2)}, u32[]{:S(2)}) collective-permute-start(bf16[256,512]{1,0:T(8,128)(2,1)S(1)} %fusion.26), channel_id=1, source_target_pairs={{0,3},{1,0},{2,1},{3,2},{4,7},{5,4},{6,5},{7,6},{8,11},{9,8},{10,9... | collective-permute-start | bytes 786440 | tf_op jit(solution)/shard_map/ppermute | solution.py:77
  140.5 25.2 %copy-start.13 = (f32[2048]{0:T(1024)S(1)}, f32[2048]{0:T(1024)}, u32[]{:S(2)}) copy-start(f32[2048]{0:T(1024)} %param.26) | copy-start | bytes 24580
  176.9 19.8 %copy-start.3 = (bf16[256,512]{1,0:T(8,128)(2,1)S(1)}, bf16[256,512]{1,0:T(8,128)(2,1)}, u32[]{:S(2)}) copy-start(bf16[256,512]{1,0:T(8,128)(2,1)} %copy-done.2) | copy-start | bytes 786436
  178.1 11.1 %collective-permute-start.13 = (bf16[256,512]{1,0:T(8,128)(2,1)S(1)}, bf16[256,512]{1,0:T(8,128)(2,1)}, u32[]{:S(2)}, u32[]{:S(2)}) collective-permute-start(bf16[256,512]{1,0:T(8,128)(2,1)S(1)} %bitcast.93), channel_id=1, source_target_pairs={{0,1},{1,2},{2,3},{3,0},{4,5},{5,6},{6,7},{7,4},{8,9},{9,10},{10,1... | collective-permute-start | bytes 786440 | tf_op jit(solution)/shard_map/ppermute | solution.py:93
  181.4 14.2 %collective-permute-start.14 = (bf16[256,512]{1,0:T(8,128)(2,1)S(1)}, bf16[256,512]{1,0:T(8,128)(2,1)}, u32[]{:S(2)}, u32[]{:S(2)}) collective-permute-start(bf16[256,512]{1,0:T(8,128)(2,1)S(1)} %bitcast.94), channel_id=1, source_target_pairs={{0,2},{1,3},{2,0},{3,1},{4,6},{5,7},{6,4},{7,5},{8,10},{9,11},{10,... | collective-permute-start | bytes 786440 | tf_op jit(solution)/shard_map/ppermute | solution.py:93
  185.9 10.8 %collective-permute-start.15 = (bf16[256,512]{1,0:T(8,128)(2,1)S(1)}, bf16[256,512]{1,0:T(8,128)(2,1)S(1)}, u32[]{:S(2)}, u32[]{:S(2)}) collective-permute-start(bf16[256,512]{1,0:T(8,128)(2,1)S(1)} %bitcast.95), channel_id=1, source_target_pairs={{0,3},{1,0},{2,1},{3,2},{4,7},{5,4},{6,5},{7,6},{8,11},{9,8},{10,9... | collective-permute-start | bytes 786440 | tf_op jit(solution)/shard_map/ppermute | solution.py:93
  (1 other events, 1.0 us)
Sparse Core Ops, SparseCore 0:
  10.5 155.1 all-gather.1

commit v5 on v4

--- a/solution.py
+++ b/solution.py
@@ -82,18 +82,28 @@
     return jnp.concatenate([gathered[k] for k in range(axis_size)], axis=1)
 
 
-def mlp_reduce_scatter(partial_value, axis_size):
+def down_and_scatter(hidden_act, down_full, axis_size):
     index = lax.axis_index("mlp")
-    width = partial_value.shape[1] // axis_size
-    blocks = partial_value.reshape(partial_value.shape[0], axis_size, width)
-    total = lax.dynamic_index_in_dim(blocks, index, 1, keepdims=False).astype(jnp.float32)
+    width = down_full.shape[0] // axis_size
+
+    def block_for(target):
+        rows = lax.dynamic_slice_in_dim(down_full, target * width, width, 0)
+        value = lax.dot_general(
+            hidden_act, rows, (((1,), (1,)), ((), ())), preferred_element_type=jnp.float32
+        )
+        return value.astype(jnp.bfloat16)
+
+    incoming = []
     for shift in range(1, axis_size):
         target = (index + shift) % axis_size
-        outgoing = lax.dynamic_index_in_dim(blocks, target, 1, keepdims=False)
-        incoming = lax.ppermute(
-            outgoing, "mlp", [(i, (i + shift) % axis_size) for i in range(axis_size)]
+        incoming.append(
+            lax.ppermute(
+                block_for(target), "mlp", [(i, (i + shift) % axis_size) for i in range(axis_size)]
+            )
         )
-        total = total + incoming.astype(jnp.float32)
+    total = block_for(index).astype(jnp.float32)
+    for received in incoming:
+        total = total + received.astype(jnp.float32)
     return total
 
 
@@ -161,13 +171,7 @@
     gate_value = jnp.dot(normed, gate_full, preferred_element_type=jnp.float32)
     up_value = jnp.dot(normed, up_full, preferred_element_type=jnp.float32)
     hidden_act = (jax.nn.silu(gate_value) * up_value).astype(jnp.bfloat16)
-    partial_value = lax.dot_general(
-        hidden_act,
-        down_full,
-        (((1,), (1,)), ((), ())),
-        preferred_element_type=jnp.float32,
-    )
-    summed = mlp_reduce_scatter(partial_value.astype(jnp.bfloat16), mlp_size)
+    summed = down_and_scatter(hidden_act, down_full, mlp_size)
     return (stream.astype(jnp.float32) + summed).astype(jnp.bfloat16)
 
 

time: 208 us -> 206 us (level)
    dynamic_slice x4 -> x0, local copies, waits for them, and re-layouts: 2.2 us -> none  [the longest x3 1.41 us: mlp_reduce_scatter(): outgoing = lax.dynamic_index_in_dim(blocks, target, 1, keepdims=False)]
    slice x0 -> x1, local copies, waits for them, and re-layouts: none -> 2.09 us  [per_device(): gathered[:, bounds[i]:bounds[i + 1]]]
    dot_general x1 -> x5, matrix products: 6.02 us -> 6.56 us  [the longest x4 3.59 us: block_for(): lax.dot_general(hidden_act, rows, (((1,), (1,)), ((), ())), preferred_ele...]
where the time goes in v5:
time: 206 us; the launch traced here: 204 us
  starting transfers between devices  73.2 us (36%)
  waiting for transfers between devices  58.5 us (28%)
  matrix products  22.7 us (11%)
  other arithmetic  16.8 us (8%)
  local copies, waits for them, and re-layouts  16.3 us (8%)
  between operations  16 us (8%)
    ppermute x7, starting transfers between devices, req_gather_by_permutes(): partner = lax.ppermute(out, 'req', [(r, r ^ 1 << bit) for r in range(size)])  40.9 us
    all_gather x1, waiting for transfers between devices, per_device(): gathered = lax.all_gather(packed, 'req', axis=0, tiled=True)  25 us
    ppermute x6, starting transfers between devices, mlp_gather(): lax.ppermute(block, 'mlp', [(i, (i + shift) % axis_size) for i in range(a...  21.7 us
    ppermute x6, waiting for transfers between devices, mlp_gather(): lax.ppermute(block, 'mlp', [(i, (i + shift) % axis_size) for i in range(a...  15.4 us
    ppermute x3, starting transfers between devices, down_and_scatter(): lax.ppermute(block_for(target), 'mlp', [(i, (i + shift) % axis_size) for...  10.6 us
    ppermute x7, waiting for transfers between devices, req_gather_by_permutes(): partner = lax.ppermute(out, 'req', [(r, r ^ 1 << bit) for r in range(size)])  10.5 us
    ppermute x3, waiting for transfers between devices, down_and_scatter(): lax.ppermute(block_for(target), 'mlp', [(i, (i + shift) % axis_size) for...  7.58 us
    dot_general x2, matrix products, one_map(): jnp.einsum('nhk,khd->nhd', exp_terms.astype(jnp.bfloat16), value_rows, pr...  7.02 us
  transfers between devices with their start and end apart: 17, of which 12 were waited for; matrix products, arithmetic and copies ran while one was open for 20% of the time, Pallas kernels for 0%

profile of v5, /device:TPU:1, one launch (start us, length us, event | category | flops | bytes accessed | tf_op | source)
XLA Modules:
  0.0 203.6 jit_solution(1007079256820882474)
XLA Ops:
  8.1 16.3 %collective-permute-start.3 = (bf16[16,512]{1,0:T(8,128)(2,1)}, bf16[16,512]{1,0:T(8,128)(2,1)S(1)}, u32[]{:S(2)}, u32[]{:S(2)}) collective-permute-start(bf16[16,512]{1,0:T(8,128)(2,1)} %param.25), channel_id=1, source_target_pairs={{0,64},{4,68},{8,72},{12,76},{16,80},{20,84},{24,88},{28,92},{32,9... | collective-permute-start | bytes 49160 | tf_op jit(solution)/shard_map/ppermute | solution.py:120
  25.1 5.1 %gather_fusion = bf16[6,128,2,512]{3,2,1,0:T(2,128)(2,1)S(1)} fusion(bf16[6,128,2,512]{3,2,1,0:T(2,128)(2,1)S(1)} %copy-done, s32[1024]{0:T(1024)S(1)} %pad_clamp_fusion.1), kind=kCustom, calls=%fused_computation.2 | custom fusion | bytes 3145752 | tf_op jit(solution)/shard_map/jit(_take)/gather | solution.py:23
  33.9 4.0 %collective-permute-start.4 = (bf16[32,512]{1,0:T(8,128)(2,1)S(1)}, bf16[32,512]{1,0:T(8,128)(2,1)S(1)}, u32[]{:S(2)}, u32[]{:S(2)}) collective-permute-start(bf16[32,512]{1,0:T(8,128)(2,1)S(1)} %maximum_select_fusion.6), channel_id=1, source_target_pairs={{0,32},{4,36},{8,40},{12,44},{16,48},{20,52},{24,56},{28,60},{32,0... | collective-permute-start | bytes 98312 | tf_op jit(solution)/shard_map/ppermute | solution.py:120
  40.1 2.4 %collective-permute-done.4 = bf16[32,512]{1,0:T(8,128)(2,1)S(1)} collective-permute-done((bf16[32,512]{1,0:T(8,128)(2,1)S(1)}, bf16[32,512]{1,0:T(8,128)(2,1)S(1)}, u32[]{:S(2)}, u32[]{:S(2)}) %collective-permute-start.4) | collective-permute-done | bytes 32800 | tf_op jit(solution)/shard_map/ppermute | solution.py:120
  42.5 4.7 %collective-permute-start.5 = (bf16[64,512]{1,0:T(8,128)(2,1)S(1)}, bf16[64,512]{1,0:T(8,128)(2,1)}, u32[]{:S(2)}, u32[]{:S(2)}) collective-permute-start(bf16[64,512]{1,0:T(8,128)(2,1)S(1)} %maximum_select_fusion.5), channel_id=1, source_target_pairs={{0,256},{4,260},{8,264},{12,268},{16,272},{20,276},{24,280},{28,28... | collective-permute-start | bytes 196616 | tf_op jit(solution)/shard_map/ppermute | solution.py:120
  50.3 3.0 %collective-permute-start.6 = (bf16[128,512]{1,0:T(8,128)(2,1)S(1)}, bf16[128,512]{1,0:T(8,128)(2,1)}, u32[]{:S(2)}, u32[]{:S(2)}) collective-permute-start(bf16[128,512]{1,0:T(8,128)(2,1)S(1)} %maximum_select_fusion.4), channel_id=1, source_target_pairs={{0,16},{4,20},{8,24},{12,28},{16,0},{20,4},{24,8},{28,12},{32,48},... | collective-permute-start | bytes 393224 | tf_op jit(solution)/shard_map/ppermute | solution.py:120
  53.4 3.2 %fusion.17 = f32[256,2,256]{0,2,1:T(8,128)} fusion(f32[256,2]{0,1:T(2,128)S(1)} %fusion.117, pred[256,1024]{0,1:T(8,128)(4,1)S(1)} %pad_add_fusion, bf16[768,2,512]{2,0,1:T(8,128)(2,1)S(1)} %bitcast_select_fusion.4, bf16[256,2,512]{2,0,1:T(8,128)(2,1)} %copy.32, bf16[256,2,128]{2,1,0:T(2,128)(2,1)} %get-tuple-element.17), kind=kOutput, calls=%fused_computation.31 | convolution fusion | flops 408552960 | bytes 5376000 | tf_op jit(solution)/shard_map/nhk,khd->nhd/dot_general | solution.py:47
  56.6 2.3 %collective-permute-done.6 = bf16[128,512]{1,0:T(8,128)(2,1)} collective-permute-done((bf16[128,512]{1,0:T(8,128)(2,1)S(1)}, bf16[128,512]{1,0:T(8,128)(2,1)}, u32[]{:S(2)}, u32[]{:S(2)}) %collective-permute-start.6) | collective-permute-done | bytes 131104 | tf_op jit(solution)/shard_map/ppermute | solution.py:120
  59.9 2.7 %collective-permute-start.7 = (bf16[256,512]{1,0:T(8,128)(2,1)S(1)}, bf16[256,512]{1,0:T(8,128)(2,1)}, u32[]{:S(2)}, u32[]{:S(2)}) collective-permute-start(bf16[256,512]{1,0:T(8,128)(2,1)S(1)} %maximum_select_fusion.3), channel_id=1, source_target_pairs={{0,128},{4,132},{8,136},{12,140},{16,144},{20,148},{24,152},{28,15... | collective-permute-start | bytes 786440 | tf_op jit(solution)/shard_map/ppermute | solution.py:120
  62.7 2.3 %fusion.122 = f32[256,2]{0,1:T(2,128)S(1)} fusion(pred[256,1024]{0,1:T(8,128)(4,1)} %copy-done.4, bf16[256,2,512]{2,0,1:T(8,128)(2,1)} %copy.32, bf16[768,2,512]{2,0,1:T(8,128)(2,1)S(1)} %bitcast_select_fusion.4, bf16[256,2,128]{2,1,0:T(2,128)(2,1)} %get-tuple-element.16), kind=kOutput, calls=%fused_computation.142 | convolution fusion | flops 137888768 | bytes 2492416 | tf_op jit(solution)/shard_map/sub | solution.py:45
  64.9 2.5 %collective-permute-done.7 = bf16[256,512]{1,0:T(8,128)(2,1)} collective-permute-done((bf16[256,512]{1,0:T(8,128)(2,1)S(1)}, bf16[256,512]{1,0:T(8,128)(2,1)}, u32[]{:S(2)}, u32[]{:S(2)}) %collective-permute-start.7) | collective-permute-done | bytes 262176 | tf_op jit(solution)/shard_map/ppermute | solution.py:120
  72.5 3.8 %multiply_reduce_fusion = (f32[256,2]{0,1:T(2,128)S(1)}, f32[256,2,256]{0,2,1:T(8,128)}) fusion(f32[256,2,256]{0,2,1:T(8,128)} %fusion.17, f32[256,2]{0,1:T(2,128)S(1)} %fusion.122, pred[256,1024]{0,1:T(8,128)(4,1)} %copy-done.4, bf16[256,2,512]{2,0,1:T(8,128)(2,1)} %copy.32, bf16[768,2,512]{2,0,1:T(8,128)(2,1)} %copy-done.2, ...), kind=kOutput, calls=%fused_computation.76 | convolution fusion | flops 409076736 | bytes 5902340 | tf_op jit(solution)/shard_map/nhk,khd->nhd/dot_general | solution.py:47
  76.4 3.4 %collective-permute-done.8 = bf16[512,512]{1,0:T(8,128)(2,1)} collective-permute-done((bf16[512,512]{1,0:T(8,128)(2,1)S(1)}, bf16[512,512]{1,0:T(8,128)(2,1)}, u32[]{:S(2)}, u32[]{:S(2)}) %collective-permute-start.8) | collective-permute-done | bytes 524320 | tf_op jit(solution)/shard_map/ppermute | solution.py:120
  81.3 8.2 %collective-permute-start.9 = (bf16[1024,512]{1,0:T(8,128)(2,1)S(1)}, bf16[1024,512]{1,0:T(8,128)(2,1)}, u32[]{:S(2)}, u32[]{:S(2)}) collective-permute-start(bf16[1024,512]{1,0:T(8,128)(2,1)S(1)} %maximum_select_fusion.1), channel_id=1, source_target_pairs={{0,4},{4,0},{8,12},{12,8},{16,20},{20,16},{24,28},{28,24},{32,36},... | collective-permute-start | bytes 3145736 | tf_op jit(solution)/shard_map/ppermute | solution.py:120
  89.7 3.2 %collective-permute-start = (bf16[256,512]{0,1:T(8,128)(2,1)S(1)}, bf16[256,512]{0,1:T(8,128)(2,1)S(1)}, u32[]{:S(2)}, u32[]{:S(2)}) collective-permute-start(bf16[256,512]{0,1:T(8,128)(2,1)S(1)} %bitcast.84), channel_id=1, source_target_pairs={{0,1},{1,2},{2,3},{3,0},{4,5},{5,6},{6,7},{7,4},{8,9},{9,10},{10,1... | collective-permute-start | bytes 786440 | tf_op jit(solution)/shard_map/ppermute | solution.py:77
  92.9 4.4 %collective-permute-start.1 = (bf16[256,512]{0,1:T(8,128)(2,1)S(1)}, bf16[256,512]{0,1:T(8,128)(2,1)S(1)}, u32[]{:S(2)}, u32[]{:S(2)}) collective-permute-start(bf16[256,512]{0,1:T(8,128)(2,1)S(1)} %bitcast.85), channel_id=1, source_target_pairs={{0,2},{1,3},{2,0},{3,1},{4,6},{5,7},{6,4},{7,5},{8,10},{9,11},{10,... | collective-permute-start | bytes 786440 | tf_op jit(solution)/shard_map/ppermute | solution.py:77
  97.3 3.0 %collective-permute-start.2 = (bf16[256,512]{0,1:T(8,128)(2,1)S(1)}, bf16[256,512]{0,1:T(8,128)(2,1)}, u32[]{:S(2)}, u32[]{:S(2)}) collective-permute-start(bf16[256,512]{0,1:T(8,128)(2,1)S(1)} %bitcast.86), channel_id=1, source_target_pairs={{0,3},{1,0},{2,1},{3,2},{4,7},{5,4},{6,5},{7,6},{8,11},{9,8},{10,9... | collective-permute-start | bytes 786440 | tf_op jit(solution)/shard_map/ppermute | solution.py:77
  100.7 6.8 %collective-permute-done.1 = bf16[256,512]{0,1:T(8,128)(2,1)S(1)} collective-permute-done((bf16[256,512]{0,1:T(8,128)(2,1)S(1)}, bf16[256,512]{0,1:T(8,128)(2,1)S(1)}, u32[]{:S(2)}, u32[]{:S(2)}) %collective-permute-start.1) | collective-permute-done | bytes 262176 | tf_op jit(solution)/shard_map/ppermute | solution.py:77
  110.7 2.9 %gather_fusion.1 = bf16[4,256,512]{1,2,0:T(8,128)(2,1)} fusion(bf16[4,256,512]{1,2,0:T(8,128)(2,1)} %pad_maximum_fusion, s32[1024]{0:T(1024)S(1)} %pad_clamp_fusion), kind=kCustom, calls=%fused_computation.clone | custom fusion | bytes 2097168 | tf_op jit(solution)/shard_map/jit(_take)/gather | solution.py:81
  115.0 2.1 %maximum_select_fusion = bf16[2048,512]{1,0:T(8,128)(2,1)S(1)} fusion(bf16[1024,512]{1,0:T(8,128)(2,1)S(1)} %maximum_select_fusion.1, bf16[1024,512]{1,0:T(8,128)(2,1)} %collective-permute-done.9, pred[]{:T(512)S(6)} %eq.36), kind=kLoop, calls=%fused_computation.18 | loop fusion | flops 9437184 | bytes 4194305 | tf_op jit(solution)/shard_map/jit(_where)/select_n | solution.py:122
  118.8 4.8 %collective-permute-start.10 = (bf16[256,512]{1,0:T(8,128)(2,1)S(1)}, bf16[256,512]{1,0:T(8,128)(2,1)S(1)}, u32[]{:S(2)}, u32[]{:S(2)}) collective-permute-start(bf16[256,512]{1,0:T(8,128)(2,1)S(1)} %fusion.21), channel_id=1, source_target_pairs={{0,1},{1,2},{2,3},{3,0},{4,5},{5,6},{6,7},{7,4},{8,9},{9,10},{10,1... | collective-permute-start | bytes 786440 | tf_op jit(solution)/shard_map/ppermute | solution.py:77
  123.6 3.2 %collective-permute-start.11 = (bf16[256,512]{1,0:T(8,128)(2,1)S(1)}, bf16[256,512]{1,0:T(8,128)(2,1)S(1)}, u32[]{:S(2)}, u32[]{:S(2)}) collective-permute-start(bf16[256,512]{1,0:T(8,128)(2,1)S(1)} %fusion.21), channel_id=1, source_target_pairs={{0,2},{1,3},{2,0},{3,1},{4,6},{5,7},{6,4},{7,5},{8,10},{9,11},{10,... | collective-permute-start | bytes 786440 | tf_op jit(solution)/shard_map/ppermute | solution.py:77
  126.8 3.0 %collective-permute-start.12 = (bf16[256,512]{1,0:T(8,128)(2,1)S(1)}, bf16[256,512]{1,0:T(8,128)(2,1)S(1)}, u32[]{:S(2)}, u32[]{:S(2)}) collective-permute-start(bf16[256,512]{1,0:T(8,128)(2,1)S(1)} %fusion.21), channel_id=1, source_target_pairs={{0,3},{1,0},{2,1},{3,2},{4,7},{5,4},{6,5},{7,6},{8,11},{9,8},{10,9... | collective-permute-start | bytes 786440 | tf_op jit(solution)/shard_map/ppermute | solution.py:77
  129.9 6.4 %collective-permute-done.11 = bf16[256,512]{1,0:T(8,128)(2,1)S(1)} collective-permute-done((bf16[256,512]{1,0:T(8,128)(2,1)S(1)}, bf16[256,512]{1,0:T(8,128)(2,1)S(1)}, u32[]{:S(2)}, u32[]{:S(2)}) %collective-permute-start.11) | collective-permute-done | bytes 262176 | tf_op jit(solution)/shard_map/ppermute | solution.py:77
  140.7 25.0 %all-gather.2.cloned.1.call-done = bf16[2048,2304]{1,0:T(8,128)(2,1)} async-done(((bf16[16,2304]{1,0:T(8,128)(2,1)}), bf16[2048,2304]{1,0:T(8,128)(2,1)}) %all-gather.2.cloned.1.call-update) | async-done | bytes 9437200 | tf_op jit(solution)/shard_map/all_gather | solution.py:153
  167.8 4.1 %fusion.4 = f32[256,768]{1,0:T(8,128)S(1)} fusion(bf16[2048,2304]{1,0:T(8,128)(2,1)} %all-gather.2.cloned.1.call-done, f32[2048]{0:T(1024)S(1)} %copy-done.12, f32[256]{0:T(256)S(1)} %add_rsqrt_fusion.1, bf16[256,512]{1,0:T(8,128)(2,1)S(1)} %get-tuple-element.9, bf16[256,512]{1,0:T(8,128)(2,1)S(1)} %get-tuple-element.10, ...), kind=kOutput, calls=%fused_computation.7 | convolution fusion | flops 811073536 | bytes 4989952 | tf_op jit(solution)/shard_map/dot_general | solution.py:171
  171.9 3.0 %fusion.14 = bf16[256,768]{1,0:T(8,128)(2,1)S(1)} fusion(bf16[2048,2304]{1,0:T(8,128)(2,1)} %all-gather.2.cloned.1.call-done, f32[256,768]{1,0:T(8,128)S(1)} %fusion.4, f32[2048]{0:T(1024)S(1)} %copy-done.12, f32[256]{0:T(256)S(1)} %add_rsqrt_fusion.1, bf16[256,512]{1,0:T(8,128)(2,1)S(1)} %get-tuple-element.9, bf16[256,512]{1,0:T(8,128)(2,1)S(1)} %get-tuple-element.10, ...), kind=kOutput, calls=%fused_computation.27 | convolution fusion | flops 812253184 | bytes 5383168 | tf_op jit(solution)/shard_map/dot_general | solution.py:172
  175.3 3.2 %collective-permute-start.13 = (bf16[256,512]{1,0:T(8,128)(2,1)S(1)}, bf16[256,512]{1,0:T(8,128)(2,1)S(1)}, u32[]{:S(2)}, u32[]{:S(2)}) collective-permute-start(bf16[256,512]{1,0:T(8,128)(2,1)S(1)} %convolution_convert_fusion.2), channel_id=1, source_target_pairs={{0,1},{1,2},{2,3},{3,0},{4,5},{5,6},{6,7},{7,4},{8,9},{9,10},{10,1... | collective-permute-start | bytes 786440 | tf_op jit(solution)/shard_map/ppermute | solution.py:100
  178.9 4.3 %collective-permute-start.14 = (bf16[256,512]{1,0:T(8,128)(2,1)S(1)}, bf16[256,512]{1,0:T(8,128)(2,1)S(1)}, u32[]{:S(2)}, u32[]{:S(2)}) collective-permute-start(bf16[256,512]{1,0:T(8,128)(2,1)S(1)} %convolution_convert_fusion.1), channel_id=1, source_target_pairs={{0,2},{1,3},{2,0},{3,1},{4,6},{5,7},{6,4},{7,5},{8,10},{9,11},{10,... | collective-permute-start | bytes 786440 | tf_op jit(solution)/shard_map/ppermute | solution.py:100
  183.7 3.1 %collective-permute-start.15 = (bf16[256,512]{1,0:T(8,128)(2,1)S(1)}, bf16[256,512]{1,0:T(8,128)(2,1)}, u32[]{:S(2)}, u32[]{:S(2)}) collective-permute-start(bf16[256,512]{1,0:T(8,128)(2,1)S(1)} %convolution_convert_fusion), channel_id=1, source_target_pairs={{0,3},{1,0},{2,1},{3,2},{4,7},{5,4},{6,5},{7,6},{8,11},{9,8},{10,9... | collective-permute-start | bytes 786440 | tf_op jit(solution)/shard_map/ppermute | solution.py:100
  186.8 5.9 %collective-permute-done.14 = bf16[256,512]{1,0:T(8,128)(2,1)S(1)} collective-permute-done((bf16[256,512]{1,0:T(8,128)(2,1)S(1)}, bf16[256,512]{1,0:T(8,128)(2,1)S(1)}, u32[]{:S(2)}, u32[]{:S(2)}) %collective-permute-start.14) | collective-permute-done | bytes 262176 | tf_op jit(solution)/shard_map/ppermute | solution.py:100
  194.3 2.4 %add_convert_fusion = bf16[256,512]{1,0:T(8,128)(2,1)} fusion(bf16[256,512]{1,0:T(8,128)(2,1)} %collective-permute-done.15, bf16[256,512]{1,0:T(8,128)(2,1)S(1)} %collective-permute-done.14, bf16[256,512]{1,0:T(8,128)(2,1)S(1)} %collective-permute-done.13, bf16[256,512]{1,0:T(8,128)(2,1)S(1)} %fusion.21, bf16[256,768]{1,0:T(8,128)(2,1)S(1)} %fusion.14, ...), kind=kOutput, calls=%fused_computation.74 | convolution fusion | flops 202768384 | bytes 2490372 | tf_op jit(solution)/shard_map/dot_general | solution.py:91
  (84 shorter events, 32.8 us)
Async XLA Ops:
  6.5 18.5 %copy-start = (bf16[6,128,2,512]{3,2,1,0:T(2,128)(2,1)S(1)}, bf16[6,128,2,512]{3,2,1,0:T(2,128)(2,1)}, u32[]{:S(2)}) copy-start(bf16[6,128,2,512]{3,2,1,0:T(2,128)(2,1)} %param.18) | copy-start | bytes 4718596
  6.5 159.2 %all-gather.2.cloned.1.call-start = ((), (), s32[]{:S(2)}) async-start(), calls=%async_computation | async-start | bytes 9510912 | tf_op jit(solution)/shard_map/all_gather | solution.py:153
  8.1 25.8 %collective-permute-start.3 = (bf16[16,512]{1,0:T(8,128)(2,1)}, bf16[16,512]{1,0:T(8,128)(2,1)S(1)}, u32[]{:S(2)}, u32[]{:S(2)}) collective-permute-start(bf16[16,512]{1,0:T(8,128)(2,1)} %param.25), channel_id=1, source_target_pairs={{0,64},{4,68},{8,72},{12,76},{16,80},{20,84},{24,88},{28,92},{32,9... | collective-permute-start | bytes 49160 | tf_op jit(solution)/shard_map/ppermute | solution.py:120
  30.2 1.0 copy-start.13
  30.2 1.7 copy-start.14
  30.2 1.8 copy-start.5
  30.5 3.4 %copy-start.8 = (bf16[16,512]{1,0:T(8,128)(2,1)S(1)}, bf16[16,512]{1,0:T(8,128)(2,1)}, u32[]{:S(2)}) copy-start(bf16[16,512]{1,0:T(8,128)(2,1)} %param.25) | copy-start | bytes 49156
  33.2 29.4 %copy-start.2 = (bf16[768,2,512]{2,0,1:T(8,128)(2,1)}, bf16[768,2,512]{2,0,1:T(8,128)(2,1)S(1)}, u32[]{:S(2)}) copy-start(bf16[768,2,512]{2,0,1:T(8,128)(2,1)S(1)} %bitcast_select_fusion.4) | copy-start | bytes 4718596
  33.9 8.6 %collective-permute-start.4 = (bf16[32,512]{1,0:T(8,128)(2,1)S(1)}, bf16[32,512]{1,0:T(8,128)(2,1)S(1)}, u32[]{:S(2)}, u32[]{:S(2)}) collective-permute-start(bf16[32,512]{1,0:T(8,128)(2,1)S(1)} %maximum_select_fusion.6), channel_id=1, source_target_pairs={{0,32},{4,36},{8,40},{12,44},{16,48},{20,52},{24,56},{28,60},{32,0... | collective-permute-start | bytes 98312 | tf_op jit(solution)/shard_map/ppermute | solution.py:120
  38.1 15.2 %copy-start.4 = (pred[256,1024]{0,1:T(8,128)(4,1)}, pred[256,1024]{0,1:T(8,128)(4,1)S(1)}, u32[]{:S(2)}) copy-start(pred[256,1024]{0,1:T(8,128)(4,1)S(1)} %pad_add_fusion) | copy-start | bytes 786436
  42.5 6.8 %copy-start.6 = (bf16[64,512]{1,0:T(8,128)(2,1)}, bf16[64,512]{1,0:T(8,128)(2,1)S(1)}, u32[]{:S(2)}) copy-start(bf16[64,512]{1,0:T(8,128)(2,1)S(1)} %maximum_select_fusion.5) | copy-start | bytes 196612
  42.5 6.8 %collective-permute-start.5 = (bf16[64,512]{1,0:T(8,128)(2,1)S(1)}, bf16[64,512]{1,0:T(8,128)(2,1)}, u32[]{:S(2)}, u32[]{:S(2)}) collective-permute-start(bf16[64,512]{1,0:T(8,128)(2,1)S(1)} %maximum_select_fusion.5), channel_id=1, source_target_pairs={{0,256},{4,260},{8,264},{12,268},{16,272},{20,276},{24,280},{28,28... | collective-permute-start | bytes 196616 | tf_op jit(solution)/shard_map/ppermute | solution.py:120
  50.3 8.5 %collective-permute-start.6 = (bf16[128,512]{1,0:T(8,128)(2,1)S(1)}, bf16[128,512]{1,0:T(8,128)(2,1)}, u32[]{:S(2)}, u32[]{:S(2)}) collective-permute-start(bf16[128,512]{1,0:T(8,128)(2,1)S(1)} %maximum_select_fusion.4), channel_id=1, source_target_pairs={{0,16},{4,20},{8,24},{12,28},{16,0},{20,4},{24,8},{28,12},{32,48},... | collective-permute-start | bytes 393224 | tf_op jit(solution)/shard_map/ppermute | solution.py:120
  59.9 7.5 %collective-permute-start.7 = (bf16[256,512]{1,0:T(8,128)(2,1)S(1)}, bf16[256,512]{1,0:T(8,128)(2,1)}, u32[]{:S(2)}, u32[]{:S(2)}) collective-permute-start(bf16[256,512]{1,0:T(8,128)(2,1)S(1)} %maximum_select_fusion.3), channel_id=1, source_target_pairs={{0,128},{4,132},{8,136},{12,140},{16,144},{20,148},{24,152},{28,15... | collective-permute-start | bytes 786440 | tf_op jit(solution)/shard_map/ppermute | solution.py:120
  62.6 7.9 %copy-start.9 = (f32[4,128]{1,0:T(4,128)S(1)}, f32[4,128]{1,0:T(4,128)}, u32[]{:S(2)}) copy-start(f32[4,128]{1,0:T(4,128)} %param.22) | copy-start | bytes 6148
  62.6 9.9 %copy-start.7 = (bf16[256,2,128]{2,1,0:T(2,128)(2,1)S(1)}, bf16[256,2,128]{2,1,0:T(2,128)(2,1)}, u32[]{:S(2)}) copy-start(bf16[256,2,128]{2,1,0:T(2,128)(2,1)} %get-tuple-element.16) | copy-start | bytes 393220
  68.6 11.2 %collective-permute-start.8 = (bf16[512,512]{1,0:T(8,128)(2,1)S(1)}, bf16[512,512]{1,0:T(8,128)(2,1)}, u32[]{:S(2)}, u32[]{:S(2)}) collective-permute-start(bf16[512,512]{1,0:T(8,128)(2,1)S(1)} %maximum_select_fusion.2), channel_id=1, source_target_pairs={{0,8},{4,12},{8,0},{12,4},{16,24},{20,28},{24,16},{28,20},{32,40},... | collective-permute-start | bytes 1572872 | tf_op jit(solution)/shard_map/ppermute | solution.py:120
  76.4 13.2 %copy-start.3 = (f32[256,2,256]{0,2,1:T(8,128)S(1)}, f32[256,2,256]{0,2,1:T(8,128)}, u32[]{:S(2)}) copy-start(f32[256,2,256]{0,2,1:T(8,128)} %get-tuple-element.19) | copy-start | bytes 1572868
  76.4 13.2 %copy-start.10 = (f32[256]{0:T(256)S(1)}, f32[256]{0:T(256)}, u32[]{:S(2)}) copy-start(f32[256]{0:T(256)} %param.23) | copy-start | bytes 3076
  81.3 33.7 %collective-permute-start.9 = (bf16[1024,512]{1,0:T(8,128)(2,1)S(1)}, bf16[1024,512]{1,0:T(8,128)(2,1)}, u32[]{:S(2)}, u32[]{:S(2)}) collective-permute-start(bf16[1024,512]{1,0:T(8,128)(2,1)S(1)} %maximum_select_fusion.1), channel_id=1, source_target_pairs={{0,4},{4,0},{8,12},{12,8},{16,20},{20,16},{24,28},{28,24},{32,36},... | collective-permute-start | bytes 3145736 | tf_op jit(solution)/shard_map/ppermute | solution.py:120
  89.7 11.0 %collective-permute-start = (bf16[256,512]{0,1:T(8,128)(2,1)S(1)}, bf16[256,512]{0,1:T(8,128)(2,1)S(1)}, u32[]{:S(2)}, u32[]{:S(2)}) collective-permute-start(bf16[256,512]{0,1:T(8,128)(2,1)S(1)} %bitcast.84), channel_id=1, source_target_pairs={{0,1},{1,2},{2,3},{3,0},{4,5},{5,6},{6,7},{7,4},{8,9},{9,10},{10,1... | collective-permute-start | bytes 786440 | tf_op jit(solution)/shard_map/ppermute | solution.py:77
  92.9 14.6 %collective-permute-start.1 = (bf16[256,512]{0,1:T(8,128)(2,1)S(1)}, bf16[256,512]{0,1:T(8,128)(2,1)S(1)}, u32[]{:S(2)}, u32[]{:S(2)}) collective-permute-start(bf16[256,512]{0,1:T(8,128)(2,1)S(1)} %bitcast.85), channel_id=1, source_target_pairs={{0,2},{1,3},{2,0},{3,1},{4,6},{5,7},{6,4},{7,5},{8,10},{9,11},{10,... | collective-permute-start | bytes 786440 | tf_op jit(solution)/shard_map/ppermute | solution.py:77
  97.3 11.3 %collective-permute-start.2 = (bf16[256,512]{0,1:T(8,128)(2,1)S(1)}, bf16[256,512]{0,1:T(8,128)(2,1)}, u32[]{:S(2)}, u32[]{:S(2)}) collective-permute-start(bf16[256,512]{0,1:T(8,128)(2,1)S(1)} %bitcast.86), channel_id=1, source_target_pairs={{0,3},{1,0},{2,1},{3,2},{4,7},{5,4},{6,5},{7,6},{8,11},{9,8},{10,9... | collective-permute-start | bytes 786440 | tf_op jit(solution)/shard_map/ppermute | solution.py:77
  117.2 1.0 copy-start.11
  118.8 11.1 %collective-permute-start.10 = (bf16[256,512]{1,0:T(8,128)(2,1)S(1)}, bf16[256,512]{1,0:T(8,128)(2,1)S(1)}, u32[]{:S(2)}, u32[]{:S(2)}) collective-permute-start(bf16[256,512]{1,0:T(8,128)(2,1)S(1)} %fusion.21), channel_id=1, source_target_pairs={{0,1},{1,2},{2,3},{3,0},{4,5},{5,6},{6,7},{7,4},{8,9},{9,10},{10,1... | collective-permute-start | bytes 786440 | tf_op jit(solution)/shard_map/ppermute | solution.py:77
  123.6 12.7 %collective-permute-start.11 = (bf16[256,512]{1,0:T(8,128)(2,1)S(1)}, bf16[256,512]{1,0:T(8,128)(2,1)S(1)}, u32[]{:S(2)}, u32[]{:S(2)}) collective-permute-start(bf16[256,512]{1,0:T(8,128)(2,1)S(1)} %fusion.21), channel_id=1, source_target_pairs={{0,2},{1,3},{2,0},{3,1},{4,6},{5,7},{6,4},{7,5},{8,10},{9,11},{10,... | collective-permute-start | bytes 786440 | tf_op jit(solution)/shard_map/ppermute | solution.py:77
  126.8 10.4 %collective-permute-start.12 = (bf16[256,512]{1,0:T(8,128)(2,1)S(1)}, bf16[256,512]{1,0:T(8,128)(2,1)S(1)}, u32[]{:S(2)}, u32[]{:S(2)}) collective-permute-start(bf16[256,512]{1,0:T(8,128)(2,1)S(1)} %fusion.21), channel_id=1, source_target_pairs={{0,3},{1,0},{2,1},{3,2},{4,7},{5,4},{6,5},{7,6},{8,11},{9,8},{10,9... | collective-permute-start | bytes 786440 | tf_op jit(solution)/shard_map/ppermute | solution.py:77
  140.7 27.1 %copy-start.12 = (f32[2048]{0:T(1024)S(1)}, f32[2048]{0:T(1024)}, u32[]{:S(2)}) copy-start(f32[2048]{0:T(1024)} %param.26) | copy-start | bytes 24580
  167.8 15.4 %copy-start.1 = (bf16[2048,768]{1,0:T(8,128)(2,1)}, bf16[2048,768]{1,0:T(8,128)(2,1)S(1)}, u32[]{:S(2)}) copy-start(bf16[2048,768]{1,0:T(8,128)(2,1)S(1)} %slice.100) | copy-start | bytes 9437188
  175.3 11.5 %collective-permute-start.13 = (bf16[256,512]{1,0:T(8,128)(2,1)S(1)}, bf16[256,512]{1,0:T(8,128)(2,1)S(1)}, u32[]{:S(2)}, u32[]{:S(2)}) collective-permute-start(bf16[256,512]{1,0:T(8,128)(2,1)S(1)} %convolution_convert_fusion.2), channel_id=1, source_target_pairs={{0,1},{1,2},{2,3},{3,0},{4,5},{5,6},{6,7},{7,4},{8,9},{9,10},{10,1... | collective-permute-start | bytes 786440 | tf_op jit(solution)/shard_map/ppermute | solution.py:100
  178.9 13.8 %collective-permute-start.14 = (bf16[256,512]{1,0:T(8,128)(2,1)S(1)}, bf16[256,512]{1,0:T(8,128)(2,1)S(1)}, u32[]{:S(2)}, u32[]{:S(2)}) collective-permute-start(bf16[256,512]{1,0:T(8,128)(2,1)S(1)} %convolution_convert_fusion.1), channel_id=1, source_target_pairs={{0,2},{1,3},{2,0},{3,1},{4,6},{5,7},{6,4},{7,5},{8,10},{9,11},{10,... | collective-permute-start | bytes 786440 | tf_op jit(solution)/shard_map/ppermute | solution.py:100
  183.7 10.7 %collective-permute-start.15 = (bf16[256,512]{1,0:T(8,128)(2,1)S(1)}, bf16[256,512]{1,0:T(8,128)(2,1)}, u32[]{:S(2)}, u32[]{:S(2)}) collective-permute-start(bf16[256,512]{1,0:T(8,128)(2,1)S(1)} %convolution_convert_fusion), channel_id=1, source_target_pairs={{0,3},{1,0},{2,1},{3,2},{4,7},{5,4},{6,5},{7,6},{8,11},{9,8},{10,9... | collective-permute-start | bytes 786440 | tf_op jit(solution)/shard_map/ppermute | solution.py:100
Sparse Core Ops, SparseCore 0:
  10.5 155.1 all-gather.1

commit v6 on v5

--- a/solution.py
+++ b/solution.py
@@ -1,7 +1,7 @@
 import jax
 import jax.numpy as jnp
 from jax import lax
-from jax.sharding import PartitionSpec as P
+from jax.sharding import Mesh, PartitionSpec as P
 
 D = 2048
 
@@ -82,16 +82,15 @@
     return jnp.concatenate([gathered[k] for k in range(axis_size)], axis=1)
 
 
-def down_and_scatter(hidden_act, down_full, axis_size):
+def down_and_scatter(hidden_act, down_full, axis_size, rows):
     index = lax.axis_index("mlp")
-    width = down_full.shape[0] // axis_size
 
     def block_for(target):
-        rows = lax.dynamic_slice_in_dim(down_full, target * width, width, 0)
+        weight_rows = down_block_rows(down_full, target, rows)
         value = lax.dot_general(
-            hidden_act, rows, (((1,), (1,)), ((), ())), preferred_element_type=jnp.float32
-        )
-        return value.astype(jnp.bfloat16)
+            hidden_act, weight_rows, (((1,), (1,)), ((), ())), preferred_element_type=jnp.float32
+        )
+        return block_to_req_order(value.astype(jnp.bfloat16), rows)
 
     incoming = []
     for shift in range(1, axis_size):
@@ -107,29 +106,39 @@
     return total
 
 
-DOUBLING_BITS = (4, 3, 6, 2, 5, 1, 0)
-
-
-def req_gather_by_permutes(block):
-    size = lax.axis_size("req")
-    index = lax.axis_index("req")
-    rows, width = block.shape
-    bits = [b for b in DOUBLING_BITS if (1 << b) < size]
-    out = block
-    for bit in bits:
-        partner = lax.ppermute(out, "req", [(r, r ^ (1 << bit)) for r in range(size)])
-        upper = (index >> bit) & 1
-        out = jnp.where(
-            upper == 1,
-            jnp.concatenate([partner, out], axis=0),
-            jnp.concatenate([out, partner], axis=0),
-        )
-    count = len(bits)
-    out = out.reshape((2,) * count + (rows, width))
-    axis_of_bit = {bits[count - 1 - j]: j for j in range(count)}
-    order = [axis_of_bit[b] for b in range(count - 1, -1, -1)]
-    out = out.transpose(order + [count, count + 1])
-    return out.reshape(size * rows, width)
+REQ_PARTS = ("x", "z", "c")
+
+
+def gather_rows(block):
+    out = lax.all_gather(block, "x", axis=0, tiled=True)
+    out = lax.all_gather(out, "z", axis=0, tiled=True)
+    other = lax.ppermute(out, "c", [(0, 1), (1, 0)])
+    return jnp.concatenate([out, other], axis=0)
+
+
+def to_gathered_order(act, rows):
+    nx, nz, nc = [lax.axis_size(name) for name in REQ_PARTS]
+    n = act.shape[0]
+    own = lax.axis_index("c")
+    split = act.reshape(n, nx, nz, nc, rows)
+    split = jnp.where(own == 0, split, split[:, :, :, ::-1, :])
+    return split.transpose(0, 3, 2, 1, 4).reshape(n, -1)
+
+
+def down_block_rows(down_full, target, rows):
+    nx, nz, nc = [lax.axis_size(name) for name in REQ_PARTS]
+    split = down_full.reshape(nc, nz, nx, rows, down_full.shape[1])
+    picked = lax.dynamic_index_in_dim(split, target, 2, keepdims=False)
+    return picked.reshape(nc * nz * rows, down_full.shape[1])
+
+
+def block_to_req_order(value, rows):
+    nx, nz, nc = [lax.axis_size(name) for name in REQ_PARTS]
+    n = value.shape[0]
+    own = lax.axis_index("c")
+    split = value.reshape(n, nc, nz, rows)
+    split = jnp.where(own == 0, split, split[:, ::-1, :, :])
+    return split.transpose(0, 2, 1, 3).reshape(n, -1)
 
 
 def per_device(
@@ -148,51 +157,56 @@
     up_weight,
     down_weight_t,
 ):
-    widths = [gate_weight.shape[1], up_weight.shape[1], down_weight_t.shape[1]]
-    packed = jnp.concatenate([gate_weight, up_weight, down_weight_t], axis=1)
-    gathered = lax.all_gather(packed, "req", axis=0, tiled=True)
+    widths = [out_weight.shape[1], gate_weight.shape[1], up_weight.shape[1], down_weight_t.shape[1]]
+    packed = jnp.concatenate([out_weight, gate_weight, up_weight, down_weight_t], axis=1)
+    gathered = gather_rows(packed)
     bounds = [0]
     for w in widths:
         bounds.append(bounds[-1] + w)
-    gate_full, up_full, down_full = [
-        gathered[:, bounds[i] : bounds[i + 1]] for i in range(3)
+    out_full, gate_full, up_full, down_full = [
+        gathered[:, bounds[i] : bounds[i + 1]] for i in range(4)
     ]
-    out_full = req_gather_by_permutes(out_weight)
     attn_out = attend(
         queries, new_kv, cache_pool, page_table, assignment, lengths, lambda_vectors, subln_gain
     )
     mlp_size = D // residual.shape[1]
     heads_all = mlp_gather(attn_out, mlp_size)
-    projected = jnp.dot(heads_all, out_full, preferred_element_type=jnp.float32)
+    rows = out_weight.shape[0]
+    projected = jnp.dot(
+        to_gathered_order(heads_all, rows), out_full, preferred_element_type=jnp.float32
+    )
     stream = (residual.astype(jnp.float32) + projected).astype(jnp.bfloat16)
     stream_all = mlp_gather(stream, mlp_size).astype(jnp.float32)
     squares = jnp.sum(stream_all * stream_all, axis=1, keepdims=True)
     normed = (stream_all * lax.rsqrt(squares / D + 1e-05) * norm_gain).astype(jnp.bfloat16)
+    normed = to_gathered_order(normed, rows)
     gate_value = jnp.dot(normed, gate_full, preferred_element_type=jnp.float32)
     up_value = jnp.dot(normed, up_full, preferred_element_type=jnp.float32)
     hidden_act = (jax.nn.silu(gate_value) * up_value).astype(jnp.bfloat16)
-    summed = down_and_scatter(hidden_act, down_full, mlp_size)
+    summed = down_and_scatter(hidden_act, down_full, mlp_size, out_weight.shape[0])
     return (stream.astype(jnp.float32) + summed).astype(jnp.bfloat16)
 
 
 def solution(mesh):
+    split = Mesh(mesh.devices.reshape(4, 16, 2, mesh.devices.shape[1]), REQ_PARTS + ("mlp",))
+    req = REQ_PARTS
     in_specs = (
-        P("req", "mlp", None),
-        P("req", "mlp", None),
-        P("req", None, "mlp", None),
-        P("req", None),
-        P("req"),
-        P(),
-        P(),
-        P(),
-        P("req", "mlp"),
-        P("req", "mlp"),
-        P(),
-        P("req", "mlp"),
-        P("req", "mlp"),
-        P("req", "mlp"),
-    )
-    out_specs = P("req", "mlp")
+        P(req, "mlp", None),
+        P(req, "mlp", None),
+        P(req, None, "mlp", None),
+        P(req, None),
+        P(req),
+        P(),
+        P(),
+        P(),
+        P(req, "mlp"),
+        P(req, "mlp"),
+        P(),
+        P(req, "mlp"),
+        P(req, "mlp"),
+        P(req, "mlp"),
+    )
+    out_specs = P(req, "mlp")
     return jax.shard_map(
-        per_device, mesh=mesh, in_specs=in_specs, out_specs=out_specs, check_vma=False
-    )
+        per_device, mesh=split, in_specs=in_specs, out_specs=out_specs, check_vma=False
+    )

time: 206 us -> 256 us (1.24)
  waiting for transfers between devices: 58.5 us -> 103 us
  starting transfers between devices: 73.2 us -> 41.2 us
  local copies, waits for them, and re-layouts: 16.3 us -> 39.1 us
  blocking collectives: 0 us -> 11.5 us
    all_gather x1, waiting for transfers between devices: 25 us -> 86.1 us  [gather_rows(): out = lax.all_gather(out, 'z', axis=0, tiled=True)]
    ppermute x7 -> x1, starting transfers between devices: 40.9 us -> 7.52 us  [gather_rows(): other = lax.ppermute(out, 'c', [(0, 1), (1, 0)])]
    all_gather x0 -> x1, blocking collectives: none -> 11.5 us  [gather_rows(): out = lax.all_gather(block, 'x', axis=0, tiled=True)]
    ppermute x7 -> x1, waiting for transfers between devices: 10.5 us -> 0.01 us  [gather_rows(): other = lax.ppermute(out, 'c', [(0, 1), (1, 0)])]
    select_n x7 -> x0, other arithmetic: 6.93 us -> none  [req_gather_by_permutes(): jnp.where(upper == 1, jnp.concatenate([partner, out], axis=0), jnp.concat...]
    unnamed x31 -> x38, local copies, waits for them, and re-layouts: 2.81 us -> 7.7 us
    convert_element_type x0 -> x6, local copies, waits for them, and re-layouts: none -> 4.79 us  [the longest x4 4.56 us: block_for(): return block_to_req_order(value.astype(jnp.bfloat16), rows)]
    convert_element_type x0 -> x3, other arithmetic: none -> 4.56 us  [the longest x1 1.91 us: per_device(): return (stream.astype(jnp.float32) + summed).astype(jnp.bfloat16)]
  transfers between devices with their start and end apart: 17 -> 11, of which waited for: 12 -> 8; matrix products, arithmetic and copies ran while one was open for 20% -> 19% of each run, Pallas kernels for 0% -> 0%
where the time goes in v6:
time: 256 us; the launch traced here: 253 us
  waiting for transfers between devices  103 us (40%)
  starting transfers between devices  41.2 us (16%)
  local copies, waits for them, and re-layouts  39.1 us (15%)
  matrix products  22.7 us (9%)
  other arithmetic  18.7 us (7%)
  between operations  16 us (6%)
  blocking collectives  11.5 us (4%)
    all_gather x1, waiting for transfers between devices, gather_rows(): out = lax.all_gather(out, 'z', axis=0, tiled=True)  86.1 us
    ppermute x6, starting transfers between devices, mlp_gather(): lax.ppermute(block, 'mlp', [(i, (i + shift) % axis_size) for i in range(a...  21.9 us
    ppermute x3, starting transfers between devices, down_and_scatter(): lax.ppermute(block_for(target), 'mlp', [(i, (i + shift) % axis_size) for...  11.8 us
    all_gather x1, blocking collectives, gather_rows(): out = lax.all_gather(block, 'x', axis=0, tiled=True)  11.5 us
    ppermute x6, waiting for transfers between devices, mlp_gather(): lax.ppermute(block, 'mlp', [(i, (i + shift) % axis_size) for i in range(a...  11.4 us
    unnamed x38, local copies, waits for them, and re-layouts  7.7 us
    ppermute x1, starting transfers between devices, gather_rows(): other = lax.ppermute(out, 'c', [(0, 1), (1, 0)])  7.52 us
    gather x2, local copies, waits for them, and re-layouts, attend(): pages = jnp.take(cache_pool, page_table[0], axis=0)  7.33 us
  transfers between devices with their start and end apart: 11, of which 8 were waited for; matrix products, arithmetic and copies ran while one was open for 19% of the time, Pallas kernels for 0%

profile of v6, /device:TPU:1, one launch (start us, length us, event | category | flops | bytes accessed | tf_op | source)
XLA Modules:
  0.0 252.6 jit_solution(10610634232479983191)
XLA Ops:
  7.4 11.5 %all_gather.6 = bf16[64,2816]{1,0:T(8,128)(2,1)} all-gather(bf16[16,2816]{1,0:T(8,128)(2,1)S(1)} %pad_maximum_fusion.15), channel_id=1, replica_groups=mesh['x'=4,'z'=16,'c'=2,'mlp'=4] {'x'}, dimensions={0}, use_global_device_ids=true | all-gather | bytes 450560 | tf_op jit(solution)/shard_map/all_gather | solution.py:113
  18.9 86.1 %all-gather.2.cloned.1.call-done = bf16[1024,2816]{1,0:T(8,128)(2,1)} async-done(((bf16[64,2816]{1,0:T(8,128)(2,1)}), bf16[1024,2816]{1,0:T(8,128)(2,1)}) %all-gather.2.cloned.1.call-update) | async-done | bytes 5767184 | tf_op jit(solution)/shard_map/all_gather | solution.py:114
  105.1 7.5 %collective-permute-start.3 = (bf16[1024,2816]{1,0:T(8,128)(2,1)}, bf16[1024,2816]{1,0:T(8,128)(2,1)}, u32[]{:S(2)}, u32[]{:S(2)}) collective-permute-start(bf16[1024,2816]{1,0:T(8,128)(2,1)} %all-gather.2.cloned.1.call-done), channel_id=1, source_target_pairs={{0,4},{4,0},{1,5},{5,1},{2,6},{6,2},{3,7},{7,3},{8,12},{12,8},{9,1... | collective-permute-start | bytes 17301512 | tf_op jit(solution)/shard_map/ppermute | solution.py:115
  113.3 5.6 %gather_fusion = bf16[6,128,2,512]{3,2,1,0:T(2,128)(2,1)} fusion(bf16[6,128,2,512]{3,2,1,0:T(2,128)(2,1)S(1)} %copy-done, s32[1024]{0:T(1024)S(1)} %pad_clamp_fusion.1), kind=kCustom, calls=%fused_computation.2 | custom fusion | bytes 3145752 | tf_op jit(solution)/shard_map/jit(_take)/gather | solution.py:23
  126.0 1.8 fusion.99
  129.3 2.3 fusion.100
  131.6 3.2 %fusion.13 = f32[256,2,256]{0,2,1:T(8,128)} fusion(f32[256,2]{0,1:T(2,128)S(1)} %fusion.100, pred[256,1024]{0,1:T(8,128)(4,1)S(1)} %pad_add_fusion, bf16[768,2,512]{2,0,1:T(8,128)(2,1)S(1)} %copy-done.3, bf16[256,2,512]{2,0,1:T(8,128)(2,1)} %copy.64, bf16[256,2,128]{2,1,0:T(2,128)(2,1)} %get-tuple-element.25), kind=kOutput, calls=%fused_computation.29 | convolution fusion | flops 408552960 | bytes 5376000 | tf_op jit(solution)/shard_map/nhk,khd->nhd/dot_general | solution.py:47
  134.8 2.0 fusion.105
  136.8 3.4 %multiply_reduce_fusion.1 = (f32[256,2]{0,1:T(2,128)S(1)}, f32[256,2,256]{0,2,1:T(8,128)}) fusion(f32[256,2,256]{0,2,1:T(8,128)} %fusion.13, f32[256,2]{0,1:T(2,128)S(1)} %fusion.105, pred[256,1024]{0,1:T(8,128)(4,1)S(1)} %pad_add_fusion, bf16[256,2,512]{2,0,1:T(8,128)(2,1)} %copy.64, bf16[768,2,512]{2,0,1:T(8,128)(2,1)S(1)} %copy-done.3, ...), kind=kOutput, calls=%fused_computation.64 | convolution fusion | flops 409076736 | bytes 5902340 | tf_op jit(solution)/shard_map/nhk,khd->nhd/dot_general | solution.py:47
  141.3 3.3 %collective-permute-start = (bf16[256,512]{0,1:T(8,128)(2,1)S(1)}, bf16[256,512]{0,1:T(8,128)(2,1)S(1)}, u32[]{:S(2)}, u32[]{:S(2)}) collective-permute-start(bf16[256,512]{0,1:T(8,128)(2,1)S(1)} %bitcast.130), channel_id=1, source_target_pairs={{0,1},{1,2},{2,3},{3,0},{4,5},{5,6},{6,7},{7,4},{8,9},{9,10},{10,1... | collective-permute-start | bytes 786440 | tf_op jit(solution)/shard_map/ppermute | solution.py:77
  144.6 4.3 %collective-permute-start.1 = (bf16[256,512]{0,1:T(8,128)(2,1)S(1)}, bf16[256,512]{0,1:T(8,128)(2,1)S(1)}, u32[]{:S(2)}, u32[]{:S(2)}) collective-permute-start(bf16[256,512]{0,1:T(8,128)(2,1)S(1)} %bitcast.131), channel_id=1, source_target_pairs={{0,2},{1,3},{2,0},{3,1},{4,6},{5,7},{6,4},{7,5},{8,10},{9,11},{10,... | collective-permute-start | bytes 786440 | tf_op jit(solution)/shard_map/ppermute | solution.py:77
  148.9 3.1 %collective-permute-start.2 = (bf16[256,512]{0,1:T(8,128)(2,1)S(1)}, bf16[256,512]{0,1:T(8,128)(2,1)S(1)}, u32[]{:S(2)}, u32[]{:S(2)}) collective-permute-start(bf16[256,512]{0,1:T(8,128)(2,1)S(1)} %bitcast.132), channel_id=1, source_target_pairs={{0,3},{1,0},{2,1},{3,2},{4,7},{5,4},{6,5},{7,6},{8,11},{9,8},{10,9... | collective-permute-start | bytes 786440 | tf_op jit(solution)/shard_map/ppermute | solution.py:77
  152.4 6.7 %collective-permute-done.1 = bf16[256,512]{0,1:T(8,128)(2,1)S(1)} collective-permute-done((bf16[256,512]{0,1:T(8,128)(2,1)S(1)}, bf16[256,512]{0,1:T(8,128)(2,1)S(1)}, u32[]{:S(2)}, u32[]{:S(2)}) %collective-permute-start.1) | collective-permute-done | bytes 262176 | tf_op jit(solution)/shard_map/ppermute | solution.py:77
  160.9 2.4 pad_maximum_fusion
  163.2 2.9 %gather_fusion.1 = bf16[4,256,512]{1,2,0:T(8,128)(2,1)} fusion(bf16[4,256,512]{1,2,0:T(8,128)(2,1)} %pad_maximum_fusion, s32[1024]{0:T(1024)S(1)} %pad_clamp_fusion), kind=kCustom, calls=%fused_computation.clone | custom fusion | bytes 2097168 | tf_op jit(solution)/shard_map/jit(_take)/gather | solution.py:81
  170.1 3.0 %constant_dynamic-update-slice_fusion = bf16[2048,2816]{1,0:T(8,128)(2,1)S(1)} fusion(bf16[2048,2816]{1,0:T(8,128)(2,1)S(1)} %constant_dynamic-update-slice_fusion.1, bf16[1024,2816]{1,0:T(8,128)(2,1)} %collective-permute-done.3), kind=kLoop, calls=%fused_computation.82 | loop fusion | bytes 11534336 | tf_op jit(solution)/shard_map/concatenate | solution.py:116
  173.1 4.3 %copy-done.1 = bf16[2048,2816]{1,0:T(8,128)(2,1)} copy-done((bf16[2048,2816]{1,0:T(8,128)(2,1)}, bf16[2048,2816]{1,0:T(8,128)(2,1)S(1)}, u32[]{:S(2)}) %copy-start.1) | copy-done | bytes 11534360
  178.2 4.8 %collective-permute-start.4 = (bf16[256,512]{1,0:T(8,128)(2,1)S(1)}, bf16[256,512]{1,0:T(8,128)(2,1)S(1)}, u32[]{:S(2)}, u32[]{:S(2)}) collective-permute-start(bf16[256,512]{1,0:T(8,128)(2,1)S(1)} %fusion.17), channel_id=1, source_target_pairs={{0,1},{1,2},{2,3},{3,0},{4,5},{5,6},{6,7},{7,4},{8,9},{9,10},{10,1... | collective-permute-start | bytes 786440 | tf_op jit(solution)/shard_map/ppermute | solution.py:77
  183.0 3.2 %collective-permute-start.5 = (bf16[256,512]{1,0:T(8,128)(2,1)S(1)}, bf16[256,512]{1,0:T(8,128)(2,1)S(1)}, u32[]{:S(2)}, u32[]{:S(2)}) collective-permute-start(bf16[256,512]{1,0:T(8,128)(2,1)S(1)} %fusion.17), channel_id=1, source_target_pairs={{0,2},{1,3},{2,0},{3,1},{4,6},{5,7},{6,4},{7,5},{8,10},{9,11},{10,... | collective-permute-start | bytes 786440 | tf_op jit(solution)/shard_map/ppermute | solution.py:77
  186.2 3.2 %collective-permute-start.6 = (bf16[256,512]{1,0:T(8,128)(2,1)S(1)}, bf16[256,512]{1,0:T(8,128)(2,1)S(1)}, u32[]{:S(2)}, u32[]{:S(2)}) collective-permute-start(bf16[256,512]{1,0:T(8,128)(2,1)S(1)} %fusion.17), channel_id=1, source_target_pairs={{0,3},{1,0},{2,1},{3,2},{4,7},{5,4},{6,5},{7,6},{8,11},{9,8},{10,9... | collective-permute-start | bytes 786440 | tf_op jit(solution)/shard_map/ppermute | solution.py:77
  189.6 2.1 slice.105
  193.2 2.6 %collective-permute-done.5 = bf16[256,512]{1,0:T(8,128)(2,1)S(1)} collective-permute-done((bf16[256,512]{1,0:T(8,128)(2,1)S(1)}, bf16[256,512]{1,0:T(8,128)(2,1)S(1)}, u32[]{:S(2)}, u32[]{:S(2)}) %collective-permute-start.5) | collective-permute-done | bytes 262176 | tf_op jit(solution)/shard_map/ppermute | solution.py:77
  197.6 1.8 gather_fusion.2
  203.3 2.9 %fusion.4 = f32[256,768]{1,0:T(8,128)S(1)} fusion(bf16[256,2048]{0,1:T(8,128)(2,1)S(1)} %bitcast.122, bf16[2048,2816]{1,0:T(8,128)(2,1)} %copy-done.1), kind=kOutput, calls=%fused_computation.7 | convolution fusion | flops 805306368 | bytes 4980736 | tf_op jit(solution)/shard_map/dot_general | solution.py:183
  206.2 3.0 %multiply_convert_fusion.1 = bf16[256,768]{1,0:T(8,128)(2,1)S(1)} fusion(f32[256,768]{1,0:T(8,128)S(1)} %fusion.4, bf16[256,2048]{0,1:T(8,128)(2,1)S(1)} %bitcast.123, bf16[2048,2816]{1,0:T(8,128)(2,1)} %copy-done.1), kind=kOutput, calls=%fused_computation.55 | convolution fusion | flops 806486016 | bytes 5373952 | tf_op jit(solution)/shard_map/dot_general | solution.py:184
  216.7 5.6 %collective-permute-start.7 = (bf16[256,512]{1,0:T(8,128)(2,1)}, bf16[256,512]{1,0:T(8,128)(2,1)}, u32[]{:S(2)}, u32[]{:S(2)}) collective-permute-start(bf16[256,512]{1,0:T(8,128)(2,1)} %copy.81), channel_id=1, source_target_pairs={{0,1},{1,2},{2,3},{3,0},{4,5},{5,6},{6,7},{7,4},{8,9},{9,10},{10,1... | collective-permute-start | bytes 786440 | tf_op jit(solution)/shard_map/ppermute | solution.py:99
  222.4 2.2 convolution_convert_fusion
  230.7 2.4 collective-permute-start.8
  233.9 3.8 %collective-permute-start.9 = (bf16[256,512]{1,0:T(8,128)(2,1)}, bf16[256,512]{1,0:T(8,128)(2,1)}, u32[]{:S(2)}, u32[]{:S(2)}) collective-permute-start(bf16[256,512]{1,0:T(8,128)(2,1)} %copy.88), channel_id=1, source_target_pairs={{0,3},{1,0},{2,1},{3,2},{4,7},{5,4},{6,5},{7,6},{8,11},{9,8},{10,9... | collective-permute-start | bytes 786440 | tf_op jit(solution)/shard_map/ppermute | solution.py:99
  238.0 3.3 %collective-permute-done.8 = bf16[256,512]{1,0:T(8,128)(2,1)S(1)} collective-permute-done((bf16[256,512]{1,0:T(8,128)(2,1)}, bf16[256,512]{1,0:T(8,128)(2,1)S(1)}, u32[]{:S(2)}, u32[]{:S(2)}) %collective-permute-start.8) | collective-permute-done | bytes 262176 | tf_op jit(solution)/shard_map/ppermute | solution.py:99
  241.3 2.6 %collective-permute-done.9 = bf16[256,512]{1,0:T(8,128)(2,1)} collective-permute-done((bf16[256,512]{1,0:T(8,128)(2,1)}, bf16[256,512]{1,0:T(8,128)(2,1)}, u32[]{:S(2)}, u32[]{:S(2)}) %collective-permute-start.9) | collective-permute-done | bytes 262176 | tf_op jit(solution)/shard_map/ppermute | solution.py:99
  243.9 1.9 add_convert_fusion
  (101 shorter events, 37.8 us)
Async XLA Ops:
  6.5 106.7 %copy-start = (bf16[6,128,2,512]{3,2,1,0:T(2,128)(2,1)S(1)}, bf16[6,128,2,512]{3,2,1,0:T(2,128)(2,1)}, u32[]{:S(2)}) copy-start(bf16[6,128,2,512]{3,2,1,0:T(2,128)(2,1)} %param.18) | copy-start | bytes 4718596
  6.5 98.5 %all-gather.2.cloned.1.call-start = ((), (), s32[]{:S(2)}) async-start(), calls=%async_computation | async-start | bytes 6127616 | tf_op jit(solution)/shard_map/all_gather | solution.py:114
  105.1 65.0 %collective-permute-start.3 = (bf16[1024,2816]{1,0:T(8,128)(2,1)}, bf16[1024,2816]{1,0:T(8,128)(2,1)}, u32[]{:S(2)}, u32[]{:S(2)}) collective-permute-start(bf16[1024,2816]{1,0:T(8,128)(2,1)} %all-gather.2.cloned.1.call-done), channel_id=1, source_target_pairs={{0,4},{4,0},{1,5},{5,1},{2,6},{6,2},{3,7},{7,3},{8,12},{12,8},{9,1... | collective-permute-start | bytes 17301512 | tf_op jit(solution)/shard_map/ppermute | solution.py:115
  118.9 1.8 copy-start.6
  118.9 3.3 %copy-start.11 = (f32[4,128]{1,0:T(4,128)S(1)}, f32[4,128]{1,0:T(4,128)}, u32[]{:S(2)}) copy-start(f32[4,128]{1,0:T(4,128)} %param.22) | copy-start | bytes 6148
  118.9 5.3 %copy-start.14 = (s32[128]{0:T(128)S(1)}, s32[128]{0:T(128)}, u32[]{:S(2)}) copy-start(s32[128]{0:T(128)} %param.21) | copy-start | bytes 1540
  118.9 6.8 %copy-start.15 = (s32[1,6]{1,0:T(1,128)S(1)}, s32[1,6]{1,0:T(1,128)}, u32[]{:S(2)}) copy-start(s32[1,6]{1,0:T(1,128)} %param.19) | copy-start | bytes 76
  129.3 2.3 copy-start.3
  136.8 3.4 %copy-start.12 = (f32[256]{0:T(256)S(1)}, f32[256]{0:T(256)}, u32[]{:S(2)}) copy-start(f32[256]{0:T(256)} %param.23) | copy-start | bytes 3076
  141.3 11.0 %collective-permute-start = (bf16[256,512]{0,1:T(8,128)(2,1)S(1)}, bf16[256,512]{0,1:T(8,128)(2,1)S(1)}, u32[]{:S(2)}, u32[]{:S(2)}) collective-permute-start(bf16[256,512]{0,1:T(8,128)(2,1)S(1)} %bitcast.130), channel_id=1, source_target_pairs={{0,1},{1,2},{2,3},{3,0},{4,5},{5,6},{6,7},{7,4},{8,9},{9,10},{10,1... | collective-permute-start | bytes 786440 | tf_op jit(solution)/shard_map/ppermute | solution.py:77
  144.6 14.5 %collective-permute-start.1 = (bf16[256,512]{0,1:T(8,128)(2,1)S(1)}, bf16[256,512]{0,1:T(8,128)(2,1)S(1)}, u32[]{:S(2)}, u32[]{:S(2)}) collective-permute-start(bf16[256,512]{0,1:T(8,128)(2,1)S(1)} %bitcast.131), channel_id=1, source_target_pairs={{0,2},{1,3},{2,0},{3,1},{4,6},{5,7},{6,4},{7,5},{8,10},{9,11},{10,... | collective-permute-start | bytes 786440 | tf_op jit(solution)/shard_map/ppermute | solution.py:77
  148.9 11.2 %collective-permute-start.2 = (bf16[256,512]{0,1:T(8,128)(2,1)S(1)}, bf16[256,512]{0,1:T(8,128)(2,1)S(1)}, u32[]{:S(2)}, u32[]{:S(2)}) collective-permute-start(bf16[256,512]{0,1:T(8,128)(2,1)S(1)} %bitcast.132), channel_id=1, source_target_pairs={{0,3},{1,0},{2,1},{3,2},{4,7},{5,4},{6,5},{7,6},{8,11},{9,8},{10,9... | collective-permute-start | bytes 786440 | tf_op jit(solution)/shard_map/ppermute | solution.py:77
  152.4 7.8 %copy-start.7 = (bf16[256,512]{0,1:T(8,128)(2,1)}, bf16[256,512]{0,1:T(8,128)(2,1)S(1)}, u32[]{:S(2)}) copy-start(bf16[256,512]{0,1:T(8,128)(2,1)S(1)} %collective-permute-done) | copy-start | bytes 786436
  159.1 1.1 copy-start.8
  160.2 0.7 copy-start.9
  160.9 7.4 %slice-start = ((s8[5767168]{0:T(1024)(128)(4,1)}), s8[1572864]{0:T(1024)(128)(4,1)S(1)}, s32[]{:S(2)}) async-start(s8[5767168]{0:T(1024)(128)(4,1)} %bitcast.112), calls=%async_computation.1 | async-start | bytes 3145728
  167.5 2.2 slice-start.1
  170.0 7.4 %copy-start.13 = (bf16[256,512]{1,0:T(8,128)(2,1)S(1)}, bf16[256,512]{1,0:T(8,128)(2,1)}, u32[]{:S(2)}) copy-start(bf16[256,512]{1,0:T(8,128)(2,1)} %param.24) | copy-start | bytes 786436
  173.1 4.3 %copy-start.1 = (bf16[2048,2816]{1,0:T(8,128)(2,1)}, bf16[2048,2816]{1,0:T(8,128)(2,1)S(1)}, u32[]{:S(2)}) copy-start(bf16[2048,2816]{1,0:T(8,128)(2,1)S(1)} %constant_dynamic-update-slice_fusion) | copy-start | bytes 34603012
  173.1 16.3 %copy-start.10 = (f32[2048]{0:T(1024)S(1)}, f32[2048]{0:T(1024)}, u32[]{:S(2)}) copy-start(f32[2048]{0:T(1024)} %param.26) | copy-start | bytes 24580
  178.2 18.3 %copy-start.4 = (bf16[256,512]{1,0:T(8,128)(2,1)}, bf16[256,512]{1,0:T(8,128)(2,1)S(1)}, u32[]{:S(2)}) copy-start(bf16[256,512]{1,0:T(8,128)(2,1)S(1)} %fusion.17) | copy-start | bytes 786436
  178.2 15.0 %collective-permute-start.4 = (bf16[256,512]{1,0:T(8,128)(2,1)S(1)}, bf16[256,512]{1,0:T(8,128)(2,1)S(1)}, u32[]{:S(2)}, u32[]{:S(2)}) collective-permute-start(bf16[256,512]{1,0:T(8,128)(2,1)S(1)} %fusion.17), channel_id=1, source_target_pairs={{0,1},{1,2},{2,3},{3,0},{4,5},{5,6},{6,7},{7,4},{8,9},{9,10},{10,1... | collective-permute-start | bytes 786440 | tf_op jit(solution)/shard_map/ppermute | solution.py:77
  183.0 12.8 %collective-permute-start.5 = (bf16[256,512]{1,0:T(8,128)(2,1)S(1)}, bf16[256,512]{1,0:T(8,128)(2,1)S(1)}, u32[]{:S(2)}, u32[]{:S(2)}) collective-permute-start(bf16[256,512]{1,0:T(8,128)(2,1)S(1)} %fusion.17), channel_id=1, source_target_pairs={{0,2},{1,3},{2,0},{3,1},{4,6},{5,7},{6,4},{7,5},{8,10},{9,11},{10,... | collective-permute-start | bytes 786440 | tf_op jit(solution)/shard_map/ppermute | solution.py:77
  186.2 10.3 %collective-permute-start.6 = (bf16[256,512]{1,0:T(8,128)(2,1)S(1)}, bf16[256,512]{1,0:T(8,128)(2,1)S(1)}, u32[]{:S(2)}, u32[]{:S(2)}) collective-permute-start(bf16[256,512]{1,0:T(8,128)(2,1)S(1)} %fusion.17), channel_id=1, source_target_pairs={{0,3},{1,0},{2,1},{3,2},{4,7},{5,4},{6,5},{7,6},{8,11},{9,8},{10,9... | collective-permute-start | bytes 786440 | tf_op jit(solution)/shard_map/ppermute | solution.py:77
  206.2 3.0 %copy-start.2 = (bf16[2,16,1,16,768]{4,3,2,1,0:T(8,128)(2,1)S(1)}, bf16[2,16,1,16,768]{4,3,2,1,0:T(8,128)(2,1)}, u32[]{:S(2)}) copy-start(bf16[2,16,1,16,768]{4,3,2,1,0:T(8,128)(2,1)} %get-tuple-element.8) | copy-start | bytes 2359300
  216.7 21.3 %collective-permute-start.7 = (bf16[256,512]{1,0:T(8,128)(2,1)}, bf16[256,512]{1,0:T(8,128)(2,1)}, u32[]{:S(2)}, u32[]{:S(2)}) collective-permute-start(bf16[256,512]{1,0:T(8,128)(2,1)} %copy.81), channel_id=1, source_target_pairs={{0,1},{1,2},{2,3},{3,0},{4,5},{5,6},{6,7},{7,4},{8,9},{9,10},{10,1... | collective-permute-start | bytes 786440 | tf_op jit(solution)/shard_map/ppermute | solution.py:99
  229.8 14.1 %copy-start.5 = (bf16[256,512]{1,0:T(8,128)(2,1)S(1)}, bf16[256,512]{1,0:T(8,128)(2,1)}, u32[]{:S(2)}) copy-start(bf16[256,512]{1,0:T(8,128)(2,1)} %copy-done.4) | copy-start | bytes 786436
  230.7 10.6 %collective-permute-start.8 = (bf16[256,512]{1,0:T(8,128)(2,1)}, bf16[256,512]{1,0:T(8,128)(2,1)S(1)}, u32[]{:S(2)}, u32[]{:S(2)}) collective-permute-start(bf16[256,512]{1,0:T(8,128)(2,1)} %copy.85), channel_id=1, source_target_pairs={{0,2},{1,3},{2,0},{3,1},{4,6},{5,7},{6,4},{7,5},{8,10},{9,11},{10,... | collective-permute-start | bytes 786440 | tf_op jit(solution)/shard_map/ppermute | solution.py:99
  233.9 9.9 %collective-permute-start.9 = (bf16[256,512]{1,0:T(8,128)(2,1)}, bf16[256,512]{1,0:T(8,128)(2,1)}, u32[]{:S(2)}, u32[]{:S(2)}) collective-permute-start(bf16[256,512]{1,0:T(8,128)(2,1)} %copy.88), channel_id=1, source_target_pairs={{0,3},{1,0},{2,1},{3,2},{4,7},{5,4},{6,5},{7,6},{8,11},{9,8},{10,9... | collective-permute-start | bytes 786440 | tf_op jit(solution)/shard_map/ppermute | solution.py:99
Sparse Core Ops, SparseCore 0:
  19.1 85.9 all-gather.1

commit v7 on v6

--- a/solution.py
+++ b/solution.py
@@ -109,11 +109,14 @@
 REQ_PARTS = ("x", "z", "c")
 
 
-def gather_rows(block):
+def gather_over_xz(block):
     out = lax.all_gather(block, "x", axis=0, tiled=True)
-    out = lax.all_gather(out, "z", axis=0, tiled=True)
-    other = lax.ppermute(out, "c", [(0, 1), (1, 0)])
-    return jnp.concatenate([out, other], axis=0)
+    return lax.all_gather(out, "z", axis=0, tiled=True)
+
+
+def swap_with_core(rows_xz):
+    other = lax.ppermute(rows_xz, "c", [(0, 1), (1, 0)])
+    return jnp.concatenate([rows_xz, other], axis=0)
 
 
 def to_gathered_order(act, rows):
@@ -159,18 +162,20 @@
 ):
     widths = [out_weight.shape[1], gate_weight.shape[1], up_weight.shape[1], down_weight_t.shape[1]]
     packed = jnp.concatenate([out_weight, gate_weight, up_weight, down_weight_t], axis=1)
-    gathered = gather_rows(packed)
+    rows_xz = gather_over_xz(packed)
+    attn_out = attend(
+        queries, new_kv, cache_pool, page_table, assignment, lengths, lambda_vectors, subln_gain
+    )
+    mlp_size = D // residual.shape[1]
+    heads_all = mlp_gather(attn_out, mlp_size)
+    rows_xz, heads_all = lax.optimization_barrier((rows_xz, heads_all))
+    gathered = swap_with_core(rows_xz)
     bounds = [0]
     for w in widths:
         bounds.append(bounds[-1] + w)
     out_full, gate_full, up_full, down_full = [
         gathered[:, bounds[i] : bounds[i + 1]] for i in range(4)
     ]
-    attn_out = attend(
-        queries, new_kv, cache_pool, page_table, assignment, lengths, lambda_vectors, subln_gain
-    )
-    mlp_size = D // residual.shape[1]
-    heads_all = mlp_gather(attn_out, mlp_size)
     rows = out_weight.shape[0]
     projected = jnp.dot(
         to_gathered_order(heads_all, rows), out_full, preferred_element_type=jnp.float32

time: 256 us -> 207 us (0.81)
  waiting for transfers between devices: 103 us -> 65.7 us
  starting transfers between devices: 41.2 us -> 34.6 us
  other arithmetic: 18.7 us -> 15 us
    all_gather x1, waiting for transfers between devices: 86.1 us -> 37.5 us  [gather_over_xz(): return lax.all_gather(out, 'z', axis=0, tiled=True)]
    slice x5 -> x4, local copies, waits for them, and re-layouts: 1.31 us -> 7.14 us  [mlp_gather(): return jnp.concatenate([gathered[k] for k in range(axis_size)], axis=1)]
    ppermute x1, waiting for transfers between devices: 0.01 us -> 5.75 us  [swap_with_core(): other = lax.ppermute(rows_xz, 'c', [(0, 1), (1, 0)])]
    ppermute x3, starting transfers between devices: 11.8 us -> 7.18 us  [down_and_scatter(): lax.ppermute(block_for(target), 'mlp', [(i, (i + shift) % axis_size) for...]
    ppermute x6, waiting for transfers between devices: 11.4 us -> 14.7 us  [mlp_gather(): lax.ppermute(block, 'mlp', [(i, (i + shift) % axis_size) for i in range(a...]
    unnamed x38 -> x28, local copies, waits for them, and re-layouts: 7.7 us -> 8.23 us
  transfers between devices with their start and end apart: 11 -> 11, of which waited for: 8 -> 8; matrix products, arithmetic and copies ran while one was open for 19% -> 21% of each run, Pallas kernels for 0% -> 0%
where the time goes in v7:
time: 207 us; the launch traced here: 205 us
  waiting for transfers between devices  65.7 us (32%)
  local copies, waits for them, and re-layouts  40.7 us (20%)
  starting transfers between devices  34.6 us (17%)
  matrix products  22 us (11%)
  between operations  15.9 us (8%)
  other arithmetic  15 us (7%)
  blocking collectives  11.5 us (6%)
    all_gather x1, waiting for transfers between devices, gather_over_xz(): return lax.all_gather(out, 'z', axis=0, tiled=True)  37.5 us
    ppermute x6, starting transfers between devices, mlp_gather(): lax.ppermute(block, 'mlp', [(i, (i + shift) % axis_size) for i in range(a...  19.7 us
    ppermute x6, waiting for transfers between devices, mlp_gather(): lax.ppermute(block, 'mlp', [(i, (i + shift) % axis_size) for i in range(a...  14.7 us
    all_gather x1, blocking collectives, gather_over_xz(): out = lax.all_gather(block, 'x', axis=0, tiled=True)  11.5 us
    unnamed x28, local copies, waits for them, and re-layouts  8.23 us
    ppermute x1, starting transfers between devices, swap_with_core(): other = lax.ppermute(rows_xz, 'c', [(0, 1), (1, 0)])  7.75 us
    ppermute x3, waiting for transfers between devices, down_and_scatter(): lax.ppermute(block_for(target), 'mlp', [(i, (i + shift) % axis_size) for...  7.71 us
    gather x2, local copies, waits for them, and re-layouts, attend(): pages = jnp.take(cache_pool, page_table[0], axis=0)  7.32 us
  transfers between devices with their start and end apart: 11, of which 8 were waited for; matrix products, arithmetic and copies ran while one was open for 21% of the time, Pallas kernels for 0%

profile of v7, /device:TPU:1, one launch (start us, length us, event | category | flops | bytes accessed | tf_op | source)
XLA Modules:
  0.0 205.4 jit_solution(14390387680062099317)
XLA Ops:
  7.4 11.5 %all_gather.6 = bf16[64,2816]{1,0:T(8,128)(2,1)} all-gather(bf16[16,2816]{1,0:T(8,128)(2,1)S(1)} %pad_maximum_fusion.15), channel_id=1, replica_groups=mesh['x'=4,'z'=16,'c'=2,'mlp'=4] {'x'}, dimensions={0}, use_global_device_ids=true | all-gather | bytes 450560 | tf_op jit(solution)/shard_map/all_gather | solution.py:113
  20.3 5.6 %gather_fusion = bf16[6,128,2,512]{3,2,1,0:T(2,128)(2,1)} fusion(bf16[6,128,2,512]{3,2,1,0:T(2,128)(2,1)S(1)} %copy-done, s32[1024]{0:T(1024)S(1)} %pad_clamp_fusion.1), kind=kCustom, calls=%fused_computation.2 | custom fusion | bytes 3145752 | tf_op jit(solution)/shard_map/jit(_take)/gather | solution.py:23
  32.1 1.8 fusion.98
  35.4 2.3 %fusion.99 = f32[256,2]{0,1:T(2,128)S(1)} fusion(pred[256,1024]{0,1:T(8,128)(4,1)S(1)} %pad_add_fusion, bf16[768,2,512]{2,0,1:T(8,128)(2,1)} %bitcast_select_fusion.4, bf16[256,2,512]{2,0,1:T(8,128)(2,1)} %copy.62, bf16[256,2,128]{2,1,0:T(2,128)(2,1)} %get-tuple-element.29), kind=kOutput, calls=%fused_computation.133 | convolution fusion | flops 137888768 | bytes 2754560 | tf_op jit(solution)/shard_map/sub | solution.py:45
  37.6 3.2 %fusion.13 = f32[256,2,256]{0,2,1:T(8,128)} fusion(f32[256,2]{0,1:T(2,128)S(1)} %fusion.99, pred[256,1024]{0,1:T(8,128)(4,1)S(1)} %pad_add_fusion, bf16[768,2,512]{2,0,1:T(8,128)(2,1)S(1)} %copy-done.3, bf16[256,2,512]{2,0,1:T(8,128)(2,1)} %copy.62, bf16[256,2,128]{2,1,0:T(2,128)(2,1)} %get-tuple-element.29), kind=kOutput, calls=%fused_computation.29 | convolution fusion | flops 408552960 | bytes 5376000 | tf_op jit(solution)/shard_map/nhk,khd->nhd/dot_general | solution.py:47
  40.9 2.0 fusion.104
  42.8 3.4 %multiply_reduce_fusion.1 = (f32[256,2]{0,1:T(2,128)S(1)}, f32[256,2,256]{0,2,1:T(8,128)}) fusion(f32[256,2,256]{0,2,1:T(8,128)} %fusion.13, f32[256,2]{0,1:T(2,128)S(1)} %fusion.104, pred[256,1024]{0,1:T(8,128)(4,1)S(1)} %pad_add_fusion, bf16[256,2,512]{2,0,1:T(8,128)(2,1)} %copy.62, bf16[768,2,512]{2,0,1:T(8,128)(2,1)S(1)} %copy-done.3, ...), kind=kOutput, calls=%fused_computation.64 | convolution fusion | flops 409076736 | bytes 5902340 | tf_op jit(solution)/shard_map/nhk,khd->nhd/dot_general | solution.py:47
  47.4 5.4 %collective-permute-start.2 = (bf16[256,512]{0,1:T(8,128)(2,1)S(1)}, bf16[256,512]{0,1:T(8,128)(2,1)S(1)}, u32[]{:S(2)}, u32[]{:S(2)}) collective-permute-start(bf16[256,512]{0,1:T(8,128)(2,1)S(1)} %bitcast.134), channel_id=1, source_target_pairs={{0,3},{1,0},{2,1},{3,2},{4,7},{5,4},{6,5},{7,6},{8,11},{9,8},{10,9... | collective-permute-start | bytes 786440 | tf_op jit(solution)/shard_map/ppermute | solution.py:77
  52.7 2.2 %collective-permute-start.1 = (bf16[256,512]{0,1:T(8,128)(2,1)S(1)}, bf16[256,512]{0,1:T(8,128)(2,1)S(1)}, u32[]{:S(2)}, u32[]{:S(2)}) collective-permute-start(bf16[256,512]{0,1:T(8,128)(2,1)S(1)} %bitcast.135), channel_id=1, source_target_pairs={{0,2},{1,3},{2,0},{3,1},{4,6},{5,7},{6,4},{7,5},{8,10},{9,11},{10,... | collective-permute-start | bytes 786440 | tf_op jit(solution)/shard_map/ppermute | solution.py:77
  55.0 2.6 %collective-permute-start = (bf16[256,512]{0,1:T(8,128)(2,1)S(1)}, bf16[256,512]{0,1:T(8,128)(2,1)S(1)}, u32[]{:S(2)}, u32[]{:S(2)}) collective-permute-start(bf16[256,512]{0,1:T(8,128)(2,1)S(1)} %bitcast.136), channel_id=1, source_target_pairs={{0,1},{1,2},{2,3},{3,0},{4,5},{5,6},{6,7},{7,4},{8,9},{9,10},{10,1... | collective-permute-start | bytes 786440 | tf_op jit(solution)/shard_map/ppermute | solution.py:77
  57.7 3.8 %collective-permute-done.1 = bf16[256,512]{0,1:T(8,128)(2,1)S(1)} collective-permute-done((bf16[256,512]{0,1:T(8,128)(2,1)S(1)}, bf16[256,512]{0,1:T(8,128)(2,1)S(1)}, u32[]{:S(2)}, u32[]{:S(2)}) %collective-permute-start.1) | collective-permute-done | bytes 262176 | tf_op jit(solution)/shard_map/ppermute | solution.py:77
  61.4 2.7 %collective-permute-done = bf16[256,512]{0,1:T(8,128)(2,1)S(1)} collective-permute-done((bf16[256,512]{0,1:T(8,128)(2,1)S(1)}, bf16[256,512]{0,1:T(8,128)(2,1)S(1)}, u32[]{:S(2)}, u32[]{:S(2)}) %collective-permute-start) | collective-permute-done | bytes 262176 | tf_op jit(solution)/shard_map/ppermute | solution.py:77
  65.3 1.9 gather_fusion.1
  67.5 37.5 %all-gather.2.cloned.1.call-done = bf16[1024,2816]{1,0:T(8,128)(2,1)} async-done(((bf16[64,2816]{1,0:T(8,128)(2,1)}), bf16[1024,2816]{1,0:T(8,128)(2,1)}) %all-gather.2.cloned.1.call-update) | async-done | bytes 5767184 | tf_op jit(solution)/shard_map/all_gather | solution.py:114
  105.0 7.8 %collective-permute-start.3 = (bf16[1024,2816]{1,0:T(8,128)(2,1)}, bf16[1024,2816]{1,0:T(8,128)(2,1)}, u32[]{:S(2)}, u32[]{:S(2)}) collective-permute-start(bf16[1024,2816]{1,0:T(8,128)(2,1)} %all-gather.2.cloned.1.call-done), channel_id=1, source_target_pairs={{0,4},{4,0},{1,5},{5,1},{2,6},{6,2},{3,7},{7,3},{8,12},{12,8},{9,1... | collective-permute-start | bytes 17301512 | tf_op jit(solution)/shard_map/ppermute | solution.py:118
  113.3 3.0 %constant_dynamic-update-slice_fusion.1 = bf16[2048,2816]{1,0:T(8,128)(2,1)S(1)} fusion(bf16[1024,2816]{1,0:T(8,128)(2,1)} %all-gather.2.cloned.1.call-done), kind=kLoop, calls=%fused_computation.87 | loop fusion | bytes 11534336
  116.4 5.8 %collective-permute-done.3 = bf16[1024,2816]{1,0:T(8,128)(2,1)} collective-permute-done((bf16[1024,2816]{1,0:T(8,128)(2,1)}, bf16[1024,2816]{1,0:T(8,128)(2,1)}, u32[]{:S(2)}, u32[]{:S(2)}) %collective-permute-start.3) | collective-permute-done | bytes 5767200 | tf_op jit(solution)/shard_map/ppermute | solution.py:118
  122.1 3.0 %constant_dynamic-update-slice_fusion = bf16[2048,2816]{1,0:T(8,128)(2,1)S(1)} fusion(bf16[2048,2816]{1,0:T(8,128)(2,1)S(1)} %constant_dynamic-update-slice_fusion.1, bf16[1024,2816]{1,0:T(8,128)(2,1)} %collective-permute-done.3), kind=kLoop, calls=%fused_computation.86 | loop fusion | bytes 11534336 | tf_op jit(solution)/shard_map/concatenate | solution.py:119
  125.1 4.3 %copy-done.1 = bf16[2048,2816]{1,0:T(8,128)(2,1)} copy-done((bf16[2048,2816]{1,0:T(8,128)(2,1)}, bf16[2048,2816]{1,0:T(8,128)(2,1)S(1)}, u32[]{:S(2)}) %copy-start.1) | copy-done | bytes 11534360
  130.2 4.3 %collective-permute-start.6 = (bf16[256,512]{1,0:T(8,128)(2,1)S(1)}, bf16[256,512]{1,0:T(8,128)(2,1)S(1)}, u32[]{:S(2)}, u32[]{:S(2)}) collective-permute-start(bf16[256,512]{1,0:T(8,128)(2,1)S(1)} %fusion.17), channel_id=1, source_target_pairs={{0,3},{1,0},{2,1},{3,2},{4,7},{5,4},{6,5},{7,6},{8,11},{9,8},{10,9... | collective-permute-start | bytes 786440 | tf_op jit(solution)/shard_map/ppermute | solution.py:77
  134.5 2.2 %collective-permute-start.5 = (bf16[256,512]{1,0:T(8,128)(2,1)S(1)}, bf16[256,512]{1,0:T(8,128)(2,1)S(1)}, u32[]{:S(2)}, u32[]{:S(2)}) collective-permute-start(bf16[256,512]{1,0:T(8,128)(2,1)S(1)} %fusion.17), channel_id=1, source_target_pairs={{0,2},{1,3},{2,0},{3,1},{4,6},{5,7},{6,4},{7,5},{8,10},{9,11},{10,... | collective-permute-start | bytes 786440 | tf_op jit(solution)/shard_map/ppermute | solution.py:77
  136.8 2.9 %collective-permute-start.4 = (bf16[256,512]{1,0:T(8,128)(2,1)S(1)}, bf16[256,512]{1,0:T(8,128)(2,1)S(1)}, u32[]{:S(2)}, u32[]{:S(2)}) collective-permute-start(bf16[256,512]{1,0:T(8,128)(2,1)S(1)} %fusion.17), channel_id=1, source_target_pairs={{0,1},{1,2},{2,3},{3,0},{4,5},{5,6},{6,7},{7,4},{8,9},{9,10},{10,1... | collective-permute-start | bytes 786440 | tf_op jit(solution)/shard_map/ppermute | solution.py:77
  139.9 2.1 %slice.105 = bf16[2048,768]{1,0:T(8,128)(2,1)S(1)} slice(bf16[2048,2816]{1,0:T(8,128)(2,1)} %copy-done.1), slice={[0:2048], [2048:2816]} | slice | bytes 6291456 | tf_op jit(solution)/shard_map/slice | solution.py:177
  145.2 6.6 %collective-permute-done.4 = bf16[256,512]{1,0:T(8,128)(2,1)S(1)} collective-permute-done((bf16[256,512]{1,0:T(8,128)(2,1)S(1)}, bf16[256,512]{1,0:T(8,128)(2,1)S(1)}, u32[]{:S(2)}, u32[]{:S(2)}) %collective-permute-start.4) | collective-permute-done | bytes 262176 | tf_op jit(solution)/shard_map/ppermute | solution.py:77
  152.9 1.8 gather_fusion.2
  165.5 2.9 %fusion.4 = f32[256,768]{1,0:T(8,128)S(1)} fusion(bf16[256,2048]{0,1:T(8,128)(2,1)S(1)} %bitcast.126, bf16[2048,2816]{1,0:T(8,128)(2,1)} %copy-done.1), kind=kOutput, calls=%fused_computation.7 | convolution fusion | flops 805306368 | bytes 4980736 | tf_op jit(solution)/shard_map/dot_general | solution.py:188
  168.5 3.0 %multiply_convert_fusion.1 = bf16[256,768]{1,0:T(8,128)(2,1)S(1)} fusion(f32[256,768]{1,0:T(8,128)S(1)} %fusion.4, bf16[256,2048]{0,1:T(8,128)(2,1)S(1)} %bitcast.127, bf16[2048,2816]{1,0:T(8,128)(2,1)} %copy-done.1), kind=kOutput, calls=%fused_computation.55 | convolution fusion | flops 806486016 | bytes 5373952 | tf_op jit(solution)/shard_map/dot_general | solution.py:189
  176.5 1.9 collective-permute-start.9
  179.3 2.2 %collective-permute-start.8 = (bf16[256,512]{1,0:T(8,128)(2,1)}, bf16[256,512]{1,0:T(8,128)(2,1)}, u32[]{:S(2)}, u32[]{:S(2)}) collective-permute-start(bf16[256,512]{1,0:T(8,128)(2,1)} %copy.83), channel_id=1, source_target_pairs={{0,2},{1,3},{2,0},{3,1},{4,6},{5,7},{6,4},{7,5},{8,10},{9,11},{10,... | collective-permute-start | bytes 786440 | tf_op jit(solution)/shard_map/ppermute | solution.py:99
  185.7 3.0 %collective-permute-start.7 = (bf16[256,512]{1,0:T(8,128)(2,1)S(1)}, bf16[256,512]{1,0:T(8,128)(2,1)S(1)}, u32[]{:S(2)}, u32[]{:S(2)}) collective-permute-start(bf16[256,512]{1,0:T(8,128)(2,1)S(1)} %copy.79), channel_id=1, source_target_pairs={{0,1},{1,2},{2,3},{3,0},{4,5},{5,6},{6,7},{7,4},{8,9},{9,10},{10,1... | collective-permute-start | bytes 786440 | tf_op jit(solution)/shard_map/ppermute | solution.py:99
  189.7 7.0 %collective-permute-done.7 = bf16[256,512]{1,0:T(8,128)(2,1)S(1)} collective-permute-done((bf16[256,512]{1,0:T(8,128)(2,1)S(1)}, bf16[256,512]{1,0:T(8,128)(2,1)S(1)}, u32[]{:S(2)}, u32[]{:S(2)}) %collective-permute-start.7) | collective-permute-done | bytes 262176 | tf_op jit(solution)/shard_map/ppermute | solution.py:99
  196.7 1.9 add_convert_fusion
  (90 shorter events, 37.9 us)
Async XLA Ops:
  6.5 13.7 %copy-start = (bf16[6,128,2,512]{3,2,1,0:T(2,128)(2,1)S(1)}, bf16[6,128,2,512]{3,2,1,0:T(2,128)(2,1)}, u32[]{:S(2)}) copy-start(bf16[6,128,2,512]{3,2,1,0:T(2,128)(2,1)} %param.18) | copy-start | bytes 4718596
  6.5 98.5 %all-gather.2.cloned.1.call-start = ((), (), s32[]{:S(2)}) async-start(), calls=%async_computation | async-start | bytes 6127616 | tf_op jit(solution)/shard_map/all_gather | solution.py:114
  25.8 1.8 copy-start.6
  25.8 2.6 %copy-start.8 = (f32[4,128]{1,0:T(4,128)S(1)}, f32[4,128]{1,0:T(4,128)}, u32[]{:S(2)}) copy-start(f32[4,128]{1,0:T(4,128)} %param.22) | copy-start | bytes 6148
  25.8 4.5 %copy-start.11 = (s32[128]{0:T(128)S(1)}, s32[128]{0:T(128)}, u32[]{:S(2)}) copy-start(s32[128]{0:T(128)} %param.21) | copy-start | bytes 1540
  25.8 5.9 %copy-start.12 = (s32[1,6]{1,0:T(1,128)S(1)}, s32[1,6]{1,0:T(1,128)}, u32[]{:S(2)}) copy-start(s32[1,6]{1,0:T(1,128)} %param.19) | copy-start | bytes 76
  35.4 2.3 %copy-start.3 = (bf16[768,2,512]{2,0,1:T(8,128)(2,1)S(1)}, bf16[768,2,512]{2,0,1:T(8,128)(2,1)}, u32[]{:S(2)}) copy-start(bf16[768,2,512]{2,0,1:T(8,128)(2,1)} %bitcast_select_fusion.4) | copy-start | bytes 4718596
  42.8 3.4 %copy-start.9 = (f32[256]{0:T(256)S(1)}, f32[256]{0:T(256)}, u32[]{:S(2)}) copy-start(f32[256]{0:T(256)} %param.23) | copy-start | bytes 3076
  47.4 10.3 %collective-permute-start.2 = (bf16[256,512]{0,1:T(8,128)(2,1)S(1)}, bf16[256,512]{0,1:T(8,128)(2,1)S(1)}, u32[]{:S(2)}, u32[]{:S(2)}) collective-permute-start(bf16[256,512]{0,1:T(8,128)(2,1)S(1)} %bitcast.134), channel_id=1, source_target_pairs={{0,3},{1,0},{2,1},{3,2},{4,7},{5,4},{6,5},{7,6},{8,11},{9,8},{10,9... | collective-permute-start | bytes 786440 | tf_op jit(solution)/shard_map/ppermute | solution.py:77
  52.7 8.7 %collective-permute-start.1 = (bf16[256,512]{0,1:T(8,128)(2,1)S(1)}, bf16[256,512]{0,1:T(8,128)(2,1)S(1)}, u32[]{:S(2)}, u32[]{:S(2)}) collective-permute-start(bf16[256,512]{0,1:T(8,128)(2,1)S(1)} %bitcast.135), channel_id=1, source_target_pairs={{0,2},{1,3},{2,0},{3,1},{4,6},{5,7},{6,4},{7,5},{8,10},{9,11},{10,... | collective-permute-start | bytes 786440 | tf_op jit(solution)/shard_map/ppermute | solution.py:77
  55.0 9.2 %collective-permute-start = (bf16[256,512]{0,1:T(8,128)(2,1)S(1)}, bf16[256,512]{0,1:T(8,128)(2,1)S(1)}, u32[]{:S(2)}, u32[]{:S(2)}) collective-permute-start(bf16[256,512]{0,1:T(8,128)(2,1)S(1)} %bitcast.136), channel_id=1, source_target_pairs={{0,1},{1,2},{2,3},{3,0},{4,5},{5,6},{6,7},{7,4},{8,9},{9,10},{10,1... | collective-permute-start | bytes 786440 | tf_op jit(solution)/shard_map/ppermute | solution.py:77
  105.0 17.1 %collective-permute-start.3 = (bf16[1024,2816]{1,0:T(8,128)(2,1)}, bf16[1024,2816]{1,0:T(8,128)(2,1)}, u32[]{:S(2)}, u32[]{:S(2)}) collective-permute-start(bf16[1024,2816]{1,0:T(8,128)(2,1)} %all-gather.2.cloned.1.call-done), channel_id=1, source_target_pairs={{0,4},{4,0},{1,5},{5,1},{2,6},{6,2},{3,7},{7,3},{8,12},{12,8},{9,1... | collective-permute-start | bytes 17301512 | tf_op jit(solution)/shard_map/ppermute | solution.py:118
  116.3 13.1 %copy-start.10 = (bf16[256,512]{1,0:T(8,128)(2,1)S(1)}, bf16[256,512]{1,0:T(8,128)(2,1)}, u32[]{:S(2)}) copy-start(bf16[256,512]{1,0:T(8,128)(2,1)} %param.24) | copy-start | bytes 786436
  125.1 4.4 %copy-start.1 = (bf16[2048,2816]{1,0:T(8,128)(2,1)}, bf16[2048,2816]{1,0:T(8,128)(2,1)S(1)}, u32[]{:S(2)}) copy-start(bf16[2048,2816]{1,0:T(8,128)(2,1)S(1)} %constant_dynamic-update-slice_fusion) | copy-start | bytes 34603012
  125.1 14.6 %copy-start.7 = (f32[2048]{0:T(1024)S(1)}, f32[2048]{0:T(1024)}, u32[]{:S(2)}) copy-start(f32[2048]{0:T(1024)} %param.26) | copy-start | bytes 24580
  130.2 21.6 %copy-start.4 = (bf16[256,512]{1,0:T(8,128)(2,1)}, bf16[256,512]{1,0:T(8,128)(2,1)S(1)}, u32[]{:S(2)}) copy-start(bf16[256,512]{1,0:T(8,128)(2,1)S(1)} %fusion.17) | copy-start | bytes 786436
  130.2 13.3 %collective-permute-start.6 = (bf16[256,512]{1,0:T(8,128)(2,1)S(1)}, bf16[256,512]{1,0:T(8,128)(2,1)S(1)}, u32[]{:S(2)}, u32[]{:S(2)}) collective-permute-start(bf16[256,512]{1,0:T(8,128)(2,1)S(1)} %fusion.17), channel_id=1, source_target_pairs={{0,3},{1,0},{2,1},{3,2},{4,7},{5,4},{6,5},{7,6},{8,11},{9,8},{10,9... | collective-permute-start | bytes 786440 | tf_op jit(solution)/shard_map/ppermute | solution.py:77
  134.5 10.6 %collective-permute-start.5 = (bf16[256,512]{1,0:T(8,128)(2,1)S(1)}, bf16[256,512]{1,0:T(8,128)(2,1)S(1)}, u32[]{:S(2)}, u32[]{:S(2)}) collective-permute-start(bf16[256,512]{1,0:T(8,128)(2,1)S(1)} %fusion.17), channel_id=1, source_target_pairs={{0,2},{1,3},{2,0},{3,1},{4,6},{5,7},{6,4},{7,5},{8,10},{9,11},{10,... | collective-permute-start | bytes 786440 | tf_op jit(solution)/shard_map/ppermute | solution.py:77
  136.8 15.0 %collective-permute-start.4 = (bf16[256,512]{1,0:T(8,128)(2,1)S(1)}, bf16[256,512]{1,0:T(8,128)(2,1)S(1)}, u32[]{:S(2)}, u32[]{:S(2)}) collective-permute-start(bf16[256,512]{1,0:T(8,128)(2,1)S(1)} %fusion.17), channel_id=1, source_target_pairs={{0,1},{1,2},{2,3},{3,0},{4,5},{5,6},{6,7},{7,4},{8,9},{9,10},{10,1... | collective-permute-start | bytes 786440 | tf_op jit(solution)/shard_map/ppermute | solution.py:77
  168.4 3.0 %copy-start.2 = (bf16[2,16,1,16,768]{4,3,2,1,0:T(8,128)(2,1)S(1)}, bf16[2,16,1,16,768]{4,3,2,1,0:T(8,128)(2,1)}, u32[]{:S(2)}) copy-start(bf16[2,16,1,16,768]{4,3,2,1,0:T(8,128)(2,1)} %get-tuple-element.14) | copy-start | bytes 2359300
  176.5 12.5 %collective-permute-start.9 = (bf16[256,512]{1,0:T(8,128)(2,1)}, bf16[256,512]{1,0:T(8,128)(2,1)}, u32[]{:S(2)}, u32[]{:S(2)}) collective-permute-start(bf16[256,512]{1,0:T(8,128)(2,1)} %copy.86), channel_id=1, source_target_pairs={{0,3},{1,0},{2,1},{3,2},{4,7},{5,4},{6,5},{7,6},{8,11},{9,8},{10,9... | collective-permute-start | bytes 786440 | tf_op jit(solution)/shard_map/ppermute | solution.py:99
  179.3 10.4 %collective-permute-start.8 = (bf16[256,512]{1,0:T(8,128)(2,1)}, bf16[256,512]{1,0:T(8,128)(2,1)}, u32[]{:S(2)}, u32[]{:S(2)}) collective-permute-start(bf16[256,512]{1,0:T(8,128)(2,1)} %copy.83), channel_id=1, source_target_pairs={{0,2},{1,3},{2,0},{3,1},{4,6},{5,7},{6,4},{7,5},{8,10},{9,11},{10,... | collective-permute-start | bytes 786440 | tf_op jit(solution)/shard_map/ppermute | solution.py:99
  185.4 11.3 %copy-start.5 = (bf16[256,512]{1,0:T(8,128)(2,1)S(1)}, bf16[256,512]{1,0:T(8,128)(2,1)}, u32[]{:S(2)}) copy-start(bf16[256,512]{1,0:T(8,128)(2,1)} %copy-done.4) | copy-start | bytes 786436
  185.7 11.0 %collective-permute-start.7 = (bf16[256,512]{1,0:T(8,128)(2,1)S(1)}, bf16[256,512]{1,0:T(8,128)(2,1)S(1)}, u32[]{:S(2)}, u32[]{:S(2)}) collective-permute-start(bf16[256,512]{1,0:T(8,128)(2,1)S(1)} %copy.79), channel_id=1, source_target_pairs={{0,1},{1,2},{2,3},{3,0},{4,5},{5,6},{6,7},{7,4},{8,9},{9,10},{10,1... | collective-permute-start | bytes 786440 | tf_op jit(solution)/shard_map/ppermute | solution.py:99
Sparse Core Ops, SparseCore 0:
  19.1 85.8 all-gather.1

commit v8 on v7

--- a/solution.py
+++ b/solution.py
@@ -115,8 +115,16 @@
 
 
 def swap_with_core(rows_xz):
-    other = lax.ppermute(rows_xz, "c", [(0, 1), (1, 0)])
-    return jnp.concatenate([rows_xz, other], axis=0)
+    return [rows_xz, lax.ppermute(rows_xz, "c", [(0, 1), (1, 0)])]
+
+
+def split_dot(act, halves):
+    size = halves[0].shape[0]
+    total = None
+    for j, half in enumerate(halves):
+        part = jnp.dot(act[:, j * size : (j + 1) * size], half, preferred_element_type=jnp.float32)
+        total = part if total is None else total + part
+    return total
 
 
 def to_gathered_order(act, rows):
@@ -128,11 +136,14 @@
     return split.transpose(0, 3, 2, 1, 4).reshape(n, -1)
 
 
-def down_block_rows(down_full, target, rows):
+def down_block_rows(down_halves, target, rows):
     nx, nz, nc = [lax.axis_size(name) for name in REQ_PARTS]
-    split = down_full.reshape(nc, nz, nx, rows, down_full.shape[1])
-    picked = lax.dynamic_index_in_dim(split, target, 2, keepdims=False)
-    return picked.reshape(nc * nz * rows, down_full.shape[1])
+    picked = []
+    for half in down_halves:
+        split = half.reshape(nz, nx, rows, half.shape[1])
+        one = lax.dynamic_index_in_dim(split, target, 1, keepdims=False)
+        picked.append(one.reshape(nz * rows, half.shape[1]))
+    return jnp.concatenate(picked, axis=0)
 
 
 def block_to_req_order(value, rows):
@@ -169,24 +180,22 @@
     mlp_size = D // residual.shape[1]
     heads_all = mlp_gather(attn_out, mlp_size)
     rows_xz, heads_all = lax.optimization_barrier((rows_xz, heads_all))
-    gathered = swap_with_core(rows_xz)
+    halves = swap_with_core(rows_xz)
     bounds = [0]
     for w in widths:
         bounds.append(bounds[-1] + w)
     out_full, gate_full, up_full, down_full = [
-        gathered[:, bounds[i] : bounds[i + 1]] for i in range(4)
+        [half[:, bounds[i] : bounds[i + 1]] for half in halves] for i in range(4)
     ]
     rows = out_weight.shape[0]
-    projected = jnp.dot(
-        to_gathered_order(heads_all, rows), out_full, preferred_element_type=jnp.float32
-    )
+    projected = split_dot(to_gathered_order(heads_all, rows), out_full)
     stream = (residual.astype(jnp.float32) + projected).astype(jnp.bfloat16)
     stream_all = mlp_gather(stream, mlp_size).astype(jnp.float32)
     squares = jnp.sum(stream_all * stream_all, axis=1, keepdims=True)
     normed = (stream_all * lax.rsqrt(squares / D + 1e-05) * norm_gain).astype(jnp.bfloat16)
     normed = to_gathered_order(normed, rows)
-    gate_value = jnp.dot(normed, gate_full, preferred_element_type=jnp.float32)
-    up_value = jnp.dot(normed, up_full, preferred_element_type=jnp.float32)
+    gate_value = split_dot(normed, gate_full)
+    up_value = split_dot(normed, up_full)
     hidden_act = (jax.nn.silu(gate_value) * up_value).astype(jnp.bfloat16)
     summed = down_and_scatter(hidden_act, down_full, mlp_size, out_weight.shape[0])
     return (stream.astype(jnp.float32) + summed).astype(jnp.bfloat16)

time: 207 us -> 201 us (0.971)
  local copies, waits for them, and re-layouts: 40.7 us -> 28.7 us
  matrix products: 22 us -> 30 us
  waiting for transfers between devices: 65.7 us -> 58.5 us
  starting transfers between devices: 34.6 us -> 40.9 us
    unnamed x28 -> x31, local copies, waits for them, and re-layouts: 8.23 us -> 1.61 us
    slice x4, local copies, waits for them, and re-layouts: 7.14 us -> 0.54 us  [mlp_gather(): return jnp.concatenate([gathered[k] for k in range(axis_size)], axis=1)]
    ppermute x6, waiting for transfers between devices: 14.7 us -> 8.48 us  [mlp_gather(): lax.ppermute(block, 'mlp', [(i, (i + shift) % axis_size) for i in range(a...]
    dot_general x3 -> x6, matrix products: 6.65 us -> 11.6 us  [split_dot(): jnp.dot(act[:, j * size:(j + 1) * size], half, preferred_element_type=jnp...]
    ppermute x3, starting transfers between devices: 7.18 us -> 11.1 us  [down_and_scatter(): lax.ppermute(block_for(target), 'mlp', [(i, (i + shift) % axis_size) for...]
    dot_general x4, matrix products: 4.56 us -> 7.66 us  [block_for(): lax.dot_general(hidden_act, weight_rows, (((1,), (1,)), ((), ())), prefer...]
    concatenate x1 -> x0, local copies, waits for them, and re-layouts: 3.01 us -> none  [swap_with_core(): return jnp.concatenate([rows_xz, other], axis=0)]
    ppermute x6, starting transfers between devices: 19.7 us -> 22 us  [mlp_gather(): lax.ppermute(block, 'mlp', [(i, (i + shift) % axis_size) for i in range(a...]
  transfers between devices with their start and end apart: 11 -> 11, of which waited for: 8 -> 8; matrix products, arithmetic and copies ran while one was open for 21% -> 23% of each run, Pallas kernels for 0% -> 0%
where the time goes in v8:
time: 201 us; the launch traced here: 199 us
  waiting for transfers between devices  58.5 us (29%)
  starting transfers between devices  40.9 us (20%)
  matrix products  30 us (15%)
  local copies, waits for them, and re-layouts  28.7 us (14%)
  between operations  16.1 us (8%)
  other arithmetic  13.5 us (7%)
  blocking collectives  11.5 us (6%)
    all_gather x1, waiting for transfers between devices, gather_over_xz(): return lax.all_gather(out, 'z', axis=0, tiled=True)  38.1 us
    ppermute x6, starting transfers between devices, mlp_gather(): lax.ppermute(block, 'mlp', [(i, (i + shift) % axis_size) for i in range(a...  22 us
    dot_general x6, matrix products, split_dot(): jnp.dot(act[:, j * size:(j + 1) * size], half, preferred_element_type=jnp...  11.6 us
    all_gather x1, blocking collectives, gather_over_xz(): out = lax.all_gather(block, 'x', axis=0, tiled=True)  11.5 us
    ppermute x3, starting transfers between devices, down_and_scatter(): lax.ppermute(block_for(target), 'mlp', [(i, (i + shift) % axis_size) for...  11.1 us
    ppermute x6, waiting for transfers between devices, mlp_gather(): lax.ppermute(block, 'mlp', [(i, (i + shift) % axis_size) for i in range(a...  8.48 us
    ppermute x1, starting transfers between devices, swap_with_core(): return [rows_xz, lax.ppermute(rows_xz, 'c', [(0, 1), (1, 0)])]  7.82 us
    dot_general x4, matrix products, block_for(): lax.dot_general(hidden_act, weight_rows, (((1,), (1,)), ((), ())), prefer...  7.66 us
  transfers between devices with their start and end apart: 11, of which 8 were waited for; matrix products, arithmetic and copies ran while one was open for 23% of the time, Pallas kernels for 0%

profile of v8, /device:TPU:1, one launch (start us, length us, event | category | flops | bytes accessed | tf_op | source)
XLA Modules:
  0.0 199.1 jit_solution(12755538315880171993)
XLA Ops:
  7.4 11.5 %all_gather.6 = bf16[64,2816]{1,0:T(8,128)(2,1)} all-gather(bf16[16,2816]{1,0:T(8,128)(2,1)S(1)} %pad_maximum_fusion.15), channel_id=1, replica_groups=mesh['x'=4,'z'=16,'c'=2,'mlp'=4] {'x'}, dimensions={0}, use_global_device_ids=true | all-gather | bytes 450560 | tf_op jit(solution)/shard_map/all_gather | solution.py:113
  19.6 5.6 %gather_fusion = bf16[6,128,2,512]{3,2,1,0:T(2,128)(2,1)} fusion(bf16[6,128,2,512]{3,2,1,0:T(2,128)(2,1)S(1)} %copy-done, s32[1024]{0:T(1024)S(1)} %pad_clamp_fusion.1), kind=kCustom, calls=%fused_computation.2 | custom fusion | bytes 3145752 | tf_op jit(solution)/shard_map/jit(_take)/gather | solution.py:23
  35.5 2.3 %fusion.132 = f32[256,2]{0,1:T(2,128)S(1)} fusion(pred[256,1024]{0,1:T(8,128)(4,1)S(1)} %pad_add_fusion, bf16[768,2,512]{2,0,1:T(8,128)(2,1)} %bitcast_select_fusion.4, bf16[256,2,512]{2,0,1:T(8,128)(2,1)} %copy.62, bf16[256,2,128]{2,1,0:T(2,128)(2,1)} %get-tuple-element.33), kind=kOutput, calls=%fused_computation.165 | convolution fusion | flops 137888768 | bytes 2754560 | tf_op jit(solution)/shard_map/sub | solution.py:45
  37.8 3.2 %fusion.18 = f32[256,2,256]{0,2,1:T(8,128)} fusion(f32[256,2]{0,1:T(2,128)S(1)} %fusion.132, pred[256,1024]{0,1:T(8,128)(4,1)S(1)} %pad_add_fusion, bf16[768,2,512]{2,0,1:T(8,128)(2,1)S(1)} %copy-done.1, bf16[256,2,512]{2,0,1:T(8,128)(2,1)} %copy.62, bf16[256,2,128]{2,1,0:T(2,128)(2,1)} %get-tuple-element.33), kind=kOutput, calls=%fused_computation.33 | convolution fusion | flops 408552960 | bytes 5376000 | tf_op jit(solution)/shard_map/nhk,khd->nhd/dot_general | solution.py:47
  41.0 2.0 fusion.137
  43.0 3.3 %multiply_reduce_fusion.1 = (f32[256,2]{0,1:T(2,128)S(1)}, f32[256,2,256]{0,2,1:T(8,128)}) fusion(f32[256,2,256]{0,2,1:T(8,128)} %fusion.18, f32[256,2]{0,1:T(2,128)S(1)} %fusion.137, pred[256,1024]{0,1:T(8,128)(4,1)S(1)} %pad_add_fusion, bf16[256,2,512]{2,0,1:T(8,128)(2,1)} %copy.62, bf16[768,2,512]{2,0,1:T(8,128)(2,1)S(1)} %copy-done.1, ...), kind=kOutput, calls=%fused_computation.86 | convolution fusion | flops 409076736 | bytes 5902340 | tf_op jit(solution)/shard_map/nhk,khd->nhd/dot_general | solution.py:47
  47.5 3.9 %collective-permute-start = (bf16[256,512]{0,1:T(8,128)(2,1)S(1)}, bf16[256,512]{0,1:T(8,128)(2,1)S(1)}, u32[]{:S(2)}, u32[]{:S(2)}) collective-permute-start(bf16[256,512]{0,1:T(8,128)(2,1)S(1)} %bitcast.132), channel_id=1, source_target_pairs={{0,1},{1,2},{2,3},{3,0},{4,5},{5,6},{6,7},{7,4},{8,9},{9,10},{10,1... | collective-permute-start | bytes 786440 | tf_op jit(solution)/shard_map/ppermute | solution.py:77
  51.4 4.5 %collective-permute-start.1 = (bf16[256,512]{0,1:T(8,128)(2,1)S(1)}, bf16[256,512]{0,1:T(8,128)(2,1)S(1)}, u32[]{:S(2)}, u32[]{:S(2)}) collective-permute-start(bf16[256,512]{0,1:T(8,128)(2,1)S(1)} %bitcast.133), channel_id=1, source_target_pairs={{0,2},{1,3},{2,0},{3,1},{4,6},{5,7},{6,4},{7,5},{8,10},{9,11},{10,... | collective-permute-start | bytes 786440 | tf_op jit(solution)/shard_map/ppermute | solution.py:77
  56.0 3.0 %collective-permute-start.2 = (bf16[256,512]{0,1:T(8,128)(2,1)S(1)}, bf16[256,512]{0,1:T(8,128)(2,1)S(1)}, u32[]{:S(2)}, u32[]{:S(2)}) collective-permute-start(bf16[256,512]{0,1:T(8,128)(2,1)S(1)} %bitcast.134), channel_id=1, source_target_pairs={{0,3},{1,0},{2,1},{3,2},{4,7},{5,4},{6,5},{7,6},{8,11},{9,8},{10,9... | collective-permute-start | bytes 786440 | tf_op jit(solution)/shard_map/ppermute | solution.py:77
  59.0 3.8 %collective-permute-done.1 = bf16[256,512]{0,1:T(8,128)(2,1)S(1)} collective-permute-done((bf16[256,512]{0,1:T(8,128)(2,1)S(1)}, bf16[256,512]{0,1:T(8,128)(2,1)S(1)}, u32[]{:S(2)}, u32[]{:S(2)}) %collective-permute-start.1) | collective-permute-done | bytes 262176 | tf_op jit(solution)/shard_map/ppermute | solution.py:77
  64.6 1.8 gather_fusion.1
  66.8 38.1 %all-gather.2.cloned.1.call-done = bf16[1024,2816]{1,0:T(8,128)(2,1)} async-done(((bf16[64,2816]{1,0:T(8,128)(2,1)}), bf16[1024,2816]{1,0:T(8,128)(2,1)}) %all-gather.2.cloned.1.call-update) | async-done | bytes 5767184 | tf_op jit(solution)/shard_map/all_gather | solution.py:114
  104.9 7.8 %collective-permute-start.3 = (bf16[1024,2816]{1,0:T(8,128)(2,1)}, bf16[1024,2816]{1,0:T(8,128)(2,1)}, u32[]{:S(2)}, u32[]{:S(2)}) collective-permute-start(bf16[1024,2816]{1,0:T(8,128)(2,1)} %all-gather.2.cloned.1.call-done), channel_id=1, source_target_pairs={{0,4},{4,0},{1,5},{5,1},{2,6},{6,2},{3,7},{7,3},{8,12},{12,8},{9,1... | collective-permute-start | bytes 17301512 | tf_op jit(solution)/shard_map/ppermute | solution.py:118
  117.4 4.7 %collective-permute-done.3 = bf16[1024,2816]{1,0:T(8,128)(2,1)} collective-permute-done((bf16[1024,2816]{1,0:T(8,128)(2,1)}, bf16[1024,2816]{1,0:T(8,128)(2,1)}, u32[]{:S(2)}, u32[]{:S(2)}) %collective-permute-start.3) | collective-permute-done | bytes 5767200 | tf_op jit(solution)/shard_map/ppermute | solution.py:118
  123.8 2.8 %collective-permute-start.4 = (bf16[256,512]{1,0:T(8,128)(2,1)S(1)}, bf16[256,512]{1,0:T(8,128)(2,1)S(1)}, u32[]{:S(2)}, u32[]{:S(2)}) collective-permute-start(bf16[256,512]{1,0:T(8,128)(2,1)S(1)} %fusion.23), channel_id=1, source_target_pairs={{0,1},{1,2},{2,3},{3,0},{4,5},{5,6},{6,7},{7,4},{8,9},{9,10},{10,1... | collective-permute-start | bytes 786440 | tf_op jit(solution)/shard_map/ppermute | solution.py:77
  126.6 4.7 %collective-permute-start.5 = (bf16[256,512]{1,0:T(8,128)(2,1)S(1)}, bf16[256,512]{1,0:T(8,128)(2,1)S(1)}, u32[]{:S(2)}, u32[]{:S(2)}) collective-permute-start(bf16[256,512]{1,0:T(8,128)(2,1)S(1)} %fusion.23), channel_id=1, source_target_pairs={{0,2},{1,3},{2,0},{3,1},{4,6},{5,7},{6,4},{7,5},{8,10},{9,11},{10,... | collective-permute-start | bytes 786440 | tf_op jit(solution)/shard_map/ppermute | solution.py:77
  131.3 3.1 %collective-permute-start.6 = (bf16[256,512]{1,0:T(8,128)(2,1)S(1)}, bf16[256,512]{1,0:T(8,128)(2,1)S(1)}, u32[]{:S(2)}, u32[]{:S(2)}) collective-permute-start(bf16[256,512]{1,0:T(8,128)(2,1)S(1)} %fusion.23), channel_id=1, source_target_pairs={{0,3},{1,0},{2,1},{3,2},{4,7},{5,4},{6,5},{7,6},{8,11},{9,8},{10,9... | collective-permute-start | bytes 786440 | tf_op jit(solution)/shard_map/ppermute | solution.py:77
  138.2 2.8 %collective-permute-done.5 = bf16[256,512]{1,0:T(8,128)(2,1)S(1)} collective-permute-done((bf16[256,512]{1,0:T(8,128)(2,1)S(1)}, bf16[256,512]{1,0:T(8,128)(2,1)S(1)}, u32[]{:S(2)}, u32[]{:S(2)}) %collective-permute-start.5) | collective-permute-done | bytes 262176 | tf_op jit(solution)/shard_map/ppermute | solution.py:77
  143.3 1.8 gather_fusion.2
  148.1 2.0 %fusion.8 = f32[256,768]{1,0:T(8,128)S(1)} fusion(bf16[1024,2816]{1,0:T(8,128)(2,1)} %all-gather.2.cloned.1.call-done, bf16[256,2048]{0,1:T(8,128)(2,1)S(1)} %bitcast.120), kind=kOutput, calls=%fused_computation.22 | convolution fusion | flops 402653184 | bytes 2883584 | tf_op jit(solution)/shard_map/dot_general | solution.py:125
  150.1 2.0 %fusion.10 = f32[256,768]{1,0:T(8,128)S(1)} fusion(bf16[1024,2816]{1,0:T(8,128)(2,1)} %all-gather.2.cloned.1.call-done, bf16[256,2048]{0,1:T(8,128)(2,1)S(1)} %bitcast.121), kind=kOutput, calls=%fused_computation.24 | convolution fusion | flops 402653184 | bytes 2883584 | tf_op jit(solution)/shard_map/dot_general | solution.py:125
  152.1 2.0 %fusion.12 = f32[256,768]{1,0:T(8,128)S(1)} fusion(f32[256,768]{1,0:T(8,128)S(1)} %fusion.10, bf16[1024,2816]{1,0:T(8,128)(2,1)} %collective-permute-done.3, bf16[256,2048]{0,1:T(8,128)(2,1)S(1)} %bitcast.122), kind=kOutput, calls=%fused_computation.28 | convolution fusion | flops 402849792 | bytes 3670016 | tf_op jit(solution)/shard_map/dot_general | solution.py:125
  154.2 2.1 %multiply_convert_fusion.1 = bf16[256,768]{1,0:T(8,128)(2,1)S(1)} fusion(f32[256,768]{1,0:T(8,128)S(1)} %fusion.12, f32[256,768]{1,0:T(8,128)S(1)} %fusion.8, bf16[1024,2816]{1,0:T(8,128)(2,1)} %collective-permute-done.3, bf16[256,2048]{0,1:T(8,128)(2,1)S(1)} %bitcast.123), kind=kOutput, calls=%fused_computation.75 | convolution fusion | flops 404029440 | bytes 4063232 | tf_op jit(solution)/shard_map/dot_general | solution.py:125
  159.3 2.1 %convolution_convert_fusion.3 = bf16[256,512]{1,0:T(8,128)(2,1)} fusion(bf16[256,768]{1,0:T(8,128)(2,1)} %copy-done.14, bf16[256,768]{1,0:T(8,128)(2,1)S(1)} %bitcast.146, bf16[256,768]{1,0:T(8,128)(2,1)S(1)} %bitcast.144), kind=kOutput, calls=%fused_computation.42 | convolution fusion | flops 203030528 | bytes 1441792 | tf_op jit(solution)/shard_map/dot_general | solution.py:90
  163.5 4.9 %collective-permute-start.7 = (bf16[256,512]{1,0:T(8,128)(2,1)}, bf16[256,512]{1,0:T(8,128)(2,1)}, u32[]{:S(2)}, u32[]{:S(2)}) collective-permute-start(bf16[256,512]{1,0:T(8,128)(2,1)} %copy.79), channel_id=1, source_target_pairs={{0,1},{1,2},{2,3},{3,0},{4,5},{5,6},{6,7},{7,4},{8,9},{9,10},{10,1... | collective-permute-start | bytes 786440 | tf_op jit(solution)/shard_map/ppermute | solution.py:99
  168.4 2.3 %convolution_convert_fusion = bf16[256,512]{1,0:T(8,128)(2,1)} fusion(bf16[256,768]{1,0:T(8,128)(2,1)} %copy-done.14, bf16[256,768]{1,0:T(8,128)(2,1)} %bitcast.143, bf16[256,768]{1,0:T(8,128)(2,1)} %bitcast.141), kind=kOutput, calls=%fused_computation.39 | convolution fusion | flops 203030528 | bytes 1441792 | tf_op jit(solution)/shard_map/dot_general | solution.py:90
  171.8 2.1 %convolution_convert_fusion.1 = bf16[256,512]{1,0:T(8,128)(2,1)} fusion(bf16[256,768]{1,0:T(8,128)(2,1)} %copy-done.14, bf16[256,768]{1,0:T(8,128)(2,1)S(1)} %bitcast.142, bf16[256,768]{1,0:T(8,128)(2,1)S(1)} %bitcast.140), kind=kOutput, calls=%fused_computation.40 | convolution fusion | flops 203030528 | bytes 1441792 | tf_op jit(solution)/shard_map/dot_general | solution.py:90
  176.0 3.4 %collective-permute-start.8 = (bf16[256,512]{1,0:T(8,128)(2,1)}, bf16[256,512]{1,0:T(8,128)(2,1)S(1)}, u32[]{:S(2)}, u32[]{:S(2)}) collective-permute-start(bf16[256,512]{1,0:T(8,128)(2,1)} %copy.83), channel_id=1, source_target_pairs={{0,2},{1,3},{2,0},{3,1},{4,6},{5,7},{6,4},{7,5},{8,10},{9,11},{10,... | collective-permute-start | bytes 786440 | tf_op jit(solution)/shard_map/ppermute | solution.py:99
  180.2 2.8 %collective-permute-start.9 = (bf16[256,512]{1,0:T(8,128)(2,1)}, bf16[256,512]{1,0:T(8,128)(2,1)S(1)}, u32[]{:S(2)}, u32[]{:S(2)}) collective-permute-start(bf16[256,512]{1,0:T(8,128)(2,1)} %copy.86), channel_id=1, source_target_pairs={{0,3},{1,0},{2,1},{3,2},{4,7},{5,4},{6,5},{7,6},{8,11},{9,8},{10,9... | collective-permute-start | bytes 786440 | tf_op jit(solution)/shard_map/ppermute | solution.py:99
  183.3 3.3 %collective-permute-done.8 = bf16[256,512]{1,0:T(8,128)(2,1)S(1)} collective-permute-done((bf16[256,512]{1,0:T(8,128)(2,1)}, bf16[256,512]{1,0:T(8,128)(2,1)S(1)}, u32[]{:S(2)}, u32[]{:S(2)}) %collective-permute-start.8) | collective-permute-done | bytes 262176 | tf_op jit(solution)/shard_map/ppermute | solution.py:99
  186.6 3.8 %collective-permute-done.9 = bf16[256,512]{1,0:T(8,128)(2,1)S(1)} collective-permute-done((bf16[256,512]{1,0:T(8,128)(2,1)}, bf16[256,512]{1,0:T(8,128)(2,1)S(1)}, u32[]{:S(2)}, u32[]{:S(2)}) %collective-permute-start.9) | collective-permute-done | bytes 262176 | tf_op jit(solution)/shard_map/ppermute | solution.py:99
  190.5 1.8 add_convert_fusion
  (97 shorter events, 37.4 us)
Async XLA Ops:
  6.5 13.1 %copy-start = (bf16[6,128,2,512]{3,2,1,0:T(2,128)(2,1)S(1)}, bf16[6,128,2,512]{3,2,1,0:T(2,128)(2,1)}, u32[]{:S(2)}) copy-start(bf16[6,128,2,512]{3,2,1,0:T(2,128)(2,1)} %param.18) | copy-start | bytes 4718596
  6.5 98.4 %all-gather.2.cloned.1.call-start = ((), (), s32[]{:S(2)}) async-start(), calls=%async_computation | async-start | bytes 6127616 | tf_op jit(solution)/shard_map/all_gather | solution.py:114
  25.2 1.8 copy-start.2
  25.2 3.3 %copy-start.9 = (f32[4,128]{1,0:T(4,128)S(1)}, f32[4,128]{1,0:T(4,128)}, u32[]{:S(2)}) copy-start(f32[4,128]{1,0:T(4,128)} %param.22) | copy-start | bytes 6148
  25.2 5.4 %copy-start.12 = (s32[128]{0:T(128)S(1)}, s32[128]{0:T(128)}, u32[]{:S(2)}) copy-start(s32[128]{0:T(128)} %param.21) | copy-start | bytes 1540
  25.2 6.7 %copy-start.13 = (s32[1,6]{1,0:T(1,128)S(1)}, s32[1,6]{1,0:T(1,128)}, u32[]{:S(2)}) copy-start(s32[1,6]{1,0:T(1,128)} %param.19) | copy-start | bytes 76
  35.5 2.3 %copy-start.1 = (bf16[768,2,512]{2,0,1:T(8,128)(2,1)S(1)}, bf16[768,2,512]{2,0,1:T(8,128)(2,1)}, u32[]{:S(2)}) copy-start(bf16[768,2,512]{2,0,1:T(8,128)(2,1)} %bitcast_select_fusion.4) | copy-start | bytes 4718596
  43.0 3.4 %copy-start.10 = (f32[256]{0:T(256)S(1)}, f32[256]{0:T(256)}, u32[]{:S(2)}) copy-start(f32[256]{0:T(256)} %param.23) | copy-start | bytes 3076
  47.5 11.5 %collective-permute-start = (bf16[256,512]{0,1:T(8,128)(2,1)S(1)}, bf16[256,512]{0,1:T(8,128)(2,1)S(1)}, u32[]{:S(2)}, u32[]{:S(2)}) collective-permute-start(bf16[256,512]{0,1:T(8,128)(2,1)S(1)} %bitcast.132), channel_id=1, source_target_pairs={{0,1},{1,2},{2,3},{3,0},{4,5},{5,6},{6,7},{7,4},{8,9},{9,10},{10,1... | collective-permute-start | bytes 786440 | tf_op jit(solution)/shard_map/ppermute | solution.py:77
  51.4 11.4 %collective-permute-start.1 = (bf16[256,512]{0,1:T(8,128)(2,1)S(1)}, bf16[256,512]{0,1:T(8,128)(2,1)S(1)}, u32[]{:S(2)}, u32[]{:S(2)}) collective-permute-start(bf16[256,512]{0,1:T(8,128)(2,1)S(1)} %bitcast.133), channel_id=1, source_target_pairs={{0,2},{1,3},{2,0},{3,1},{4,6},{5,7},{6,4},{7,5},{8,10},{9,11},{10,... | collective-permute-start | bytes 786440 | tf_op jit(solution)/shard_map/ppermute | solution.py:77
  56.0 7.5 %collective-permute-start.2 = (bf16[256,512]{0,1:T(8,128)(2,1)S(1)}, bf16[256,512]{0,1:T(8,128)(2,1)S(1)}, u32[]{:S(2)}, u32[]{:S(2)}) collective-permute-start(bf16[256,512]{0,1:T(8,128)(2,1)S(1)} %bitcast.134), channel_id=1, source_target_pairs={{0,3},{1,0},{2,1},{3,2},{4,7},{5,4},{6,5},{7,6},{8,11},{9,8},{10,9... | collective-permute-start | bytes 786440 | tf_op jit(solution)/shard_map/ppermute | solution.py:77
  66.6 46.2 %copy-start.8 = (f32[2048]{0:T(1024)S(1)}, f32[2048]{0:T(1024)}, u32[]{:S(2)}) copy-start(f32[2048]{0:T(1024)} %param.26) | copy-start | bytes 24580
  104.9 17.2 %collective-permute-start.3 = (bf16[1024,2816]{1,0:T(8,128)(2,1)}, bf16[1024,2816]{1,0:T(8,128)(2,1)}, u32[]{:S(2)}, u32[]{:S(2)}) collective-permute-start(bf16[1024,2816]{1,0:T(8,128)(2,1)} %all-gather.2.cloned.1.call-done), channel_id=1, source_target_pairs={{0,4},{4,0},{1,5},{5,1},{2,6},{6,2},{3,7},{7,3},{8,12},{12,8},{9,1... | collective-permute-start | bytes 17301512 | tf_op jit(solution)/shard_map/ppermute | solution.py:118
  115.5 6.6 %copy-start.11 = (bf16[256,512]{1,0:T(8,128)(2,1)S(1)}, bf16[256,512]{1,0:T(8,128)(2,1)}, u32[]{:S(2)}) copy-start(bf16[256,512]{1,0:T(8,128)(2,1)} %param.24) | copy-start | bytes 786436
  123.8 14.4 %collective-permute-start.4 = (bf16[256,512]{1,0:T(8,128)(2,1)S(1)}, bf16[256,512]{1,0:T(8,128)(2,1)S(1)}, u32[]{:S(2)}, u32[]{:S(2)}) collective-permute-start(bf16[256,512]{1,0:T(8,128)(2,1)S(1)} %fusion.23), channel_id=1, source_target_pairs={{0,1},{1,2},{2,3},{3,0},{4,5},{5,6},{6,7},{7,4},{8,9},{9,10},{10,1... | collective-permute-start | bytes 786440 | tf_op jit(solution)/shard_map/ppermute | solution.py:77
  126.6 14.4 %collective-permute-start.5 = (bf16[256,512]{1,0:T(8,128)(2,1)S(1)}, bf16[256,512]{1,0:T(8,128)(2,1)S(1)}, u32[]{:S(2)}, u32[]{:S(2)}) collective-permute-start(bf16[256,512]{1,0:T(8,128)(2,1)S(1)} %fusion.23), channel_id=1, source_target_pairs={{0,2},{1,3},{2,0},{3,1},{4,6},{5,7},{6,4},{7,5},{8,10},{9,11},{10,... | collective-permute-start | bytes 786440 | tf_op jit(solution)/shard_map/ppermute | solution.py:77
  131.3 10.9 %collective-permute-start.6 = (bf16[256,512]{1,0:T(8,128)(2,1)S(1)}, bf16[256,512]{1,0:T(8,128)(2,1)S(1)}, u32[]{:S(2)}, u32[]{:S(2)}) collective-permute-start(bf16[256,512]{1,0:T(8,128)(2,1)S(1)} %fusion.23), channel_id=1, source_target_pairs={{0,3},{1,0},{2,1},{3,2},{4,7},{5,4},{6,5},{7,6},{8,11},{9,8},{10,9... | collective-permute-start | bytes 786440 | tf_op jit(solution)/shard_map/ppermute | solution.py:77
  154.2 2.9 %copy-start.5 = (bf16[16,1,16,768]{3,2,1,0:T(8,128)(2,1)S(1)}, bf16[16,1,16,768]{3,2,1,0:T(8,128)(2,1)}, u32[]{:S(2)}) copy-start(bf16[16,1,16,768]{3,2,1,0:T(8,128)(2,1)} %get-tuple-element.12) | copy-start | bytes 1179652
  154.2 2.9 %copy-start.7 = (bf16[16,1,16,768]{3,2,1,0:T(8,128)(2,1)S(1)}, bf16[16,1,16,768]{3,2,1,0:T(8,128)(2,1)}, u32[]{:S(2)}) copy-start(bf16[16,1,16,768]{3,2,1,0:T(8,128)(2,1)} %get-tuple-element.16) | copy-start | bytes 1179652
  156.3 0.7 copy-start.14
  156.3 3.0 %copy-start.4 = (bf16[16,1,16,768]{3,2,1,0:T(8,128)(2,1)S(1)}, bf16[16,1,16,768]{3,2,1,0:T(8,128)(2,1)}, u32[]{:S(2)}) copy-start(bf16[16,1,16,768]{3,2,1,0:T(8,128)(2,1)} %get-tuple-element.15) | copy-start | bytes 1179652
  156.4 3.0 %copy-start.6 = (bf16[16,1,16,768]{3,2,1,0:T(8,128)(2,1)S(1)}, bf16[16,1,16,768]{3,2,1,0:T(8,128)(2,1)}, u32[]{:S(2)}) copy-start(bf16[16,1,16,768]{3,2,1,0:T(8,128)(2,1)} %get-tuple-element.19) | copy-start | bytes 1179652
  162.6 9.2 %copy-start.3 = (bf16[16,1,16,768]{3,2,1,0:T(8,128)(2,1)S(1)}, bf16[16,1,16,768]{3,2,1,0:T(8,128)(2,1)}, u32[]{:S(2)}) copy-start(bf16[16,1,16,768]{3,2,1,0:T(8,128)(2,1)} %get-tuple-element.18) | copy-start | bytes 1179652
  163.5 19.8 %collective-permute-start.7 = (bf16[256,512]{1,0:T(8,128)(2,1)}, bf16[256,512]{1,0:T(8,128)(2,1)}, u32[]{:S(2)}, u32[]{:S(2)}) collective-permute-start(bf16[256,512]{1,0:T(8,128)(2,1)} %copy.79), channel_id=1, source_target_pairs={{0,1},{1,2},{2,3},{3,0},{4,5},{5,6},{6,7},{7,4},{8,9},{9,10},{10,1... | collective-permute-start | bytes 786440 | tf_op jit(solution)/shard_map/ppermute | solution.py:99
  176.0 10.6 %collective-permute-start.8 = (bf16[256,512]{1,0:T(8,128)(2,1)}, bf16[256,512]{1,0:T(8,128)(2,1)S(1)}, u32[]{:S(2)}, u32[]{:S(2)}) collective-permute-start(bf16[256,512]{1,0:T(8,128)(2,1)} %copy.83), channel_id=1, source_target_pairs={{0,2},{1,3},{2,0},{3,1},{4,6},{5,7},{6,4},{7,5},{8,10},{9,11},{10,... | collective-permute-start | bytes 786440 | tf_op jit(solution)/shard_map/ppermute | solution.py:99
  180.2 10.3 %collective-permute-start.9 = (bf16[256,512]{1,0:T(8,128)(2,1)}, bf16[256,512]{1,0:T(8,128)(2,1)S(1)}, u32[]{:S(2)}, u32[]{:S(2)}) collective-permute-start(bf16[256,512]{1,0:T(8,128)(2,1)} %copy.86), channel_id=1, source_target_pairs={{0,3},{1,0},{2,1},{3,2},{4,7},{5,4},{6,5},{7,6},{8,11},{9,8},{10,9... | collective-permute-start | bytes 786440 | tf_op jit(solution)/shard_map/ppermute | solution.py:99
Sparse Core Ops, SparseCore 0:
  19.1 85.7 all-gather.1

commit v9 on v8

--- a/solution.py
+++ b/solution.py
@@ -110,7 +110,18 @@
 
 
 def gather_over_xz(block):
-    out = lax.all_gather(block, "x", axis=0, tiled=True)
+    size = lax.axis_size("x")
+    index = lax.axis_index("x")
+    out = block
+    bit = 1
+    while bit < size:
+        partner = lax.ppermute(out, "x", [(i, i ^ bit) for i in range(size)])
+        out = jnp.where(
+            (index & bit) == 0,
+            jnp.concatenate([out, partner], axis=0),
+            jnp.concatenate([partner, out], axis=0),
+        )
+        bit *= 2
     return lax.all_gather(out, "z", axis=0, tiled=True)
 
 

time: 201 us -> 207 us (1.030)
  blocking collectives: 11.5 us -> 0 us
  starting transfers between devices: 40.9 us -> 49.7 us
  waiting for transfers between devices: 58.5 us -> 62.8 us
  local copies, waits for them, and re-layouts: 28.7 us -> 31.8 us
    all_gather x1 -> x0, blocking collectives: 11.5 us -> none  [gather_over_xz(): out = lax.all_gather(block, 'x', axis=0, tiled=True)]
    ppermute x0 -> x2, starting transfers between devices: none -> 8.83 us  [gather_over_xz(): partner = lax.ppermute(out, 'x', [(i, i ^ bit) for i in range(size)])]
    ppermute x0 -> x2, waiting for transfers between devices: none -> 4.76 us  [gather_over_xz(): partner = lax.ppermute(out, 'x', [(i, i ^ bit) for i in range(size)])]
    unnamed x31 -> x34, local copies, waits for them, and re-layouts: 1.61 us -> 3.94 us
  transfers between devices with their start and end apart: 11 -> 13, of which waited for: 8 -> 10; matrix products, arithmetic and copies ran while one was open for 23% -> 23% of each run, Pallas kernels for 0% -> 0%
where the time goes in v9:
time: 207 us; the launch traced here: 204 us
  waiting for transfers between devices  62.8 us (30%)
  starting transfers between devices  49.7 us (24%)
  local copies, waits for them, and re-layouts  31.8 us (15%)
  matrix products  30 us (14%)
  between operations  16 us (8%)
  other arithmetic  13.4 us (6%)
    all_gather x1, waiting for transfers between devices, gather_over_xz(): return lax.all_gather(out, 'z', axis=0, tiled=True)  38.6 us
    ppermute x6, starting transfers between devices, mlp_gather(): lax.ppermute(block, 'mlp', [(i, (i + shift) % axis_size) for i in range(a...  21.7 us
    dot_general x6, matrix products, split_dot(): jnp.dot(act[:, j * size:(j + 1) * size], half, preferred_element_type=jnp...  11.6 us
    ppermute x3, starting transfers between devices, down_and_scatter(): lax.ppermute(block_for(target), 'mlp', [(i, (i + shift) % axis_size) for...  11.4 us
    ppermute x2, starting transfers between devices, gather_over_xz(): partner = lax.ppermute(out, 'x', [(i, i ^ bit) for i in range(size)])  8.83 us
    ppermute x6, waiting for transfers between devices, mlp_gather(): lax.ppermute(block, 'mlp', [(i, (i + shift) % axis_size) for i in range(a...  8.21 us
    ppermute x1, starting transfers between devices, swap_with_core(): return [rows_xz, lax.ppermute(rows_xz, 'c', [(0, 1), (1, 0)])]  7.71 us
    dot_general x4, matrix products, block_for(): lax.dot_general(hidden_act, weight_rows, (((1,), (1,)), ((), ())), prefer...  7.65 us
  transfers between devices with their start and end apart: 13, of which 10 were waited for; matrix products, arithmetic and copies ran while one was open for 23% of the time, Pallas kernels for 0%

profile of v9, /device:TPU:1, one launch (start us, length us, event | category | flops | bytes accessed | tf_op | source)
XLA Modules:
  0.0 203.7 jit_solution(48156884652574491)
XLA Ops:
  9.6 3.9 %collective-permute-start = (bf16[16,2816]{1,0:T(8,128)(2,1)S(1)}, bf16[16,2816]{1,0:T(8,128)(2,1)S(1)}, u32[]{:S(2)}, u32[]{:S(2)}) collective-permute-start(bf16[16,2816]{1,0:T(8,128)(2,1)S(1)} %constant_dynamic-update-slice_fusion), channel_id=1, source_target_pairs={{0,128},{128,0},{256,384},{384,256},{1,129},{129,1},{257,385},{385... | collective-permute-start | bytes 270344 | tf_op jit(solution)/shard_map/ppermute | solution.py:118
  13.5 1.9 collective-permute-done
  15.5 4.9 %collective-permute-start.1 = (bf16[32,2816]{1,0:T(8,128)(2,1)S(1)}, bf16[32,2816]{1,0:T(8,128)(2,1)S(1)}, u32[]{:S(2)}, u32[]{:S(2)}) collective-permute-start(bf16[32,2816]{1,0:T(8,128)(2,1)S(1)} %maximum_select_fusion.1), channel_id=1, source_target_pairs={{0,256},{128,384},{256,0},{384,128},{1,257},{129,385},{257,1},{385... | collective-permute-start | bytes 540680 | tf_op jit(solution)/shard_map/ppermute | solution.py:118
  20.4 2.9 %collective-permute-done.1 = bf16[32,2816]{1,0:T(8,128)(2,1)S(1)} collective-permute-done((bf16[32,2816]{1,0:T(8,128)(2,1)S(1)}, bf16[32,2816]{1,0:T(8,128)(2,1)S(1)}, u32[]{:S(2)}, u32[]{:S(2)}) %collective-permute-start.1) | collective-permute-done | bytes 180256 | tf_op jit(solution)/shard_map/ppermute | solution.py:118
  24.8 5.6 %gather_fusion = bf16[6,128,2,512]{3,2,1,0:T(2,128)(2,1)} fusion(bf16[6,128,2,512]{3,2,1,0:T(2,128)(2,1)S(1)} %copy-done, s32[1024]{0:T(1024)S(1)} %pad_clamp_fusion.1), kind=kCustom, calls=%fused_computation.2 | custom fusion | bytes 3145752 | tf_op jit(solution)/shard_map/jit(_take)/gather | solution.py:23
  40.5 2.3 %fusion.132 = f32[256,2]{0,1:T(2,128)S(1)} fusion(pred[256,1024]{0,1:T(8,128)(4,1)S(1)} %pad_add_fusion, bf16[768,2,512]{2,0,1:T(8,128)(2,1)} %bitcast_select_fusion.4, bf16[256,2,512]{2,0,1:T(8,128)(2,1)} %copy.62, bf16[256,2,128]{2,1,0:T(2,128)(2,1)} %get-tuple-element.33), kind=kOutput, calls=%fused_computation.170 | convolution fusion | flops 137888768 | bytes 2754560 | tf_op jit(solution)/shard_map/sub | solution.py:45
  42.8 3.2 %fusion.18 = f32[256,2,256]{0,2,1:T(8,128)} fusion(f32[256,2]{0,1:T(2,128)S(1)} %fusion.132, pred[256,1024]{0,1:T(8,128)(4,1)S(1)} %pad_add_fusion, bf16[768,2,512]{2,0,1:T(8,128)(2,1)S(1)} %copy-done.1, bf16[256,2,512]{2,0,1:T(8,128)(2,1)} %copy.62, bf16[256,2,128]{2,1,0:T(2,128)(2,1)} %get-tuple-element.33), kind=kOutput, calls=%fused_computation.33 | convolution fusion | flops 408552960 | bytes 5376000 | tf_op jit(solution)/shard_map/nhk,khd->nhd/dot_general | solution.py:47
  46.0 2.0 fusion.137
  48.0 3.3 %multiply_reduce_fusion.1 = (f32[256,2]{0,1:T(2,128)S(1)}, f32[256,2,256]{0,2,1:T(8,128)}) fusion(f32[256,2,256]{0,2,1:T(8,128)} %fusion.18, f32[256,2]{0,1:T(2,128)S(1)} %fusion.137, pred[256,1024]{0,1:T(8,128)(4,1)S(1)} %pad_add_fusion, bf16[256,2,512]{2,0,1:T(8,128)(2,1)} %copy.62, bf16[768,2,512]{2,0,1:T(8,128)(2,1)S(1)} %copy-done.1, ...), kind=kOutput, calls=%fused_computation.86 | convolution fusion | flops 409076736 | bytes 5902340 | tf_op jit(solution)/shard_map/nhk,khd->nhd/dot_general | solution.py:47
  52.5 3.4 %collective-permute-start.2 = (bf16[256,512]{0,1:T(8,128)(2,1)S(1)}, bf16[256,512]{0,1:T(8,128)(2,1)S(1)}, u32[]{:S(2)}, u32[]{:S(2)}) collective-permute-start(bf16[256,512]{0,1:T(8,128)(2,1)S(1)} %bitcast.132), channel_id=1, source_target_pairs={{0,1},{1,2},{2,3},{3,0},{4,5},{5,6},{6,7},{7,4},{8,9},{9,10},{10,1... | collective-permute-start | bytes 786440 | tf_op jit(solution)/shard_map/ppermute | solution.py:77
  55.9 4.5 %collective-permute-start.3 = (bf16[256,512]{0,1:T(8,128)(2,1)S(1)}, bf16[256,512]{0,1:T(8,128)(2,1)S(1)}, u32[]{:S(2)}, u32[]{:S(2)}) collective-permute-start(bf16[256,512]{0,1:T(8,128)(2,1)S(1)} %bitcast.133), channel_id=1, source_target_pairs={{0,2},{1,3},{2,0},{3,1},{4,6},{5,7},{6,4},{7,5},{8,10},{9,11},{10,... | collective-permute-start | bytes 786440 | tf_op jit(solution)/shard_map/ppermute | solution.py:77
  60.4 3.0 %collective-permute-start.4 = (bf16[256,512]{0,1:T(8,128)(2,1)S(1)}, bf16[256,512]{0,1:T(8,128)(2,1)S(1)}, u32[]{:S(2)}, u32[]{:S(2)}) collective-permute-start(bf16[256,512]{0,1:T(8,128)(2,1)S(1)} %bitcast.134), channel_id=1, source_target_pairs={{0,3},{1,0},{2,1},{3,2},{4,7},{5,4},{6,5},{7,6},{8,11},{9,8},{10,9... | collective-permute-start | bytes 786440 | tf_op jit(solution)/shard_map/ppermute | solution.py:77
  63.5 3.7 %collective-permute-done.3 = bf16[256,512]{0,1:T(8,128)(2,1)S(1)} collective-permute-done((bf16[256,512]{0,1:T(8,128)(2,1)S(1)}, bf16[256,512]{0,1:T(8,128)(2,1)S(1)}, u32[]{:S(2)}, u32[]{:S(2)}) %collective-permute-start.3) | collective-permute-done | bytes 262176 | tf_op jit(solution)/shard_map/ppermute | solution.py:77
  71.3 38.6 %all-gather.2.cloned.1.call-done = bf16[1024,2816]{1,0:T(8,128)(2,1)} async-done(((bf16[64,2816]{1,0:T(8,128)(2,1)}), bf16[1024,2816]{1,0:T(8,128)(2,1)}) %all-gather.2.cloned.1.call-update) | async-done | bytes 5767184 | tf_op jit(solution)/shard_map/all_gather | solution.py:125
  109.9 7.7 %collective-permute-start.5 = (bf16[1024,2816]{1,0:T(8,128)(2,1)}, bf16[1024,2816]{1,0:T(8,128)(2,1)}, u32[]{:S(2)}, u32[]{:S(2)}) collective-permute-start(bf16[1024,2816]{1,0:T(8,128)(2,1)} %all-gather.2.cloned.1.call-done), channel_id=1, source_target_pairs={{0,4},{4,0},{1,5},{5,1},{2,6},{6,2},{3,7},{7,3},{8,12},{12,8},{9,1... | collective-permute-start | bytes 17301512 | tf_op jit(solution)/shard_map/ppermute | solution.py:129
  122.2 4.7 %collective-permute-done.5 = bf16[1024,2816]{1,0:T(8,128)(2,1)} collective-permute-done((bf16[1024,2816]{1,0:T(8,128)(2,1)}, bf16[1024,2816]{1,0:T(8,128)(2,1)}, u32[]{:S(2)}, u32[]{:S(2)}) %collective-permute-start.5) | collective-permute-done | bytes 5767200 | tf_op jit(solution)/shard_map/ppermute | solution.py:129
  128.6 2.7 %collective-permute-start.6 = (bf16[256,512]{1,0:T(8,128)(2,1)S(1)}, bf16[256,512]{1,0:T(8,128)(2,1)S(1)}, u32[]{:S(2)}, u32[]{:S(2)}) collective-permute-start(bf16[256,512]{1,0:T(8,128)(2,1)S(1)} %fusion.23), channel_id=1, source_target_pairs={{0,1},{1,2},{2,3},{3,0},{4,5},{5,6},{6,7},{7,4},{8,9},{9,10},{10,1... | collective-permute-start | bytes 786440 | tf_op jit(solution)/shard_map/ppermute | solution.py:77
  131.4 4.9 %collective-permute-start.7 = (bf16[256,512]{1,0:T(8,128)(2,1)S(1)}, bf16[256,512]{1,0:T(8,128)(2,1)S(1)}, u32[]{:S(2)}, u32[]{:S(2)}) collective-permute-start(bf16[256,512]{1,0:T(8,128)(2,1)S(1)} %fusion.23), channel_id=1, source_target_pairs={{0,2},{1,3},{2,0},{3,1},{4,6},{5,7},{6,4},{7,5},{8,10},{9,11},{10,... | collective-permute-start | bytes 786440 | tf_op jit(solution)/shard_map/ppermute | solution.py:77
  136.2 3.2 %collective-permute-start.8 = (bf16[256,512]{1,0:T(8,128)(2,1)S(1)}, bf16[256,512]{1,0:T(8,128)(2,1)S(1)}, u32[]{:S(2)}, u32[]{:S(2)}) collective-permute-start(bf16[256,512]{1,0:T(8,128)(2,1)S(1)} %fusion.23), channel_id=1, source_target_pairs={{0,3},{1,0},{2,1},{3,2},{4,7},{5,4},{6,5},{7,6},{8,11},{9,8},{10,9... | collective-permute-start | bytes 786440 | tf_op jit(solution)/shard_map/ppermute | solution.py:77
  143.3 2.7 %collective-permute-done.7 = bf16[256,512]{1,0:T(8,128)(2,1)S(1)} collective-permute-done((bf16[256,512]{1,0:T(8,128)(2,1)S(1)}, bf16[256,512]{1,0:T(8,128)(2,1)S(1)}, u32[]{:S(2)}, u32[]{:S(2)}) %collective-permute-start.7) | collective-permute-done | bytes 262176 | tf_op jit(solution)/shard_map/ppermute | solution.py:77
  153.0 2.0 fusion.8
  155.0 2.0 fusion.10
  157.0 2.0 fusion.12
  159.1 2.1 %multiply_convert_fusion.1 = bf16[256,768]{1,0:T(8,128)(2,1)S(1)} fusion(f32[256,768]{1,0:T(8,128)S(1)} %fusion.12, f32[256,768]{1,0:T(8,128)S(1)} %fusion.8, bf16[1024,2816]{1,0:T(8,128)(2,1)} %collective-permute-done.5, bf16[256,2048]{0,1:T(8,128)(2,1)S(1)} %bitcast.123), kind=kOutput, calls=%fused_computation.75 | convolution fusion | flops 404029440 | bytes 4063232 | tf_op jit(solution)/shard_map/dot_general | solution.py:136
  164.2 2.1 %convolution_convert_fusion.3 = bf16[256,512]{1,0:T(8,128)(2,1)} fusion(bf16[256,768]{1,0:T(8,128)(2,1)} %copy-done.14, bf16[256,768]{1,0:T(8,128)(2,1)S(1)} %bitcast.146, bf16[256,768]{1,0:T(8,128)(2,1)S(1)} %bitcast.144), kind=kOutput, calls=%fused_computation.42 | convolution fusion | flops 203030528 | bytes 1441792 | tf_op jit(solution)/shard_map/dot_general | solution.py:90
  168.4 5.2 %collective-permute-start.9 = (bf16[256,512]{1,0:T(8,128)(2,1)}, bf16[256,512]{1,0:T(8,128)(2,1)}, u32[]{:S(2)}, u32[]{:S(2)}) collective-permute-start(bf16[256,512]{1,0:T(8,128)(2,1)} %copy.79), channel_id=1, source_target_pairs={{0,1},{1,2},{2,3},{3,0},{4,5},{5,6},{6,7},{7,4},{8,9},{9,10},{10,1... | collective-permute-start | bytes 786440 | tf_op jit(solution)/shard_map/ppermute | solution.py:99
  173.6 2.3 %convolution_convert_fusion = bf16[256,512]{1,0:T(8,128)(2,1)} fusion(bf16[256,768]{1,0:T(8,128)(2,1)} %copy-done.14, bf16[256,768]{1,0:T(8,128)(2,1)} %bitcast.143, bf16[256,768]{1,0:T(8,128)(2,1)} %bitcast.141), kind=kOutput, calls=%fused_computation.39 | convolution fusion | flops 203030528 | bytes 1441792 | tf_op jit(solution)/shard_map/dot_general | solution.py:90
  177.0 2.1 %convolution_convert_fusion.1 = bf16[256,512]{1,0:T(8,128)(2,1)} fusion(bf16[256,768]{1,0:T(8,128)(2,1)} %copy-done.14, bf16[256,768]{1,0:T(8,128)(2,1)S(1)} %bitcast.142, bf16[256,768]{1,0:T(8,128)(2,1)S(1)} %bitcast.140), kind=kOutput, calls=%fused_computation.40 | convolution fusion | flops 203030528 | bytes 1441792 | tf_op jit(solution)/shard_map/dot_general | solution.py:90
  181.2 2.9 %collective-permute-start.10 = (bf16[256,512]{1,0:T(8,128)(2,1)}, bf16[256,512]{1,0:T(8,128)(2,1)S(1)}, u32[]{:S(2)}, u32[]{:S(2)}) collective-permute-start(bf16[256,512]{1,0:T(8,128)(2,1)} %copy.83), channel_id=1, source_target_pairs={{0,2},{1,3},{2,0},{3,1},{4,6},{5,7},{6,4},{7,5},{8,10},{9,11},{10,... | collective-permute-start | bytes 786440 | tf_op jit(solution)/shard_map/ppermute | solution.py:99
  184.9 3.3 %collective-permute-start.11 = (bf16[256,512]{1,0:T(8,128)(2,1)}, bf16[256,512]{1,0:T(8,128)(2,1)S(1)}, u32[]{:S(2)}, u32[]{:S(2)}) collective-permute-start(bf16[256,512]{1,0:T(8,128)(2,1)} %copy.86), channel_id=1, source_target_pairs={{0,3},{1,0},{2,1},{3,2},{4,7},{5,4},{6,5},{7,6},{8,11},{9,8},{10,9... | collective-permute-start | bytes 786440 | tf_op jit(solution)/shard_map/ppermute | solution.py:99
  188.5 3.3 %collective-permute-done.10 = bf16[256,512]{1,0:T(8,128)(2,1)S(1)} collective-permute-done((bf16[256,512]{1,0:T(8,128)(2,1)}, bf16[256,512]{1,0:T(8,128)(2,1)S(1)}, u32[]{:S(2)}, u32[]{:S(2)}) %collective-permute-start.10) | collective-permute-done | bytes 262176 | tf_op jit(solution)/shard_map/ppermute | solution.py:99
  191.8 3.1 %collective-permute-done.11 = bf16[256,512]{1,0:T(8,128)(2,1)S(1)} collective-permute-done((bf16[256,512]{1,0:T(8,128)(2,1)}, bf16[256,512]{1,0:T(8,128)(2,1)S(1)}, u32[]{:S(2)}, u32[]{:S(2)}) %collective-permute-start.11) | collective-permute-done | bytes 262176 | tf_op jit(solution)/shard_map/ppermute | solution.py:99
  (105 shorter events, 45.9 us)
Async XLA Ops:
  6.5 18.2 %copy-start = (bf16[6,128,2,512]{3,2,1,0:T(2,128)(2,1)S(1)}, bf16[6,128,2,512]{3,2,1,0:T(2,128)(2,1)}, u32[]{:S(2)}) copy-start(bf16[6,128,2,512]{3,2,1,0:T(2,128)(2,1)} %param.18) | copy-start | bytes 4718596
  6.5 103.3 %all-gather.2.cloned.1.call-start = ((), (), s32[]{:S(2)}) async-start(), calls=%async_computation | async-start | bytes 6127616 | tf_op jit(solution)/shard_map/all_gather | solution.py:125
  9.6 5.8 %collective-permute-start = (bf16[16,2816]{1,0:T(8,128)(2,1)S(1)}, bf16[16,2816]{1,0:T(8,128)(2,1)S(1)}, u32[]{:S(2)}, u32[]{:S(2)}) collective-permute-start(bf16[16,2816]{1,0:T(8,128)(2,1)S(1)} %constant_dynamic-update-slice_fusion), channel_id=1, source_target_pairs={{0,128},{128,0},{256,384},{384,256},{1,129},{129,1},{257,385},{385... | collective-permute-start | bytes 270344 | tf_op jit(solution)/shard_map/ppermute | solution.py:118
  15.5 7.8 %collective-permute-start.1 = (bf16[32,2816]{1,0:T(8,128)(2,1)S(1)}, bf16[32,2816]{1,0:T(8,128)(2,1)S(1)}, u32[]{:S(2)}, u32[]{:S(2)}) collective-permute-start(bf16[32,2816]{1,0:T(8,128)(2,1)S(1)} %maximum_select_fusion.1), channel_id=1, source_target_pairs={{0,256},{128,384},{256,0},{384,128},{1,257},{129,385},{257,1},{385... | collective-permute-start | bytes 540680 | tf_op jit(solution)/shard_map/ppermute | solution.py:118
  30.3 1.8 copy-start.2
  30.3 3.3 %copy-start.9 = (f32[4,128]{1,0:T(4,128)S(1)}, f32[4,128]{1,0:T(4,128)}, u32[]{:S(2)}) copy-start(f32[4,128]{1,0:T(4,128)} %param.22) | copy-start | bytes 6148
  30.3 5.3 %copy-start.12 = (s32[128]{0:T(128)S(1)}, s32[128]{0:T(128)}, u32[]{:S(2)}) copy-start(s32[128]{0:T(128)} %param.21) | copy-start | bytes 1540
  30.3 6.6 %copy-start.13 = (s32[1,6]{1,0:T(1,128)S(1)}, s32[1,6]{1,0:T(1,128)}, u32[]{:S(2)}) copy-start(s32[1,6]{1,0:T(1,128)} %param.19) | copy-start | bytes 76
  40.5 2.3 %copy-start.1 = (bf16[768,2,512]{2,0,1:T(8,128)(2,1)S(1)}, bf16[768,2,512]{2,0,1:T(8,128)(2,1)}, u32[]{:S(2)}) copy-start(bf16[768,2,512]{2,0,1:T(8,128)(2,1)} %bitcast_select_fusion.4) | copy-start | bytes 4718596
  48.0 3.4 %copy-start.10 = (f32[256]{0:T(256)S(1)}, f32[256]{0:T(256)}, u32[]{:S(2)}) copy-start(f32[256]{0:T(256)} %param.23) | copy-start | bytes 3076
  52.5 11.0 %collective-permute-start.2 = (bf16[256,512]{0,1:T(8,128)(2,1)S(1)}, bf16[256,512]{0,1:T(8,128)(2,1)S(1)}, u32[]{:S(2)}, u32[]{:S(2)}) collective-permute-start(bf16[256,512]{0,1:T(8,128)(2,1)S(1)} %bitcast.132), channel_id=1, source_target_pairs={{0,1},{1,2},{2,3},{3,0},{4,5},{5,6},{6,7},{7,4},{8,9},{9,10},{10,1... | collective-permute-start | bytes 786440 | tf_op jit(solution)/shard_map/ppermute | solution.py:77
  55.9 11.3 %collective-permute-start.3 = (bf16[256,512]{0,1:T(8,128)(2,1)S(1)}, bf16[256,512]{0,1:T(8,128)(2,1)S(1)}, u32[]{:S(2)}, u32[]{:S(2)}) collective-permute-start(bf16[256,512]{0,1:T(8,128)(2,1)S(1)} %bitcast.133), channel_id=1, source_target_pairs={{0,2},{1,3},{2,0},{3,1},{4,6},{5,7},{6,4},{7,5},{8,10},{9,11},{10,... | collective-permute-start | bytes 786440 | tf_op jit(solution)/shard_map/ppermute | solution.py:77
  60.4 7.5 %collective-permute-start.4 = (bf16[256,512]{0,1:T(8,128)(2,1)S(1)}, bf16[256,512]{0,1:T(8,128)(2,1)S(1)}, u32[]{:S(2)}, u32[]{:S(2)}) collective-permute-start(bf16[256,512]{0,1:T(8,128)(2,1)S(1)} %bitcast.134), channel_id=1, source_target_pairs={{0,3},{1,0},{2,1},{3,2},{4,7},{5,4},{6,5},{7,6},{8,11},{9,8},{10,9... | collective-permute-start | bytes 786440 | tf_op jit(solution)/shard_map/ppermute | solution.py:77
  71.1 46.5 %copy-start.8 = (f32[2048]{0:T(1024)S(1)}, f32[2048]{0:T(1024)}, u32[]{:S(2)}) copy-start(f32[2048]{0:T(1024)} %param.26) | copy-start | bytes 24580
  109.9 17.1 %collective-permute-start.5 = (bf16[1024,2816]{1,0:T(8,128)(2,1)}, bf16[1024,2816]{1,0:T(8,128)(2,1)}, u32[]{:S(2)}, u32[]{:S(2)}) collective-permute-start(bf16[1024,2816]{1,0:T(8,128)(2,1)} %all-gather.2.cloned.1.call-done), channel_id=1, source_target_pairs={{0,4},{4,0},{1,5},{5,1},{2,6},{6,2},{3,7},{7,3},{8,12},{12,8},{9,1... | collective-permute-start | bytes 17301512 | tf_op jit(solution)/shard_map/ppermute | solution.py:129
  120.4 6.6 %copy-start.11 = (bf16[256,512]{1,0:T(8,128)(2,1)S(1)}, bf16[256,512]{1,0:T(8,128)(2,1)}, u32[]{:S(2)}) copy-start(bf16[256,512]{1,0:T(8,128)(2,1)} %param.24) | copy-start | bytes 786436
  128.6 14.7 %collective-permute-start.6 = (bf16[256,512]{1,0:T(8,128)(2,1)S(1)}, bf16[256,512]{1,0:T(8,128)(2,1)S(1)}, u32[]{:S(2)}, u32[]{:S(2)}) collective-permute-start(bf16[256,512]{1,0:T(8,128)(2,1)S(1)} %fusion.23), channel_id=1, source_target_pairs={{0,1},{1,2},{2,3},{3,0},{4,5},{5,6},{6,7},{7,4},{8,9},{9,10},{10,1... | collective-permute-start | bytes 786440 | tf_op jit(solution)/shard_map/ppermute | solution.py:77
  131.4 14.6 %collective-permute-start.7 = (bf16[256,512]{1,0:T(8,128)(2,1)S(1)}, bf16[256,512]{1,0:T(8,128)(2,1)S(1)}, u32[]{:S(2)}, u32[]{:S(2)}) collective-permute-start(bf16[256,512]{1,0:T(8,128)(2,1)S(1)} %fusion.23), channel_id=1, source_target_pairs={{0,2},{1,3},{2,0},{3,1},{4,6},{5,7},{6,4},{7,5},{8,10},{9,11},{10,... | collective-permute-start | bytes 786440 | tf_op jit(solution)/shard_map/ppermute | solution.py:77
  136.2 10.8 %collective-permute-start.8 = (bf16[256,512]{1,0:T(8,128)(2,1)S(1)}, bf16[256,512]{1,0:T(8,128)(2,1)S(1)}, u32[]{:S(2)}, u32[]{:S(2)}) collective-permute-start(bf16[256,512]{1,0:T(8,128)(2,1)S(1)} %fusion.23), channel_id=1, source_target_pairs={{0,3},{1,0},{2,1},{3,2},{4,7},{5,4},{6,5},{7,6},{8,11},{9,8},{10,9... | collective-permute-start | bytes 786440 | tf_op jit(solution)/shard_map/ppermute | solution.py:77
  159.0 2.9 %copy-start.5 = (bf16[16,1,16,768]{3,2,1,0:T(8,128)(2,1)S(1)}, bf16[16,1,16,768]{3,2,1,0:T(8,128)(2,1)}, u32[]{:S(2)}) copy-start(bf16[16,1,16,768]{3,2,1,0:T(8,128)(2,1)} %get-tuple-element.12) | copy-start | bytes 1179652
  159.1 2.9 %copy-start.7 = (bf16[16,1,16,768]{3,2,1,0:T(8,128)(2,1)S(1)}, bf16[16,1,16,768]{3,2,1,0:T(8,128)(2,1)}, u32[]{:S(2)}) copy-start(bf16[16,1,16,768]{3,2,1,0:T(8,128)(2,1)} %get-tuple-element.16) | copy-start | bytes 1179652
  161.2 0.8 copy-start.14
  161.2 3.0 %copy-start.4 = (bf16[16,1,16,768]{3,2,1,0:T(8,128)(2,1)S(1)}, bf16[16,1,16,768]{3,2,1,0:T(8,128)(2,1)}, u32[]{:S(2)}) copy-start(bf16[16,1,16,768]{3,2,1,0:T(8,128)(2,1)} %get-tuple-element.15) | copy-start | bytes 1179652
  161.2 3.0 %copy-start.6 = (bf16[16,1,16,768]{3,2,1,0:T(8,128)(2,1)S(1)}, bf16[16,1,16,768]{3,2,1,0:T(8,128)(2,1)}, u32[]{:S(2)}) copy-start(bf16[16,1,16,768]{3,2,1,0:T(8,128)(2,1)} %get-tuple-element.19) | copy-start | bytes 1179652
  167.5 9.5 %copy-start.3 = (bf16[16,1,16,768]{3,2,1,0:T(8,128)(2,1)S(1)}, bf16[16,1,16,768]{3,2,1,0:T(8,128)(2,1)}, u32[]{:S(2)}) copy-start(bf16[16,1,16,768]{3,2,1,0:T(8,128)(2,1)} %get-tuple-element.18) | copy-start | bytes 1179652
  168.4 20.1 %collective-permute-start.9 = (bf16[256,512]{1,0:T(8,128)(2,1)}, bf16[256,512]{1,0:T(8,128)(2,1)}, u32[]{:S(2)}, u32[]{:S(2)}) collective-permute-start(bf16[256,512]{1,0:T(8,128)(2,1)} %copy.79), channel_id=1, source_target_pairs={{0,1},{1,2},{2,3},{3,0},{4,5},{5,6},{6,7},{7,4},{8,9},{9,10},{10,1... | collective-permute-start | bytes 786440 | tf_op jit(solution)/shard_map/ppermute | solution.py:99
  181.2 10.7 %collective-permute-start.10 = (bf16[256,512]{1,0:T(8,128)(2,1)}, bf16[256,512]{1,0:T(8,128)(2,1)S(1)}, u32[]{:S(2)}, u32[]{:S(2)}) collective-permute-start(bf16[256,512]{1,0:T(8,128)(2,1)} %copy.83), channel_id=1, source_target_pairs={{0,2},{1,3},{2,0},{3,1},{4,6},{5,7},{6,4},{7,5},{8,10},{9,11},{10,... | collective-permute-start | bytes 786440 | tf_op jit(solution)/shard_map/ppermute | solution.py:99
  184.9 10.1 %collective-permute-start.11 = (bf16[256,512]{1,0:T(8,128)(2,1)}, bf16[256,512]{1,0:T(8,128)(2,1)S(1)}, u32[]{:S(2)}, u32[]{:S(2)}) collective-permute-start(bf16[256,512]{1,0:T(8,128)(2,1)} %copy.86), channel_id=1, source_target_pairs={{0,3},{1,0},{2,1},{3,2},{4,7},{5,4},{6,5},{7,6},{8,11},{9,8},{10,9... | collective-permute-start | bytes 786440 | tf_op jit(solution)/shard_map/ppermute | solution.py:99
Sparse Core Ops, SparseCore 0:
  24.2 85.6 all-gather.1

commit v10 on v8

--- a/solution.py
+++ b/solution.py
@@ -82,15 +82,23 @@
     return jnp.concatenate([gathered[k] for k in range(axis_size)], axis=1)
 
 
-def down_and_scatter(hidden_act, down_full, axis_size, rows):
+def down_and_scatter(hidden_act, down_halves, axis_size, rows):
     index = lax.axis_index("mlp")
+    nx, nz, nc = [lax.axis_size(name) for name in REQ_PARTS]
+    n = hidden_act.shape[0]
+    own = lax.axis_index("c")
+    parts = []
+    for half in down_halves:
+        value = lax.dot_general(
+            hidden_act, half, (((1,), (1,)), ((), ())), preferred_element_type=jnp.float32
+        )
+        parts.append(value.astype(jnp.bfloat16).reshape(n, nz, nx, rows))
+    both = jnp.stack(parts, axis=1)
+    both = jnp.where(own == 0, both, both[:, ::-1])
 
     def block_for(target):
-        weight_rows = down_block_rows(down_full, target, rows)
-        value = lax.dot_general(
-            hidden_act, weight_rows, (((1,), (1,)), ((), ())), preferred_element_type=jnp.float32
-        )
-        return block_to_req_order(value.astype(jnp.bfloat16), rows)
+        picked = lax.dynamic_index_in_dim(both, target, 3, keepdims=False)
+        return picked.transpose(0, 2, 1, 3).reshape(n, -1)
 
     incoming = []
     for shift in range(1, axis_size):
@@ -134,25 +142,6 @@
     split = act.reshape(n, nx, nz, nc, rows)
     split = jnp.where(own == 0, split, split[:, :, :, ::-1, :])
     return split.transpose(0, 3, 2, 1, 4).reshape(n, -1)
-
-
-def down_block_rows(down_halves, target, rows):
-    nx, nz, nc = [lax.axis_size(name) for name in REQ_PARTS]
-    picked = []
-    for half in down_halves:
-        split = half.reshape(nz, nx, rows, half.shape[1])
-        one = lax.dynamic_index_in_dim(split, target, 1, keepdims=False)
-        picked.append(one.reshape(nz * rows, half.shape[1]))
-    return jnp.concatenate(picked, axis=0)
-
-
-def block_to_req_order(value, rows):
-    nx, nz, nc = [lax.axis_size(name) for name in REQ_PARTS]
-    n = value.shape[0]
-    own = lax.axis_index("c")
-    split = value.reshape(n, nc, nz, rows)
-    split = jnp.where(own == 0, split, split[:, ::-1, :, :])
-    return split.transpose(0, 2, 1, 3).reshape(n, -1)
 
 
 def per_device(

time: 201 us -> 193 us (0.960)
  local copies, waits for them, and re-layouts: 28.7 us -> 18.9 us
  waiting for transfers between devices: 58.5 us -> 64.2 us
  matrix products: 30 us -> 26.5 us
    convert_element_type x4 -> x2, local copies, waits for them, and re-layouts: 4.32 us -> 0.41 us  [down_and_scatter(): parts.append(value.astype(jnp.bfloat16).reshape(n, nz, nx, rows))]
    ppermute x6, waiting for transfers between devices: 8.48 us -> 12.1 us  [mlp_gather(): lax.ppermute(block, 'mlp', [(i, (i + shift) % axis_size) for i in range(a...]
    dot_general x4 -> x2, matrix products: 7.66 us -> 4.15 us  [down_and_scatter(): lax.dot_general(hidden_act, half, (((1,), (1,)), ((), ())), preferred_ele...]
    slice x2 -> x0, local copies, waits for them, and re-layouts: 3.02 us -> none  [per_device(): half[:, bounds[i]:bounds[i + 1]]]
    dynamic_slice x2 -> x0, local copies, waits for them, and re-layouts: 2.32 us -> none  [down_block_rows(): one = lax.dynamic_index_in_dim(split, target, 1, keepdims=False)]
    ppermute x1, waiting for transfers between devices: 4.73 us -> 7.05 us  [swap_with_core(): return [rows_xz, lax.ppermute(rows_xz, 'c', [(0, 1), (1, 0)])]]
  transfers between devices with their start and end apart: 11 -> 11, of which waited for: 8 -> 8; matrix products, arithmetic and copies ran while one was open for 23% -> 18% of each run, Pallas kernels for 0% -> 0%
where the time goes in v10:
time: 193 us; the launch traced here: 191 us
  waiting for transfers between devices  64.2 us (33%)
  starting transfers between devices  40.9 us (21%)
  matrix products  26.5 us (14%)
  local copies, waits for them, and re-layouts  18.9 us (10%)
  between operations  16 us (8%)
  other arithmetic  13.1 us (7%)
  blocking collectives  11.5 us (6%)
    all_gather x1, waiting for transfers between devices, gather_over_xz(): return lax.all_gather(out, 'z', axis=0, tiled=True)  38.1 us
    ppermute x6, starting transfers between devices, mlp_gather(): lax.ppermute(block, 'mlp', [(i, (i + shift) % axis_size) for i in range(a...  22.6 us
    ppermute x6, waiting for transfers between devices, mlp_gather(): lax.ppermute(block, 'mlp', [(i, (i + shift) % axis_size) for i in range(a...  12.1 us
    dot_general x6, matrix products, split_dot(): jnp.dot(act[:, j * size:(j + 1) * size], half, preferred_element_type=jnp...  11.5 us
    all_gather x1, blocking collectives, gather_over_xz(): out = lax.all_gather(block, 'x', axis=0, tiled=True)  11.5 us
    ppermute x3, starting transfers between devices, down_and_scatter(): lax.ppermute(block_for(target), 'mlp', [(i, (i + shift) % axis_size) for...  11.1 us
    gather x2, local copies, waits for them, and re-layouts, attend(): pages = jnp.take(cache_pool, page_table[0], axis=0)  7.33 us
    ppermute x1, starting transfers between devices, swap_with_core(): return [rows_xz, lax.ppermute(rows_xz, 'c', [(0, 1), (1, 0)])]  7.24 us
  transfers between devices with their start and end apart: 11, of which 8 were waited for; matrix products, arithmetic and copies ran while one was open for 18% of the time, Pallas kernels for 0%

profile of v10, /device:TPU:1, one launch (start us, length us, event | category | flops | bytes accessed | tf_op | source)
XLA Modules:
  0.0 190.9 jit_solution(3541181415488043765)
XLA Ops:
  7.4 11.5 %all_gather.6 = bf16[64,2816]{1,0:T(8,128)(2,1)} all-gather(bf16[16,2816]{1,0:T(8,128)(2,1)S(1)} %pad_maximum_fusion.16), channel_id=1, replica_groups=mesh['x'=4,'z'=16,'c'=2,'mlp'=4] {'x'}, dimensions={0}, use_global_device_ids=true | all-gather | bytes 450560 | tf_op jit(solution)/shard_map/all_gather | solution.py:121
  19.6 5.6 %gather_fusion = bf16[6,128,2,512]{3,2,1,0:T(2,128)(2,1)} fusion(bf16[6,128,2,512]{3,2,1,0:T(2,128)(2,1)S(1)} %copy-done, s32[1024]{0:T(1024)S(1)} %pad_clamp_fusion.1), kind=kCustom, calls=%fused_computation.2 | custom fusion | bytes 3145752 | tf_op jit(solution)/shard_map/jit(_take)/gather | solution.py:23
  32.3 1.8 fusion.122
  35.6 2.3 %fusion.123 = f32[256,2]{0,1:T(2,128)S(1)} fusion(pred[256,1024]{0,1:T(8,128)(4,1)S(1)} %pad_add_fusion, bf16[768,2,512]{2,0,1:T(8,128)(2,1)} %bitcast_select_fusion.4, bf16[256,2,512]{2,0,1:T(8,128)(2,1)} %copy.51, bf16[256,2,128]{2,1,0:T(2,128)(2,1)} %get-tuple-element.29), kind=kOutput, calls=%fused_computation.141 | convolution fusion | flops 137888768 | bytes 2754560 | tf_op jit(solution)/shard_map/sub | solution.py:45
  37.9 3.2 %fusion.28 = f32[256,2,256]{0,2,1:T(8,128)} fusion(f32[256,2]{0,1:T(2,128)S(1)} %fusion.123, pred[256,1024]{0,1:T(8,128)(4,1)S(1)} %pad_add_fusion, bf16[768,2,512]{2,0,1:T(8,128)(2,1)S(1)} %copy-done.1, bf16[256,2,512]{2,0,1:T(8,128)(2,1)} %copy.51, bf16[256,2,128]{2,1,0:T(2,128)(2,1)} %get-tuple-element.29), kind=kOutput, calls=%fused_computation.40 | convolution fusion | flops 408552960 | bytes 5376000 | tf_op jit(solution)/shard_map/nhk,khd->nhd/dot_general | solution.py:47
  41.1 2.0 %fusion.128 = f32[256,2]{0,1:T(2,128)S(1)} fusion(pred[256,1024]{0,1:T(8,128)(4,1)S(1)} %pad_add_fusion, bf16[256,2,512]{2,0,1:T(8,128)(2,1)} %copy.51, bf16[768,2,512]{2,0,1:T(8,128)(2,1)S(1)} %copy-done.1, bf16[256,2,128]{2,1,0:T(2,128)(2,1)S(1)} %get-tuple-element.28), kind=kOutput, calls=%fused_computation.142 | convolution fusion | flops 137888768 | bytes 2492416 | tf_op jit(solution)/shard_map/sub | solution.py:45
  43.1 3.4 %multiply_reduce_fusion.1 = (f32[256,2]{0,1:T(2,128)S(1)}, f32[256,2,256]{0,2,1:T(8,128)}) fusion(f32[256,2,256]{0,2,1:T(8,128)} %fusion.28, f32[256,2]{0,1:T(2,128)S(1)} %fusion.128, pred[256,1024]{0,1:T(8,128)(4,1)S(1)} %pad_add_fusion, bf16[256,2,512]{2,0,1:T(8,128)(2,1)} %copy.51, bf16[768,2,512]{2,0,1:T(8,128)(2,1)S(1)} %copy-done.1, ...), kind=kOutput, calls=%fused_computation.78 | convolution fusion | flops 409076736 | bytes 5902340 | tf_op jit(solution)/shard_map/nhk,khd->nhd/dot_general | solution.py:47
  47.6 3.9 %collective-permute-start = (bf16[256,512]{0,1:T(8,128)(2,1)S(1)}, bf16[256,512]{0,1:T(8,128)(2,1)S(1)}, u32[]{:S(2)}, u32[]{:S(2)}) collective-permute-start(bf16[256,512]{0,1:T(8,128)(2,1)S(1)} %bitcast.123), channel_id=1, source_target_pairs={{0,1},{1,2},{2,3},{3,0},{4,5},{5,6},{6,7},{7,4},{8,9},{9,10},{10,1... | collective-permute-start | bytes 786440 | tf_op jit(solution)/shard_map/ppermute | solution.py:77
  51.5 4.5 %collective-permute-start.1 = (bf16[256,512]{0,1:T(8,128)(2,1)S(1)}, bf16[256,512]{0,1:T(8,128)(2,1)S(1)}, u32[]{:S(2)}, u32[]{:S(2)}) collective-permute-start(bf16[256,512]{0,1:T(8,128)(2,1)S(1)} %bitcast.124), channel_id=1, source_target_pairs={{0,2},{1,3},{2,0},{3,1},{4,6},{5,7},{6,4},{7,5},{8,10},{9,11},{10,... | collective-permute-start | bytes 786440 | tf_op jit(solution)/shard_map/ppermute | solution.py:77
  56.1 3.0 %collective-permute-start.2 = (bf16[256,512]{0,1:T(8,128)(2,1)S(1)}, bf16[256,512]{0,1:T(8,128)(2,1)S(1)}, u32[]{:S(2)}, u32[]{:S(2)}) collective-permute-start(bf16[256,512]{0,1:T(8,128)(2,1)S(1)} %bitcast.125), channel_id=1, source_target_pairs={{0,3},{1,0},{2,1},{3,2},{4,7},{5,4},{6,5},{7,6},{8,11},{9,8},{10,9... | collective-permute-start | bytes 786440 | tf_op jit(solution)/shard_map/ppermute | solution.py:77
  59.1 3.9 %collective-permute-done.1 = bf16[256,512]{0,1:T(8,128)(2,1)S(1)} collective-permute-done((bf16[256,512]{0,1:T(8,128)(2,1)S(1)}, bf16[256,512]{0,1:T(8,128)(2,1)S(1)}, u32[]{:S(2)}, u32[]{:S(2)}) %collective-permute-start.1) | collective-permute-done | bytes 262176 | tf_op jit(solution)/shard_map/ppermute | solution.py:77
  64.7 1.8 gather_fusion.1
  66.9 38.1 %all-gather.2.cloned.1.call-done = bf16[1024,2816]{1,0:T(8,128)(2,1)} async-done(((bf16[64,2816]{1,0:T(8,128)(2,1)}), bf16[1024,2816]{1,0:T(8,128)(2,1)}) %all-gather.2.cloned.1.call-update) | async-done | bytes 5767184 | tf_op jit(solution)/shard_map/all_gather | solution.py:122
  104.9 7.2 %collective-permute-start.3 = (bf16[1024,2816]{1,0:T(8,128)(2,1)}, bf16[1024,2816]{1,0:T(8,128)(2,1)}, u32[]{:S(2)}, u32[]{:S(2)}) collective-permute-start(bf16[1024,2816]{1,0:T(8,128)(2,1)} %all-gather.2.cloned.1.call-done), channel_id=1, source_target_pairs={{0,4},{4,0},{1,5},{5,1},{2,6},{6,2},{3,7},{7,3},{8,12},{12,8},{9,1... | collective-permute-start | bytes 17301512 | tf_op jit(solution)/shard_map/ppermute | solution.py:126
  114.5 7.0 %collective-permute-done.3 = bf16[1024,2816]{1,0:T(8,128)(2,1)} collective-permute-done((bf16[1024,2816]{1,0:T(8,128)(2,1)}, bf16[1024,2816]{1,0:T(8,128)(2,1)}, u32[]{:S(2)}, u32[]{:S(2)}) %collective-permute-start.3) | collective-permute-done | bytes 5767200 | tf_op jit(solution)/shard_map/ppermute | solution.py:126
  123.2 3.4 %collective-permute-start.4 = (bf16[256,512]{1,0:T(8,128)(2,1)S(1)}, bf16[256,512]{1,0:T(8,128)(2,1)S(1)}, u32[]{:S(2)}, u32[]{:S(2)}) collective-permute-start(bf16[256,512]{1,0:T(8,128)(2,1)S(1)} %fusion.33), channel_id=1, source_target_pairs={{0,1},{1,2},{2,3},{3,0},{4,5},{5,6},{6,7},{7,4},{8,9},{9,10},{10,1... | collective-permute-start | bytes 786440 | tf_op jit(solution)/shard_map/ppermute | solution.py:77
  126.7 4.5 %collective-permute-start.5 = (bf16[256,512]{1,0:T(8,128)(2,1)S(1)}, bf16[256,512]{1,0:T(8,128)(2,1)S(1)}, u32[]{:S(2)}, u32[]{:S(2)}) collective-permute-start(bf16[256,512]{1,0:T(8,128)(2,1)S(1)} %fusion.33), channel_id=1, source_target_pairs={{0,2},{1,3},{2,0},{3,1},{4,6},{5,7},{6,4},{7,5},{8,10},{9,11},{10,... | collective-permute-start | bytes 786440 | tf_op jit(solution)/shard_map/ppermute | solution.py:77
  131.2 3.2 %collective-permute-start.6 = (bf16[256,512]{1,0:T(8,128)(2,1)S(1)}, bf16[256,512]{1,0:T(8,128)(2,1)S(1)}, u32[]{:S(2)}, u32[]{:S(2)}) collective-permute-start(bf16[256,512]{1,0:T(8,128)(2,1)S(1)} %fusion.33), channel_id=1, source_target_pairs={{0,3},{1,0},{2,1},{3,2},{4,7},{5,4},{6,5},{7,6},{8,11},{9,8},{10,9... | collective-permute-start | bytes 786440 | tf_op jit(solution)/shard_map/ppermute | solution.py:77
  134.7 6.3 %collective-permute-done.5 = bf16[256,512]{1,0:T(8,128)(2,1)S(1)} collective-permute-done((bf16[256,512]{1,0:T(8,128)(2,1)S(1)}, bf16[256,512]{1,0:T(8,128)(2,1)S(1)}, u32[]{:S(2)}, u32[]{:S(2)}) %collective-permute-start.5) | collective-permute-done | bytes 262176 | tf_op jit(solution)/shard_map/ppermute | solution.py:77
  143.4 1.8 gather_fusion.2
  147.3 2.0 %fusion.12 = f32[256,768]{1,0:T(8,128)S(1)} fusion(bf16[1024,2816]{1,0:T(8,128)(2,1)} %all-gather.2.cloned.1.call-done, bf16[256,2048]{0,1:T(8,128)(2,1)S(1)} %bitcast.115), kind=kOutput, calls=%fused_computation.27 | convolution fusion | flops 402653184 | bytes 2883584 | tf_op jit(solution)/shard_map/dot_general | solution.py:133
  149.4 2.0 %fusion.14 = f32[256,768]{1,0:T(8,128)S(1)} fusion(bf16[1024,2816]{1,0:T(8,128)(2,1)} %all-gather.2.cloned.1.call-done, bf16[256,2048]{0,1:T(8,128)(2,1)S(1)} %bitcast.116), kind=kOutput, calls=%fused_computation.29 | convolution fusion | flops 402653184 | bytes 2883584 | tf_op jit(solution)/shard_map/dot_general | solution.py:133
  151.4 2.0 %fusion.19 = f32[256,768]{1,0:T(8,128)S(1)} fusion(f32[256,768]{1,0:T(8,128)S(1)} %fusion.14, bf16[1024,2816]{1,0:T(8,128)(2,1)} %collective-permute-done.3, bf16[256,2048]{0,1:T(8,128)(2,1)S(1)} %bitcast.117), kind=kOutput, calls=%fused_computation.34 | convolution fusion | flops 402849792 | bytes 3670016 | tf_op jit(solution)/shard_map/dot_general | solution.py:133
  153.4 2.1 %multiply_convert_fusion.1 = bf16[256,768]{1,0:T(8,128)(2,1)S(1)} fusion(f32[256,768]{1,0:T(8,128)S(1)} %fusion.19, f32[256,768]{1,0:T(8,128)S(1)} %fusion.12, bf16[1024,2816]{1,0:T(8,128)(2,1)} %collective-permute-done.3, bf16[256,2048]{0,1:T(8,128)(2,1)S(1)} %bitcast.118), kind=kOutput, calls=%fused_computation.67 | convolution fusion | flops 404029440 | bytes 4063232 | tf_op jit(solution)/shard_map/dot_general | solution.py:133
  156.2 2.0 %fusion.16 = bf16[256,1024]{1,0:T(8,128)(2,1)S(1)} fusion(bf16[256,768]{1,0:T(8,128)(2,1)S(1)} %multiply_convert_fusion.1, bf16[1024,2816]{1,0:T(8,128)(2,1)} %all-gather.2.cloned.1.call-done), kind=kOutput, calls=%fused_computation.33 | convolution fusion | flops 402915328 | bytes 2490368 | tf_op jit(solution)/shard_map/dot_general | solution.py:92
  158.5 2.1 %fusion.25 = bf16[256,1024]{1,0:T(8,128)(2,1)S(1)} fusion(bf16[256,768]{1,0:T(8,128)(2,1)} %copy-done.9, bf16[1024,2816]{1,0:T(8,128)(2,1)} %collective-permute-done.3), kind=kOutput, calls=%fused_computation.36 | convolution fusion | flops 402915328 | bytes 2490368 | tf_op jit(solution)/shard_map/dot_general | solution.py:92
  162.2 4.9 %collective-permute-start.7 = (bf16[256,512]{1,0:T(8,128)(2,1)}, bf16[256,512]{1,0:T(8,128)(2,1)S(1)}, u32[]{:S(2)}, u32[]{:S(2)}) collective-permute-start(bf16[256,512]{1,0:T(8,128)(2,1)} %copy.68), channel_id=1, source_target_pairs={{0,1},{1,2},{2,3},{3,0},{4,5},{5,6},{6,7},{7,4},{8,9},{9,10},{10,1... | collective-permute-start | bytes 786440 | tf_op jit(solution)/shard_map/ppermute | solution.py:107
  168.0 3.0 %collective-permute-start.8 = (bf16[256,512]{1,0:T(8,128)(2,1)}, bf16[256,512]{1,0:T(8,128)(2,1)S(1)}, u32[]{:S(2)}, u32[]{:S(2)}) collective-permute-start(bf16[256,512]{1,0:T(8,128)(2,1)} %copy.71), channel_id=1, source_target_pairs={{0,2},{1,3},{2,0},{3,1},{4,6},{5,7},{6,4},{7,5},{8,10},{9,11},{10,... | collective-permute-start | bytes 786440 | tf_op jit(solution)/shard_map/ppermute | solution.py:107
  171.9 3.2 %collective-permute-start.9 = (bf16[256,512]{1,0:T(8,128)(2,1)}, bf16[256,512]{1,0:T(8,128)(2,1)}, u32[]{:S(2)}, u32[]{:S(2)}) collective-permute-start(bf16[256,512]{1,0:T(8,128)(2,1)} %copy.73), channel_id=1, source_target_pairs={{0,3},{1,0},{2,1},{3,2},{4,7},{5,4},{6,5},{7,6},{8,11},{9,8},{10,9... | collective-permute-start | bytes 786440 | tf_op jit(solution)/shard_map/ppermute | solution.py:107
  175.3 4.6 %collective-permute-done.8 = bf16[256,512]{1,0:T(8,128)(2,1)S(1)} collective-permute-done((bf16[256,512]{1,0:T(8,128)(2,1)}, bf16[256,512]{1,0:T(8,128)(2,1)S(1)}, u32[]{:S(2)}, u32[]{:S(2)}) %collective-permute-start.8) | collective-permute-done | bytes 262176 | tf_op jit(solution)/shard_map/ppermute | solution.py:107
  180.0 2.3 %collective-permute-done.9 = bf16[256,512]{1,0:T(8,128)(2,1)} collective-permute-done((bf16[256,512]{1,0:T(8,128)(2,1)}, bf16[256,512]{1,0:T(8,128)(2,1)}, u32[]{:S(2)}, u32[]{:S(2)}) %collective-permute-start.9) | collective-permute-done | bytes 262176 | tf_op jit(solution)/shard_map/ppermute | solution.py:107
  182.3 1.8 add_convert_fusion
  (80 shorter events, 24.3 us)
Async XLA Ops:
  6.5 13.1 %copy-start = (bf16[6,128,2,512]{3,2,1,0:T(2,128)(2,1)S(1)}, bf16[6,128,2,512]{3,2,1,0:T(2,128)(2,1)}, u32[]{:S(2)}) copy-start(bf16[6,128,2,512]{3,2,1,0:T(2,128)(2,1)} %param.18) | copy-start | bytes 4718596
  6.5 98.4 %all-gather.2.cloned.1.call-start = ((), (), s32[]{:S(2)}) async-start(), calls=%async_computation | async-start | bytes 6127616 | tf_op jit(solution)/shard_map/all_gather | solution.py:122
  25.2 1.8 copy-start.2
  25.2 3.3 %copy-start.4 = (f32[4,128]{1,0:T(4,128)S(1)}, f32[4,128]{1,0:T(4,128)}, u32[]{:S(2)}) copy-start(f32[4,128]{1,0:T(4,128)} %param.22) | copy-start | bytes 6148
  25.2 5.3 %copy-start.7 = (s32[128]{0:T(128)S(1)}, s32[128]{0:T(128)}, u32[]{:S(2)}) copy-start(s32[128]{0:T(128)} %param.21) | copy-start | bytes 1540
  25.2 6.8 %copy-start.8 = (s32[1,6]{1,0:T(1,128)S(1)}, s32[1,6]{1,0:T(1,128)}, u32[]{:S(2)}) copy-start(s32[1,6]{1,0:T(1,128)} %param.19) | copy-start | bytes 76
  35.6 2.3 %copy-start.1 = (bf16[768,2,512]{2,0,1:T(8,128)(2,1)S(1)}, bf16[768,2,512]{2,0,1:T(8,128)(2,1)}, u32[]{:S(2)}) copy-start(bf16[768,2,512]{2,0,1:T(8,128)(2,1)} %bitcast_select_fusion.4) | copy-start | bytes 4718596
  43.1 3.4 %copy-start.5 = (f32[256]{0:T(256)S(1)}, f32[256]{0:T(256)}, u32[]{:S(2)}) copy-start(f32[256]{0:T(256)} %param.23) | copy-start | bytes 3076
  47.6 11.5 %collective-permute-start = (bf16[256,512]{0,1:T(8,128)(2,1)S(1)}, bf16[256,512]{0,1:T(8,128)(2,1)S(1)}, u32[]{:S(2)}, u32[]{:S(2)}) collective-permute-start(bf16[256,512]{0,1:T(8,128)(2,1)S(1)} %bitcast.123), channel_id=1, source_target_pairs={{0,1},{1,2},{2,3},{3,0},{4,5},{5,6},{6,7},{7,4},{8,9},{9,10},{10,1... | collective-permute-start | bytes 786440 | tf_op jit(solution)/shard_map/ppermute | solution.py:77
  51.5 11.4 %collective-permute-start.1 = (bf16[256,512]{0,1:T(8,128)(2,1)S(1)}, bf16[256,512]{0,1:T(8,128)(2,1)S(1)}, u32[]{:S(2)}, u32[]{:S(2)}) collective-permute-start(bf16[256,512]{0,1:T(8,128)(2,1)S(1)} %bitcast.124), channel_id=1, source_target_pairs={{0,2},{1,3},{2,0},{3,1},{4,6},{5,7},{6,4},{7,5},{8,10},{9,11},{10,... | collective-permute-start | bytes 786440 | tf_op jit(solution)/shard_map/ppermute | solution.py:77
  56.1 7.5 %collective-permute-start.2 = (bf16[256,512]{0,1:T(8,128)(2,1)S(1)}, bf16[256,512]{0,1:T(8,128)(2,1)S(1)}, u32[]{:S(2)}, u32[]{:S(2)}) collective-permute-start(bf16[256,512]{0,1:T(8,128)(2,1)S(1)} %bitcast.125), channel_id=1, source_target_pairs={{0,3},{1,0},{2,1},{3,2},{4,7},{5,4},{6,5},{7,6},{8,11},{9,8},{10,9... | collective-permute-start | bytes 786440 | tf_op jit(solution)/shard_map/ppermute | solution.py:77
  104.9 16.6 %collective-permute-start.3 = (bf16[1024,2816]{1,0:T(8,128)(2,1)}, bf16[1024,2816]{1,0:T(8,128)(2,1)}, u32[]{:S(2)}, u32[]{:S(2)}) collective-permute-start(bf16[1024,2816]{1,0:T(8,128)(2,1)} %all-gather.2.cloned.1.call-done), channel_id=1, source_target_pairs={{0,4},{4,0},{1,5},{5,1},{2,6},{6,2},{3,7},{7,3},{8,12},{12,8},{9,1... | collective-permute-start | bytes 17301512 | tf_op jit(solution)/shard_map/ppermute | solution.py:126
  112.6 8.9 %copy-start.6 = (bf16[256,512]{1,0:T(8,128)(2,1)S(1)}, bf16[256,512]{1,0:T(8,128)(2,1)}, u32[]{:S(2)}) copy-start(bf16[256,512]{1,0:T(8,128)(2,1)} %param.24) | copy-start | bytes 786436
  114.5 20.0 %copy-start.3 = (f32[2048]{0:T(1024)S(1)}, f32[2048]{0:T(1024)}, u32[]{:S(2)}) copy-start(f32[2048]{0:T(1024)} %param.26) | copy-start | bytes 24580
  123.2 11.4 %collective-permute-start.4 = (bf16[256,512]{1,0:T(8,128)(2,1)S(1)}, bf16[256,512]{1,0:T(8,128)(2,1)S(1)}, u32[]{:S(2)}, u32[]{:S(2)}) collective-permute-start(bf16[256,512]{1,0:T(8,128)(2,1)S(1)} %fusion.33), channel_id=1, source_target_pairs={{0,1},{1,2},{2,3},{3,0},{4,5},{5,6},{6,7},{7,4},{8,9},{9,10},{10,1... | collective-permute-start | bytes 786440 | tf_op jit(solution)/shard_map/ppermute | solution.py:77
  126.7 14.3 %collective-permute-start.5 = (bf16[256,512]{1,0:T(8,128)(2,1)S(1)}, bf16[256,512]{1,0:T(8,128)(2,1)S(1)}, u32[]{:S(2)}, u32[]{:S(2)}) collective-permute-start(bf16[256,512]{1,0:T(8,128)(2,1)S(1)} %fusion.33), channel_id=1, source_target_pairs={{0,2},{1,3},{2,0},{3,1},{4,6},{5,7},{6,4},{7,5},{8,10},{9,11},{10,... | collective-permute-start | bytes 786440 | tf_op jit(solution)/shard_map/ppermute | solution.py:77
  131.2 11.1 %collective-permute-start.6 = (bf16[256,512]{1,0:T(8,128)(2,1)S(1)}, bf16[256,512]{1,0:T(8,128)(2,1)S(1)}, u32[]{:S(2)}, u32[]{:S(2)}) collective-permute-start(bf16[256,512]{1,0:T(8,128)(2,1)S(1)} %fusion.33), channel_id=1, source_target_pairs={{0,3},{1,0},{2,1},{3,2},{4,7},{5,4},{6,5},{7,6},{8,11},{9,8},{10,9... | collective-permute-start | bytes 786440 | tf_op jit(solution)/shard_map/ppermute | solution.py:77
  155.5 0.8 copy-start.9
  162.2 13.1 %collective-permute-start.7 = (bf16[256,512]{1,0:T(8,128)(2,1)}, bf16[256,512]{1,0:T(8,128)(2,1)S(1)}, u32[]{:S(2)}, u32[]{:S(2)}) collective-permute-start(bf16[256,512]{1,0:T(8,128)(2,1)} %copy.68), channel_id=1, source_target_pairs={{0,1},{1,2},{2,3},{3,0},{4,5},{5,6},{6,7},{7,4},{8,9},{9,10},{10,1... | collective-permute-start | bytes 786440 | tf_op jit(solution)/shard_map/ppermute | solution.py:107
  168.0 12.0 %collective-permute-start.8 = (bf16[256,512]{1,0:T(8,128)(2,1)}, bf16[256,512]{1,0:T(8,128)(2,1)S(1)}, u32[]{:S(2)}, u32[]{:S(2)}) collective-permute-start(bf16[256,512]{1,0:T(8,128)(2,1)} %copy.71), channel_id=1, source_target_pairs={{0,2},{1,3},{2,0},{3,1},{4,6},{5,7},{6,4},{7,5},{8,10},{9,11},{10,... | collective-permute-start | bytes 786440 | tf_op jit(solution)/shard_map/ppermute | solution.py:107
  171.9 10.4 %collective-permute-start.9 = (bf16[256,512]{1,0:T(8,128)(2,1)}, bf16[256,512]{1,0:T(8,128)(2,1)}, u32[]{:S(2)}, u32[]{:S(2)}) collective-permute-start(bf16[256,512]{1,0:T(8,128)(2,1)} %copy.73), channel_id=1, source_target_pairs={{0,3},{1,0},{2,1},{3,2},{4,7},{5,4},{6,5},{7,6},{8,11},{9,8},{10,9... | collective-permute-start | bytes 786440 | tf_op jit(solution)/shard_map/ppermute | solution.py:107
Sparse Core Ops, SparseCore 0:
  19.1 85.8 all-gather.1

commit v11 on v10

--- a/solution.py
+++ b/solution.py
@@ -183,8 +183,11 @@
     squares = jnp.sum(stream_all * stream_all, axis=1, keepdims=True)
     normed = (stream_all * lax.rsqrt(squares / D + 1e-05) * norm_gain).astype(jnp.bfloat16)
     normed = to_gathered_order(normed, rows)
-    gate_value = split_dot(normed, gate_full)
-    up_value = split_dot(normed, up_full)
+    gate_up = split_dot(
+        normed, [half[:, bounds[1] : bounds[3]] for half in halves]
+    )
+    gate_value = gate_up[:, : widths[1]]
+    up_value = gate_up[:, widths[1] :]
     hidden_act = (jax.nn.silu(gate_value) * up_value).astype(jnp.bfloat16)
     summed = down_and_scatter(hidden_act, down_full, mlp_size, out_weight.shape[0])
     return (stream.astype(jnp.float32) + summed).astype(jnp.bfloat16)

time: 193 us -> 191 us (0.990)
  matrix products: 26.5 us -> 24.1 us
    dot_general x6 -> x4, matrix products: 11.5 us -> 9.13 us  [split_dot(): jnp.dot(act[:, j * size:(j + 1) * size], half, preferred_element_type=jnp...]
where the time goes in v11:
time: 191 us; the launch traced here: 189 us
  waiting for transfers between devices  64.3 us (34%)
  starting transfers between devices  40.9 us (21%)
  matrix products  24.1 us (13%)
  local copies, waits for them, and re-layouts  18.9 us (10%)
  between operations  16 us (8%)
  other arithmetic  13.3 us (7%)
  blocking collectives  11.5 us (6%)
    all_gather x1, waiting for transfers between devices, gather_over_xz(): return lax.all_gather(out, 'z', axis=0, tiled=True)  38 us
    ppermute x6, starting transfers between devices, mlp_gather(): lax.ppermute(block, 'mlp', [(i, (i + shift) % axis_size) for i in range(a...  22.4 us
    ppermute x6, waiting for transfers between devices, mlp_gather(): lax.ppermute(block, 'mlp', [(i, (i + shift) % axis_size) for i in range(a...  12.1 us
    all_gather x1, blocking collectives, gather_over_xz(): out = lax.all_gather(block, 'x', axis=0, tiled=True)  11.5 us
    ppermute x3, starting transfers between devices, down_and_scatter(): lax.ppermute(block_for(target), 'mlp', [(i, (i + shift) % axis_size) for...  11.1 us
    dot_general x4, matrix products, split_dot(): jnp.dot(act[:, j * size:(j + 1) * size], half, preferred_element_type=jnp...  9.13 us
    ppermute x1, starting transfers between devices, swap_with_core(): return [rows_xz, lax.ppermute(rows_xz, 'c', [(0, 1), (1, 0)])]  7.45 us
    gather x2, local copies, waits for them, and re-layouts, attend(): pages = jnp.take(cache_pool, page_table[0], axis=0)  7.33 us
  transfers between devices with their start and end apart: 11, of which 8 were waited for; matrix products, arithmetic and copies ran while one was open for 18% of the time, Pallas kernels for 0%

profile of v11, /device:TPU:1, one launch (start us, length us, event | category | flops | bytes accessed | tf_op | source)
XLA Modules:
  0.0 188.9 jit_solution(7171871650857875737)
XLA Ops:
  7.4 11.5 %all_gather.6 = bf16[64,2816]{1,0:T(8,128)(2,1)} all-gather(bf16[16,2816]{1,0:T(8,128)(2,1)S(1)} %pad_maximum_fusion.16), channel_id=1, replica_groups=mesh['x'=4,'z'=16,'c'=2,'mlp'=4] {'x'}, dimensions={0}, use_global_device_ids=true | all-gather | bytes 450560 | tf_op jit(solution)/shard_map/all_gather | solution.py:121
  19.6 5.6 %gather_fusion = bf16[6,128,2,512]{3,2,1,0:T(2,128)(2,1)} fusion(bf16[6,128,2,512]{3,2,1,0:T(2,128)(2,1)S(1)} %copy-done, s32[1024]{0:T(1024)S(1)} %pad_clamp_fusion.1), kind=kCustom, calls=%fused_computation.2 | custom fusion | bytes 3145752 | tf_op jit(solution)/shard_map/jit(_take)/gather | solution.py:23
  25.2 1.7 copy.50
  32.3 1.8 fusion.110
  35.6 2.3 %fusion.111 = f32[256,2]{0,1:T(2,128)S(1)} fusion(pred[256,1024]{0,1:T(8,128)(4,1)S(1)} %pad_add_fusion, bf16[768,2,512]{2,0,1:T(8,128)(2,1)} %bitcast_select_fusion.4, bf16[256,2,512]{2,0,1:T(8,128)(2,1)} %copy.51, bf16[256,2,128]{2,1,0:T(2,128)(2,1)} %get-tuple-element.29), kind=kOutput, calls=%fused_computation.135 | convolution fusion | flops 137888768 | bytes 2754560 | tf_op jit(solution)/shard_map/sub | solution.py:45
  37.9 3.2 %fusion.21 = f32[256,2,256]{0,2,1:T(8,128)} fusion(f32[256,2]{0,1:T(2,128)S(1)} %fusion.111, pred[256,1024]{0,1:T(8,128)(4,1)S(1)} %pad_add_fusion, bf16[768,2,512]{2,0,1:T(8,128)(2,1)S(1)} %copy-done.1, bf16[256,2,512]{2,0,1:T(8,128)(2,1)} %copy.51, bf16[256,2,128]{2,1,0:T(2,128)(2,1)} %get-tuple-element.29), kind=kOutput, calls=%fused_computation.35 | convolution fusion | flops 408552960 | bytes 5376000 | tf_op jit(solution)/shard_map/nhk,khd->nhd/dot_general | solution.py:47
  41.1 2.0 %fusion.116 = f32[256,2]{0,1:T(2,128)S(1)} fusion(pred[256,1024]{0,1:T(8,128)(4,1)S(1)} %pad_add_fusion, bf16[256,2,512]{2,0,1:T(8,128)(2,1)} %copy.51, bf16[768,2,512]{2,0,1:T(8,128)(2,1)S(1)} %copy-done.1, bf16[256,2,128]{2,1,0:T(2,128)(2,1)S(1)} %get-tuple-element.28), kind=kOutput, calls=%fused_computation.136 | convolution fusion | flops 137888768 | bytes 2492416 | tf_op jit(solution)/shard_map/sub | solution.py:45
  43.1 3.4 %multiply_reduce_fusion.1 = (f32[256,2]{0,1:T(2,128)S(1)}, f32[256,2,256]{0,2,1:T(8,128)}) fusion(f32[256,2,256]{0,2,1:T(8,128)} %fusion.21, f32[256,2]{0,1:T(2,128)S(1)} %fusion.116, pred[256,1024]{0,1:T(8,128)(4,1)S(1)} %pad_add_fusion, bf16[256,2,512]{2,0,1:T(8,128)(2,1)} %copy.51, bf16[768,2,512]{2,0,1:T(8,128)(2,1)S(1)} %copy-done.1, ...), kind=kOutput, calls=%fused_computation.76 | convolution fusion | flops 409076736 | bytes 5902340 | tf_op jit(solution)/shard_map/nhk,khd->nhd/dot_general | solution.py:47
  47.6 3.9 %collective-permute-start = (bf16[256,512]{0,1:T(8,128)(2,1)S(1)}, bf16[256,512]{0,1:T(8,128)(2,1)S(1)}, u32[]{:S(2)}, u32[]{:S(2)}) collective-permute-start(bf16[256,512]{0,1:T(8,128)(2,1)S(1)} %bitcast.121), channel_id=1, source_target_pairs={{0,1},{1,2},{2,3},{3,0},{4,5},{5,6},{6,7},{7,4},{8,9},{9,10},{10,1... | collective-permute-start | bytes 786440 | tf_op jit(solution)/shard_map/ppermute | solution.py:77
  51.5 4.5 %collective-permute-start.1 = (bf16[256,512]{0,1:T(8,128)(2,1)S(1)}, bf16[256,512]{0,1:T(8,128)(2,1)S(1)}, u32[]{:S(2)}, u32[]{:S(2)}) collective-permute-start(bf16[256,512]{0,1:T(8,128)(2,1)S(1)} %bitcast.122), channel_id=1, source_target_pairs={{0,2},{1,3},{2,0},{3,1},{4,6},{5,7},{6,4},{7,5},{8,10},{9,11},{10,... | collective-permute-start | bytes 786440 | tf_op jit(solution)/shard_map/ppermute | solution.py:77
  56.1 3.0 %collective-permute-start.2 = (bf16[256,512]{0,1:T(8,128)(2,1)S(1)}, bf16[256,512]{0,1:T(8,128)(2,1)S(1)}, u32[]{:S(2)}, u32[]{:S(2)}) collective-permute-start(bf16[256,512]{0,1:T(8,128)(2,1)S(1)} %bitcast.123), channel_id=1, source_target_pairs={{0,3},{1,0},{2,1},{3,2},{4,7},{5,4},{6,5},{7,6},{8,11},{9,8},{10,9... | collective-permute-start | bytes 786440 | tf_op jit(solution)/shard_map/ppermute | solution.py:77
  59.1 3.9 %collective-permute-done.1 = bf16[256,512]{0,1:T(8,128)(2,1)S(1)} collective-permute-done((bf16[256,512]{0,1:T(8,128)(2,1)S(1)}, bf16[256,512]{0,1:T(8,128)(2,1)S(1)}, u32[]{:S(2)}, u32[]{:S(2)}) %collective-permute-start.1) | collective-permute-done | bytes 262176 | tf_op jit(solution)/shard_map/ppermute | solution.py:77
  64.7 1.8 gather_fusion.1
  66.9 38.0 %all-gather.2.cloned.1.call-done = bf16[1024,2816]{1,0:T(8,128)(2,1)} async-done(((bf16[64,2816]{1,0:T(8,128)(2,1)}), bf16[1024,2816]{1,0:T(8,128)(2,1)}) %all-gather.2.cloned.1.call-update) | async-done | bytes 5767184 | tf_op jit(solution)/shard_map/all_gather | solution.py:122
  104.9 7.4 %collective-permute-start.3 = (bf16[1024,2816]{1,0:T(8,128)(2,1)}, bf16[1024,2816]{1,0:T(8,128)(2,1)}, u32[]{:S(2)}, u32[]{:S(2)}) collective-permute-start(bf16[1024,2816]{1,0:T(8,128)(2,1)} %all-gather.2.cloned.1.call-done), channel_id=1, source_target_pairs={{0,4},{4,0},{1,5},{5,1},{2,6},{6,2},{3,7},{7,3},{8,12},{12,8},{9,1... | collective-permute-start | bytes 17301512 | tf_op jit(solution)/shard_map/ppermute | solution.py:126
  114.6 7.0 %collective-permute-done.3 = bf16[1024,2816]{1,0:T(8,128)(2,1)} collective-permute-done((bf16[1024,2816]{1,0:T(8,128)(2,1)}, bf16[1024,2816]{1,0:T(8,128)(2,1)}, u32[]{:S(2)}, u32[]{:S(2)}) %collective-permute-start.3) | collective-permute-done | bytes 5767200 | tf_op jit(solution)/shard_map/ppermute | solution.py:126
  121.7 1.7 fusion.26
  123.4 3.3 %collective-permute-start.4 = (bf16[256,512]{1,0:T(8,128)(2,1)S(1)}, bf16[256,512]{1,0:T(8,128)(2,1)S(1)}, u32[]{:S(2)}, u32[]{:S(2)}) collective-permute-start(bf16[256,512]{1,0:T(8,128)(2,1)S(1)} %fusion.26), channel_id=1, source_target_pairs={{0,1},{1,2},{2,3},{3,0},{4,5},{5,6},{6,7},{7,4},{8,9},{9,10},{10,1... | collective-permute-start | bytes 786440 | tf_op jit(solution)/shard_map/ppermute | solution.py:77
  126.7 4.6 %collective-permute-start.5 = (bf16[256,512]{1,0:T(8,128)(2,1)S(1)}, bf16[256,512]{1,0:T(8,128)(2,1)S(1)}, u32[]{:S(2)}, u32[]{:S(2)}) collective-permute-start(bf16[256,512]{1,0:T(8,128)(2,1)S(1)} %fusion.26), channel_id=1, source_target_pairs={{0,2},{1,3},{2,0},{3,1},{4,6},{5,7},{6,4},{7,5},{8,10},{9,11},{10,... | collective-permute-start | bytes 786440 | tf_op jit(solution)/shard_map/ppermute | solution.py:77
  131.3 3.1 %collective-permute-start.6 = (bf16[256,512]{1,0:T(8,128)(2,1)S(1)}, bf16[256,512]{1,0:T(8,128)(2,1)S(1)}, u32[]{:S(2)}, u32[]{:S(2)}) collective-permute-start(bf16[256,512]{1,0:T(8,128)(2,1)S(1)} %fusion.26), channel_id=1, source_target_pairs={{0,3},{1,0},{2,1},{3,2},{4,7},{5,4},{6,5},{7,6},{8,11},{9,8},{10,9... | collective-permute-start | bytes 786440 | tf_op jit(solution)/shard_map/ppermute | solution.py:77
  134.6 6.4 %collective-permute-done.5 = bf16[256,512]{1,0:T(8,128)(2,1)S(1)} collective-permute-done((bf16[256,512]{1,0:T(8,128)(2,1)S(1)}, bf16[256,512]{1,0:T(8,128)(2,1)S(1)}, u32[]{:S(2)}, u32[]{:S(2)}) %collective-permute-start.5) | collective-permute-done | bytes 262176 | tf_op jit(solution)/shard_map/ppermute | solution.py:77
  143.3 1.8 gather_fusion.2
  147.3 2.9 %fusion.4 = f32[256,1536]{1,0:T(8,128)S(1)} fusion(bf16[1024,2816]{1,0:T(8,128)(2,1)} %all-gather.2.cloned.1.call-done, bf16[256,2048]{0,1:T(8,128)(2,1)S(1)} %bitcast.110), kind=kOutput, calls=%fused_computation.7 | convolution fusion | flops 805306368 | bytes 5242880 | tf_op jit(solution)/shard_map/dot_general | solution.py:133
  150.2 2.9 %fusion.6 = f32[256,1536]{1,0:T(8,128)S(1)} fusion(f32[256,1536]{1,0:T(8,128)S(1)} %fusion.4, bf16[1024,2816]{1,0:T(8,128)(2,1)} %collective-permute-done.3, bf16[256,2048]{0,1:T(8,128)(2,1)S(1)} %bitcast.111), kind=kOutput, calls=%fused_computation.9 | convolution fusion | flops 805699584 | bytes 6815744 | tf_op jit(solution)/shard_map/dot_general | solution.py:133
  154.1 2.0 %fusion.15 = bf16[256,1024]{1,0:T(8,128)(2,1)S(1)} fusion(bf16[256,768]{1,0:T(8,128)(2,1)S(1)} %fusion.41, bf16[1024,2816]{1,0:T(8,128)(2,1)} %all-gather.2.cloned.1.call-done), kind=kOutput, calls=%fused_computation.30 | convolution fusion | flops 402915328 | bytes 2490368 | tf_op jit(solution)/shard_map/dot_general | solution.py:92
  156.3 2.1 %fusion.18 = bf16[256,1024]{1,0:T(8,128)(2,1)S(1)} fusion(bf16[256,768]{1,0:T(8,128)(2,1)} %copy-done.3, bf16[1024,2816]{1,0:T(8,128)(2,1)} %collective-permute-done.3), kind=kOutput, calls=%fused_computation.31 | convolution fusion | flops 402915328 | bytes 2490368 | tf_op jit(solution)/shard_map/dot_general | solution.py:92
  160.1 4.9 %collective-permute-start.7 = (bf16[256,512]{1,0:T(8,128)(2,1)}, bf16[256,512]{1,0:T(8,128)(2,1)S(1)}, u32[]{:S(2)}, u32[]{:S(2)}) collective-permute-start(bf16[256,512]{1,0:T(8,128)(2,1)} %copy.68), channel_id=1, source_target_pairs={{0,1},{1,2},{2,3},{3,0},{4,5},{5,6},{6,7},{7,4},{8,9},{9,10},{10,1... | collective-permute-start | bytes 786440 | tf_op jit(solution)/shard_map/ppermute | solution.py:107
  165.8 3.2 %collective-permute-start.8 = (bf16[256,512]{1,0:T(8,128)(2,1)}, bf16[256,512]{1,0:T(8,128)(2,1)S(1)}, u32[]{:S(2)}, u32[]{:S(2)}) collective-permute-start(bf16[256,512]{1,0:T(8,128)(2,1)} %copy.71), channel_id=1, source_target_pairs={{0,2},{1,3},{2,0},{3,1},{4,6},{5,7},{6,4},{7,5},{8,10},{9,11},{10,... | collective-permute-start | bytes 786440 | tf_op jit(solution)/shard_map/ppermute | solution.py:107
  169.9 3.0 %collective-permute-start.9 = (bf16[256,512]{1,0:T(8,128)(2,1)}, bf16[256,512]{1,0:T(8,128)(2,1)}, u32[]{:S(2)}, u32[]{:S(2)}) collective-permute-start(bf16[256,512]{1,0:T(8,128)(2,1)} %copy.73), channel_id=1, source_target_pairs={{0,3},{1,0},{2,1},{3,2},{4,7},{5,4},{6,5},{7,6},{8,11},{9,8},{10,9... | collective-permute-start | bytes 786440 | tf_op jit(solution)/shard_map/ppermute | solution.py:107
  173.2 4.6 %collective-permute-done.8 = bf16[256,512]{1,0:T(8,128)(2,1)S(1)} collective-permute-done((bf16[256,512]{1,0:T(8,128)(2,1)}, bf16[256,512]{1,0:T(8,128)(2,1)S(1)}, u32[]{:S(2)}, u32[]{:S(2)}) %collective-permute-start.8) | collective-permute-done | bytes 262176 | tf_op jit(solution)/shard_map/ppermute | solution.py:107
  177.8 2.5 %collective-permute-done.9 = bf16[256,512]{1,0:T(8,128)(2,1)} collective-permute-done((bf16[256,512]{1,0:T(8,128)(2,1)}, bf16[256,512]{1,0:T(8,128)(2,1)}, u32[]{:S(2)}, u32[]{:S(2)}) %collective-permute-start.9) | collective-permute-done | bytes 262176 | tf_op jit(solution)/shard_map/ppermute | solution.py:107
  180.2 1.8 add_convert_fusion
  (79 shorter events, 21.1 us)
Async XLA Ops:
  6.5 13.1 %copy-start = (bf16[6,128,2,512]{3,2,1,0:T(2,128)(2,1)S(1)}, bf16[6,128,2,512]{3,2,1,0:T(2,128)(2,1)}, u32[]{:S(2)}) copy-start(bf16[6,128,2,512]{3,2,1,0:T(2,128)(2,1)} %param.18) | copy-start | bytes 4718596
  6.5 98.3 %all-gather.2.cloned.1.call-start = ((), (), s32[]{:S(2)}) async-start(), calls=%async_computation | async-start | bytes 6127616 | tf_op jit(solution)/shard_map/all_gather | solution.py:122
  25.2 1.8 copy-start.2
  25.2 3.3 %copy-start.5 = (f32[4,128]{1,0:T(4,128)S(1)}, f32[4,128]{1,0:T(4,128)}, u32[]{:S(2)}) copy-start(f32[4,128]{1,0:T(4,128)} %param.22) | copy-start | bytes 6148
  25.2 5.3 %copy-start.8 = (s32[128]{0:T(128)S(1)}, s32[128]{0:T(128)}, u32[]{:S(2)}) copy-start(s32[128]{0:T(128)} %param.21) | copy-start | bytes 1540
  25.2 6.8 %copy-start.9 = (s32[1,6]{1,0:T(1,128)S(1)}, s32[1,6]{1,0:T(1,128)}, u32[]{:S(2)}) copy-start(s32[1,6]{1,0:T(1,128)} %param.19) | copy-start | bytes 76
  35.6 2.3 %copy-start.1 = (bf16[768,2,512]{2,0,1:T(8,128)(2,1)S(1)}, bf16[768,2,512]{2,0,1:T(8,128)(2,1)}, u32[]{:S(2)}) copy-start(bf16[768,2,512]{2,0,1:T(8,128)(2,1)} %bitcast_select_fusion.4) | copy-start | bytes 4718596
  43.1 3.4 %copy-start.6 = (f32[256]{0:T(256)S(1)}, f32[256]{0:T(256)}, u32[]{:S(2)}) copy-start(f32[256]{0:T(256)} %param.23) | copy-start | bytes 3076
  47.6 11.5 %collective-permute-start = (bf16[256,512]{0,1:T(8,128)(2,1)S(1)}, bf16[256,512]{0,1:T(8,128)(2,1)S(1)}, u32[]{:S(2)}, u32[]{:S(2)}) collective-permute-start(bf16[256,512]{0,1:T(8,128)(2,1)S(1)} %bitcast.121), channel_id=1, source_target_pairs={{0,1},{1,2},{2,3},{3,0},{4,5},{5,6},{6,7},{7,4},{8,9},{9,10},{10,1... | collective-permute-start | bytes 786440 | tf_op jit(solution)/shard_map/ppermute | solution.py:77
  51.5 11.4 %collective-permute-start.1 = (bf16[256,512]{0,1:T(8,128)(2,1)S(1)}, bf16[256,512]{0,1:T(8,128)(2,1)S(1)}, u32[]{:S(2)}, u32[]{:S(2)}) collective-permute-start(bf16[256,512]{0,1:T(8,128)(2,1)S(1)} %bitcast.122), channel_id=1, source_target_pairs={{0,2},{1,3},{2,0},{3,1},{4,6},{5,7},{6,4},{7,5},{8,10},{9,11},{10,... | collective-permute-start | bytes 786440 | tf_op jit(solution)/shard_map/ppermute | solution.py:77
  56.1 7.5 %collective-permute-start.2 = (bf16[256,512]{0,1:T(8,128)(2,1)S(1)}, bf16[256,512]{0,1:T(8,128)(2,1)S(1)}, u32[]{:S(2)}, u32[]{:S(2)}) collective-permute-start(bf16[256,512]{0,1:T(8,128)(2,1)S(1)} %bitcast.123), channel_id=1, source_target_pairs={{0,3},{1,0},{2,1},{3,2},{4,7},{5,4},{6,5},{7,6},{8,11},{9,8},{10,9... | collective-permute-start | bytes 786440 | tf_op jit(solution)/shard_map/ppermute | solution.py:77
  104.9 16.8 %collective-permute-start.3 = (bf16[1024,2816]{1,0:T(8,128)(2,1)}, bf16[1024,2816]{1,0:T(8,128)(2,1)}, u32[]{:S(2)}, u32[]{:S(2)}) collective-permute-start(bf16[1024,2816]{1,0:T(8,128)(2,1)} %all-gather.2.cloned.1.call-done), channel_id=1, source_target_pairs={{0,4},{4,0},{1,5},{5,1},{2,6},{6,2},{3,7},{7,3},{8,12},{12,8},{9,1... | collective-permute-start | bytes 17301512 | tf_op jit(solution)/shard_map/ppermute | solution.py:126
  112.8 8.9 %copy-start.7 = (bf16[256,512]{1,0:T(8,128)(2,1)S(1)}, bf16[256,512]{1,0:T(8,128)(2,1)}, u32[]{:S(2)}) copy-start(bf16[256,512]{1,0:T(8,128)(2,1)} %param.24) | copy-start | bytes 786436
  114.6 19.8 %copy-start.4 = (f32[2048]{0:T(1024)S(1)}, f32[2048]{0:T(1024)}, u32[]{:S(2)}) copy-start(f32[2048]{0:T(1024)} %param.26) | copy-start | bytes 24580
  123.4 11.2 %collective-permute-start.4 = (bf16[256,512]{1,0:T(8,128)(2,1)S(1)}, bf16[256,512]{1,0:T(8,128)(2,1)S(1)}, u32[]{:S(2)}, u32[]{:S(2)}) collective-permute-start(bf16[256,512]{1,0:T(8,128)(2,1)S(1)} %fusion.26), channel_id=1, source_target_pairs={{0,1},{1,2},{2,3},{3,0},{4,5},{5,6},{6,7},{7,4},{8,9},{9,10},{10,1... | collective-permute-start | bytes 786440 | tf_op jit(solution)/shard_map/ppermute | solution.py:77
  126.7 14.3 %collective-permute-start.5 = (bf16[256,512]{1,0:T(8,128)(2,1)S(1)}, bf16[256,512]{1,0:T(8,128)(2,1)S(1)}, u32[]{:S(2)}, u32[]{:S(2)}) collective-permute-start(bf16[256,512]{1,0:T(8,128)(2,1)S(1)} %fusion.26), channel_id=1, source_target_pairs={{0,2},{1,3},{2,0},{3,1},{4,6},{5,7},{6,4},{7,5},{8,10},{9,11},{10,... | collective-permute-start | bytes 786440 | tf_op jit(solution)/shard_map/ppermute | solution.py:77
  131.3 11.0 %collective-permute-start.6 = (bf16[256,512]{1,0:T(8,128)(2,1)S(1)}, bf16[256,512]{1,0:T(8,128)(2,1)S(1)}, u32[]{:S(2)}, u32[]{:S(2)}) collective-permute-start(bf16[256,512]{1,0:T(8,128)(2,1)S(1)} %fusion.26), channel_id=1, source_target_pairs={{0,3},{1,0},{2,1},{3,2},{4,7},{5,4},{6,5},{7,6},{8,11},{9,8},{10,9... | collective-permute-start | bytes 786440 | tf_op jit(solution)/shard_map/ppermute | solution.py:77
  153.3 0.8 copy-start.3
  160.1 13.1 %collective-permute-start.7 = (bf16[256,512]{1,0:T(8,128)(2,1)}, bf16[256,512]{1,0:T(8,128)(2,1)S(1)}, u32[]{:S(2)}, u32[]{:S(2)}) collective-permute-start(bf16[256,512]{1,0:T(8,128)(2,1)} %copy.68), channel_id=1, source_target_pairs={{0,1},{1,2},{2,3},{3,0},{4,5},{5,6},{6,7},{7,4},{8,9},{9,10},{10,1... | collective-permute-start | bytes 786440 | tf_op jit(solution)/shard_map/ppermute | solution.py:107
  165.8 12.0 %collective-permute-start.8 = (bf16[256,512]{1,0:T(8,128)(2,1)}, bf16[256,512]{1,0:T(8,128)(2,1)S(1)}, u32[]{:S(2)}, u32[]{:S(2)}) collective-permute-start(bf16[256,512]{1,0:T(8,128)(2,1)} %copy.71), channel_id=1, source_target_pairs={{0,2},{1,3},{2,0},{3,1},{4,6},{5,7},{6,4},{7,5},{8,10},{9,11},{10,... | collective-permute-start | bytes 786440 | tf_op jit(solution)/shard_map/ppermute | solution.py:107
  169.9 10.4 %collective-permute-start.9 = (bf16[256,512]{1,0:T(8,128)(2,1)}, bf16[256,512]{1,0:T(8,128)(2,1)}, u32[]{:S(2)}, u32[]{:S(2)}) collective-permute-start(bf16[256,512]{1,0:T(8,128)(2,1)} %copy.73), channel_id=1, source_target_pairs={{0,3},{1,0},{2,1},{3,2},{4,7},{5,4},{6,5},{7,6},{8,11},{9,8},{10,9... | collective-permute-start | bytes 786440 | tf_op jit(solution)/shard_map/ppermute | solution.py:107
Sparse Core Ops, SparseCore 0:
  19.1 85.7 all-gather.1

commit v12 on v11

--- a/solution.py
+++ b/solution.py
@@ -76,10 +76,13 @@
         pieces.append(
             lax.ppermute(block, "mlp", [(i, (i + shift) % axis_size) for i in range(axis_size)])
         )
-    stacked = jnp.stack(pieces, axis=0)
-    source_of = (index - jnp.arange(axis_size, dtype=jnp.int32)) % axis_size
-    gathered = jnp.take(stacked, source_of, axis=0)
-    return jnp.concatenate([gathered[k] for k in range(axis_size)], axis=1)
+    slots = []
+    for j in range(axis_size):
+        chosen = pieces[0]
+        for k in range(1, axis_size):
+            chosen = jnp.where((index - k) % axis_size == j, pieces[k], chosen)
+        slots.append(chosen)
+    return jnp.concatenate(slots, axis=1)
 
 
 def down_and_scatter(hidden_act, down_halves, axis_size, rows):

time: 191 us -> 192 us (level)
  waiting for transfers between devices: 64.3 us -> 72.4 us
  starting transfers between devices: 40.9 us -> 35.6 us
    ppermute x6, waiting for transfers between devices: 12.1 us -> 18.4 us  [mlp_gather(): lax.ppermute(block, 'mlp', [(i, (i + shift) % axis_size) for i in range(a...]
    gather x2 -> x0, local copies, waits for them, and re-layouts: 3.67 us -> none  [mlp_gather(): gathered = jnp.take(stacked, source_of, axis=0)]
    ppermute x3, starting transfers between devices: 11.1 us -> 8.38 us  [down_and_scatter(): lax.ppermute(block_for(target), 'mlp', [(i, (i + shift) % axis_size) for...]
    ppermute x6, starting transfers between devices: 22.4 us -> 20 us  [mlp_gather(): lax.ppermute(block, 'mlp', [(i, (i + shift) % axis_size) for i in range(a...]
    another operation x2 -> x0, other arithmetic: 2.23 us -> none  [mlp_gather(): stacked = jnp.stack(pieces, axis=0)]
    ppermute x3, waiting for transfers between devices: 7.08 us -> 9.19 us  [down_and_scatter(): lax.ppermute(block_for(target), 'mlp', [(i, (i + shift) % axis_size) for...]
where the time goes in v12:
time: 192 us; the launch traced here: 191 us
  waiting for transfers between devices  72.4 us (38%)
  starting transfers between devices  35.6 us (19%)
  matrix products  24.1 us (13%)
  local copies, waits for them, and re-layouts  17.3 us (9%)
  between operations  16 us (8%)
  other arithmetic  13.9 us (7%)
  blocking collectives  11.5 us (6%)
    all_gather x1, waiting for transfers between devices, gather_over_xz(): return lax.all_gather(out, 'z', axis=0, tiled=True)  39.2 us
    ppermute x6, starting transfers between devices, mlp_gather(): lax.ppermute(block, 'mlp', [(i, (i + shift) % axis_size) for i in range(a...  20 us
    ppermute x6, waiting for transfers between devices, mlp_gather(): lax.ppermute(block, 'mlp', [(i, (i + shift) % axis_size) for i in range(a...  18.4 us
    all_gather x1, blocking collectives, gather_over_xz(): out = lax.all_gather(block, 'x', axis=0, tiled=True)  11.5 us
    ppermute x3, waiting for transfers between devices, down_and_scatter(): lax.ppermute(block_for(target), 'mlp', [(i, (i + shift) % axis_size) for...  9.19 us
    dot_general x4, matrix products, split_dot(): jnp.dot(act[:, j * size:(j + 1) * size], half, preferred_element_type=jnp...  9.13 us
    ppermute x3, starting transfers between devices, down_and_scatter(): lax.ppermute(block_for(target), 'mlp', [(i, (i + shift) % axis_size) for...  8.38 us
    gather x2, local copies, waits for them, and re-layouts, attend(): pages = jnp.take(cache_pool, page_table[0], axis=0)  7.33 us
  transfers between devices with their start and end apart: 11, of which 8 were waited for; matrix products, arithmetic and copies ran while one was open for 18% of the time, Pallas kernels for 0%

profile of v12, /device:TPU:1, one launch (start us, length us, event | category | flops | bytes accessed | tf_op | source)
XLA Modules:
  0.0 190.9 jit_solution(9383692709614010337)
XLA Ops:
  7.4 11.5 %all_gather.6 = bf16[64,2816]{1,0:T(8,128)(2,1)} all-gather(bf16[16,2816]{1,0:T(8,128)(2,1)S(1)} %pad_maximum_fusion.14), channel_id=1, replica_groups=mesh['x'=4,'z'=16,'c'=2,'mlp'=4] {'x'}, dimensions={0}, use_global_device_ids=true | all-gather | bytes 450560 | tf_op jit(solution)/shard_map/all_gather | solution.py:124
  19.6 5.6 %gather_fusion = bf16[6,128,2,512]{3,2,1,0:T(2,128)(2,1)} fusion(bf16[6,128,2,512]{3,2,1,0:T(2,128)(2,1)S(1)} %copy-done, s32[1024]{0:T(1024)S(1)} %pad_clamp_fusion), kind=kCustom, calls=%fused_computation | custom fusion | bytes 3145752 | tf_op jit(solution)/shard_map/jit(_take)/gather | solution.py:23
  25.2 1.7 copy.63
  32.3 1.8 fusion.109
  35.6 2.3 %fusion.110 = f32[256,2]{0,1:T(2,128)S(1)} fusion(pred[256,1024]{0,1:T(8,128)(4,1)S(1)} %pad_add_fusion, bf16[768,2,512]{2,0,1:T(8,128)(2,1)} %bitcast_select_fusion.4, bf16[256,2,512]{2,0,1:T(8,128)(2,1)} %copy.64, bf16[256,2,128]{2,1,0:T(2,128)(2,1)} %get-tuple-element.24), kind=kOutput, calls=%fused_computation.122 | convolution fusion | flops 137888768 | bytes 2754560 | tf_op jit(solution)/shard_map/sub | solution.py:45
  37.9 3.2 %fusion.21 = f32[256,2,256]{0,2,1:T(8,128)} fusion(f32[256,2]{0,1:T(2,128)S(1)} %fusion.110, pred[256,1024]{0,1:T(8,128)(4,1)S(1)} %pad_add_fusion, bf16[768,2,512]{2,0,1:T(8,128)(2,1)S(1)} %copy-done.1, bf16[256,2,512]{2,0,1:T(8,128)(2,1)} %copy.64, bf16[256,2,128]{2,1,0:T(2,128)(2,1)} %get-tuple-element.24), kind=kOutput, calls=%fused_computation.33 | convolution fusion | flops 408552960 | bytes 5376000 | tf_op jit(solution)/shard_map/nhk,khd->nhd/dot_general | solution.py:47
  41.1 2.0 %fusion.115 = f32[256,2]{0,1:T(2,128)S(1)} fusion(pred[256,1024]{0,1:T(8,128)(4,1)S(1)} %pad_add_fusion, bf16[256,2,512]{2,0,1:T(8,128)(2,1)} %copy.64, bf16[768,2,512]{2,0,1:T(8,128)(2,1)S(1)} %copy-done.1, bf16[256,2,128]{2,1,0:T(2,128)(2,1)S(1)} %get-tuple-element.23), kind=kOutput, calls=%fused_computation.123 | convolution fusion | flops 137888768 | bytes 2492416 | tf_op jit(solution)/shard_map/sub | solution.py:45
  43.1 3.4 %multiply_reduce_fusion.1 = (f32[256,2]{0,1:T(2,128)S(1)}, f32[256,2,256]{0,2,1:T(8,128)}) fusion(f32[256,2,256]{0,2,1:T(8,128)} %fusion.21, f32[256,2]{0,1:T(2,128)S(1)} %fusion.115, pred[256,1024]{0,1:T(8,128)(4,1)S(1)} %pad_add_fusion, bf16[256,2,512]{2,0,1:T(8,128)(2,1)} %copy.64, bf16[768,2,512]{2,0,1:T(8,128)(2,1)S(1)} %copy-done.1, ...), kind=kOutput, calls=%fused_computation.70 | convolution fusion | flops 409076736 | bytes 5902340 | tf_op jit(solution)/shard_map/nhk,khd->nhd/dot_general | solution.py:47
  47.8 5.3 %collective-permute-start = (bf16[256,512]{1,0:T(8,128)(2,1)S(1)}, bf16[256,512]{1,0:T(8,128)(2,1)S(1)}, u32[]{:S(2)}, u32[]{:S(2)}) collective-permute-start(bf16[256,512]{1,0:T(8,128)(2,1)S(1)} %copy.71), channel_id=1, source_target_pairs={{0,3},{1,0},{2,1},{3,2},{4,7},{5,4},{6,5},{7,6},{8,11},{9,8},{10,9... | collective-permute-start | bytes 786440 | tf_op jit(solution)/shard_map/ppermute | solution.py:77
  53.1 2.3 %collective-permute-start.1 = (bf16[256,512]{1,0:T(8,128)(2,1)S(1)}, bf16[256,512]{1,0:T(8,128)(2,1)S(1)}, u32[]{:S(2)}, u32[]{:S(2)}) collective-permute-start(bf16[256,512]{1,0:T(8,128)(2,1)S(1)} %copy.71), channel_id=1, source_target_pairs={{0,2},{1,3},{2,0},{3,1},{4,6},{5,7},{6,4},{7,5},{8,10},{9,11},{10,... | collective-permute-start | bytes 786440 | tf_op jit(solution)/shard_map/ppermute | solution.py:77
  55.4 2.6 %collective-permute-start.2 = (bf16[256,512]{1,0:T(8,128)(2,1)S(1)}, bf16[256,512]{1,0:T(8,128)(2,1)S(1)}, u32[]{:S(2)}, u32[]{:S(2)}) collective-permute-start(bf16[256,512]{1,0:T(8,128)(2,1)S(1)} %copy.71), channel_id=1, source_target_pairs={{0,1},{1,2},{2,3},{3,0},{4,5},{5,6},{6,7},{7,4},{8,9},{9,10},{10,1... | collective-permute-start | bytes 786440 | tf_op jit(solution)/shard_map/ppermute | solution.py:77
  58.1 3.7 %collective-permute-done.1 = bf16[256,512]{1,0:T(8,128)(2,1)S(1)} collective-permute-done((bf16[256,512]{1,0:T(8,128)(2,1)S(1)}, bf16[256,512]{1,0:T(8,128)(2,1)S(1)}, u32[]{:S(2)}, u32[]{:S(2)}) %collective-permute-start.1) | collective-permute-done | bytes 262176 | tf_op jit(solution)/shard_map/ppermute | solution.py:77
  61.8 2.7 %collective-permute-done.2 = bf16[256,512]{1,0:T(8,128)(2,1)S(1)} collective-permute-done((bf16[256,512]{1,0:T(8,128)(2,1)S(1)}, bf16[256,512]{1,0:T(8,128)(2,1)S(1)}, u32[]{:S(2)}, u32[]{:S(2)}) %collective-permute-start.2) | collective-permute-done | bytes 262176 | tf_op jit(solution)/shard_map/ppermute | solution.py:77
  65.8 39.2 %all-gather.2.cloned.1.call-done = bf16[1024,2816]{1,0:T(8,128)(2,1)} async-done(((bf16[64,2816]{1,0:T(8,128)(2,1)}), bf16[1024,2816]{1,0:T(8,128)(2,1)}) %all-gather.2.cloned.1.call-update) | async-done | bytes 5767184 | tf_op jit(solution)/shard_map/all_gather | solution.py:125
  105.0 7.3 %collective-permute-start.3 = (bf16[1024,2816]{1,0:T(8,128)(2,1)}, bf16[1024,2816]{1,0:T(8,128)(2,1)}, u32[]{:S(2)}, u32[]{:S(2)}) collective-permute-start(bf16[1024,2816]{1,0:T(8,128)(2,1)} %all-gather.2.cloned.1.call-done), channel_id=1, source_target_pairs={{0,4},{4,0},{1,5},{5,1},{2,6},{6,2},{3,7},{7,3},{8,12},{12,8},{9,1... | collective-permute-start | bytes 17301512 | tf_op jit(solution)/shard_map/ppermute | solution.py:129
  116.1 5.6 %collective-permute-done.3 = bf16[1024,2816]{1,0:T(8,128)(2,1)} collective-permute-done((bf16[1024,2816]{1,0:T(8,128)(2,1)}, bf16[1024,2816]{1,0:T(8,128)(2,1)}, u32[]{:S(2)}, u32[]{:S(2)}) %collective-permute-start.3) | collective-permute-done | bytes 5767200 | tf_op jit(solution)/shard_map/ppermute | solution.py:129
  121.6 1.7 fusion.26
  123.3 4.6 %collective-permute-start.4 = (bf16[256,512]{1,0:T(8,128)(2,1)S(1)}, bf16[256,512]{1,0:T(8,128)(2,1)S(1)}, u32[]{:S(2)}, u32[]{:S(2)}) collective-permute-start(bf16[256,512]{1,0:T(8,128)(2,1)S(1)} %fusion.26), channel_id=1, source_target_pairs={{0,3},{1,0},{2,1},{3,2},{4,7},{5,4},{6,5},{7,6},{8,11},{9,8},{10,9... | collective-permute-start | bytes 786440 | tf_op jit(solution)/shard_map/ppermute | solution.py:77
  128.0 2.5 %collective-permute-start.5 = (bf16[256,512]{1,0:T(8,128)(2,1)S(1)}, bf16[256,512]{1,0:T(8,128)(2,1)S(1)}, u32[]{:S(2)}, u32[]{:S(2)}) collective-permute-start(bf16[256,512]{1,0:T(8,128)(2,1)S(1)} %fusion.26), channel_id=1, source_target_pairs={{0,2},{1,3},{2,0},{3,1},{4,6},{5,7},{6,4},{7,5},{8,10},{9,11},{10,... | collective-permute-start | bytes 786440 | tf_op jit(solution)/shard_map/ppermute | solution.py:77
  130.4 2.7 %collective-permute-start.6 = (bf16[256,512]{1,0:T(8,128)(2,1)S(1)}, bf16[256,512]{1,0:T(8,128)(2,1)}, u32[]{:S(2)}, u32[]{:S(2)}) collective-permute-start(bf16[256,512]{1,0:T(8,128)(2,1)S(1)} %fusion.26), channel_id=1, source_target_pairs={{0,1},{1,2},{2,3},{3,0},{4,5},{5,6},{6,7},{7,4},{8,9},{9,10},{10,1... | collective-permute-start | bytes 786440 | tf_op jit(solution)/shard_map/ppermute | solution.py:77
  133.3 5.4 %collective-permute-done.4 = bf16[256,512]{1,0:T(8,128)(2,1)S(1)} collective-permute-done((bf16[256,512]{1,0:T(8,128)(2,1)S(1)}, bf16[256,512]{1,0:T(8,128)(2,1)S(1)}, u32[]{:S(2)}, u32[]{:S(2)}) %collective-permute-start.4) | collective-permute-done | bytes 262176 | tf_op jit(solution)/shard_map/ppermute | solution.py:77
  138.7 6.6 %collective-permute-done.6 = bf16[256,512]{1,0:T(8,128)(2,1)} collective-permute-done((bf16[256,512]{1,0:T(8,128)(2,1)S(1)}, bf16[256,512]{1,0:T(8,128)(2,1)}, u32[]{:S(2)}, u32[]{:S(2)}) %collective-permute-start.6) | collective-permute-done | bytes 262176 | tf_op jit(solution)/shard_map/ppermute | solution.py:77
  149.8 2.9 %fusion.4 = f32[256,1536]{1,0:T(8,128)S(1)} fusion(bf16[1024,2816]{1,0:T(8,128)(2,1)} %all-gather.2.cloned.1.call-done, bf16[256,2048]{0,1:T(8,128)(2,1)S(1)} %bitcast.86), kind=kOutput, calls=%fused_computation.5 | convolution fusion | flops 805306368 | bytes 5242880 | tf_op jit(solution)/shard_map/dot_general | solution.py:136
  152.7 2.9 %fusion.6 = f32[256,1536]{1,0:T(8,128)S(1)} fusion(f32[256,1536]{1,0:T(8,128)S(1)} %fusion.4, bf16[1024,2816]{1,0:T(8,128)(2,1)} %collective-permute-done.3, bf16[256,2048]{0,1:T(8,128)(2,1)S(1)} %bitcast.87), kind=kOutput, calls=%fused_computation.7 | convolution fusion | flops 805699584 | bytes 6815744 | tf_op jit(solution)/shard_map/dot_general | solution.py:136
  156.6 2.0 %fusion.15 = bf16[256,1024]{1,0:T(8,128)(2,1)S(1)} fusion(bf16[256,768]{1,0:T(8,128)(2,1)S(1)} %fusion.41, bf16[1024,2816]{1,0:T(8,128)(2,1)} %all-gather.2.cloned.1.call-done), kind=kOutput, calls=%fused_computation.28 | convolution fusion | flops 402915328 | bytes 2490368 | tf_op jit(solution)/shard_map/dot_general | solution.py:95
  158.9 2.1 %fusion.18 = bf16[256,1024]{1,0:T(8,128)(2,1)S(1)} fusion(bf16[256,768]{1,0:T(8,128)(2,1)} %copy-done.3, bf16[1024,2816]{1,0:T(8,128)(2,1)} %collective-permute-done.3), kind=kOutput, calls=%fused_computation.29 | convolution fusion | flops 402915328 | bytes 2490368 | tf_op jit(solution)/shard_map/dot_general | solution.py:95
  162.6 1.9 collective-permute-start.7
  165.4 2.5 %collective-permute-start.8 = (bf16[256,512]{1,0:T(8,128)(2,1)}, bf16[256,512]{1,0:T(8,128)(2,1)S(1)}, u32[]{:S(2)}, u32[]{:S(2)}) collective-permute-start(bf16[256,512]{1,0:T(8,128)(2,1)} %copy.92), channel_id=1, source_target_pairs={{0,2},{1,3},{2,0},{3,1},{4,6},{5,7},{6,4},{7,5},{8,10},{9,11},{10,... | collective-permute-start | bytes 786440 | tf_op jit(solution)/shard_map/ppermute | solution.py:110
  168.7 4.0 %collective-permute-start.9 = (bf16[256,512]{1,0:T(8,128)(2,1)}, bf16[256,512]{1,0:T(8,128)(2,1)}, u32[]{:S(2)}, u32[]{:S(2)}) collective-permute-start(bf16[256,512]{1,0:T(8,128)(2,1)} %copy.94), channel_id=1, source_target_pairs={{0,3},{1,0},{2,1},{3,2},{4,7},{5,4},{6,5},{7,6},{8,11},{9,8},{10,9... | collective-permute-start | bytes 786440 | tf_op jit(solution)/shard_map/ppermute | solution.py:110
  173.0 5.9 %collective-permute-done.7 = bf16[256,512]{1,0:T(8,128)(2,1)S(1)} collective-permute-done((bf16[256,512]{1,0:T(8,128)(2,1)}, bf16[256,512]{1,0:T(8,128)(2,1)S(1)}, u32[]{:S(2)}, u32[]{:S(2)}) %collective-permute-start.7) | collective-permute-done | bytes 262176 | tf_op jit(solution)/shard_map/ppermute | solution.py:110
  178.9 3.3 %collective-permute-done.9 = bf16[256,512]{1,0:T(8,128)(2,1)} collective-permute-done((bf16[256,512]{1,0:T(8,128)(2,1)}, bf16[256,512]{1,0:T(8,128)(2,1)}, u32[]{:S(2)}, u32[]{:S(2)}) %collective-permute-start.9) | collective-permute-done | bytes 262176 | tf_op jit(solution)/shard_map/ppermute | solution.py:110
  182.2 1.8 add_convert_fusion
  (72 shorter events, 22.0 us)
Async XLA Ops:
  6.5 13.1 %copy-start = (bf16[6,128,2,512]{3,2,1,0:T(2,128)(2,1)S(1)}, bf16[6,128,2,512]{3,2,1,0:T(2,128)(2,1)}, u32[]{:S(2)}) copy-start(bf16[6,128,2,512]{3,2,1,0:T(2,128)(2,1)} %param.16) | copy-start | bytes 4718596
  6.5 98.5 %all-gather.2.cloned.1.call-start = ((), (), s32[]{:S(2)}) async-start(), calls=%async_computation | async-start | bytes 6127616 | tf_op jit(solution)/shard_map/all_gather | solution.py:125
  25.2 1.8 copy-start.2
  25.2 3.3 %copy-start.5 = (f32[4,128]{1,0:T(4,128)S(1)}, f32[4,128]{1,0:T(4,128)}, u32[]{:S(2)}) copy-start(f32[4,128]{1,0:T(4,128)} %param.20) | copy-start | bytes 6148
  25.2 5.3 %copy-start.8 = (s32[128]{0:T(128)S(1)}, s32[128]{0:T(128)}, u32[]{:S(2)}) copy-start(s32[128]{0:T(128)} %param.19) | copy-start | bytes 1540
  25.2 6.8 %copy-start.9 = (s32[1,6]{1,0:T(1,128)S(1)}, s32[1,6]{1,0:T(1,128)}, u32[]{:S(2)}) copy-start(s32[1,6]{1,0:T(1,128)} %param.17) | copy-start | bytes 76
  35.6 2.3 %copy-start.1 = (bf16[768,2,512]{2,0,1:T(8,128)(2,1)S(1)}, bf16[768,2,512]{2,0,1:T(8,128)(2,1)}, u32[]{:S(2)}) copy-start(bf16[768,2,512]{2,0,1:T(8,128)(2,1)} %bitcast_select_fusion.4) | copy-start | bytes 4718596
  43.1 3.4 %copy-start.6 = (f32[256]{0:T(256)S(1)}, f32[256]{0:T(256)}, u32[]{:S(2)}) copy-start(f32[256]{0:T(256)} %param.21) | copy-start | bytes 3076
  47.8 10.3 %collective-permute-start = (bf16[256,512]{1,0:T(8,128)(2,1)S(1)}, bf16[256,512]{1,0:T(8,128)(2,1)S(1)}, u32[]{:S(2)}, u32[]{:S(2)}) collective-permute-start(bf16[256,512]{1,0:T(8,128)(2,1)S(1)} %copy.71), channel_id=1, source_target_pairs={{0,3},{1,0},{2,1},{3,2},{4,7},{5,4},{6,5},{7,6},{8,11},{9,8},{10,9... | collective-permute-start | bytes 786440 | tf_op jit(solution)/shard_map/ppermute | solution.py:77
  53.1 8.7 %collective-permute-start.1 = (bf16[256,512]{1,0:T(8,128)(2,1)S(1)}, bf16[256,512]{1,0:T(8,128)(2,1)S(1)}, u32[]{:S(2)}, u32[]{:S(2)}) collective-permute-start(bf16[256,512]{1,0:T(8,128)(2,1)S(1)} %copy.71), channel_id=1, source_target_pairs={{0,2},{1,3},{2,0},{3,1},{4,6},{5,7},{6,4},{7,5},{8,10},{9,11},{10,... | collective-permute-start | bytes 786440 | tf_op jit(solution)/shard_map/ppermute | solution.py:77
  55.4 9.2 %collective-permute-start.2 = (bf16[256,512]{1,0:T(8,128)(2,1)S(1)}, bf16[256,512]{1,0:T(8,128)(2,1)S(1)}, u32[]{:S(2)}, u32[]{:S(2)}) collective-permute-start(bf16[256,512]{1,0:T(8,128)(2,1)S(1)} %copy.71), channel_id=1, source_target_pairs={{0,1},{1,2},{2,3},{3,0},{4,5},{5,6},{6,7},{7,4},{8,9},{9,10},{10,1... | collective-permute-start | bytes 786440 | tf_op jit(solution)/shard_map/ppermute | solution.py:77
  105.0 16.7 %collective-permute-start.3 = (bf16[1024,2816]{1,0:T(8,128)(2,1)}, bf16[1024,2816]{1,0:T(8,128)(2,1)}, u32[]{:S(2)}, u32[]{:S(2)}) collective-permute-start(bf16[1024,2816]{1,0:T(8,128)(2,1)} %all-gather.2.cloned.1.call-done), channel_id=1, source_target_pairs={{0,4},{4,0},{1,5},{5,1},{2,6},{6,2},{3,7},{7,3},{8,12},{12,8},{9,1... | collective-permute-start | bytes 17301512 | tf_op jit(solution)/shard_map/ppermute | solution.py:129
  114.2 7.4 %copy-start.7 = (bf16[256,512]{1,0:T(8,128)(2,1)S(1)}, bf16[256,512]{1,0:T(8,128)(2,1)}, u32[]{:S(2)}) copy-start(bf16[256,512]{1,0:T(8,128)(2,1)} %param.22) | copy-start | bytes 786436
  116.1 17.1 %copy-start.4 = (f32[2048]{0:T(1024)S(1)}, f32[2048]{0:T(1024)}, u32[]{:S(2)}) copy-start(f32[2048]{0:T(1024)} %param.24) | copy-start | bytes 24580
  123.3 15.4 %collective-permute-start.4 = (bf16[256,512]{1,0:T(8,128)(2,1)S(1)}, bf16[256,512]{1,0:T(8,128)(2,1)S(1)}, u32[]{:S(2)}, u32[]{:S(2)}) collective-permute-start(bf16[256,512]{1,0:T(8,128)(2,1)S(1)} %fusion.26), channel_id=1, source_target_pairs={{0,3},{1,0},{2,1},{3,2},{4,7},{5,4},{6,5},{7,6},{8,11},{9,8},{10,9... | collective-permute-start | bytes 786440 | tf_op jit(solution)/shard_map/ppermute | solution.py:77
  128.0 10.8 %collective-permute-start.5 = (bf16[256,512]{1,0:T(8,128)(2,1)S(1)}, bf16[256,512]{1,0:T(8,128)(2,1)S(1)}, u32[]{:S(2)}, u32[]{:S(2)}) collective-permute-start(bf16[256,512]{1,0:T(8,128)(2,1)S(1)} %fusion.26), channel_id=1, source_target_pairs={{0,2},{1,3},{2,0},{3,1},{4,6},{5,7},{6,4},{7,5},{8,10},{9,11},{10,... | collective-permute-start | bytes 786440 | tf_op jit(solution)/shard_map/ppermute | solution.py:77
  130.4 14.9 %collective-permute-start.6 = (bf16[256,512]{1,0:T(8,128)(2,1)S(1)}, bf16[256,512]{1,0:T(8,128)(2,1)}, u32[]{:S(2)}, u32[]{:S(2)}) collective-permute-start(bf16[256,512]{1,0:T(8,128)(2,1)S(1)} %fusion.26), channel_id=1, source_target_pairs={{0,1},{1,2},{2,3},{3,0},{4,5},{5,6},{6,7},{7,4},{8,9},{9,10},{10,1... | collective-permute-start | bytes 786440 | tf_op jit(solution)/shard_map/ppermute | solution.py:77
  155.9 0.8 copy-start.3
  162.6 16.3 %collective-permute-start.7 = (bf16[256,512]{1,0:T(8,128)(2,1)}, bf16[256,512]{1,0:T(8,128)(2,1)S(1)}, u32[]{:S(2)}, u32[]{:S(2)}) collective-permute-start(bf16[256,512]{1,0:T(8,128)(2,1)} %copy.89), channel_id=1, source_target_pairs={{0,1},{1,2},{2,3},{3,0},{4,5},{5,6},{6,7},{7,4},{8,9},{9,10},{10,1... | collective-permute-start | bytes 786440 | tf_op jit(solution)/shard_map/ppermute | solution.py:110
  165.4 13.5 %collective-permute-start.8 = (bf16[256,512]{1,0:T(8,128)(2,1)}, bf16[256,512]{1,0:T(8,128)(2,1)S(1)}, u32[]{:S(2)}, u32[]{:S(2)}) collective-permute-start(bf16[256,512]{1,0:T(8,128)(2,1)} %copy.92), channel_id=1, source_target_pairs={{0,2},{1,3},{2,0},{3,1},{4,6},{5,7},{6,4},{7,5},{8,10},{9,11},{10,... | collective-permute-start | bytes 786440 | tf_op jit(solution)/shard_map/ppermute | solution.py:110
  168.7 13.5 %collective-permute-start.9 = (bf16[256,512]{1,0:T(8,128)(2,1)}, bf16[256,512]{1,0:T(8,128)(2,1)}, u32[]{:S(2)}, u32[]{:S(2)}) collective-permute-start(bf16[256,512]{1,0:T(8,128)(2,1)} %copy.94), channel_id=1, source_target_pairs={{0,3},{1,0},{2,1},{3,2},{4,7},{5,4},{6,5},{7,6},{8,11},{9,8},{10,9... | collective-permute-start | bytes 786440 | tf_op jit(solution)/shard_map/ppermute | solution.py:110
Sparse Core Ops, SparseCore 0:
  19.1 85.8 all-gather.1

commit v13 on v11

--- a/solution.py
+++ b/solution.py
@@ -169,12 +169,14 @@
     mlp_size = D // residual.shape[1]
     heads_all = mlp_gather(attn_out, mlp_size)
     rows_xz, heads_all = lax.optimization_barrier((rows_xz, heads_all))
-    halves = swap_with_core(rows_xz)
     bounds = [0]
     for w in widths:
         bounds.append(bounds[-1] + w)
-    out_full, gate_full, up_full, down_full = [
-        [half[:, bounds[i] : bounds[i + 1]] for half in halves] for i in range(4)
+    out_full = swap_with_core(rows_xz[:, : bounds[1]])
+    halves = swap_with_core(rows_xz[:, bounds[1] :])
+    gate_full, up_full, down_full = [
+        [half[:, bounds[i] - bounds[1] : bounds[i + 1] - bounds[1]] for half in halves]
+        for i in range(1, 4)
     ]
     rows = out_weight.shape[0]
     projected = split_dot(to_gathered_order(heads_all, rows), out_full)
@@ -184,7 +186,7 @@
     normed = (stream_all * lax.rsqrt(squares / D + 1e-05) * norm_gain).astype(jnp.bfloat16)
     normed = to_gathered_order(normed, rows)
     gate_up = split_dot(
-        normed, [half[:, bounds[1] : bounds[3]] for half in halves]
+        normed, [half[:, : bounds[3] - bounds[1]] for half in halves]
     )
     gate_value = gate_up[:, : widths[1]]
     up_value = gate_up[:, widths[1] :]

time: 191 us -> 201 us (1.052)
  local copies, waits for them, and re-layouts: 18.9 us -> 29.1 us
  waiting for transfers between devices: 64.3 us -> 61.1 us
    slice x0 -> x2, local copies, waits for them, and re-layouts: none -> 7.15 us  [the longest x1 4.85 us: per_device(): halves = swap_with_core(rows_xz[:, bounds[1]:])]
    ppermute x1 -> x2, waiting for transfers between devices: 7.05 us -> 2.82 us  [swap_with_core(): return [rows_xz, lax.ppermute(rows_xz, 'c', [(0, 1), (1, 0)])]]
    slice x4, local copies, waits for them, and re-layouts: 0.54 us -> 3.61 us  [mlp_gather(): return jnp.concatenate([gathered[k] for k in range(axis_size)], axis=1)]
    ppermute x1 -> x2, starting transfers between devices: 7.45 us -> 9.26 us  [swap_with_core(): return [rows_xz, lax.ppermute(rows_xz, 'c', [(0, 1), (1, 0)])]]
  transfers between devices with their start and end apart: 11 -> 12, of which waited for: 8 -> 8; matrix products, arithmetic and copies ran while one was open for 18% -> 26% of each run, Pallas kernels for 0% -> 0%
where the time goes in v13:
time: 201 us; the launch traced here: 198 us
  waiting for transfers between devices  61.1 us (30%)
  starting transfers between devices  42.3 us (21%)
  local copies, waits for them, and re-layouts  29.1 us (14%)
  matrix products  24 us (12%)
  between operations  16 us (8%)
  other arithmetic  14.4 us (7%)
  blocking collectives  11.5 us (6%)
    all_gather x1, waiting for transfers between devices, gather_over_xz(): return lax.all_gather(out, 'z', axis=0, tiled=True)  38.1 us
    ppermute x6, starting transfers between devices, mlp_gather(): lax.ppermute(block, 'mlp', [(i, (i + shift) % axis_size) for i in range(a...  22.5 us
    ppermute x6, waiting for transfers between devices, mlp_gather(): lax.ppermute(block, 'mlp', [(i, (i + shift) % axis_size) for i in range(a...  12 us
    all_gather x1, blocking collectives, gather_over_xz(): out = lax.all_gather(block, 'x', axis=0, tiled=True)  11.5 us
    ppermute x3, starting transfers between devices, down_and_scatter(): lax.ppermute(block_for(target), 'mlp', [(i, (i + shift) % axis_size) for...  10.6 us
    ppermute x2, starting transfers between devices, swap_with_core(): return [rows_xz, lax.ppermute(rows_xz, 'c', [(0, 1), (1, 0)])]  9.26 us
    dot_general x4, matrix products, split_dot(): jnp.dot(act[:, j * size:(j + 1) * size], half, preferred_element_type=jnp...  9.13 us
    ppermute x3, waiting for transfers between devices, down_and_scatter(): lax.ppermute(block_for(target), 'mlp', [(i, (i + shift) % axis_size) for...  8.17 us
  transfers between devices with their start and end apart: 12, of which 8 were waited for; matrix products, arithmetic and copies ran while one was open for 26% of the time, Pallas kernels for 0%

profile of v13, /device:TPU:1, one launch (start us, length us, event | category | flops | bytes accessed | tf_op | source)
XLA Modules:
  0.0 198.3 jit_solution(10852075165350120561)
XLA Ops:
  7.4 11.5 %all_gather.6 = bf16[64,2816]{1,0:T(8,128)(2,1)} all-gather(bf16[16,2816]{1,0:T(8,128)(2,1)S(1)} %pad_maximum_fusion.16), channel_id=1, replica_groups=mesh['x'=4,'z'=16,'c'=2,'mlp'=4] {'x'}, dimensions={0}, use_global_device_ids=true | all-gather | bytes 450560 | tf_op jit(solution)/shard_map/all_gather | solution.py:121
  19.6 5.6 %gather_fusion = bf16[6,128,2,512]{3,2,1,0:T(2,128)(2,1)} fusion(bf16[6,128,2,512]{3,2,1,0:T(2,128)(2,1)S(1)} %copy-done, s32[1024]{0:T(1024)S(1)} %pad_clamp_fusion.1), kind=kCustom, calls=%fused_computation.2 | custom fusion | bytes 3145752 | tf_op jit(solution)/shard_map/jit(_take)/gather | solution.py:23
  35.6 2.3 %fusion.110 = f32[256,2]{0,1:T(2,128)S(1)} fusion(pred[256,1024]{0,1:T(8,128)(4,1)S(1)} %pad_add_fusion, bf16[768,2,512]{2,0,1:T(8,128)(2,1)} %bitcast_select_fusion.4, bf16[256,2,512]{2,0,1:T(8,128)(2,1)} %copy.51, bf16[256,2,128]{2,1,0:T(2,128)(2,1)} %get-tuple-element.29), kind=kOutput, calls=%fused_computation.134 | convolution fusion | flops 137888768 | bytes 2754560 | tf_op jit(solution)/shard_map/sub | solution.py:45
  37.9 3.2 %fusion.21 = f32[256,2,256]{0,2,1:T(8,128)} fusion(f32[256,2]{0,1:T(2,128)S(1)} %fusion.110, pred[256,1024]{0,1:T(8,128)(4,1)S(1)} %pad_add_fusion, bf16[768,2,512]{2,0,1:T(8,128)(2,1)S(1)} %copy-done.1, bf16[256,2,512]{2,0,1:T(8,128)(2,1)} %copy.51, bf16[256,2,128]{2,1,0:T(2,128)(2,1)} %get-tuple-element.29), kind=kOutput, calls=%fused_computation.35 | convolution fusion | flops 408552960 | bytes 5376000 | tf_op jit(solution)/shard_map/nhk,khd->nhd/dot_general | solution.py:47
  41.1 2.0 fusion.115
  43.1 3.4 %multiply_reduce_fusion.1 = (f32[256,2]{0,1:T(2,128)S(1)}, f32[256,2,256]{0,2,1:T(8,128)}) fusion(f32[256,2,256]{0,2,1:T(8,128)} %fusion.21, f32[256,2]{0,1:T(2,128)S(1)} %fusion.115, pred[256,1024]{0,1:T(8,128)(4,1)S(1)} %pad_add_fusion, bf16[256,2,512]{2,0,1:T(8,128)(2,1)} %copy.51, bf16[768,2,512]{2,0,1:T(8,128)(2,1)S(1)} %copy-done.1, ...), kind=kOutput, calls=%fused_computation.74 | convolution fusion | flops 409076736 | bytes 5902340 | tf_op jit(solution)/shard_map/nhk,khd->nhd/dot_general | solution.py:47
  47.6 3.9 %collective-permute-start = (bf16[256,512]{0,1:T(8,128)(2,1)S(1)}, bf16[256,512]{0,1:T(8,128)(2,1)S(1)}, u32[]{:S(2)}, u32[]{:S(2)}) collective-permute-start(bf16[256,512]{0,1:T(8,128)(2,1)S(1)} %bitcast.122), channel_id=1, source_target_pairs={{0,1},{1,2},{2,3},{3,0},{4,5},{5,6},{6,7},{7,4},{8,9},{9,10},{10,1... | collective-permute-start | bytes 786440 | tf_op jit(solution)/shard_map/ppermute | solution.py:77
  51.5 4.5 %collective-permute-start.1 = (bf16[256,512]{0,1:T(8,128)(2,1)S(1)}, bf16[256,512]{0,1:T(8,128)(2,1)S(1)}, u32[]{:S(2)}, u32[]{:S(2)}) collective-permute-start(bf16[256,512]{0,1:T(8,128)(2,1)S(1)} %bitcast.123), channel_id=1, source_target_pairs={{0,2},{1,3},{2,0},{3,1},{4,6},{5,7},{6,4},{7,5},{8,10},{9,11},{10,... | collective-permute-start | bytes 786440 | tf_op jit(solution)/shard_map/ppermute | solution.py:77
  56.1 3.0 %collective-permute-start.2 = (bf16[256,512]{0,1:T(8,128)(2,1)S(1)}, bf16[256,512]{0,1:T(8,128)(2,1)S(1)}, u32[]{:S(2)}, u32[]{:S(2)}) collective-permute-start(bf16[256,512]{0,1:T(8,128)(2,1)S(1)} %bitcast.124), channel_id=1, source_target_pairs={{0,3},{1,0},{2,1},{3,2},{4,7},{5,4},{6,5},{7,6},{8,11},{9,8},{10,9... | collective-permute-start | bytes 786440 | tf_op jit(solution)/shard_map/ppermute | solution.py:77
  59.1 3.9 %collective-permute-done.1 = bf16[256,512]{0,1:T(8,128)(2,1)S(1)} collective-permute-done((bf16[256,512]{0,1:T(8,128)(2,1)S(1)}, bf16[256,512]{0,1:T(8,128)(2,1)S(1)}, u32[]{:S(2)}, u32[]{:S(2)}) %collective-permute-start.1) | collective-permute-done | bytes 262176 | tf_op jit(solution)/shard_map/ppermute | solution.py:77
  64.7 1.8 gather_fusion.1
  66.9 38.1 %all-gather.2.cloned.1.call-done = bf16[1024,2816]{1,0:T(8,128)(2,1)} async-done(((bf16[64,2816]{1,0:T(8,128)(2,1)}), bf16[1024,2816]{1,0:T(8,128)(2,1)}) %all-gather.2.cloned.1.call-update) | async-done | bytes 5767184 | tf_op jit(solution)/shard_map/all_gather | solution.py:122
  105.0 4.8 %slice.112 = bf16[1024,2304]{1,0:T(8,128)(2,1)} slice(bf16[1024,2816]{1,0:T(8,128)(2,1)} %all-gather.2.cloned.1.call-done), slice={[0:1024], [512:2816]} | slice | bytes 9437184 | tf_op jit(solution)/shard_map/slice | solution.py:176
  109.8 7.4 %collective-permute-start.7 = (bf16[1024,2304]{1,0:T(8,128)(2,1)}, bf16[1024,2304]{1,0:T(8,128)(2,1)}, u32[]{:S(2)}, u32[]{:S(2)}) collective-permute-start(bf16[1024,2304]{1,0:T(8,128)(2,1)} %slice.112), channel_id=1, source_target_pairs={{0,4},{4,0},{1,5},{5,1},{2,6},{6,2},{3,7},{7,3},{8,12},{12,8},{9,1... | collective-permute-start | bytes 14155784 | tf_op jit(solution)/shard_map/ppermute | solution.py:126
  117.2 2.3 %slice.103 = bf16[1024,512]{1,0:T(8,128)(2,1)} slice(bf16[1024,2816]{1,0:T(8,128)(2,1)} %all-gather.2.cloned.1.call-done), slice={[0:1024], [0:512]} | slice | bytes 2097152 | tf_op jit(solution)/shard_map/slice | solution.py:175
  119.5 1.9 collective-permute-start.3
  123.7 2.8 %collective-permute-done.3 = bf16[1024,512]{1,0:T(8,128)(2,1)} collective-permute-done((bf16[1024,512]{1,0:T(8,128)(2,1)}, bf16[1024,512]{1,0:T(8,128)(2,1)}, u32[]{:S(2)}, u32[]{:S(2)}) %collective-permute-start.3) | collective-permute-done | bytes 1048608 | tf_op jit(solution)/shard_map/ppermute | solution.py:126
  128.2 3.3 %collective-permute-start.4 = (bf16[256,512]{1,0:T(8,128)(2,1)S(1)}, bf16[256,512]{1,0:T(8,128)(2,1)S(1)}, u32[]{:S(2)}, u32[]{:S(2)}) collective-permute-start(bf16[256,512]{1,0:T(8,128)(2,1)S(1)} %fusion.26), channel_id=1, source_target_pairs={{0,1},{1,2},{2,3},{3,0},{4,5},{5,6},{6,7},{7,4},{8,9},{9,10},{10,1... | collective-permute-start | bytes 786440 | tf_op jit(solution)/shard_map/ppermute | solution.py:77
  131.5 4.5 %collective-permute-start.5 = (bf16[256,512]{1,0:T(8,128)(2,1)S(1)}, bf16[256,512]{1,0:T(8,128)(2,1)S(1)}, u32[]{:S(2)}, u32[]{:S(2)}) collective-permute-start(bf16[256,512]{1,0:T(8,128)(2,1)S(1)} %fusion.26), channel_id=1, source_target_pairs={{0,2},{1,3},{2,0},{3,1},{4,6},{5,7},{6,4},{7,5},{8,10},{9,11},{10,... | collective-permute-start | bytes 786440 | tf_op jit(solution)/shard_map/ppermute | solution.py:77
  136.1 3.2 %collective-permute-start.6 = (bf16[256,512]{1,0:T(8,128)(2,1)S(1)}, bf16[256,512]{1,0:T(8,128)(2,1)S(1)}, u32[]{:S(2)}, u32[]{:S(2)}) collective-permute-start(bf16[256,512]{1,0:T(8,128)(2,1)S(1)} %fusion.26), channel_id=1, source_target_pairs={{0,3},{1,0},{2,1},{3,2},{4,7},{5,4},{6,5},{7,6},{8,11},{9,8},{10,9... | collective-permute-start | bytes 786440 | tf_op jit(solution)/shard_map/ppermute | solution.py:77
  139.5 6.3 %collective-permute-done.5 = bf16[256,512]{1,0:T(8,128)(2,1)S(1)} collective-permute-done((bf16[256,512]{1,0:T(8,128)(2,1)S(1)}, bf16[256,512]{1,0:T(8,128)(2,1)S(1)}, u32[]{:S(2)}, u32[]{:S(2)}) %collective-permute-start.5) | collective-permute-done | bytes 262176 | tf_op jit(solution)/shard_map/ppermute | solution.py:77
  148.1 1.8 gather_fusion.2
  156.9 2.9 %fusion.4 = f32[256,1536]{1,0:T(8,128)S(1)} fusion(bf16[1024,2816]{1,0:T(8,128)(2,1)} %all-gather.2.cloned.1.call-done, bf16[256,2048]{0,1:T(8,128)(2,1)S(1)} %bitcast.111), kind=kOutput, calls=%fused_computation.7 | convolution fusion | flops 805306368 | bytes 5242880 | tf_op jit(solution)/shard_map/dot_general | solution.py:133
  159.9 2.9 %fusion.6 = f32[256,1536]{1,0:T(8,128)S(1)} fusion(f32[256,1536]{1,0:T(8,128)S(1)} %fusion.4, bf16[1024,2304]{1,0:T(8,128)(2,1)} %collective-permute-done.7, bf16[256,2048]{0,1:T(8,128)(2,1)S(1)} %bitcast.112), kind=kOutput, calls=%fused_computation.9 | convolution fusion | flops 805699584 | bytes 6815744 | tf_op jit(solution)/shard_map/dot_general | solution.py:133
  163.0 2.0 %fusion.15 = bf16[256,1024]{1,0:T(8,128)(2,1)S(1)} fusion(bf16[256,768]{1,0:T(8,128)(2,1)S(1)} %fusion.38, bf16[1024,2816]{1,0:T(8,128)(2,1)} %all-gather.2.cloned.1.call-done), kind=kOutput, calls=%fused_computation.30 | convolution fusion | flops 402915328 | bytes 2490368 | tf_op jit(solution)/shard_map/dot_general | solution.py:92
  165.2 2.0 %fusion.18 = bf16[256,1024]{1,0:T(8,128)(2,1)S(1)} fusion(bf16[256,768]{1,0:T(8,128)(2,1)S(1)} %fusion.38, bf16[1024,2304]{1,0:T(8,128)(2,1)} %collective-permute-done.7), kind=kOutput, calls=%fused_computation.31 | convolution fusion | flops 402915328 | bytes 2490368 | tf_op jit(solution)/shard_map/dot_general | solution.py:92
  168.8 4.9 %collective-permute-start.10 = (bf16[256,512]{1,0:T(8,128)(2,1)}, bf16[256,512]{1,0:T(8,128)(2,1)S(1)}, u32[]{:S(2)}, u32[]{:S(2)}) collective-permute-start(bf16[256,512]{1,0:T(8,128)(2,1)} %copy.73), channel_id=1, source_target_pairs={{0,3},{1,0},{2,1},{3,2},{4,7},{5,4},{6,5},{7,6},{8,11},{9,8},{10,9... | collective-permute-start | bytes 786440 | tf_op jit(solution)/shard_map/ppermute | solution.py:107
  174.6 2.0 %collective-permute-start.8 = (bf16[256,512]{1,0:T(8,128)(2,1)}, bf16[256,512]{1,0:T(8,128)(2,1)S(1)}, u32[]{:S(2)}, u32[]{:S(2)}) collective-permute-start(bf16[256,512]{1,0:T(8,128)(2,1)} %copy.68), channel_id=1, source_target_pairs={{0,1},{1,2},{2,3},{3,0},{4,5},{5,6},{6,7},{7,4},{8,9},{9,10},{10,1... | collective-permute-start | bytes 786440 | tf_op jit(solution)/shard_map/ppermute | solution.py:107
  177.5 3.7 %collective-permute-start.9 = (bf16[256,512]{1,0:T(8,128)(2,1)}, bf16[256,512]{1,0:T(8,128)(2,1)}, u32[]{:S(2)}, u32[]{:S(2)}) collective-permute-start(bf16[256,512]{1,0:T(8,128)(2,1)} %copy.71), channel_id=1, source_target_pairs={{0,2},{1,3},{2,0},{3,1},{4,6},{5,7},{6,4},{7,5},{8,10},{9,11},{10,... | collective-permute-start | bytes 786440 | tf_op jit(solution)/shard_map/ppermute | solution.py:107
  181.5 4.1 %collective-permute-done.8 = bf16[256,512]{1,0:T(8,128)(2,1)S(1)} collective-permute-done((bf16[256,512]{1,0:T(8,128)(2,1)}, bf16[256,512]{1,0:T(8,128)(2,1)S(1)}, u32[]{:S(2)}, u32[]{:S(2)}) %collective-permute-start.8) | collective-permute-done | bytes 262176 | tf_op jit(solution)/shard_map/ppermute | solution.py:107
  185.6 4.0 %collective-permute-done.9 = bf16[256,512]{1,0:T(8,128)(2,1)} collective-permute-done((bf16[256,512]{1,0:T(8,128)(2,1)}, bf16[256,512]{1,0:T(8,128)(2,1)}, u32[]{:S(2)}, u32[]{:S(2)}) %collective-permute-start.9) | collective-permute-done | bytes 262176 | tf_op jit(solution)/shard_map/ppermute | solution.py:107
  189.7 1.8 add_convert_fusion
  (87 shorter events, 30.4 us)
Async XLA Ops:
  6.5 13.1 %copy-start = (bf16[6,128,2,512]{3,2,1,0:T(2,128)(2,1)S(1)}, bf16[6,128,2,512]{3,2,1,0:T(2,128)(2,1)}, u32[]{:S(2)}) copy-start(bf16[6,128,2,512]{3,2,1,0:T(2,128)(2,1)} %param.18) | copy-start | bytes 4718596
  6.5 98.4 %all-gather.2.cloned.1.call-start = ((), (), s32[]{:S(2)}) async-start(), calls=%async_computation | async-start | bytes 6127616 | tf_op jit(solution)/shard_map/all_gather | solution.py:122
  25.2 1.8 copy-start.5
  25.2 3.3 %copy-start.7 = (f32[4,128]{1,0:T(4,128)S(1)}, f32[4,128]{1,0:T(4,128)}, u32[]{:S(2)}) copy-start(f32[4,128]{1,0:T(4,128)} %param.22) | copy-start | bytes 6148
  25.2 5.3 %copy-start.10 = (s32[128]{0:T(128)S(1)}, s32[128]{0:T(128)}, u32[]{:S(2)}) copy-start(s32[128]{0:T(128)} %param.21) | copy-start | bytes 1540
  25.2 6.8 %copy-start.11 = (s32[1,6]{1,0:T(1,128)S(1)}, s32[1,6]{1,0:T(1,128)}, u32[]{:S(2)}) copy-start(s32[1,6]{1,0:T(1,128)} %param.19) | copy-start | bytes 76
  35.6 2.3 %copy-start.1 = (bf16[768,2,512]{2,0,1:T(8,128)(2,1)S(1)}, bf16[768,2,512]{2,0,1:T(8,128)(2,1)}, u32[]{:S(2)}) copy-start(bf16[768,2,512]{2,0,1:T(8,128)(2,1)} %bitcast_select_fusion.4) | copy-start | bytes 4718596
  43.1 3.4 %copy-start.8 = (f32[256]{0:T(256)S(1)}, f32[256]{0:T(256)}, u32[]{:S(2)}) copy-start(f32[256]{0:T(256)} %param.23) | copy-start | bytes 3076
  47.6 11.5 %collective-permute-start = (bf16[256,512]{0,1:T(8,128)(2,1)S(1)}, bf16[256,512]{0,1:T(8,128)(2,1)S(1)}, u32[]{:S(2)}, u32[]{:S(2)}) collective-permute-start(bf16[256,512]{0,1:T(8,128)(2,1)S(1)} %bitcast.122), channel_id=1, source_target_pairs={{0,1},{1,2},{2,3},{3,0},{4,5},{5,6},{6,7},{7,4},{8,9},{9,10},{10,1... | collective-permute-start | bytes 786440 | tf_op jit(solution)/shard_map/ppermute | solution.py:77
  51.5 11.4 %collective-permute-start.1 = (bf16[256,512]{0,1:T(8,128)(2,1)S(1)}, bf16[256,512]{0,1:T(8,128)(2,1)S(1)}, u32[]{:S(2)}, u32[]{:S(2)}) collective-permute-start(bf16[256,512]{0,1:T(8,128)(2,1)S(1)} %bitcast.123), channel_id=1, source_target_pairs={{0,2},{1,3},{2,0},{3,1},{4,6},{5,7},{6,4},{7,5},{8,10},{9,11},{10,... | collective-permute-start | bytes 786440 | tf_op jit(solution)/shard_map/ppermute | solution.py:77
  56.1 7.5 %collective-permute-start.2 = (bf16[256,512]{0,1:T(8,128)(2,1)S(1)}, bf16[256,512]{0,1:T(8,128)(2,1)S(1)}, u32[]{:S(2)}, u32[]{:S(2)}) collective-permute-start(bf16[256,512]{0,1:T(8,128)(2,1)S(1)} %bitcast.124), channel_id=1, source_target_pairs={{0,3},{1,0},{2,1},{3,2},{4,7},{5,4},{6,5},{7,6},{8,11},{9,8},{10,9... | collective-permute-start | bytes 786440 | tf_op jit(solution)/shard_map/ppermute | solution.py:77
  109.8 50.0 %collective-permute-start.7 = (bf16[1024,2304]{1,0:T(8,128)(2,1)}, bf16[1024,2304]{1,0:T(8,128)(2,1)}, u32[]{:S(2)}, u32[]{:S(2)}) collective-permute-start(bf16[1024,2304]{1,0:T(8,128)(2,1)} %slice.112), channel_id=1, source_target_pairs={{0,4},{4,0},{1,5},{5,1},{2,6},{6,2},{3,7},{7,3},{8,12},{12,8},{9,1... | collective-permute-start | bytes 14155784 | tf_op jit(solution)/shard_map/ppermute | solution.py:126
  119.5 7.0 %collective-permute-start.3 = (bf16[1024,512]{1,0:T(8,128)(2,1)}, bf16[1024,512]{1,0:T(8,128)(2,1)}, u32[]{:S(2)}, u32[]{:S(2)}) collective-permute-start(bf16[1024,512]{1,0:T(8,128)(2,1)} %slice.103), channel_id=1, source_target_pairs={{0,4},{4,0},{1,5},{5,1},{2,6},{6,2},{3,7},{7,3},{8,12},{12,8},{9,1... | collective-permute-start | bytes 3145736 | tf_op jit(solution)/shard_map/ppermute | solution.py:126
  121.9 4.7 %copy-start.9 = (bf16[256,512]{1,0:T(8,128)(2,1)S(1)}, bf16[256,512]{1,0:T(8,128)(2,1)}, u32[]{:S(2)}) copy-start(bf16[256,512]{1,0:T(8,128)(2,1)} %param.24) | copy-start | bytes 786436
  122.0 17.3 %copy-start.6 = (f32[2048]{0:T(1024)S(1)}, f32[2048]{0:T(1024)}, u32[]{:S(2)}) copy-start(f32[2048]{0:T(1024)} %param.26) | copy-start | bytes 24580
  128.2 18.8 %copy-start.2 = (bf16[256,512]{1,0:T(8,128)(2,1)}, bf16[256,512]{1,0:T(8,128)(2,1)S(1)}, u32[]{:S(2)}) copy-start(bf16[256,512]{1,0:T(8,128)(2,1)S(1)} %fusion.26) | copy-start | bytes 786436
  128.2 11.3 %collective-permute-start.4 = (bf16[256,512]{1,0:T(8,128)(2,1)S(1)}, bf16[256,512]{1,0:T(8,128)(2,1)S(1)}, u32[]{:S(2)}, u32[]{:S(2)}) collective-permute-start(bf16[256,512]{1,0:T(8,128)(2,1)S(1)} %fusion.26), channel_id=1, source_target_pairs={{0,1},{1,2},{2,3},{3,0},{4,5},{5,6},{6,7},{7,4},{8,9},{9,10},{10,1... | collective-permute-start | bytes 786440 | tf_op jit(solution)/shard_map/ppermute | solution.py:77
  131.5 14.3 %collective-permute-start.5 = (bf16[256,512]{1,0:T(8,128)(2,1)S(1)}, bf16[256,512]{1,0:T(8,128)(2,1)S(1)}, u32[]{:S(2)}, u32[]{:S(2)}) collective-permute-start(bf16[256,512]{1,0:T(8,128)(2,1)S(1)} %fusion.26), channel_id=1, source_target_pairs={{0,2},{1,3},{2,0},{3,1},{4,6},{5,7},{6,4},{7,5},{8,10},{9,11},{10,... | collective-permute-start | bytes 786440 | tf_op jit(solution)/shard_map/ppermute | solution.py:77
  136.1 10.9 %collective-permute-start.6 = (bf16[256,512]{1,0:T(8,128)(2,1)S(1)}, bf16[256,512]{1,0:T(8,128)(2,1)S(1)}, u32[]{:S(2)}, u32[]{:S(2)}) collective-permute-start(bf16[256,512]{1,0:T(8,128)(2,1)S(1)} %fusion.26), channel_id=1, source_target_pairs={{0,3},{1,0},{2,1},{3,2},{4,7},{5,4},{6,5},{7,6},{8,11},{9,8},{10,9... | collective-permute-start | bytes 786440 | tf_op jit(solution)/shard_map/ppermute | solution.py:77
  153.7 1.3 copy-start.4
  168.8 12.6 %collective-permute-start.10 = (bf16[256,512]{1,0:T(8,128)(2,1)}, bf16[256,512]{1,0:T(8,128)(2,1)S(1)}, u32[]{:S(2)}, u32[]{:S(2)}) collective-permute-start(bf16[256,512]{1,0:T(8,128)(2,1)} %copy.73), channel_id=1, source_target_pairs={{0,3},{1,0},{2,1},{3,2},{4,7},{5,4},{6,5},{7,6},{8,11},{9,8},{10,9... | collective-permute-start | bytes 786440 | tf_op jit(solution)/shard_map/ppermute | solution.py:107
  173.8 15.9 %copy-start.3 = (bf16[256,512]{1,0:T(8,128)(2,1)S(1)}, bf16[256,512]{1,0:T(8,128)(2,1)}, u32[]{:S(2)}) copy-start(bf16[256,512]{1,0:T(8,128)(2,1)} %copy-done.2) | copy-start | bytes 786436
  174.6 11.0 %collective-permute-start.8 = (bf16[256,512]{1,0:T(8,128)(2,1)}, bf16[256,512]{1,0:T(8,128)(2,1)S(1)}, u32[]{:S(2)}, u32[]{:S(2)}) collective-permute-start(bf16[256,512]{1,0:T(8,128)(2,1)} %copy.68), channel_id=1, source_target_pairs={{0,1},{1,2},{2,3},{3,0},{4,5},{5,6},{6,7},{7,4},{8,9},{9,10},{10,1... | collective-permute-start | bytes 786440 | tf_op jit(solution)/shard_map/ppermute | solution.py:107
  177.5 12.1 %collective-permute-start.9 = (bf16[256,512]{1,0:T(8,128)(2,1)}, bf16[256,512]{1,0:T(8,128)(2,1)}, u32[]{:S(2)}, u32[]{:S(2)}) collective-permute-start(bf16[256,512]{1,0:T(8,128)(2,1)} %copy.71), channel_id=1, source_target_pairs={{0,2},{1,3},{2,0},{3,1},{4,6},{5,7},{6,4},{7,5},{8,10},{9,11},{10,... | collective-permute-start | bytes 786440 | tf_op jit(solution)/shard_map/ppermute | solution.py:107
Sparse Core Ops, SparseCore 0:
  19.1 85.8 all-gather.1

commit v14 on v11

--- a/solution.py
+++ b/solution.py
@@ -93,12 +93,12 @@
             hidden_act, half, (((1,), (1,)), ((), ())), preferred_element_type=jnp.float32
         )
         parts.append(value.astype(jnp.bfloat16).reshape(n, nz, nx, rows))
-    both = jnp.stack(parts, axis=1)
-    both = jnp.where(own == 0, both, both[:, ::-1])
 
     def block_for(target):
-        picked = lax.dynamic_index_in_dim(both, target, 3, keepdims=False)
-        return picked.transpose(0, 2, 1, 3).reshape(n, -1)
+        picks = [lax.dynamic_index_in_dim(p, target, 2, keepdims=False) for p in parts]
+        first = jnp.where(own == 0, picks[0], picks[1])
+        second = jnp.where(own == 0, picks[1], picks[0])
+        return jnp.stack([first, second], axis=2).reshape(n, -1)
 
     incoming = []
     for shift in range(1, axis_size):

time: 191 us -> 190 us (level)
  no operation moved by 1% of the time
where the time goes in v14:
time: 190 us; the launch traced here: 189 us
  waiting for transfers between devices  64.4 us (34%)
  starting transfers between devices  40.7 us (21%)
  matrix products  24.1 us (13%)
  local copies, waits for them, and re-layouts  18.8 us (10%)
  between operations  15.9 us (8%)
  other arithmetic  13 us (7%)
  blocking collectives  11.5 us (6%)
    all_gather x1, waiting for transfers between devices, gather_over_xz(): return lax.all_gather(out, 'z', axis=0, tiled=True)  38 us
    ppermute x6, starting transfers between devices, mlp_gather(): lax.ppermute(block, 'mlp', [(i, (i + shift) % axis_size) for i in range(a...  22.5 us
    ppermute x6, waiting for transfers between devices, mlp_gather(): lax.ppermute(block, 'mlp', [(i, (i + shift) % axis_size) for i in range(a...  12.2 us
    all_gather x1, blocking collectives, gather_over_xz(): out = lax.all_gather(block, 'x', axis=0, tiled=True)  11.5 us
    ppermute x3, starting transfers between devices, down_and_scatter(): lax.ppermute(block_for(target), 'mlp', [(i, (i + shift) % axis_size) for...  11 us
    dot_general x4, matrix products, split_dot(): jnp.dot(act[:, j * size:(j + 1) * size], half, preferred_element_type=jnp...  9.13 us
    gather x2, local copies, waits for them, and re-layouts, attend(): pages = jnp.take(cache_pool, page_table[0], axis=0)  7.33 us
    ppermute x1, starting transfers between devices, swap_with_core(): return [rows_xz, lax.ppermute(rows_xz, 'c', [(0, 1), (1, 0)])]  7.31 us
  transfers between devices with their start and end apart: 11, of which 8 were waited for; matrix products, arithmetic and copies ran while one was open for 18% of the time, Pallas kernels for 0%

profile of v14, /device:TPU:1, one launch (start us, length us, event | category | flops | bytes accessed | tf_op | source)
XLA Modules:
  0.0 188.6 jit_solution(5457327461825373114)
XLA Ops:
  7.4 11.5 %all_gather.6 = bf16[64,2816]{1,0:T(8,128)(2,1)} all-gather(bf16[16,2816]{1,0:T(8,128)(2,1)S(1)} %pad_maximum_fusion.19), channel_id=1, replica_groups=mesh['x'=4,'z'=16,'c'=2,'mlp'=4] {'x'}, dimensions={0}, use_global_device_ids=true | all-gather | bytes 450560 | tf_op jit(solution)/shard_map/all_gather | solution.py:121
  19.6 5.6 %gather_fusion = bf16[6,128,2,512]{3,2,1,0:T(2,128)(2,1)} fusion(bf16[6,128,2,512]{3,2,1,0:T(2,128)(2,1)S(1)} %copy-done, s32[1024]{0:T(1024)S(1)} %pad_clamp_fusion.1), kind=kCustom, calls=%fused_computation.2 | custom fusion | bytes 3145752 | tf_op jit(solution)/shard_map/jit(_take)/gather | solution.py:23
  25.2 1.7 copy.47
  32.3 1.8 fusion.110
  35.6 2.3 %fusion.111 = f32[256,2]{0,1:T(2,128)S(1)} fusion(pred[256,1024]{0,1:T(8,128)(4,1)S(1)} %pad_add_fusion, bf16[768,2,512]{2,0,1:T(8,128)(2,1)} %bitcast_select_fusion.4, bf16[256,2,512]{2,0,1:T(8,128)(2,1)} %copy.48, bf16[256,2,128]{2,1,0:T(2,128)(2,1)} %get-tuple-element.33), kind=kOutput, calls=%fused_computation.142 | convolution fusion | flops 137888768 | bytes 2754560 | tf_op jit(solution)/shard_map/sub | solution.py:45
  37.9 3.2 %fusion.21 = f32[256,2,256]{0,2,1:T(8,128)} fusion(f32[256,2]{0,1:T(2,128)S(1)} %fusion.111, pred[256,1024]{0,1:T(8,128)(4,1)S(1)} %pad_add_fusion, bf16[768,2,512]{2,0,1:T(8,128)(2,1)S(1)} %copy-done.1, bf16[256,2,512]{2,0,1:T(8,128)(2,1)} %copy.48, bf16[256,2,128]{2,1,0:T(2,128)(2,1)} %get-tuple-element.33), kind=kOutput, calls=%fused_computation.34 | convolution fusion | flops 408552960 | bytes 5376000 | tf_op jit(solution)/shard_map/nhk,khd->nhd/dot_general | solution.py:47
  41.1 2.0 %fusion.116 = f32[256,2]{0,1:T(2,128)S(1)} fusion(pred[256,1024]{0,1:T(8,128)(4,1)S(1)} %pad_add_fusion, bf16[256,2,512]{2,0,1:T(8,128)(2,1)} %copy.48, bf16[768,2,512]{2,0,1:T(8,128)(2,1)S(1)} %copy-done.1, bf16[256,2,128]{2,1,0:T(2,128)(2,1)S(1)} %get-tuple-element.32), kind=kOutput, calls=%fused_computation.143 | convolution fusion | flops 137888768 | bytes 2492416 | tf_op jit(solution)/shard_map/sub | solution.py:45
  43.1 3.4 %multiply_reduce_fusion.1 = (f32[256,2]{0,1:T(2,128)S(1)}, f32[256,2,256]{0,2,1:T(8,128)}) fusion(f32[256,2,256]{0,2,1:T(8,128)} %fusion.21, f32[256,2]{0,1:T(2,128)S(1)} %fusion.116, pred[256,1024]{0,1:T(8,128)(4,1)S(1)} %pad_add_fusion, bf16[256,2,512]{2,0,1:T(8,128)(2,1)} %copy.48, bf16[768,2,512]{2,0,1:T(8,128)(2,1)S(1)} %copy-done.1, ...), kind=kOutput, calls=%fused_computation.73 | convolution fusion | flops 409076736 | bytes 5902340 | tf_op jit(solution)/shard_map/nhk,khd->nhd/dot_general | solution.py:47
  47.6 3.9 %collective-permute-start = (bf16[256,512]{0,1:T(8,128)(2,1)S(1)}, bf16[256,512]{0,1:T(8,128)(2,1)S(1)}, u32[]{:S(2)}, u32[]{:S(2)}) collective-permute-start(bf16[256,512]{0,1:T(8,128)(2,1)S(1)} %bitcast.105), channel_id=1, source_target_pairs={{0,1},{1,2},{2,3},{3,0},{4,5},{5,6},{6,7},{7,4},{8,9},{9,10},{10,1... | collective-permute-start | bytes 786440 | tf_op jit(solution)/shard_map/ppermute | solution.py:77
  51.5 4.5 %collective-permute-start.1 = (bf16[256,512]{0,1:T(8,128)(2,1)S(1)}, bf16[256,512]{0,1:T(8,128)(2,1)S(1)}, u32[]{:S(2)}, u32[]{:S(2)}) collective-permute-start(bf16[256,512]{0,1:T(8,128)(2,1)S(1)} %bitcast.106), channel_id=1, source_target_pairs={{0,2},{1,3},{2,0},{3,1},{4,6},{5,7},{6,4},{7,5},{8,10},{9,11},{10,... | collective-permute-start | bytes 786440 | tf_op jit(solution)/shard_map/ppermute | solution.py:77
  56.1 3.0 %collective-permute-start.2 = (bf16[256,512]{0,1:T(8,128)(2,1)S(1)}, bf16[256,512]{0,1:T(8,128)(2,1)S(1)}, u32[]{:S(2)}, u32[]{:S(2)}) collective-permute-start(bf16[256,512]{0,1:T(8,128)(2,1)S(1)} %bitcast.107), channel_id=1, source_target_pairs={{0,3},{1,0},{2,1},{3,2},{4,7},{5,4},{6,5},{7,6},{8,11},{9,8},{10,9... | collective-permute-start | bytes 786440 | tf_op jit(solution)/shard_map/ppermute | solution.py:77
  59.1 3.8 %collective-permute-done.1 = bf16[256,512]{0,1:T(8,128)(2,1)S(1)} collective-permute-done((bf16[256,512]{0,1:T(8,128)(2,1)S(1)}, bf16[256,512]{0,1:T(8,128)(2,1)S(1)}, u32[]{:S(2)}, u32[]{:S(2)}) %collective-permute-start.1) | collective-permute-done | bytes 262176 | tf_op jit(solution)/shard_map/ppermute | solution.py:77
  64.7 1.8 gather_fusion.1
  66.9 38.0 %all-gather.2.cloned.1.call-done = bf16[1024,2816]{1,0:T(8,128)(2,1)} async-done(((bf16[64,2816]{1,0:T(8,128)(2,1)}), bf16[1024,2816]{1,0:T(8,128)(2,1)}) %all-gather.2.cloned.1.call-update) | async-done | bytes 5767184 | tf_op jit(solution)/shard_map/all_gather | solution.py:122
  104.9 7.3 %collective-permute-start.3 = (bf16[1024,2816]{1,0:T(8,128)(2,1)}, bf16[1024,2816]{1,0:T(8,128)(2,1)}, u32[]{:S(2)}, u32[]{:S(2)}) collective-permute-start(bf16[1024,2816]{1,0:T(8,128)(2,1)} %all-gather.2.cloned.1.call-done), channel_id=1, source_target_pairs={{0,4},{4,0},{1,5},{5,1},{2,6},{6,2},{3,7},{7,3},{8,12},{12,8},{9,1... | collective-permute-start | bytes 17301512 | tf_op jit(solution)/shard_map/ppermute | solution.py:126
  114.5 7.0 %collective-permute-done.3 = bf16[1024,2816]{1,0:T(8,128)(2,1)} collective-permute-done((bf16[1024,2816]{1,0:T(8,128)(2,1)}, bf16[1024,2816]{1,0:T(8,128)(2,1)}, u32[]{:S(2)}, u32[]{:S(2)}) %collective-permute-start.3) | collective-permute-done | bytes 5767200 | tf_op jit(solution)/shard_map/ppermute | solution.py:126
  121.6 1.7 fusion.26
  123.2 3.5 %collective-permute-start.4 = (bf16[256,512]{1,0:T(8,128)(2,1)S(1)}, bf16[256,512]{1,0:T(8,128)(2,1)S(1)}, u32[]{:S(2)}, u32[]{:S(2)}) collective-permute-start(bf16[256,512]{1,0:T(8,128)(2,1)S(1)} %fusion.26), channel_id=1, source_target_pairs={{0,1},{1,2},{2,3},{3,0},{4,5},{5,6},{6,7},{7,4},{8,9},{9,10},{10,1... | collective-permute-start | bytes 786440 | tf_op jit(solution)/shard_map/ppermute | solution.py:77
  126.8 4.5 %collective-permute-start.5 = (bf16[256,512]{1,0:T(8,128)(2,1)S(1)}, bf16[256,512]{1,0:T(8,128)(2,1)S(1)}, u32[]{:S(2)}, u32[]{:S(2)}) collective-permute-start(bf16[256,512]{1,0:T(8,128)(2,1)S(1)} %fusion.26), channel_id=1, source_target_pairs={{0,2},{1,3},{2,0},{3,1},{4,6},{5,7},{6,4},{7,5},{8,10},{9,11},{10,... | collective-permute-start | bytes 786440 | tf_op jit(solution)/shard_map/ppermute | solution.py:77
  131.3 3.1 %collective-permute-start.6 = (bf16[256,512]{1,0:T(8,128)(2,1)S(1)}, bf16[256,512]{1,0:T(8,128)(2,1)S(1)}, u32[]{:S(2)}, u32[]{:S(2)}) collective-permute-start(bf16[256,512]{1,0:T(8,128)(2,1)S(1)} %fusion.26), channel_id=1, source_target_pairs={{0,3},{1,0},{2,1},{3,2},{4,7},{5,4},{6,5},{7,6},{8,11},{9,8},{10,9... | collective-permute-start | bytes 786440 | tf_op jit(solution)/shard_map/ppermute | solution.py:77
  134.6 6.4 %collective-permute-done.5 = bf16[256,512]{1,0:T(8,128)(2,1)S(1)} collective-permute-done((bf16[256,512]{1,0:T(8,128)(2,1)S(1)}, bf16[256,512]{1,0:T(8,128)(2,1)S(1)}, u32[]{:S(2)}, u32[]{:S(2)}) %collective-permute-start.5) | collective-permute-done | bytes 262176 | tf_op jit(solution)/shard_map/ppermute | solution.py:77
  143.4 1.8 gather_fusion.2
  147.4 2.9 %fusion.4 = f32[256,1536]{1,0:T(8,128)S(1)} fusion(bf16[1024,2816]{1,0:T(8,128)(2,1)} %all-gather.2.cloned.1.call-done, bf16[256,2048]{0,1:T(8,128)(2,1)S(1)} %bitcast.95), kind=kOutput, calls=%fused_computation.7 | convolution fusion | flops 805306368 | bytes 5242880 | tf_op jit(solution)/shard_map/dot_general | solution.py:133
  150.3 2.9 %fusion.6 = f32[256,1536]{1,0:T(8,128)S(1)} fusion(f32[256,1536]{1,0:T(8,128)S(1)} %fusion.4, bf16[1024,2816]{1,0:T(8,128)(2,1)} %collective-permute-done.3, bf16[256,2048]{0,1:T(8,128)(2,1)S(1)} %bitcast.96), kind=kOutput, calls=%fused_computation.9 | convolution fusion | flops 805699584 | bytes 6815744 | tf_op jit(solution)/shard_map/dot_general | solution.py:133
  154.2 2.0 %fusion.15 = bf16[256,1024]{1,0:T(8,128)(2,1)S(1)} fusion(bf16[256,768]{1,0:T(8,128)(2,1)S(1)} %fusion.41, bf16[1024,2816]{1,0:T(8,128)(2,1)} %all-gather.2.cloned.1.call-done), kind=kOutput, calls=%fused_computation.29 | convolution fusion | flops 402915328 | bytes 2490368 | tf_op jit(solution)/shard_map/dot_general | solution.py:92
  156.4 2.1 %fusion.18 = bf16[256,1024]{1,0:T(8,128)(2,1)S(1)} fusion(bf16[256,768]{1,0:T(8,128)(2,1)} %copy-done.3, bf16[1024,2816]{1,0:T(8,128)(2,1)} %collective-permute-done.3), kind=kOutput, calls=%fused_computation.30 | convolution fusion | flops 402915328 | bytes 2490368 | tf_op jit(solution)/shard_map/dot_general | solution.py:92
  159.7 4.8 %collective-permute-start.7 = (bf16[256,512]{1,0:T(8,128)(2,1)}, bf16[256,512]{1,0:T(8,128)(2,1)}, u32[]{:S(2)}, u32[]{:S(2)}) collective-permute-start(bf16[256,512]{1,0:T(8,128)(2,1)} %copy.63), channel_id=1, source_target_pairs={{0,1},{1,2},{2,3},{3,0},{4,5},{5,6},{6,7},{7,4},{8,9},{9,10},{10,1... | collective-permute-start | bytes 786440 | tf_op jit(solution)/shard_map/ppermute | solution.py:107
  165.4 3.2 %collective-permute-start.8 = (bf16[256,512]{1,0:T(8,128)(2,1)}, bf16[256,512]{1,0:T(8,128)(2,1)S(1)}, u32[]{:S(2)}, u32[]{:S(2)}) collective-permute-start(bf16[256,512]{1,0:T(8,128)(2,1)} %copy.65), channel_id=1, source_target_pairs={{0,2},{1,3},{2,0},{3,1},{4,6},{5,7},{6,4},{7,5},{8,10},{9,11},{10,... | collective-permute-start | bytes 786440 | tf_op jit(solution)/shard_map/ppermute | solution.py:107
  169.5 3.0 %collective-permute-start.9 = (bf16[256,512]{1,0:T(8,128)(2,1)}, bf16[256,512]{1,0:T(8,128)(2,1)S(1)}, u32[]{:S(2)}, u32[]{:S(2)}) collective-permute-start(bf16[256,512]{1,0:T(8,128)(2,1)} %copy.66), channel_id=1, source_target_pairs={{0,3},{1,0},{2,1},{3,2},{4,7},{5,4},{6,5},{7,6},{8,11},{9,8},{10,9... | collective-permute-start | bytes 786440 | tf_op jit(solution)/shard_map/ppermute | solution.py:107
  172.7 4.7 %collective-permute-done.8 = bf16[256,512]{1,0:T(8,128)(2,1)S(1)} collective-permute-done((bf16[256,512]{1,0:T(8,128)(2,1)}, bf16[256,512]{1,0:T(8,128)(2,1)S(1)}, u32[]{:S(2)}, u32[]{:S(2)}) %collective-permute-start.8) | collective-permute-done | bytes 262176 | tf_op jit(solution)/shard_map/ppermute | solution.py:107
  177.5 2.4 %collective-permute-done.9 = bf16[256,512]{1,0:T(8,128)(2,1)S(1)} collective-permute-done((bf16[256,512]{1,0:T(8,128)(2,1)}, bf16[256,512]{1,0:T(8,128)(2,1)S(1)}, u32[]{:S(2)}, u32[]{:S(2)}) %collective-permute-start.9) | collective-permute-done | bytes 262176 | tf_op jit(solution)/shard_map/ppermute | solution.py:107
  179.9 1.8 add_convert_fusion
  (76 shorter events, 20.8 us)
Async XLA Ops:
  6.5 13.1 %copy-start = (bf16[6,128,2,512]{3,2,1,0:T(2,128)(2,1)S(1)}, bf16[6,128,2,512]{3,2,1,0:T(2,128)(2,1)}, u32[]{:S(2)}) copy-start(bf16[6,128,2,512]{3,2,1,0:T(2,128)(2,1)} %param.18) | copy-start | bytes 4718596
  6.5 98.3 %all-gather.2.cloned.1.call-start = ((), (), s32[]{:S(2)}) async-start(), calls=%async_computation | async-start | bytes 6127616 | tf_op jit(solution)/shard_map/all_gather | solution.py:122
  25.2 1.8 copy-start.2
  25.2 3.3 %copy-start.5 = (f32[4,128]{1,0:T(4,128)S(1)}, f32[4,128]{1,0:T(4,128)}, u32[]{:S(2)}) copy-start(f32[4,128]{1,0:T(4,128)} %param.22) | copy-start | bytes 6148
  25.2 5.3 %copy-start.8 = (s32[128]{0:T(128)S(1)}, s32[128]{0:T(128)}, u32[]{:S(2)}) copy-start(s32[128]{0:T(128)} %param.21) | copy-start | bytes 1540
  25.2 6.8 %copy-start.9 = (s32[1,6]{1,0:T(1,128)S(1)}, s32[1,6]{1,0:T(1,128)}, u32[]{:S(2)}) copy-start(s32[1,6]{1,0:T(1,128)} %param.19) | copy-start | bytes 76
  35.6 2.3 %copy-start.1 = (bf16[768,2,512]{2,0,1:T(8,128)(2,1)S(1)}, bf16[768,2,512]{2,0,1:T(8,128)(2,1)}, u32[]{:S(2)}) copy-start(bf16[768,2,512]{2,0,1:T(8,128)(2,1)} %bitcast_select_fusion.4) | copy-start | bytes 4718596
  43.1 3.4 %copy-start.6 = (f32[256]{0:T(256)S(1)}, f32[256]{0:T(256)}, u32[]{:S(2)}) copy-start(f32[256]{0:T(256)} %param.23) | copy-start | bytes 3076
  47.6 11.5 %collective-permute-start = (bf16[256,512]{0,1:T(8,128)(2,1)S(1)}, bf16[256,512]{0,1:T(8,128)(2,1)S(1)}, u32[]{:S(2)}, u32[]{:S(2)}) collective-permute-start(bf16[256,512]{0,1:T(8,128)(2,1)S(1)} %bitcast.105), channel_id=1, source_target_pairs={{0,1},{1,2},{2,3},{3,0},{4,5},{5,6},{6,7},{7,4},{8,9},{9,10},{10,1... | collective-permute-start | bytes 786440 | tf_op jit(solution)/shard_map/ppermute | solution.py:77
  51.5 11.4 %collective-permute-start.1 = (bf16[256,512]{0,1:T(8,128)(2,1)S(1)}, bf16[256,512]{0,1:T(8,128)(2,1)S(1)}, u32[]{:S(2)}, u32[]{:S(2)}) collective-permute-start(bf16[256,512]{0,1:T(8,128)(2,1)S(1)} %bitcast.106), channel_id=1, source_target_pairs={{0,2},{1,3},{2,0},{3,1},{4,6},{5,7},{6,4},{7,5},{8,10},{9,11},{10,... | collective-permute-start | bytes 786440 | tf_op jit(solution)/shard_map/ppermute | solution.py:77
  56.1 7.5 %collective-permute-start.2 = (bf16[256,512]{0,1:T(8,128)(2,1)S(1)}, bf16[256,512]{0,1:T(8,128)(2,1)S(1)}, u32[]{:S(2)}, u32[]{:S(2)}) collective-permute-start(bf16[256,512]{0,1:T(8,128)(2,1)S(1)} %bitcast.107), channel_id=1, source_target_pairs={{0,3},{1,0},{2,1},{3,2},{4,7},{5,4},{6,5},{7,6},{8,11},{9,8},{10,9... | collective-permute-start | bytes 786440 | tf_op jit(solution)/shard_map/ppermute | solution.py:77
  104.9 16.7 %collective-permute-start.3 = (bf16[1024,2816]{1,0:T(8,128)(2,1)}, bf16[1024,2816]{1,0:T(8,128)(2,1)}, u32[]{:S(2)}, u32[]{:S(2)}) collective-permute-start(bf16[1024,2816]{1,0:T(8,128)(2,1)} %all-gather.2.cloned.1.call-done), channel_id=1, source_target_pairs={{0,4},{4,0},{1,5},{5,1},{2,6},{6,2},{3,7},{7,3},{8,12},{12,8},{9,1... | collective-permute-start | bytes 17301512 | tf_op jit(solution)/shard_map/ppermute | solution.py:126
  112.7 8.9 %copy-start.7 = (bf16[256,512]{1,0:T(8,128)(2,1)S(1)}, bf16[256,512]{1,0:T(8,128)(2,1)}, u32[]{:S(2)}) copy-start(bf16[256,512]{1,0:T(8,128)(2,1)} %param.24) | copy-start | bytes 786436
  114.5 19.9 %copy-start.4 = (f32[2048]{0:T(1024)S(1)}, f32[2048]{0:T(1024)}, u32[]{:S(2)}) copy-start(f32[2048]{0:T(1024)} %param.26) | copy-start | bytes 24580
  123.2 11.3 %collective-permute-start.4 = (bf16[256,512]{1,0:T(8,128)(2,1)S(1)}, bf16[256,512]{1,0:T(8,128)(2,1)S(1)}, u32[]{:S(2)}, u32[]{:S(2)}) collective-permute-start(bf16[256,512]{1,0:T(8,128)(2,1)S(1)} %fusion.26), channel_id=1, source_target_pairs={{0,1},{1,2},{2,3},{3,0},{4,5},{5,6},{6,7},{7,4},{8,9},{9,10},{10,1... | collective-permute-start | bytes 786440 | tf_op jit(solution)/shard_map/ppermute | solution.py:77
  126.8 14.2 %collective-permute-start.5 = (bf16[256,512]{1,0:T(8,128)(2,1)S(1)}, bf16[256,512]{1,0:T(8,128)(2,1)S(1)}, u32[]{:S(2)}, u32[]{:S(2)}) collective-permute-start(bf16[256,512]{1,0:T(8,128)(2,1)S(1)} %fusion.26), channel_id=1, source_target_pairs={{0,2},{1,3},{2,0},{3,1},{4,6},{5,7},{6,4},{7,5},{8,10},{9,11},{10,... | collective-permute-start | bytes 786440 | tf_op jit(solution)/shard_map/ppermute | solution.py:77
  131.3 11.1 %collective-permute-start.6 = (bf16[256,512]{1,0:T(8,128)(2,1)S(1)}, bf16[256,512]{1,0:T(8,128)(2,1)S(1)}, u32[]{:S(2)}, u32[]{:S(2)}) collective-permute-start(bf16[256,512]{1,0:T(8,128)(2,1)S(1)} %fusion.26), channel_id=1, source_target_pairs={{0,3},{1,0},{2,1},{3,2},{4,7},{5,4},{6,5},{7,6},{8,11},{9,8},{10,9... | collective-permute-start | bytes 786440 | tf_op jit(solution)/shard_map/ppermute | solution.py:77
  153.4 0.8 copy-start.3
  159.7 13.0 %collective-permute-start.7 = (bf16[256,512]{1,0:T(8,128)(2,1)}, bf16[256,512]{1,0:T(8,128)(2,1)}, u32[]{:S(2)}, u32[]{:S(2)}) collective-permute-start(bf16[256,512]{1,0:T(8,128)(2,1)} %copy.63), channel_id=1, source_target_pairs={{0,1},{1,2},{2,3},{3,0},{4,5},{5,6},{6,7},{7,4},{8,9},{9,10},{10,1... | collective-permute-start | bytes 786440 | tf_op jit(solution)/shard_map/ppermute | solution.py:107
  165.4 12.1 %collective-permute-start.8 = (bf16[256,512]{1,0:T(8,128)(2,1)}, bf16[256,512]{1,0:T(8,128)(2,1)S(1)}, u32[]{:S(2)}, u32[]{:S(2)}) collective-permute-start(bf16[256,512]{1,0:T(8,128)(2,1)} %copy.65), channel_id=1, source_target_pairs={{0,2},{1,3},{2,0},{3,1},{4,6},{5,7},{6,4},{7,5},{8,10},{9,11},{10,... | collective-permute-start | bytes 786440 | tf_op jit(solution)/shard_map/ppermute | solution.py:107
  169.5 10.4 %collective-permute-start.9 = (bf16[256,512]{1,0:T(8,128)(2,1)}, bf16[256,512]{1,0:T(8,128)(2,1)S(1)}, u32[]{:S(2)}, u32[]{:S(2)}) collective-permute-start(bf16[256,512]{1,0:T(8,128)(2,1)} %copy.66), channel_id=1, source_target_pairs={{0,3},{1,0},{2,1},{3,2},{4,7},{5,4},{6,5},{7,6},{8,11},{9,8},{10,9... | collective-permute-start | bytes 786440 | tf_op jit(solution)/shard_map/ppermute | solution.py:107
Sparse Core Ops, SparseCore 0:
  19.1 85.7 all-gather.1

commit v15 on v14

--- a/solution.py
+++ b/solution.py
@@ -76,10 +76,10 @@
         pieces.append(
             lax.ppermute(block, "mlp", [(i, (i + shift) % axis_size) for i in range(axis_size)])
         )
-    stacked = jnp.stack(pieces, axis=0)
-    source_of = (index - jnp.arange(axis_size, dtype=jnp.int32)) % axis_size
-    gathered = jnp.take(stacked, source_of, axis=0)
-    return jnp.concatenate([gathered[k] for k in range(axis_size)], axis=1)
+    ring = jnp.concatenate(pieces[::-1] + pieces[::-1], axis=1)
+    width = block.shape[1]
+    start = ((axis_size - 1 - index) % axis_size) * width
+    return lax.dynamic_slice_in_dim(ring, start, axis_size * width, 1)
 
 
 def down_and_scatter(hidden_act, down_halves, axis_size, rows):

time: 190 us -> 191 us (level)
  waiting for transfers between devices: 64.4 us -> 75.1 us
  starting transfers between devices: 40.7 us -> 35.8 us
  local copies, waits for them, and re-layouts: 18.8 us -> 16.1 us
    ppermute x6, waiting for transfers between devices: 12.2 us -> 18.6 us  [mlp_gather(): lax.ppermute(block, 'mlp', [(i, (i + shift) % axis_size) for i in range(a...]
    gather x2 -> x0, local copies, waits for them, and re-layouts: 3.67 us -> none  [mlp_gather(): gathered = jnp.take(stacked, source_of, axis=0)]
    ppermute x3, starting transfers between devices: 11 us -> 8.38 us  [down_and_scatter(): lax.ppermute(block_for(target), 'mlp', [(i, (i + shift) % axis_size) for...]
    ppermute x6, starting transfers between devices: 22.5 us -> 20.1 us  [mlp_gather(): lax.ppermute(block, 'mlp', [(i, (i + shift) % axis_size) for i in range(a...]
    another operation x2 -> x0, other arithmetic: 2.23 us -> none  [mlp_gather(): stacked = jnp.stack(pieces, axis=0)]
    all_gather x1, waiting for transfers between devices: 38 us -> 40.2 us  [gather_over_xz(): return lax.all_gather(out, 'z', axis=0, tiled=True)]
    ppermute x3, waiting for transfers between devices: 7.14 us -> 9.2 us  [down_and_scatter(): lax.ppermute(block_for(target), 'mlp', [(i, (i + shift) % axis_size) for...]
  transfers between devices with their start and end apart: 11 -> 11, of which waited for: 8 -> 8; matrix products, arithmetic and copies ran while one was open for 18% -> 16% of each run, Pallas kernels for 0% -> 0%
where the time goes in v15:
time: 191 us; the launch traced here: 190 us
  waiting for transfers between devices  75.1 us (39%)
  starting transfers between devices  35.8 us (19%)
  matrix products  24.1 us (13%)
  local copies, waits for them, and re-layouts  16.1 us (8%)
  between operations  16 us (8%)
  blocking collectives  11.5 us (6%)
  other arithmetic  11.3 us (6%)
    all_gather x1, waiting for transfers between devices, gather_over_xz(): return lax.all_gather(out, 'z', axis=0, tiled=True)  40.2 us
    ppermute x6, starting transfers between devices, mlp_gather(): lax.ppermute(block, 'mlp', [(i, (i + shift) % axis_size) for i in range(a...  20.1 us
    ppermute x6, waiting for transfers between devices, mlp_gather(): lax.ppermute(block, 'mlp', [(i, (i + shift) % axis_size) for i in range(a...  18.6 us
    all_gather x1, blocking collectives, gather_over_xz(): out = lax.all_gather(block, 'x', axis=0, tiled=True)  11.5 us
    ppermute x3, waiting for transfers between devices, down_and_scatter(): lax.ppermute(block_for(target), 'mlp', [(i, (i + shift) % axis_size) for...  9.2 us
    dot_general x4, matrix products, split_dot(): jnp.dot(act[:, j * size:(j + 1) * size], half, preferred_element_type=jnp...  9.13 us
    ppermute x3, starting transfers between devices, down_and_scatter(): lax.ppermute(block_for(target), 'mlp', [(i, (i + shift) % axis_size) for...  8.38 us
    ppermute x1, starting transfers between devices, swap_with_core(): return [rows_xz, lax.ppermute(rows_xz, 'c', [(0, 1), (1, 0)])]  7.35 us
  transfers between devices with their start and end apart: 11, of which 8 were waited for; matrix products, arithmetic and copies ran while one was open for 16% of the time, Pallas kernels for 0%

profile of v15, /device:TPU:1, one launch (start us, length us, event | category | flops | bytes accessed | tf_op | source)
XLA Modules:
  0.0 189.9 jit_solution(10626357677645802815)
XLA Ops:
  7.4 11.5 %all_gather.6 = bf16[64,2816]{1,0:T(8,128)(2,1)} all-gather(bf16[16,2816]{1,0:T(8,128)(2,1)S(1)} %pad_maximum_fusion.16), channel_id=1, replica_groups=mesh['x'=4,'z'=16,'c'=2,'mlp'=4] {'x'}, dimensions={0}, use_global_device_ids=true | all-gather | bytes 450560 | tf_op jit(solution)/shard_map/all_gather | solution.py:121
  19.6 5.6 %gather_fusion = bf16[6,128,2,512]{3,2,1,0:T(2,128)(2,1)} fusion(bf16[6,128,2,512]{3,2,1,0:T(2,128)(2,1)S(1)} %copy-done, s32[1024]{0:T(1024)S(1)} %pad_clamp_fusion), kind=kCustom, calls=%fused_computation | custom fusion | bytes 3145752 | tf_op jit(solution)/shard_map/jit(_take)/gather | solution.py:23
  25.2 1.7 copy.42
  32.3 1.8 fusion.112
  35.6 2.3 %fusion.113 = f32[256,2]{0,1:T(2,128)S(1)} fusion(pred[256,1024]{0,1:T(8,128)(4,1)S(1)} %pad_add_fusion, bf16[768,2,512]{2,0,1:T(8,128)(2,1)} %bitcast_select_fusion.4, bf16[256,2,512]{2,0,1:T(8,128)(2,1)} %copy.43, bf16[256,2,128]{2,1,0:T(2,128)(2,1)} %get-tuple-element.20), kind=kOutput, calls=%fused_computation.140 | convolution fusion | flops 137888768 | bytes 2754560 | tf_op jit(solution)/shard_map/sub | solution.py:45
  37.9 3.2 %fusion.24 = f32[256,2,256]{0,2,1:T(8,128)} fusion(f32[256,2]{0,1:T(2,128)S(1)} %fusion.113, pred[256,1024]{0,1:T(8,128)(4,1)S(1)} %pad_add_fusion, bf16[768,2,512]{2,0,1:T(8,128)(2,1)S(1)} %copy-done.1, bf16[256,2,512]{2,0,1:T(8,128)(2,1)} %copy.43, bf16[256,2,128]{2,1,0:T(2,128)(2,1)} %get-tuple-element.20), kind=kOutput, calls=%fused_computation.35 | convolution fusion | flops 408552960 | bytes 5376000 | tf_op jit(solution)/shard_map/nhk,khd->nhd/dot_general | solution.py:47
  41.1 2.0 %fusion.118 = f32[256,2]{0,1:T(2,128)S(1)} fusion(pred[256,1024]{0,1:T(8,128)(4,1)S(1)} %pad_add_fusion, bf16[256,2,512]{2,0,1:T(8,128)(2,1)} %copy.43, bf16[768,2,512]{2,0,1:T(8,128)(2,1)S(1)} %copy-done.1, bf16[256,2,128]{2,1,0:T(2,128)(2,1)S(1)} %get-tuple-element.19), kind=kOutput, calls=%fused_computation.141 | convolution fusion | flops 137888768 | bytes 2492416 | tf_op jit(solution)/shard_map/sub | solution.py:45
  43.1 3.4 %multiply_reduce_fusion = (f32[256,2]{0,1:T(2,128)S(1)}, f32[256,2,256]{0,2,1:T(8,128)}) fusion(f32[256,2,256]{0,2,1:T(8,128)} %fusion.24, f32[256,2]{0,1:T(2,128)S(1)} %fusion.118, pred[256,1024]{0,1:T(8,128)(4,1)S(1)} %pad_add_fusion, bf16[256,2,512]{2,0,1:T(8,128)(2,1)} %copy.43, bf16[768,2,512]{2,0,1:T(8,128)(2,1)S(1)} %copy-done.1, ...), kind=kOutput, calls=%fused_computation.69 | convolution fusion | flops 409076736 | bytes 5902340 | tf_op jit(solution)/shard_map/nhk,khd->nhd/dot_general | solution.py:47
  47.6 5.3 %collective-permute-start = (bf16[256,512]{0,1:T(8,128)(2,1)S(1)}, bf16[256,512]{0,1:T(8,128)(2,1)S(1)}, u32[]{:S(2)}, u32[]{:S(2)}) collective-permute-start(bf16[256,512]{0,1:T(8,128)(2,1)S(1)} %bitcast.69), channel_id=1, source_target_pairs={{0,3},{1,0},{2,1},{3,2},{4,7},{5,4},{6,5},{7,6},{8,11},{9,8},{10,9... | collective-permute-start | bytes 786440 | tf_op jit(solution)/shard_map/ppermute | solution.py:77
  53.0 2.3 %collective-permute-start.1 = (bf16[256,512]{0,1:T(8,128)(2,1)S(1)}, bf16[256,512]{0,1:T(8,128)(2,1)S(1)}, u32[]{:S(2)}, u32[]{:S(2)}) collective-permute-start(bf16[256,512]{0,1:T(8,128)(2,1)S(1)} %bitcast.70), channel_id=1, source_target_pairs={{0,2},{1,3},{2,0},{3,1},{4,6},{5,7},{6,4},{7,5},{8,10},{9,11},{10,... | collective-permute-start | bytes 786440 | tf_op jit(solution)/shard_map/ppermute | solution.py:77
  55.2 2.6 %collective-permute-start.2 = (bf16[256,512]{0,1:T(8,128)(2,1)S(1)}, bf16[256,512]{0,1:T(8,128)(2,1)S(1)}, u32[]{:S(2)}, u32[]{:S(2)}) collective-permute-start(bf16[256,512]{0,1:T(8,128)(2,1)S(1)} %bitcast.71), channel_id=1, source_target_pairs={{0,1},{1,2},{2,3},{3,0},{4,5},{5,6},{6,7},{7,4},{8,9},{9,10},{10,1... | collective-permute-start | bytes 786440 | tf_op jit(solution)/shard_map/ppermute | solution.py:77
  57.9 3.8 %collective-permute-done.1 = bf16[256,512]{0,1:T(8,128)(2,1)S(1)} collective-permute-done((bf16[256,512]{0,1:T(8,128)(2,1)S(1)}, bf16[256,512]{0,1:T(8,128)(2,1)S(1)}, u32[]{:S(2)}, u32[]{:S(2)}) %collective-permute-start.1) | collective-permute-done | bytes 262176 | tf_op jit(solution)/shard_map/ppermute | solution.py:77
  61.7 2.7 %collective-permute-done.2 = bf16[256,512]{0,1:T(8,128)(2,1)S(1)} collective-permute-done((bf16[256,512]{0,1:T(8,128)(2,1)S(1)}, bf16[256,512]{0,1:T(8,128)(2,1)S(1)}, u32[]{:S(2)}, u32[]{:S(2)}) %collective-permute-start.2) | collective-permute-done | bytes 262176 | tf_op jit(solution)/shard_map/ppermute | solution.py:77
  64.6 40.2 %all-gather.2.cloned.1.call-done = bf16[1024,2816]{1,0:T(8,128)(2,1)} async-done(((bf16[64,2816]{1,0:T(8,128)(2,1)}), bf16[1024,2816]{1,0:T(8,128)(2,1)}) %all-gather.2.cloned.1.call-update) | async-done | bytes 5767184 | tf_op jit(solution)/shard_map/all_gather | solution.py:122
  104.8 7.3 %collective-permute-start.3 = (bf16[1024,2816]{1,0:T(8,128)(2,1)}, bf16[1024,2816]{1,0:T(8,128)(2,1)}, u32[]{:S(2)}, u32[]{:S(2)}) collective-permute-start(bf16[1024,2816]{1,0:T(8,128)(2,1)} %all-gather.2.cloned.1.call-done), channel_id=1, source_target_pairs={{0,4},{4,0},{1,5},{5,1},{2,6},{6,2},{3,7},{7,3},{8,12},{12,8},{9,1... | collective-permute-start | bytes 17301512 | tf_op jit(solution)/shard_map/ppermute | solution.py:126
  114.5 7.1 %collective-permute-done.3 = bf16[1024,2816]{1,0:T(8,128)(2,1)} collective-permute-done((bf16[1024,2816]{1,0:T(8,128)(2,1)}, bf16[1024,2816]{1,0:T(8,128)(2,1)}, u32[]{:S(2)}, u32[]{:S(2)}) %collective-permute-start.3) | collective-permute-done | bytes 5767200 | tf_op jit(solution)/shard_map/ppermute | solution.py:126
  121.5 1.7 fusion.29
  123.2 4.9 %collective-permute-start.4 = (bf16[256,512]{1,0:T(8,128)(2,1)S(1)}, bf16[256,512]{1,0:T(8,128)(2,1)S(1)}, u32[]{:S(2)}, u32[]{:S(2)}) collective-permute-start(bf16[256,512]{1,0:T(8,128)(2,1)S(1)} %fusion.29), channel_id=1, source_target_pairs={{0,3},{1,0},{2,1},{3,2},{4,7},{5,4},{6,5},{7,6},{8,11},{9,8},{10,9... | collective-permute-start | bytes 786440 | tf_op jit(solution)/shard_map/ppermute | solution.py:77
  128.2 2.4 %collective-permute-start.5 = (bf16[256,512]{1,0:T(8,128)(2,1)S(1)}, bf16[256,512]{1,0:T(8,128)(2,1)S(1)}, u32[]{:S(2)}, u32[]{:S(2)}) collective-permute-start(bf16[256,512]{1,0:T(8,128)(2,1)S(1)} %fusion.29), channel_id=1, source_target_pairs={{0,2},{1,3},{2,0},{3,1},{4,6},{5,7},{6,4},{7,5},{8,10},{9,11},{10,... | collective-permute-start | bytes 786440 | tf_op jit(solution)/shard_map/ppermute | solution.py:77
  130.5 2.6 %collective-permute-start.6 = (bf16[256,512]{1,0:T(8,128)(2,1)S(1)}, bf16[256,512]{1,0:T(8,128)(2,1)S(1)}, u32[]{:S(2)}, u32[]{:S(2)}) collective-permute-start(bf16[256,512]{1,0:T(8,128)(2,1)S(1)} %fusion.29), channel_id=1, source_target_pairs={{0,1},{1,2},{2,3},{3,0},{4,5},{5,6},{6,7},{7,4},{8,9},{9,10},{10,1... | collective-permute-start | bytes 786440 | tf_op jit(solution)/shard_map/ppermute | solution.py:77
  133.2 5.8 %collective-permute-done.4 = bf16[256,512]{1,0:T(8,128)(2,1)S(1)} collective-permute-done((bf16[256,512]{1,0:T(8,128)(2,1)S(1)}, bf16[256,512]{1,0:T(8,128)(2,1)S(1)}, u32[]{:S(2)}, u32[]{:S(2)}) %collective-permute-start.4) | collective-permute-done | bytes 262176 | tf_op jit(solution)/shard_map/ppermute | solution.py:77
  139.0 6.4 %collective-permute-done.6 = bf16[256,512]{1,0:T(8,128)(2,1)S(1)} collective-permute-done((bf16[256,512]{1,0:T(8,128)(2,1)S(1)}, bf16[256,512]{1,0:T(8,128)(2,1)S(1)}, u32[]{:S(2)}, u32[]{:S(2)}) %collective-permute-start.6) | collective-permute-done | bytes 262176 | tf_op jit(solution)/shard_map/ppermute | solution.py:77
  149.3 2.9 %fusion.4 = f32[256,1536]{1,0:T(8,128)S(1)} fusion(bf16[1024,2816]{1,0:T(8,128)(2,1)} %all-gather.2.cloned.1.call-done, bf16[256,2048]{0,1:T(8,128)(2,1)S(1)} %bitcast.74), kind=kOutput, calls=%fused_computation.5 | convolution fusion | flops 805306368 | bytes 5242880 | tf_op jit(solution)/shard_map/dot_general | solution.py:133
  152.2 2.9 %fusion.6 = f32[256,1536]{1,0:T(8,128)S(1)} fusion(f32[256,1536]{1,0:T(8,128)S(1)} %fusion.4, bf16[1024,2816]{1,0:T(8,128)(2,1)} %collective-permute-done.3, bf16[256,2048]{0,1:T(8,128)(2,1)S(1)} %bitcast.75), kind=kOutput, calls=%fused_computation.7 | convolution fusion | flops 805699584 | bytes 6815744 | tf_op jit(solution)/shard_map/dot_general | solution.py:133
  156.1 2.0 %fusion.18 = bf16[256,1024]{1,0:T(8,128)(2,1)S(1)} fusion(bf16[256,768]{1,0:T(8,128)(2,1)S(1)} %fusion.44, bf16[1024,2816]{1,0:T(8,128)(2,1)} %all-gather.2.cloned.1.call-done), kind=kOutput, calls=%fused_computation.30 | convolution fusion | flops 402915328 | bytes 2490368 | tf_op jit(solution)/shard_map/dot_general | solution.py:92
  158.3 2.1 %fusion.21 = bf16[256,1024]{1,0:T(8,128)(2,1)S(1)} fusion(bf16[256,768]{1,0:T(8,128)(2,1)} %copy-done.3, bf16[1024,2816]{1,0:T(8,128)(2,1)} %collective-permute-done.3), kind=kOutput, calls=%fused_computation.31 | convolution fusion | flops 402915328 | bytes 2490368 | tf_op jit(solution)/shard_map/dot_general | solution.py:92
  161.6 1.9 %collective-permute-start.7 = (bf16[256,512]{1,0:T(8,128)(2,1)}, bf16[256,512]{1,0:T(8,128)(2,1)}, u32[]{:S(2)}, u32[]{:S(2)}) collective-permute-start(bf16[256,512]{1,0:T(8,128)(2,1)} %copy.55), channel_id=1, source_target_pairs={{0,1},{1,2},{2,3},{3,0},{4,5},{5,6},{6,7},{7,4},{8,9},{9,10},{10,1... | collective-permute-start | bytes 786440 | tf_op jit(solution)/shard_map/ppermute | solution.py:107
  164.4 2.4 %collective-permute-start.8 = (bf16[256,512]{1,0:T(8,128)(2,1)}, bf16[256,512]{1,0:T(8,128)(2,1)S(1)}, u32[]{:S(2)}, u32[]{:S(2)}) collective-permute-start(bf16[256,512]{1,0:T(8,128)(2,1)} %copy.57), channel_id=1, source_target_pairs={{0,2},{1,3},{2,0},{3,1},{4,6},{5,7},{6,4},{7,5},{8,10},{9,11},{10,... | collective-permute-start | bytes 786440 | tf_op jit(solution)/shard_map/ppermute | solution.py:107
  167.7 4.1 %collective-permute-start.9 = (bf16[256,512]{1,0:T(8,128)(2,1)}, bf16[256,512]{1,0:T(8,128)(2,1)S(1)}, u32[]{:S(2)}, u32[]{:S(2)}) collective-permute-start(bf16[256,512]{1,0:T(8,128)(2,1)} %copy.58), channel_id=1, source_target_pairs={{0,3},{1,0},{2,1},{3,2},{4,7},{5,4},{6,5},{7,6},{8,11},{9,8},{10,9... | collective-permute-start | bytes 786440 | tf_op jit(solution)/shard_map/ppermute | solution.py:107
  172.0 6.0 %collective-permute-done.7 = bf16[256,512]{1,0:T(8,128)(2,1)} collective-permute-done((bf16[256,512]{1,0:T(8,128)(2,1)}, bf16[256,512]{1,0:T(8,128)(2,1)}, u32[]{:S(2)}, u32[]{:S(2)}) %collective-permute-start.7) | collective-permute-done | bytes 262176 | tf_op jit(solution)/shard_map/ppermute | solution.py:107
  178.0 3.2 %collective-permute-done.9 = bf16[256,512]{1,0:T(8,128)(2,1)S(1)} collective-permute-done((bf16[256,512]{1,0:T(8,128)(2,1)}, bf16[256,512]{1,0:T(8,128)(2,1)S(1)}, u32[]{:S(2)}, u32[]{:S(2)}) %collective-permute-start.9) | collective-permute-done | bytes 262176 | tf_op jit(solution)/shard_map/ppermute | solution.py:107
  181.2 1.8 add_convert_fusion
  (77 shorter events, 18.2 us)
Async XLA Ops:
  6.5 13.1 %copy-start = (bf16[6,128,2,512]{3,2,1,0:T(2,128)(2,1)S(1)}, bf16[6,128,2,512]{3,2,1,0:T(2,128)(2,1)}, u32[]{:S(2)}) copy-start(bf16[6,128,2,512]{3,2,1,0:T(2,128)(2,1)} %param.16) | copy-start | bytes 4718596
  6.5 98.3 %all-gather.2.cloned.1.call-start = ((), (), s32[]{:S(2)}) async-start(), calls=%async_computation | async-start | bytes 6127616 | tf_op jit(solution)/shard_map/all_gather | solution.py:122
  25.2 1.8 copy-start.2
  25.2 3.3 %copy-start.5 = (f32[4,128]{1,0:T(4,128)S(1)}, f32[4,128]{1,0:T(4,128)}, u32[]{:S(2)}) copy-start(f32[4,128]{1,0:T(4,128)} %param.20) | copy-start | bytes 6148
  25.2 5.3 %copy-start.8 = (s32[128]{0:T(128)S(1)}, s32[128]{0:T(128)}, u32[]{:S(2)}) copy-start(s32[128]{0:T(128)} %param.19) | copy-start | bytes 1540
  25.2 6.8 %copy-start.9 = (s32[1,6]{1,0:T(1,128)S(1)}, s32[1,6]{1,0:T(1,128)}, u32[]{:S(2)}) copy-start(s32[1,6]{1,0:T(1,128)} %param.17) | copy-start | bytes 76
  35.6 2.3 %copy-start.1 = (bf16[768,2,512]{2,0,1:T(8,128)(2,1)S(1)}, bf16[768,2,512]{2,0,1:T(8,128)(2,1)}, u32[]{:S(2)}) copy-start(bf16[768,2,512]{2,0,1:T(8,128)(2,1)} %bitcast_select_fusion.4) | copy-start | bytes 4718596
  43.1 3.4 %copy-start.6 = (f32[256]{0:T(256)S(1)}, f32[256]{0:T(256)}, u32[]{:S(2)}) copy-start(f32[256]{0:T(256)} %param.21) | copy-start | bytes 3076
  47.6 10.2 %collective-permute-start = (bf16[256,512]{0,1:T(8,128)(2,1)S(1)}, bf16[256,512]{0,1:T(8,128)(2,1)S(1)}, u32[]{:S(2)}, u32[]{:S(2)}) collective-permute-start(bf16[256,512]{0,1:T(8,128)(2,1)S(1)} %bitcast.69), channel_id=1, source_target_pairs={{0,3},{1,0},{2,1},{3,2},{4,7},{5,4},{6,5},{7,6},{8,11},{9,8},{10,9... | collective-permute-start | bytes 786440 | tf_op jit(solution)/shard_map/ppermute | solution.py:77
  53.0 8.7 %collective-permute-start.1 = (bf16[256,512]{0,1:T(8,128)(2,1)S(1)}, bf16[256,512]{0,1:T(8,128)(2,1)S(1)}, u32[]{:S(2)}, u32[]{:S(2)}) collective-permute-start(bf16[256,512]{0,1:T(8,128)(2,1)S(1)} %bitcast.70), channel_id=1, source_target_pairs={{0,2},{1,3},{2,0},{3,1},{4,6},{5,7},{6,4},{7,5},{8,10},{9,11},{10,... | collective-permute-start | bytes 786440 | tf_op jit(solution)/shard_map/ppermute | solution.py:77
  55.2 9.2 %collective-permute-start.2 = (bf16[256,512]{0,1:T(8,128)(2,1)S(1)}, bf16[256,512]{0,1:T(8,128)(2,1)S(1)}, u32[]{:S(2)}, u32[]{:S(2)}) collective-permute-start(bf16[256,512]{0,1:T(8,128)(2,1)S(1)} %bitcast.71), channel_id=1, source_target_pairs={{0,1},{1,2},{2,3},{3,0},{4,5},{5,6},{6,7},{7,4},{8,9},{9,10},{10,1... | collective-permute-start | bytes 786440 | tf_op jit(solution)/shard_map/ppermute | solution.py:77
  104.8 16.7 %collective-permute-start.3 = (bf16[1024,2816]{1,0:T(8,128)(2,1)}, bf16[1024,2816]{1,0:T(8,128)(2,1)}, u32[]{:S(2)}, u32[]{:S(2)}) collective-permute-start(bf16[1024,2816]{1,0:T(8,128)(2,1)} %all-gather.2.cloned.1.call-done), channel_id=1, source_target_pairs={{0,4},{4,0},{1,5},{5,1},{2,6},{6,2},{3,7},{7,3},{8,12},{12,8},{9,1... | collective-permute-start | bytes 17301512 | tf_op jit(solution)/shard_map/ppermute | solution.py:126
  112.6 8.9 %copy-start.7 = (bf16[256,512]{1,0:T(8,128)(2,1)S(1)}, bf16[256,512]{1,0:T(8,128)(2,1)}, u32[]{:S(2)}) copy-start(bf16[256,512]{1,0:T(8,128)(2,1)} %param.22) | copy-start | bytes 786436
  123.2 15.7 %collective-permute-start.4 = (bf16[256,512]{1,0:T(8,128)(2,1)S(1)}, bf16[256,512]{1,0:T(8,128)(2,1)S(1)}, u32[]{:S(2)}, u32[]{:S(2)}) collective-permute-start(bf16[256,512]{1,0:T(8,128)(2,1)S(1)} %fusion.29), channel_id=1, source_target_pairs={{0,3},{1,0},{2,1},{3,2},{4,7},{5,4},{6,5},{7,6},{8,11},{9,8},{10,9... | collective-permute-start | bytes 786440 | tf_op jit(solution)/shard_map/ppermute | solution.py:77
  128.2 10.8 %collective-permute-start.5 = (bf16[256,512]{1,0:T(8,128)(2,1)S(1)}, bf16[256,512]{1,0:T(8,128)(2,1)S(1)}, u32[]{:S(2)}, u32[]{:S(2)}) collective-permute-start(bf16[256,512]{1,0:T(8,128)(2,1)S(1)} %fusion.29), channel_id=1, source_target_pairs={{0,2},{1,3},{2,0},{3,1},{4,6},{5,7},{6,4},{7,5},{8,10},{9,11},{10,... | collective-permute-start | bytes 786440 | tf_op jit(solution)/shard_map/ppermute | solution.py:77
  130.5 14.9 %collective-permute-start.6 = (bf16[256,512]{1,0:T(8,128)(2,1)S(1)}, bf16[256,512]{1,0:T(8,128)(2,1)S(1)}, u32[]{:S(2)}, u32[]{:S(2)}) collective-permute-start(bf16[256,512]{1,0:T(8,128)(2,1)S(1)} %fusion.29), channel_id=1, source_target_pairs={{0,1},{1,2},{2,3},{3,0},{4,5},{5,6},{6,7},{7,4},{8,9},{9,10},{10,1... | collective-permute-start | bytes 786440 | tf_op jit(solution)/shard_map/ppermute | solution.py:77
  139.0 6.9 %copy-start.4 = (f32[2048]{0:T(1024)S(1)}, f32[2048]{0:T(1024)}, u32[]{:S(2)}) copy-start(f32[2048]{0:T(1024)} %param.24) | copy-start | bytes 24580
  155.3 0.8 copy-start.3
  161.6 16.4 %collective-permute-start.7 = (bf16[256,512]{1,0:T(8,128)(2,1)}, bf16[256,512]{1,0:T(8,128)(2,1)}, u32[]{:S(2)}, u32[]{:S(2)}) collective-permute-start(bf16[256,512]{1,0:T(8,128)(2,1)} %copy.55), channel_id=1, source_target_pairs={{0,1},{1,2},{2,3},{3,0},{4,5},{5,6},{6,7},{7,4},{8,9},{9,10},{10,1... | collective-permute-start | bytes 786440 | tf_op jit(solution)/shard_map/ppermute | solution.py:107
  164.4 13.6 %collective-permute-start.8 = (bf16[256,512]{1,0:T(8,128)(2,1)}, bf16[256,512]{1,0:T(8,128)(2,1)S(1)}, u32[]{:S(2)}, u32[]{:S(2)}) collective-permute-start(bf16[256,512]{1,0:T(8,128)(2,1)} %copy.57), channel_id=1, source_target_pairs={{0,2},{1,3},{2,0},{3,1},{4,6},{5,7},{6,4},{7,5},{8,10},{9,11},{10,... | collective-permute-start | bytes 786440 | tf_op jit(solution)/shard_map/ppermute | solution.py:107
  167.7 13.6 %collective-permute-start.9 = (bf16[256,512]{1,0:T(8,128)(2,1)}, bf16[256,512]{1,0:T(8,128)(2,1)S(1)}, u32[]{:S(2)}, u32[]{:S(2)}) collective-permute-start(bf16[256,512]{1,0:T(8,128)(2,1)} %copy.58), channel_id=1, source_target_pairs={{0,3},{1,0},{2,1},{3,2},{4,7},{5,4},{6,5},{7,6},{8,11},{9,8},{10,9... | collective-permute-start | bytes 786440 | tf_op jit(solution)/shard_map/ppermute | solution.py:107
Sparse Core Ops, SparseCore 0:
  19.1 85.7 all-gather.1
